TPU v7x, 32 devices: a whole 2x2x4 slice. The times are simulated.
32 devices in a mesh: group: 4 (over y, core), tile: 8 (over z, x).
Axes of the slice: x: 2, y: 2, z: 4, core: 2. Of those that a mesh axis runs over, the one named last changes fastest.
Arguments:
- maps: bfloat16 [32, 256, 128, 128], P('group', 'tile'), may hold values from -6 to 6
- first_weight: bfloat16 [3, 3, 128, 256], replicated, may hold values from -0.1875 to 0.1875
- second_weight: bfloat16 [3, 3, 256, 256], replicated, may hold values from -0.125 to 0.125
- out_grad: bfloat16 [32, 128, 64, 256], P(('group', 'tile')), may hold values from -0.0234375 to 0.0234375
Outputs:
- conv_out: bfloat16 [32, 128, 64, 256], P(('group', 'tile'))
- weight_grad: float32 [256, 3, 3, 256], P(('group', 'tile'))
All inputs are finite; a program needn't handle non-finite values.
Results may differ from a plain program's by a relative error of at most 0.0051.
Values may be sent and summed in bfloat16 or wider, within the bound.
No kernel may reach another device: no remote copies, remote signals or barrier semaphores. Data moves between devices by JAX's collectives and lax.ppermute only.
A program may use at most 192 MiB of HBM per device.

v0:
```python
import jax
import jax.numpy as jnp
from jax import lax
from jax.sharding import PartitionSpec as P


def shifted_2(shard, axis, by):
    length = lax.axis_size(axis)
    pairs = [(i, i + by) for i in range(length) if 0 <= i + by < length]
    return lax.ppermute(shard, axis, pairs)


def shift_cols_right(slab):
    zero_col = jnp.zeros_like(slab[:, :, :1])
    return jnp.concatenate([zero_col, slab[:, :, :-1]], axis=2)


def shift_cols_left(slab):
    zero_col = jnp.zeros_like(slab[:, :, :1])
    return jnp.concatenate([slab[:, :, 1:], zero_col], axis=2)


def first_conv(source, upper_row, first_weight):
    images, rows, width, inputs = source.shape
    outputs = first_weight.shape[3]
    paired = source.reshape(images, rows // 2, 2, width // 2, 2 * inputs)
    even_rows = paired[:, :, 0]
    odd_rows = paired[:, :, 1]
    upper_paired = upper_row.reshape(images, 1, width // 2, 2 * inputs)
    odd_above = jnp.concatenate([upper_paired, odd_rows[:, :-1]], axis=1)
    sources = [odd_above, even_rows, odd_rows]
    total = jnp.zeros((images, rows // 2, width // 2, outputs), jnp.float32)
    for tap_row in range(3):
        wide_kernel = first_weight[tap_row, 1:3].reshape(2 * inputs, outputs)
        total = total + jnp.dot(sources[tap_row], wide_kernel, preferred_element_type=jnp.float32)
    halves = jnp.concatenate([piece[..., inputs:] for piece in sources], axis=-1)
    narrow_kernel = first_weight[:, 0].reshape(3 * inputs, outputs)
    total = total + jnp.dot(
        shift_cols_right(halves), narrow_kernel, preferred_element_type=jnp.float32
    )
    return jnp.maximum(total, 0.0).astype(jnp.bfloat16)


def local(maps, first_weight, second_weight, out_grad):
    tiles = lax.axis_size("tile")
    images, height, width, inputs = maps.shape
    outputs = first_weight.shape[3]
    owned = images // tiles
    upper_row = shifted_2(maps[:, height - 1 : height], "tile", 1)
    local_hidden = first_conv(maps, upper_row, first_weight)
    half_rows = height // 2
    arrived = lax.all_to_all(
        local_hidden.reshape(tiles, owned, half_rows, width // 2, outputs),
        "tile",
        split_axis=0,
        concat_axis=2,
        tiled=True,
    )
    hidden = arrived.reshape(owned, half_rows * tiles, width // 2, outputs)
    out_rows = hidden.shape[1]
    out_cols = hidden.shape[2]
    row_padded = jnp.pad(hidden, ((0, 0), (1, 1), (0, 0), (0, 0)))
    shifted = [shift_cols_right(row_padded), row_padded, shift_cols_left(row_padded)]
    total = jnp.zeros((owned, out_rows, out_cols, outputs), jnp.float32)
    for tap_row in range(3):
        for tap_col in range(3):
            window = shifted[tap_col][:, tap_row : tap_row + out_rows]
            total = total + jnp.dot(
                window, second_weight[tap_row, tap_col], preferred_element_type=jnp.float32
            )
    conv_out = total.astype(jnp.bfloat16)
    devices = lax.axis_size("group") * tiles
    selected = out_grad.reshape(-1, lax.axis_size(("group", "tile")) * (outputs // devices))
    terms = []
    for tap_row in range(3):
        for tap_col in range(3):
            window = shifted[tap_col][:, tap_row : tap_row + out_rows].reshape(-1, outputs)
            terms.append(
                lax.dot_general(
                    selected, window, (((0,), (0,)), ((), ())), preferred_element_type=jnp.float32
                )
            )
    summed = lax.psum_scatter(
        jnp.stack(terms, axis=1).reshape(
            lax.axis_size(("group", "tile")) * (outputs // devices), 9 * outputs
        ),
        ("group", "tile"),
        scatter_dimension=0,
        tiled=True,
    )
    weight_grad = summed.reshape(-1, 3, 3, outputs)
    return (conv_out, weight_grad)


def solution(mesh):
    return jax.shard_map(
        local,
        mesh=mesh,
        in_specs=(P("group", "tile", None, None), P(), P(), P(("group", "tile"), None, None, None)),
        out_specs=(P(("group", "tile"), None, None, None), P(("group", "tile"), None, None, None)),
        check_vma=False,
    )
```

profile of v0, /device:TPU:0, one launch (start us, length us, event | category | flops | bytes accessed | tf_op | source)
XLA Modules:
  0.0 348.4 jit_solution(9022107546819320369)
XLA Ops:
  7.2 0.0 reduce-scatter.2.cloned.1.call-start
  7.2 1.0 slice.103
  8.2 0.0 copy-start.4
  8.2 5.0 %collective-permute-start = (bf16[8,1,128,128]{3,2,1,0:T(8,128)(2,1)S(1)}, bf16[8,1,128,128]{3,2,1,0:T(8,128)(2,1)S(1)}, u32[]{:S(2)}, u32[]{:S(2)}) collective-permute-start(bf16[8,1,128,128]{3,2,1,0:T(8,128)(2,1)S(1)} %slice.103), channel_id=1, source_target_pairs={{0,1},{1,2},{2,3},{3,4},{4,5},{5,6},{6,7},{8,9},{9,10},{10,11},{11... | collective-permute-start | bytes 786440 | tf_op jit(solution)/shard_map/ppermute | solution.py:10
  13.2 12.9 %reshape.106 = bf16[8,16,2,64,256]{4,3,2,1,0:T(8,128)(2,1)} reshape(bf16[8,32,128,128]{3,2,1,0:T(8,128)(2,1)} %param.4) | data formatting | bytes 16777216 | tf_op jit(solution)/shard_map/reshape | solution.py:26
  26.1 0.0 copy-done.4
  26.2 0.0 slice-start
  26.2 0.0 slice-start.1
  26.2 6.8 %fusion.185 = f32[8,16,64,256]{3,2,1,0:T(8,128)} fusion(bf16[256,256,1,1]{1,0,3,2:T(8,128)(2,1)S(1)} %bitcast.263, bf16[8,16,2,64,256]{4,3,2,1,0:T(8,128)(2,1)} %reshape.106), kind=kOutput, calls=%fused_computation.155 | convolution fusion | flops 1073741824 | bytes 12713984 | tf_op jit(solution)/shard_map/dot_general | solution.py:35
  33.0 0.0 slice-done
  33.0 4.5 %fusion.186 = f32[8,16,64,256]{3,2,1,0:T(8,128)} fusion(bf16[256,256,1,1]{1,0,3,2:T(8,128)(2,1)S(1)} %bitcast.262, bf16[8,16,2,64,256]{4,3,2,1,0:T(8,128)(2,1)S(1)} %bitcast.242), kind=kOutput, calls=%fused_computation.156 | convolution fusion | flops 1073741824 | bytes 12713984 | tf_op jit(solution)/shard_map/dot_general | solution.py:35
  37.5 1.2 slice_bitcast_fusion
  38.7 2.4 slice.135
  41.1 1.8 slice.138
  42.9 1.8 slice.137
  44.7 0.0 collective-permute-done
  44.7 0.1 reshape.105
  44.8 0.0 copy-start.1
  44.8 0.0 slice-start.2
  44.8 3.5 %fusion.19 = f32[8,16,64,256]{3,2,1,0:T(8,128)S(1)} fusion(bf16[256,256,1,1]{1,0,3,2:T(8,128)(2,1)S(1)} %bitcast.261, bf16[8,15,64,256]{3,2,1,0:T(8,128)(2,1)} %slice.135, bf16[8,1,64,256]{3,2,1,0:T(8,128)(2,1)S(1)} %reshape.105), kind=kOutput, calls=%fused_computation.20 | convolution fusion | flops 1075838976 | bytes 12713984 | tf_op jit(solution)/shard_map/dot_general | solution.py:35
  48.3 10.3 %fusion.17 = bf16[8,1,16,64,256]{4,3,2,1,0:T(8,128)(2,1)} fusion(f32[8,16,64,256]{3,2,1,0:T(8,128)} %fusion.185, f32[8,16,64,256]{3,2,1,0:T(8,128)S(1)} %fusion.19, f32[8,16,64,256]{3,2,1,0:T(8,128)} %fusion.186, bf16[384,256,1,1]{1,0,3,2:T(8,128)(2,1)S(1)} %bitcast.260, bf16[8,16,64,128]{3,2,1,0:T(8,128)(2,1)} %slice.138, ...), kind=kOutput, calls=%fused_computation.16 | convolution fusion | flops 1661992960 | bytes 37945344 | tf_op jit(solution)/shard_map/dot_general | solution.py:38
  58.6 98.4 %all_to_all.4 = bf16[8,1,16,64,256]{4,3,2,1,0:T(8,128)(2,1)S(1)} all-to-all(bf16[8,1,16,64,256]{4,3,2,1,0:T(8,128)(2,1)} %fusion.17), channel_id=1, replica_groups=mesh['group'=4,'tile'=8] {'tile'}, dimensions={0} | all-to-all | bytes 8388608 | tf_op jit(solution)/shard_map/all_to_all | solution.py:52
  157.1 2.4 copy.51
  159.5 0.0 copy-start
  159.5 0.0 copy-start.3
  159.5 4.8 %pad_slice_fusion.1 = (bf16[1,130,63,256]{3,1,2,0:T(8,128)(2,1)S(1)}, bf16[1,130,63,256]{3,1,2,0:T(8,128)(2,1)S(1)}) fusion(bf16[1,128,64,256]{3,1,2,0:T(8,128)(2,1)S(1)} %bitcast.243), kind=kLoop, calls=%fused_computation.78 | loop fusion | bytes 12580864 | tf_op jit(solution)/shard_map/slice | solution.py:15
  164.4 4.5 %fusion.25 = f32[128,64,256]{2,0,1:T(8,128)} fusion(bf16[1,130,63,256]{3,1,2,0:T(8,128)(2,1)S(1)} %get-tuple-element.11, bf16[3,3,256,256]{3,2,1,0:T(8,128)(2,1)S(1)} %copy-done.3), kind=kOutput, calls=%fused_computation.26 | convolution fusion | flops 1073741824 | bytes 12906496 | tf_op jit(solution)/shard_map/dot_general | solution.py:68
  168.9 4.5 %fusion.37 = f32[128,64,256]{2,0,1:T(8,128)} fusion(bf16[1,130,63,256]{3,1,2,0:T(8,128)(2,1)S(1)} %get-tuple-element.11, bf16[3,3,256,256]{3,2,1,0:T(8,128)(2,1)S(1)} %copy-done.3), kind=kOutput, calls=%fused_computation.38 | convolution fusion | flops 1073741824 | bytes 12906496 | tf_op jit(solution)/shard_map/dot_general | solution.py:68
  173.4 4.5 %fusion.33 = f32[128,64,256]{2,0,1:T(8,128)} fusion(bf16[1,130,63,256]{3,1,2,0:T(8,128)(2,1)S(1)} %get-tuple-element.10, bf16[3,3,256,256]{3,2,1,0:T(8,128)(2,1)S(1)} %copy-done.3), kind=kOutput, calls=%fused_computation.34 | convolution fusion | flops 1073741824 | bytes 12906496 | tf_op jit(solution)/shard_map/dot_general | solution.py:68
  177.8 4.5 %fusion.41 = f32[128,64,256]{2,0,1:T(8,128)} fusion(bf16[1,130,63,256]{3,1,2,0:T(8,128)(2,1)S(1)} %get-tuple-element.10, bf16[3,3,256,256]{3,2,1,0:T(8,128)(2,1)S(1)} %copy-done.3), kind=kOutput, calls=%fused_computation.42 | convolution fusion | flops 1073741824 | bytes 12906496 | tf_op jit(solution)/shard_map/dot_general | solution.py:68
  182.3 4.5 %fusion.45 = f32[128,64,256]{2,0,1:T(8,128)} fusion(bf16[1,130,63,256]{3,1,2,0:T(8,128)(2,1)S(1)} %get-tuple-element.11, bf16[3,3,256,256]{3,2,1,0:T(8,128)(2,1)S(1)} %copy-done.3), kind=kOutput, calls=%fused_computation.46 | convolution fusion | flops 1073741824 | bytes 12906496 | tf_op jit(solution)/shard_map/dot_general | solution.py:68
  186.8 4.5 %fusion.53 = f32[128,64,256]{2,0,1:T(8,128)} fusion(bf16[1,130,63,256]{3,1,2,0:T(8,128)(2,1)S(1)} %get-tuple-element.10, bf16[3,3,256,256]{3,2,1,0:T(8,128)(2,1)S(1)} %copy-done.3), kind=kOutput, calls=%fused_computation.54 | convolution fusion | flops 1073741824 | bytes 12906496 | tf_op jit(solution)/shard_map/dot_general | solution.py:68
  191.3 4.5 %fusion.29 = f32[128,64,256]{2,0,1:T(8,128)} fusion(bf16[1,128,64,256]{3,1,2,0:T(8,128)(2,1)S(1)} %bitcast.244, bf16[3,3,256,256]{3,2,1,0:T(8,128)(2,1)S(1)} %copy-done.3), kind=kOutput, calls=%fused_computation.30 | convolution fusion | flops 1073741824 | bytes 12713984 | tf_op jit(solution)/shard_map/dot_general | solution.py:68
  195.8 5.1 %fusion.93 = f32[256,9,256]{0,2,1:T(8,128)S(1)} fusion(bf16[1,130,63,256]{3,1,2,0:T(8,128)(2,1)S(1)} %get-tuple-element.10, bf16[128,64,256]{2,1,0:T(8,128)(2,1)S(1)} %bitcast.250), kind=kOutput, calls=%fused_computation.92 | convolution fusion | flops 1073741824 | bytes 8649728 | tf_op jit(solution)/shard_map/dot_general | solution.py:79
  200.9 5.6 %fusion.99 = f32[256,9,256]{0,2,1:T(8,128)S(1)} fusion(f32[256,9,256]{0,2,1:T(8,128)S(1)} %fusion.93, bf16[1,128,64,256]{3,1,2,0:T(8,128)(2,1)S(1)} %bitcast.245, bf16[128,64,256]{2,1,0:T(8,128)(2,1)S(1)} %bitcast.251), kind=kOutput, calls=%fused_computation.94 | convolution fusion | flops 1073741824 | bytes 8650752 | tf_op jit(solution)/shard_map/dot_general | solution.py:79
  206.5 5.3 %fusion.105 = f32[256,9,256]{0,2,1:T(8,128)S(1)} fusion(f32[256,9,256]{0,2,1:T(8,128)S(1)} %fusion.99, bf16[1,130,63,256]{3,1,2,0:T(8,128)(2,1)S(1)} %get-tuple-element.11, bf16[128,64,256]{2,1,0:T(8,128)(2,1)S(1)} %bitcast.252), kind=kOutput, calls=%fused_computation.96 | convolution fusion | flops 1073741824 | bytes 8843264 | tf_op jit(solution)/shard_map/dot_general | solution.py:79
  211.8 5.5 %fusion.111 = f32[256,9,256]{0,2,1:T(8,128)S(1)} fusion(f32[256,9,256]{0,2,1:T(8,128)S(1)} %fusion.105, bf16[1,130,63,256]{3,1,2,0:T(8,128)(2,1)S(1)} %get-tuple-element.10, bf16[128,64,256]{2,1,0:T(8,128)(2,1)S(1)} %bitcast.253), kind=kOutput, calls=%fused_computation.98 | convolution fusion | flops 1073741824 | bytes 8843264 | tf_op jit(solution)/shard_map/dot_general | solution.py:79
  217.3 1.3 fusion.138
  218.7 5.6 %fusion.117 = f32[256,9,256]{0,2,1:T(8,128)S(1)} fusion(f32[256,9,256]{0,2,1:T(8,128)S(1)} %fusion.138, bf16[1,130,63,256]{3,1,2,0:T(8,128)(2,1)S(1)} %get-tuple-element.11, bf16[128,64,256]{2,1,0:T(8,128)(2,1)S(1)} %bitcast.255), kind=kOutput, calls=%fused_computation.100 | convolution fusion | flops 1073741824 | bytes 8843264 | tf_op jit(solution)/shard_map/dot_general | solution.py:79
  224.3 5.7 %fusion.123 = f32[256,9,256]{0,2,1:T(8,128)S(1)} fusion(f32[256,9,256]{0,2,1:T(8,128)S(1)} %fusion.117, bf16[1,130,63,256]{3,1,2,0:T(8,128)(2,1)S(1)} %get-tuple-element.10, bf16[128,64,256]{2,1,0:T(8,128)(2,1)S(1)} %bitcast.256), kind=kOutput, calls=%fused_computation.102 | convolution fusion | flops 1073741824 | bytes 8843264 | tf_op jit(solution)/shard_map/dot_general | solution.py:79
  230.0 5.6 %fusion.129 = f32[256,9,256]{0,2,1:T(8,128)S(1)} fusion(f32[256,9,256]{0,2,1:T(8,128)S(1)} %fusion.123, bf16[1,128,64,256]{3,1,2,0:T(8,128)(2,1)S(1)} %bitcast.246, bf16[128,64,256]{2,1,0:T(8,128)(2,1)S(1)} %bitcast.257), kind=kOutput, calls=%fused_computation.104 | convolution fusion | flops 1073741824 | bytes 8650752 | tf_op jit(solution)/shard_map/dot_general | solution.py:79
  235.6 5.7 %fusion.135 = f32[256,9,256]{0,2,1:T(8,128)S(1)} fusion(f32[256,9,256]{0,2,1:T(8,128)S(1)} %fusion.129, bf16[1,130,63,256]{3,1,2,0:T(8,128)(2,1)S(1)} %get-tuple-element.11, bf16[128,64,256]{2,1,0:T(8,128)(2,1)S(1)} %bitcast.258), kind=kOutput, calls=%fused_computation.106 | convolution fusion | flops 1073741824 | bytes 8843264 | tf_op jit(solution)/shard_map/dot_general | solution.py:79
  241.4 2.0 copy.69
  243.3 0.0 reduce-scatter.2.cloned.1.call-update
  243.4 6.7 %fusion.49 = f32[128,64,256]{2,0,1:T(8,128)} fusion(bf16[1,128,64,256]{3,1,2,0:T(8,128)(2,1)} %bitcast.247, bf16[3,3,256,256]{3,2,1,0:T(8,128)(2,1)S(1)} %copy-done.3), kind=kOutput, calls=%fused_computation.50 | convolution fusion | flops 1073741824 | bytes 12713984 | tf_op jit(solution)/shard_map/dot_general | solution.py:68
  250.1 25.8 %fusion.18 = bf16[1,128,64,256]{3,1,2,0:T(8,128)(2,1)} fusion(f32[128,64,256]{2,0,1:T(8,128)} %fusion.25, f32[128,64,256]{2,0,1:T(8,128)} %fusion.29, f32[128,64,256]{2,0,1:T(8,128)} %fusion.33, f32[128,64,256]{2,0,1:T(8,128)} %fusion.37, f32[128,64,256]{2,0,1:T(8,128)} %fusion.41, f32[128,64,256]{2,0,1:T(8,128)} %fusion.45, f32[128,64,256]{2,0,1:T(8,128)} %fusion.53, ...), kind=kOutput, calls=%fused_computation.17 | convolution fusion | flops 1092616192 | bytes 75628544 | tf_op jit(solution)/shard_map/dot_general | solution.py:68
  275.9 6.6 %copy.70 = bf16[1,128,64,256]{3,2,1,0:T(8,128)(2,1)} copy(bf16[1,128,64,256]{3,1,2,0:T(8,128)(2,1)} %fusion.18) | data formatting | bytes 8388608
  282.5 58.8 %reduce-scatter.2.cloned.1.call-done = f32[8,2304]{1,0:T(8,128)} async-done(((f32[256,2304]{1,0:T(8,128)}), f32[8,2304]{1,0:T(8,128)}) %reduce-scatter.2.cloned.1.call-update) | async-done | bytes 73744 | tf_op jit(solution)/shard_map/reduce_scatter | solution.py:83
  (9 shorter events, 0.0 us)
Async XLA Ops:
  7.2 334.2 %reduce-scatter.2.cloned.1.call-start = ((), (), s32[]{:S(2)}) async-start(), calls=%async_computation.2 | async-start | bytes 2433024 | tf_op jit(solution)/shard_map/reduce_scatter | solution.py:83
  8.2 17.9 %copy-start.4 = (bf16[3,3,128,256]{3,2,1,0:T(8,128)(2,1)S(1)}, bf16[3,3,128,256]{3,2,1,0:T(8,128)(2,1)}, u32[]{:S(2)}) copy-start(bf16[3,3,128,256]{3,2,1,0:T(8,128)(2,1)} %param.5) | copy-start | bytes 1769476
  8.2 36.5 %collective-permute-start = (bf16[8,1,128,128]{3,2,1,0:T(8,128)(2,1)S(1)}, bf16[8,1,128,128]{3,2,1,0:T(8,128)(2,1)S(1)}, u32[]{:S(2)}, u32[]{:S(2)}) collective-permute-start(bf16[8,1,128,128]{3,2,1,0:T(8,128)(2,1)S(1)} %slice.103), channel_id=1, source_target_pairs={{0,1},{1,2},{2,3},{3,4},{4,5},{5,6},{6,7},{8,9},{9,10},{10,11},{11... | collective-permute-start | bytes 786440 | tf_op jit(solution)/shard_map/ppermute | solution.py:10
  26.2 6.9 %slice-start = ((s8[8388608]{0:T(1024)(128)(4,1)}), s8[4194304]{0:T(1024)(128)(4,1)S(1)}, s32[]{:S(2)}) async-start(s8[8388608]{0:T(1024)(128)(4,1)} %bitcast.241), calls=%async_computation.3 | async-start | bytes 8388608
  26.2 6.8 %slice-start.1 = ((s8[8388608]{0:T(1024)(128)(4,1)}), s8[4194304]{0:T(1024)(128)(4,1)S(1)}, s32[]{:S(2)}) async-start(s8[8388608]{0:T(1024)(128)(4,1)} %bitcast.241), calls=%async_computation.4 | async-start | bytes 8388608
  44.8 3.5 %copy-start.1 = (bf16[8,15,64,256]{3,2,1,0:T(8,128)(2,1)S(1)}, bf16[8,15,64,256]{3,2,1,0:T(8,128)(2,1)}, u32[]{:S(2)}) copy-start(bf16[8,15,64,256]{3,2,1,0:T(8,128)(2,1)} %slice.135) | copy-start | bytes 11796484
  44.8 3.5 %slice-start.2 = ((bf16[3,3,128,256]{3,2,1,0:T(8,128)(2,1)}), bf16[3,1,128,256]{3,2,1,0:T(8,128)(2,1)S(1)}, s32[]{:S(2)}) async-start(bf16[3,3,128,256]{3,2,1,0:T(8,128)(2,1)} %param.5), calls=%async_computation.5 | async-start | bytes 393216 | tf_op jit(solution)/shard_map/slice | solution.py:37
  159.5 70.5 %copy-start = (bf16[8,1,16,64,256]{4,2,0,3,1:T(8,128)(2,1)}, bf16[8,1,16,64,256]{4,2,0,3,1:T(8,128)(2,1)S(1)}, u32[]{:S(2)}) copy-start(bf16[8,1,16,64,256]{4,2,0,3,1:T(8,128)(2,1)S(1)} %copy.51) | copy-start | bytes 12582916
  159.5 4.8 %copy-start.3 = (bf16[3,3,256,256]{3,2,1,0:T(8,128)(2,1)S(1)}, bf16[3,3,256,256]{3,2,1,0:T(8,128)(2,1)}, u32[]{:S(2)}) copy-start(bf16[3,3,256,256]{3,2,1,0:T(8,128)(2,1)} %param.6) | copy-start | bytes 3538948
  191.3 4.5 %copy-start.2 = (bf16[1,128,64,256]{3,2,1,0:T(8,128)(2,1)S(1)}, bf16[1,128,64,256]{3,2,1,0:T(8,128)(2,1)}, u32[]{:S(2)}) copy-start(bf16[1,128,64,256]{3,2,1,0:T(8,128)(2,1)} %param.7) | copy-start | bytes 12582916
Sparse Core Ops, SparseCore 0:
  243.5 97.8 reduce-scatter.1
where the time goes:
time: 355 us; the launch traced here: 348 us
  matrix products  135 us (38%)
  blocking collectives  98.4 us (28%)
  waiting for transfers between devices  58.8 us (17%)
  local copies, waits for them, and re-layouts  37 us (10%)
  between operations  14.4 us (4%)
  starting transfers between devices  5.03 us (1%)
    all_to_all x1, blocking collectives, local(): lax.all_to_all(local_hidden.reshape(tiles, owned, half_rows, width // 2,...  98.4 us
    dot_general x9, matrix products, local(): jnp.dot(window, second_weight[tap_row, tap_col], preferred_element_type=j...  63.9 us
    reduce_scatter x1, waiting for transfers between devices, local(): lax.psum_scatter(jnp.stack(terms, axis=1).reshape(lax.axis_size(('group',...  58.8 us
    dot_general x9, matrix products, local(): lax.dot_general(selected, window, (((0,), (0,)), ((), ())), preferred_ele...  45.5 us
    dot_general x3, matrix products, first_conv(): jnp.dot(sources[tap_row], wide_kernel, preferred_element_type=jnp.float32)  14.8 us
    reshape x1, local copies, waits for them, and re-layouts, first_conv(): paired = source.reshape(images, rows // 2, 2, width // 2, 2 * inputs)  12.9 us
    dot_general x1, matrix products, first_conv(): jnp.dot(shift_cols_right(halves), narrow_kernel, preferred_element_type=j...  10.3 us
  transfers between devices with their start and end apart: 2, of which 1 were waited for; matrix products, arithmetic and copies ran while one was open for 20% of the time, Pallas kernels for 0%

commit v1 on v0

--- a/solution.py
+++ b/solution.py
@@ -1,6 +1,10 @@
+import functools
+
 import jax
 import jax.numpy as jnp
 from jax import lax
+from jax.experimental import pallas as pl
+from jax.experimental.pallas import tpu as pltpu
 from jax.sharding import PartitionSpec as P
 
 
@@ -41,6 +45,87 @@
     return jnp.maximum(total, 0.0).astype(jnp.bfloat16)
 
 
+def second_kernel(left_ref, mid_ref, right_ref, weight_ref, grad_ref, out_ref, wgrad_ref, *, rows):
+    step = pl.program_id(1)
+    _, width, channels = out_ref.shape
+
+    @pl.when(step == 0)
+    def _():
+        wgrad_ref[...] = jnp.zeros_like(wgrad_ref)
+
+    grad_t = grad_ref[...]
+    acc = jnp.zeros((rows * width, channels), jnp.float32)
+    for tap_row in range(3):
+        for tap_col, src in enumerate((left_ref, mid_ref, right_ref)):
+            window = src[pl.ds(step * rows + tap_row, rows)].reshape(rows * width, channels)
+            acc = acc + jnp.dot(window, weight_ref[tap_row, tap_col], preferred_element_type=jnp.float32)
+            tap = tap_row * 3 + tap_col
+            wgrad_ref[:, tap * channels:(tap + 1) * channels] += jnp.dot(
+                grad_t, window, preferred_element_type=jnp.float32
+            )
+    out_ref[...] = acc.astype(out_ref.dtype).reshape(rows, width, channels)
+
+
+def second_stage(hidden, second_weight, out_grad):
+    owned, out_rows, out_cols, channels = hidden.shape
+    rows = min(16, out_rows)
+    row_padded = jnp.pad(hidden, ((0, 0), (1, 1), (0, 0), (0, 0)))
+    shifted = [shift_cols_right(row_padded), row_padded, shift_cols_left(row_padded)]
+    grad_t = out_grad.reshape(owned, out_rows * out_cols, channels).transpose(0, 2, 1)
+    full = pl.BlockSpec((None, out_rows + 2, out_cols, channels), lambda n, i: (n, 0, 0, 0))
+    flops = 4 * owned * out_rows * out_cols * 9 * channels * channels
+    conv_out, wgrad = pl.pallas_call(
+        functools.partial(second_kernel, rows=rows),
+        grid=(owned, out_rows // rows),
+        in_specs=[
+            full,
+            full,
+            full,
+            pl.BlockSpec((3, 3, channels, channels), lambda n, i: (0, 0, 0, 0)),
+            pl.BlockSpec((None, channels, rows * out_cols), lambda n, i: (n, 0, i)),
+        ],
+        out_specs=[
+            pl.BlockSpec((None, rows, out_cols, channels), lambda n, i: (n, i, 0, 0)),
+            pl.BlockSpec((None, channels, 9 * channels), lambda n, i: (n, 0, 0)),
+        ],
+        out_shape=[
+            jax.ShapeDtypeStruct(hidden.shape, jnp.bfloat16),
+            jax.ShapeDtypeStruct((owned, channels, 9 * channels), jnp.float32),
+        ],
+        compiler_params=pltpu.CompilerParams(
+            dimension_semantics=("arbitrary", "arbitrary"), vmem_limit_bytes=60 * 1024 * 1024
+        ),
+        cost_estimate=pl.CostEstimate(
+            flops=flops, transcendentals=0, bytes_accessed=hidden.size * 2 * 5 + wgrad_bytes(owned, channels)
+        ),
+    )(*shifted, second_weight, grad_t)
+    return conv_out, wgrad.sum(axis=0)
+
+
+def wgrad_bytes(owned, channels):
+    return owned * channels * 9 * channels * 4
+
+
+def halving_reduce_scatter(partial, axes):
+    devices = lax.axis_size(axes)
+    tiles = lax.axis_size(axes[-1])
+    bits = devices.bit_length() - 1
+    me = lax.axis_index(axes)
+    order = [tiles.bit_length() - 1] + [b for b in range(bits) if b != tiles.bit_length() - 1]
+    rows = partial.shape[0] // devices
+    buf = partial.reshape((2,) * bits + (rows,) + partial.shape[1:])
+    remaining = list(range(bits - 1, -1, -1))
+    for bit in order:
+        axis = remaining.index(bit)
+        mine = (me >> bit) & 1
+        keep = lax.dynamic_index_in_dim(buf, mine, axis=axis, keepdims=False)
+        send = lax.dynamic_index_in_dim(buf, 1 - mine, axis=axis, keepdims=False)
+        pairs = [(i, i ^ (1 << bit)) for i in range(devices)]
+        buf = keep + lax.ppermute(send, axes, pairs)
+        remaining.pop(axis)
+    return buf
+
+
 def local(maps, first_weight, second_weight, out_grad):
     tiles = lax.axis_size("tile")
     images, height, width, inputs = maps.shape
@@ -57,37 +142,8 @@
         tiled=True,
     )
     hidden = arrived.reshape(owned, half_rows * tiles, width // 2, outputs)
-    out_rows = hidden.shape[1]
-    out_cols = hidden.shape[2]
-    row_padded = jnp.pad(hidden, ((0, 0), (1, 1), (0, 0), (0, 0)))
-    shifted = [shift_cols_right(row_padded), row_padded, shift_cols_left(row_padded)]
-    total = jnp.zeros((owned, out_rows, out_cols, outputs), jnp.float32)
-    for tap_row in range(3):
-        for tap_col in range(3):
-            window = shifted[tap_col][:, tap_row : tap_row + out_rows]
-            total = total + jnp.dot(
-                window, second_weight[tap_row, tap_col], preferred_element_type=jnp.float32
-            )
-    conv_out = total.astype(jnp.bfloat16)
-    devices = lax.axis_size("group") * tiles
-    selected = out_grad.reshape(-1, lax.axis_size(("group", "tile")) * (outputs // devices))
-    terms = []
-    for tap_row in range(3):
-        for tap_col in range(3):
-            window = shifted[tap_col][:, tap_row : tap_row + out_rows].reshape(-1, outputs)
-            terms.append(
-                lax.dot_general(
-                    selected, window, (((0,), (0,)), ((), ())), preferred_element_type=jnp.float32
-                )
-            )
-    summed = lax.psum_scatter(
-        jnp.stack(terms, axis=1).reshape(
-            lax.axis_size(("group", "tile")) * (outputs // devices), 9 * outputs
-        ),
-        ("group", "tile"),
-        scatter_dimension=0,
-        tiled=True,
-    )
+    conv_out, partial = second_stage(hidden, second_weight, out_grad)
+    summed = halving_reduce_scatter(partial, ("group", "tile"))
     weight_grad = summed.reshape(-1, 3, 3, outputs)
     return (conv_out, weight_grad)
 

time: 355 us -> 239 us (0.67); the launches traced: 348 us -> 238 us
  matrix products: 135 us -> 25.2 us
  blocking collectives: 98.4 us -> 0 us
  waiting for transfers between devices: 58.8 us -> 121 us
  Pallas kernels: 0 us -> 28 us
  between operations: 14.4 us -> 0.81 us
  local copies, waits for them, and re-layouts: 37 us -> 46.5 us
  starting transfers between devices: 5.03 us -> 14.4 us
    dot_general x18 -> x0, matrix products: 109 us -> none  [the longest x9 63.9 us: local(): jnp.dot(window, second_weight[tap_row, tap_col], preferred_element_type=j...]
    all_to_all x1 -> x0, blocking collectives: 98.4 us -> none  [local(): lax.all_to_all(local_hidden.reshape(tiles, owned, half_rows, width // 2,...]
    all_to_all x0 -> x1, waiting for transfers between devices: none -> 86.6 us  [local(): lax.all_to_all(local_hidden.reshape(tiles, owned, half_rows, width // 2,...]
    reduce_scatter x1 -> x0, waiting for transfers between devices: 58.8 us -> none  [local(): lax.psum_scatter(jnp.stack(terms, axis=1).reshape(lax.axis_size(('group',...]
    ppermute x0 -> x5, waiting for transfers between devices: none -> 34.8 us  [halving_reduce_scatter(): buf = keep + lax.ppermute(send, axes, pairs)]
    pallas_call x0 -> x1, Pallas kernels: none -> 28 us  [second_stage(): pl.pallas_call(functools.partial(second_kernel, rows=rows), grid=(owned,...]
    concatenate x0 -> x2, local copies, waits for them, and re-layouts: none -> 7.85 us  [the longest x1 5.29 us: shift_cols_right(): return jnp.concatenate([zero_col, slab[:, :, :-1]], axis=2)]
    unnamed x15 -> x8, local copies, waits for them, and re-layouts: 6.66 us -> 0.02 us
  transfers between devices with their start and end apart: 2 -> 7, of which waited for: 1 -> 6; matrix products, arithmetic and copies ran while one was open for 20% -> 16% of each run, Pallas kernels for 0% -> 0%
where the time goes in v1:
time: 239 us; the launch traced here: 238 us
  waiting for transfers between devices  121 us (51%)
  local copies, waits for them, and re-layouts  46.5 us (19%)
  Pallas kernels  28 us (12%)
  matrix products  25.2 us (11%)
  starting transfers between devices  14.4 us (6%)
    all_to_all x1, waiting for transfers between devices, local(): lax.all_to_all(local_hidden.reshape(tiles, owned, half_rows, width // 2,...  86.6 us
    ppermute x5, waiting for transfers between devices, halving_reduce_scatter(): buf = keep + lax.ppermute(send, axes, pairs)  34.8 us
    pallas_call x1, Pallas kernels, second_stage(): pl.pallas_call(functools.partial(second_kernel, rows=rows), grid=(owned,...  28 us
    dot_general x3, matrix products, first_conv(): jnp.dot(sources[tap_row], wide_kernel, preferred_element_type=jnp.float32)  14.9 us
    reshape x1, local copies, waits for them, and re-layouts, first_conv(): paired = source.reshape(images, rows // 2, 2, width // 2, 2 * inputs)  12.9 us
    dot_general x1, matrix products, first_conv(): jnp.dot(shift_cols_right(halves), narrow_kernel, preferred_element_type=j...  10.3 us
    reshape x1, local copies, waits for them, and re-layouts, second_stage(): out_grad.reshape(owned, out_rows * out_cols, channels).transpose(0, 2, 1)  6.4 us
    concatenate x1, local copies, waits for them, and re-layouts, shift_cols_right(): return jnp.concatenate([zero_col, slab[:, :, :-1]], axis=2)  5.29 us
  transfers between devices with their start and end apart: 7, of which 6 were waited for; matrix products, arithmetic and copies ran while one was open for 16% of the time, Pallas kernels for 0%

profile of v1, /device:TPU:0, one launch (start us, length us, event | category | flops | bytes accessed | tf_op | source)
XLA Modules:
  0.0 238.4 jit_solution(5636517189056269141)
XLA Ops:
  0.6 1.0 slice.42
  1.6 0.0 copy-start.1
  1.6 5.0 %collective-permute-start = (bf16[8,1,128,128]{3,2,1,0:T(8,128)(2,1)S(1)}, bf16[8,1,128,128]{3,2,1,0:T(8,128)(2,1)S(1)}, u32[]{:S(2)}, u32[]{:S(2)}) collective-permute-start(bf16[8,1,128,128]{3,2,1,0:T(8,128)(2,1)S(1)} %slice.42), channel_id=1, source_target_pairs={{0,1},{1,2},{2,3},{3,4},{4,5},{5,6},{6,7},{8,9},{9,10},{10,11},{11... | collective-permute-start | bytes 786440 | tf_op jit(solution)/shard_map/ppermute | solution.py:14
  6.6 12.9 %reshape.32 = bf16[8,16,2,64,256]{4,3,2,1,0:T(8,128)(2,1)} reshape(bf16[8,32,128,128]{3,2,1,0:T(8,128)(2,1)} %param.4) | data formatting | bytes 16777216 | tf_op jit(solution)/shard_map/reshape | solution.py:30
  19.6 0.0 copy-done.1
  19.6 0.0 slice-start
  19.6 0.0 slice-start.1
  19.6 6.8 %fusion.29 = f32[8,16,64,256]{3,2,1,0:T(8,128)} fusion(bf16[256,256,1,1]{1,0,3,2:T(8,128)(2,1)S(1)} %bitcast.76, bf16[8,16,2,64,256]{4,3,2,1,0:T(8,128)(2,1)} %reshape.32), kind=kOutput, calls=%fused_computation.37 | convolution fusion | flops 1073741824 | bytes 12713984 | tf_op jit(solution)/shard_map/dot_general | solution.py:39
  26.5 0.0 slice-done
  26.5 0.0 slice-done.1
  26.5 4.5 %fusion.30 = f32[8,16,64,256]{3,2,1,0:T(8,128)} fusion(bf16[256,256,1,1]{1,0,3,2:T(8,128)(2,1)S(1)} %bitcast.75, bf16[8,16,2,64,256]{4,3,2,1,0:T(8,128)(2,1)S(1)} %bitcast.68), kind=kOutput, calls=%fused_computation.38 | convolution fusion | flops 1073741824 | bytes 12713984 | tf_op jit(solution)/shard_map/dot_general | solution.py:39
  31.0 1.2 slice_bitcast_fusion
  32.1 1.8 slice.60
  33.9 2.4 %slice.57 = bf16[8,15,64,256]{3,2,1,0:T(8,128)(2,1)} slice(bf16[8,16,64,256]{3,2,1,0:T(8,128)(2,1)S(1)} %get-tuple-element.7), slice={[0:8], [0:15], [0:64], [0:256]} | slice | bytes 7864320 | tf_op jit(solution)/shard_map/slice | solution.py:34
  36.3 1.8 slice.59
  38.1 0.0 collective-permute-done
  38.1 0.1 reshape.31
  38.2 0.0 copy-start
  38.2 0.0 slice-start.2
  38.2 3.5 %fusion.18 = f32[8,16,64,256]{3,2,1,0:T(8,128)S(1)} fusion(bf16[256,256,1,1]{1,0,3,2:T(8,128)(2,1)S(1)} %bitcast.74, bf16[8,15,64,256]{3,2,1,0:T(8,128)(2,1)} %slice.57, bf16[8,1,64,256]{3,2,1,0:T(8,128)(2,1)S(1)} %reshape.31), kind=kOutput, calls=%fused_computation.18 | convolution fusion | flops 1075838976 | bytes 12713984 | tf_op jit(solution)/shard_map/dot_general | solution.py:39
  41.7 0.0 copy-done
  41.8 0.0 slice-done.2
  41.8 10.3 %fusion.17 = bf16[8,1,16,64,256]{4,3,2,1,0:T(8,128)(2,1)} fusion(f32[8,16,64,256]{3,2,1,0:T(8,128)} %fusion.29, f32[8,16,64,256]{3,2,1,0:T(8,128)S(1)} %fusion.18, f32[8,16,64,256]{3,2,1,0:T(8,128)} %fusion.30, bf16[384,256,1,1]{1,0,3,2:T(8,128)(2,1)S(1)} %bitcast.73, bf16[8,16,64,128]{3,2,1,0:T(8,128)(2,1)} %slice.60, bf16[8,16,64,128]{3,2,1,0:T(8,128)(2,1)} %slice.59, ...), kind=kOutput, calls=%fused_computation.15 | convolution fusion | flops 1661992960 | bytes 37945344 | tf_op jit(solution)/shard_map/dot_general | solution.py:42
  52.1 4.9 %all-to-all-start = ((bf16[8,1,16,64,256]{4,3,2,1,0:T(8,128)(2,1)}), bf16[8,1,16,64,256]{4,3,2,1,0:T(8,128)(2,1)}, u32[]{:S(2)}, u32[]{:S(2)}) async-start(bf16[8,1,16,64,256]{4,3,2,1,0:T(8,128)(2,1)} %fusion.17), calls=%async_computation | async-start | bytes 8388608 | tf_op jit(solution)/shard_map/all_to_all | solution.py:137
  57.0 6.4 %copy.13 = bf16[1,8192,256]{1,2,0:T(8,128)(2,1)} copy(bf16[1,8192,256]{2,1,0:T(8,128)(2,1)} %bitcast.69) | data formatting | bytes 8388608 | tf_op jit(solution)/shard_map/reshape | solution.py:74
  63.4 86.6 %all-to-all-done = bf16[8,1,16,64,256]{4,3,2,1,0:T(8,128)(2,1)} async-done(((bf16[8,1,16,64,256]{4,3,2,1,0:T(8,128)(2,1)}), bf16[8,1,16,64,256]{4,3,2,1,0:T(8,128)(2,1)}, u32[]{:S(2)}, u32[]{:S(2)}) %all-to-all-start) | async-done | bytes 4194336 | tf_op jit(solution)/shard_map/all_to_all | solution.py:137
  150.0 4.8 %pad_slice_fusion = (bf16[1,130,63,256]{3,2,1,0:T(8,128)(2,1)S(1)}, bf16[1,130,63,256]{3,2,1,0:T(8,128)(2,1)S(1)}) fusion(bf16[1,128,64,256]{3,2,1,0:T(8,128)(2,1)} %bitcast.16), kind=kLoop, calls=%fused_computation.39 | loop fusion | bytes 12580864 | tf_op jit(solution)/shard_map/slice | solution.py:24
  154.8 4.7 %pad.7.mid_ref = bf16[1,130,64,256]{3,2,1,0:T(8,128)(2,1)} pad(bf16[1,128,64,256]{3,2,1,0:T(8,128)(2,1)} %bitcast.16, bf16[]{:T(256)} %constant.52.clone.1), padding=0_0x1_1x0_0x0_0 | pad | bytes 8454146 | tf_op jit(solution)/shard_map/jit(_pad)/pad | solution.py:72
  159.6 2.6 %concatenate.19.right_ref = bf16[1,130,64,256]{3,2,1,0:T(8,128)(2,1)} pad(bf16[1,130,63,256]{3,2,1,0:T(8,128)(2,1)S(1)} %get-tuple-element.8, bf16[]{:T(256)} %constant.52.clone.1), padding=0_0x0_0x0_1x0_0 | pad | bytes 8453122 | tf_op jit(solution)/shard_map/concatenate | solution.py:24
  162.1 5.3 %concatenate.18.left_ref = bf16[1,130,64,256]{3,2,1,0:T(8,128)(2,1)} pad(bf16[1,130,63,256]{3,2,1,0:T(8,128)(2,1)S(1)} %get-tuple-element.9, bf16[]{:T(256)} %constant.52.clone.1), padding=0_0x0_0x1_0x0_0 | pad | bytes 8453122 | tf_op jit(solution)/shard_map/concatenate | solution.py:19
  167.4 28.0 %shard_map.59 = (bf16[1,128,64,256]{3,2,1,0:T(8,128)(2,1)}, f32[1,256,2304]{2,1,0:T(8,128)}) custom-call(bf16[1,130,64,256]{3,2,1,0:T(8,128)(2,1)} %concatenate.18.left_ref, bf16[1,130,64,256]{3,2,1,0:T(8,128)(2,1)} %pad.7.mid_ref, bf16[1,130,64,256]{3,2,1,0:T(8,128)(2,1)} %concatenate.19.right_ref, bf16[3,3,256,256]{3,2,1,0:T(8,128)(2,1)} %weight_ref.1, ...), custom_call_target="tpu_custom_call" | custom-call | flops 19327352832 | bytes 23330816 | tf_op jit(solution)/shard_map/pallas_call | solution.py:77
  195.4 1.4 dynamic-slice_bitcast_fusion
  196.8 0.1 collective-permute-start.1
  196.9 2.8 %collective-permute-done.1 = f32[2,2,2,2,8,2304]{5,4,3,2,1,0:T(8,128)S(1)} collective-permute-done((f32[2,2,2,2,8,2304]{5,4,3,2,1,0:T(8,128)S(1)}, f32[2,2,2,2,8,2304]{5,4,3,2,1,0:T(8,128)S(1)}, u32[]{:S(2)}, u32[]{:S(2)}) %collective-permute-start.1) | collective-permute-done | bytes 1179680 | tf_op jit(solution)/shard_map/ppermute | solution.py:124
  199.7 1.4 bitcast_add_fusion
  201.2 1.6 collective-permute-start.2
  202.7 13.9 %collective-permute-done.2 = f32[2,2,2,8,2304]{4,3,2,1,0:T(8,128)S(1)} collective-permute-done((f32[2,2,2,8,2304]{4,3,2,1,0:T(8,128)S(1)}, f32[2,2,2,8,2304]{4,3,2,1,0:T(8,128)S(1)}, u32[]{:S(2)}, u32[]{:S(2)}) %collective-permute-start.2) | collective-permute-done | bytes 589856 | tf_op jit(solution)/shard_map/ppermute | solution.py:124
  216.6 0.1 bitcast_add_fusion.1
  216.7 0.1 collective-permute-start.3
  216.8 8.2 %collective-permute-done.3 = f32[2,2,8,2304]{3,2,1,0:T(8,128)S(1)} collective-permute-done((f32[2,2,8,2304]{3,2,1,0:T(8,128)S(1)}, f32[2,2,8,2304]{3,2,1,0:T(8,128)S(1)}, u32[]{:S(2)}, u32[]{:S(2)}) %collective-permute-start.3) | collective-permute-done | bytes 294944 | tf_op jit(solution)/shard_map/ppermute | solution.py:124
  225.0 1.2 collective-permute-start.4
  226.3 7.0 %collective-permute-done.4 = f32[2,8,2304]{2,1,0:T(8,128)S(1)} collective-permute-done((f32[2,8,2304]{2,1,0:T(8,128)S(1)}, f32[2,8,2304]{2,1,0:T(8,128)S(1)}, u32[]{:S(2)}, u32[]{:S(2)}) %collective-permute-start.4) | collective-permute-done | bytes 147488 | tf_op jit(solution)/shard_map/ppermute | solution.py:124
  233.4 1.6 collective-permute-start.5
  234.9 2.8 %collective-permute-done.5 = f32[8,2304]{1,0:T(8,128)S(1)} collective-permute-done((f32[8,2304]{1,0:T(8,128)S(1)}, f32[8,2304]{1,0:T(8,128)S(1)}, u32[]{:S(2)}, u32[]{:S(2)}) %collective-permute-start.5) | collective-permute-done | bytes 73760 | tf_op jit(solution)/shard_map/ppermute | solution.py:124
  237.8 0.6 bitcast_add_fusion.4
  (8 shorter events, 0.2 us)
Async XLA Ops:
  1.6 17.9 %copy-start.1 = (bf16[3,3,128,256]{3,2,1,0:T(8,128)(2,1)S(1)}, bf16[3,3,128,256]{3,2,1,0:T(8,128)(2,1)}, u32[]{:S(2)}) copy-start(bf16[3,3,128,256]{3,2,1,0:T(8,128)(2,1)} %param.5) | copy-start | bytes 1769476
  1.6 36.5 %collective-permute-start = (bf16[8,1,128,128]{3,2,1,0:T(8,128)(2,1)S(1)}, bf16[8,1,128,128]{3,2,1,0:T(8,128)(2,1)S(1)}, u32[]{:S(2)}, u32[]{:S(2)}) collective-permute-start(bf16[8,1,128,128]{3,2,1,0:T(8,128)(2,1)S(1)} %slice.42), channel_id=1, source_target_pairs={{0,1},{1,2},{2,3},{3,4},{4,5},{5,6},{6,7},{8,9},{9,10},{10,11},{11... | collective-permute-start | bytes 786440 | tf_op jit(solution)/shard_map/ppermute | solution.py:14
  19.6 6.9 %slice-start = ((s8[8388608]{0:T(1024)(128)(4,1)}), s8[4194304]{0:T(1024)(128)(4,1)S(1)}, s32[]{:S(2)}) async-start(s8[8388608]{0:T(1024)(128)(4,1)} %bitcast.67), calls=%async_computation.1 | async-start | bytes 8388608
  19.6 6.9 %slice-start.1 = ((s8[8388608]{0:T(1024)(128)(4,1)}), s8[4194304]{0:T(1024)(128)(4,1)S(1)}, s32[]{:S(2)}) async-start(s8[8388608]{0:T(1024)(128)(4,1)} %bitcast.67), calls=%async_computation.2 | async-start | bytes 8388608
  38.2 3.5 %copy-start = (bf16[8,15,64,256]{3,2,1,0:T(8,128)(2,1)S(1)}, bf16[8,15,64,256]{3,2,1,0:T(8,128)(2,1)}, u32[]{:S(2)}) copy-start(bf16[8,15,64,256]{3,2,1,0:T(8,128)(2,1)} %slice.57) | copy-start | bytes 11796484
  38.2 3.5 %slice-start.2 = ((bf16[3,3,128,256]{3,2,1,0:T(8,128)(2,1)}), bf16[3,1,128,256]{3,2,1,0:T(8,128)(2,1)S(1)}, s32[]{:S(2)}) async-start(bf16[3,3,128,256]{3,2,1,0:T(8,128)(2,1)} %param.5), calls=%async_computation.3 | async-start | bytes 393216 | tf_op jit(solution)/shard_map/slice | solution.py:41
  52.1 97.9 %all-to-all-start = ((bf16[8,1,16,64,256]{4,3,2,1,0:T(8,128)(2,1)}), bf16[8,1,16,64,256]{4,3,2,1,0:T(8,128)(2,1)}, u32[]{:S(2)}, u32[]{:S(2)}) async-start(bf16[8,1,16,64,256]{4,3,2,1,0:T(8,128)(2,1)} %fusion.17), calls=%async_computation | async-start | bytes 8388608 | tf_op jit(solution)/shard_map/all_to_all | solution.py:137
  196.8 2.9 %collective-permute-start.1 = (f32[2,2,2,2,8,2304]{5,4,3,2,1,0:T(8,128)S(1)}, f32[2,2,2,2,8,2304]{5,4,3,2,1,0:T(8,128)S(1)}, u32[]{:S(2)}, u32[]{:S(2)}) collective-permute-start(f32[2,2,2,2,8,2304]{5,4,3,2,1,0:T(8,128)S(1)} %dynamic-slice_bitcast_fusion), channel_id=1, source_target_pairs={{0,8},{1,9},{2,10},{3,11},{4,12},{5,13},{6,14},{7,15},{8,0},{9,1},... | collective-permute-start | bytes 3538952 | tf_op jit(solution)/shard_map/ppermute | solution.py:124
  201.2 15.4 %collective-permute-start.2 = (f32[2,2,2,8,2304]{4,3,2,1,0:T(8,128)S(1)}, f32[2,2,2,8,2304]{4,3,2,1,0:T(8,128)S(1)}, u32[]{:S(2)}, u32[]{:S(2)}) collective-permute-start(f32[2,2,2,8,2304]{4,3,2,1,0:T(8,128)S(1)} %dynamic-slice_bitcast_fusion.1), channel_id=1, source_target_pairs={{0,1},{1,0},{2,3},{3,2},{4,5},{5,4},{6,7},{7,6},{8,9},{9,8},{10,11... | collective-permute-start | bytes 1769480 | tf_op jit(solution)/shard_map/ppermute | solution.py:124
  216.7 8.3 %collective-permute-start.3 = (f32[2,2,8,2304]{3,2,1,0:T(8,128)S(1)}, f32[2,2,8,2304]{3,2,1,0:T(8,128)S(1)}, u32[]{:S(2)}, u32[]{:S(2)}) collective-permute-start(f32[2,2,8,2304]{3,2,1,0:T(8,128)S(1)} %dynamic-slice_bitcast_fusion.2), channel_id=1, source_target_pairs={{0,2},{1,3},{2,0},{3,1},{4,6},{5,7},{6,4},{7,5},{8,10},{9,11},{10,... | collective-permute-start | bytes 884744 | tf_op jit(solution)/shard_map/ppermute | solution.py:124
  225.0 8.3 %collective-permute-start.4 = (f32[2,8,2304]{2,1,0:T(8,128)S(1)}, f32[2,8,2304]{2,1,0:T(8,128)S(1)}, u32[]{:S(2)}, u32[]{:S(2)}) collective-permute-start(f32[2,8,2304]{2,1,0:T(8,128)S(1)} %dynamic-slice_bitcast_fusion.3), channel_id=1, source_target_pairs={{0,4},{1,5},{2,6},{3,7},{4,0},{5,1},{6,2},{7,3},{8,12},{9,13},{10,... | collective-permute-start | bytes 442376 | tf_op jit(solution)/shard_map/ppermute | solution.py:124
  233.4 4.4 %collective-permute-start.5 = (f32[8,2304]{1,0:T(8,128)S(1)}, f32[8,2304]{1,0:T(8,128)S(1)}, u32[]{:S(2)}, u32[]{:S(2)}) collective-permute-start(f32[8,2304]{1,0:T(8,128)S(1)} %dynamic-slice_bitcast_fusion.4), channel_id=1, source_target_pairs={{0,16},{1,17},{2,18},{3,19},{4,20},{5,21},{6,22},{7,23},{8,24},{9,... | collective-permute-start | bytes 221192 | tf_op jit(solution)/shard_map/ppermute | solution.py:124

commit v2 on v1

v2 whole, which is shorter than its diff:
```python
import functools

import jax
import jax.numpy as jnp
from jax import lax
from jax.experimental import pallas as pl
from jax.experimental.pallas import tpu as pltpu
from jax.sharding import PartitionSpec as P


def shifted_2(shard, axis, by):
    length = lax.axis_size(axis)
    pairs = [(i, i + by) for i in range(length) if 0 <= i + by < length]
    return lax.ppermute(shard, axis, pairs)


def shift_cols_right(slab):
    zero_col = jnp.zeros_like(slab[:, :, :1])
    return jnp.concatenate([zero_col, slab[:, :, :-1]], axis=2)


def shift_cols_left(slab):
    zero_col = jnp.zeros_like(slab[:, :, :1])
    return jnp.concatenate([slab[:, :, 1:], zero_col], axis=2)


def first_conv(source, upper_row, first_weight):
    images, rows, width, inputs = source.shape
    outputs = first_weight.shape[3]
    paired = source.reshape(images, rows // 2, 2, width // 2, 2 * inputs)
    even_rows = paired[:, :, 0]
    odd_rows = paired[:, :, 1]
    upper_paired = upper_row.reshape(images, 1, width // 2, 2 * inputs)
    odd_above = jnp.concatenate([upper_paired, odd_rows[:, :-1]], axis=1)
    sources = [odd_above, even_rows, odd_rows]
    total = jnp.zeros((images, rows // 2, width // 2, outputs), jnp.float32)
    for tap_row in range(3):
        wide_kernel = first_weight[tap_row, 1:3].reshape(2 * inputs, outputs)
        total = total + jnp.dot(sources[tap_row], wide_kernel, preferred_element_type=jnp.float32)
    halves = jnp.concatenate([piece[..., inputs:] for piece in sources], axis=-1)
    narrow_kernel = first_weight[:, 0].reshape(3 * inputs, outputs)
    total = total + jnp.dot(
        shift_cols_right(halves), narrow_kernel, preferred_element_type=jnp.float32
    )
    return jnp.maximum(total, 0.0).astype(jnp.bfloat16)


def second_kernel(*refs, rows, carry):
    if carry:
        left_ref, mid_ref, right_ref, weight_ref, grad_ref, prev_ref, out_ref, wgrad_ref = refs
    else:
        left_ref, mid_ref, right_ref, weight_ref, grad_ref, out_ref, wgrad_ref = refs
    step = pl.program_id(1)
    _, width, outputs = out_ref.shape
    inputs = mid_ref.shape[-1]
    grad_t = grad_ref[...]
    if carry:
        acc = prev_ref[...].reshape(rows * width, outputs)
    else:
        acc = jnp.zeros((rows * width, outputs), jnp.float32)
    for tap_row in range(3):
        for tap_col, src in enumerate((left_ref, mid_ref, right_ref)):
            window = src[pl.ds(step * rows + tap_row, rows)].reshape(rows * width, inputs)
            acc = acc + jnp.dot(window, weight_ref[tap_row, tap_col], preferred_element_type=jnp.float32)
            term = jnp.dot(grad_t, window, preferred_element_type=jnp.float32)
            tap = tap_row * 3 + tap_col

            @pl.when(step == 0)
            def _():
                wgrad_ref[:, tap * inputs:(tap + 1) * inputs] = term

            @pl.when(step > 0)
            def _():
                wgrad_ref[:, tap * inputs:(tap + 1) * inputs] += term

    out_ref[...] = acc.astype(out_ref.dtype).reshape(rows, width, outputs)


def second_stage(hidden, weight, grad_t, prev, out_dtype):
    owned, out_rows, out_cols, inputs = hidden.shape
    outputs = weight.shape[-1]
    rows = min(16, out_rows)
    row_padded = jnp.pad(hidden, ((0, 0), (1, 1), (0, 0), (0, 0)))
    shifted = [shift_cols_right(row_padded), row_padded, shift_cols_left(row_padded)]
    full = pl.BlockSpec((None, out_rows + 2, out_cols, inputs), lambda n, i: (n, 0, 0, 0))
    block = pl.BlockSpec((None, rows, out_cols, outputs), lambda n, i: (n, i, 0, 0))
    in_specs = [
        full,
        full,
        full,
        pl.BlockSpec((3, 3, inputs, outputs), lambda n, i: (0, 0, 0, 0)),
        pl.BlockSpec((None, outputs, rows * out_cols), lambda n, i: (n, 0, i)),
    ]
    operands = [*shifted, weight, grad_t]
    if prev is not None:
        in_specs.append(block)
        operands.append(prev)
    flops = 4 * owned * out_rows * out_cols * 9 * inputs * outputs
    return pl.pallas_call(
        functools.partial(second_kernel, rows=rows, carry=prev is not None),
        grid=(owned, out_rows // rows),
        in_specs=in_specs,
        out_specs=[block, pl.BlockSpec((None, outputs, 9 * inputs), lambda n, i: (n, 0, 0))],
        out_shape=[
            jax.ShapeDtypeStruct((owned, out_rows, out_cols, outputs), out_dtype),
            jax.ShapeDtypeStruct((owned, outputs, 9 * inputs), jnp.float32),
        ],
        compiler_params=pltpu.CompilerParams(
            dimension_semantics=("arbitrary", "arbitrary"), vmem_limit_bytes=60 * 1024 * 1024
        ),
        cost_estimate=pl.CostEstimate(
            flops=flops,
            transcendentals=0,
            bytes_accessed=hidden.size * 2 * 4 + owned * out_rows * out_cols * outputs * 8
            + owned * outputs * 9 * inputs * 4,
        ),
    )(*operands)


def halving_reduce_scatter(partial, axes):
    devices = lax.axis_size(axes)
    tiles = lax.axis_size(axes[-1])
    bits = devices.bit_length() - 1
    me = lax.axis_index(axes)
    core = tiles.bit_length() - 1
    order = [core] + [b for b in range(bits) if b > core] + [b for b in range(core)]
    rows = partial.shape[0] // devices
    buf = partial.reshape((2,) * bits + (rows,) + partial.shape[1:])
    remaining = list(range(bits - 1, -1, -1))
    for bit in order:
        axis = remaining.index(bit)
        mine = (me >> bit) & 1
        keep = lax.dynamic_index_in_dim(buf, mine, axis=axis, keepdims=False)
        send = lax.dynamic_index_in_dim(buf, 1 - mine, axis=axis, keepdims=False)
        pairs = [(i, i ^ (1 << bit)) for i in range(devices)]
        buf = keep + lax.ppermute(send, axes, pairs)
        remaining.pop(axis)
    return buf


def local(maps, first_weight, second_weight, out_grad):
    tiles = lax.axis_size("tile")
    images, height, width, inputs = maps.shape
    outputs = first_weight.shape[3]
    owned = images // tiles
    half_rows = height // 2
    chunks = 2 if outputs % 256 == 0 else 1
    part = outputs // chunks
    upper_row = shifted_2(maps[:, height - 1 : height], "tile", 1)
    grad_t = out_grad.reshape(owned, -1, outputs).transpose(0, 2, 1)
    conv = None
    pieces = []
    for chunk in range(chunks):
        channels = slice(chunk * part, (chunk + 1) * part)
        local_hidden = first_conv(maps, upper_row, first_weight[..., channels])
        arrived = lax.all_to_all(
            local_hidden.reshape(tiles, owned, half_rows, width // 2, part),
            "tile",
            split_axis=0,
            concat_axis=2,
            tiled=True,
        )
        if conv is not None:
            arrived, conv = lax.optimization_barrier((arrived, conv))
        hidden = arrived.reshape(owned, half_rows * tiles, width // 2, part)
        last = chunk == chunks - 1
        conv, partial = second_stage(
            hidden, second_weight[:, :, channels], grad_t, conv, jnp.bfloat16 if last else jnp.float32
        )
        summed = halving_reduce_scatter(partial.sum(axis=0).reshape(outputs, 9 * part), ("group", "tile"))
        pieces.append(summed.reshape(-1, 9, part))
    weight_grad = jnp.concatenate(pieces, axis=-1).reshape(-1, 3, 3, outputs)
    return (conv, weight_grad)


def solution(mesh):
    return jax.shard_map(
        local,
        mesh=mesh,
        in_specs=(P("group", "tile", None, None), P(), P(), P(("group", "tile"), None, None, None)),
        out_specs=(P(("group", "tile"), None, None, None), P(("group", "tile"), None, None, None)),
        check_vma=False,
    )
```

time: 239 us -> 240 us (level)
  waiting for transfers between devices: 121 us -> 51.2 us
  Pallas kernels: 28 us -> 72 us
  starting transfers between devices: 14.4 us -> 29.5 us
  local copies, waits for them, and re-layouts: 46.5 us -> 55.1 us
  matrix products: 25.2 us -> 27.9 us
    all_to_all x1 -> x2, waiting for transfers between devices: 86.6 us -> 34.5 us  [local(): lax.all_to_all(local_hidden.reshape(tiles, owned, half_rows, width // 2,...]
    pallas_call x1 -> x2, Pallas kernels: 28 us -> 72 us  [second_stage(): pl.pallas_call(functools.partial(second_kernel, rows=rows, carry=prev is...]
    ppermute x5 -> x10, waiting for transfers between devices: 34.8 us -> 16.7 us  [halving_reduce_scatter(): buf = keep + lax.ppermute(send, axes, pairs)]
    ppermute x5 -> x10, starting transfers between devices: 4.52 us -> 15.1 us  [halving_reduce_scatter(): buf = keep + lax.ppermute(send, axes, pairs)]
    all_to_all x1 -> x2, starting transfers between devices: 4.88 us -> 9.39 us  [local(): lax.all_to_all(local_hidden.reshape(tiles, owned, half_rows, width // 2,...]
    unnamed x8 -> x26, local copies, waits for them, and re-layouts: 0.02 us -> 4.42 us
    dot_general x3 -> x6, matrix products: 14.9 us -> 18.3 us  [first_conv(): jnp.dot(sources[tap_row], wide_kernel, preferred_element_type=jnp.float32)]
    squeeze x1, local copies, waits for them, and re-layouts: 1.18 us -> 4.22 us  [first_conv(): even_rows = paired[:, :, 0]]
  transfers between devices with their start and end apart: 7 -> 13, of which waited for: 6 -> 7; matrix products, arithmetic and copies ran while one was open for 16% -> 24% of each run, Pallas kernels for 0% -> 15%
where the time goes in v2:
time: 240 us; the launch traced here: 239 us
  Pallas kernels  72 us (30%)
  local copies, waits for them, and re-layouts  55.1 us (23%)
  waiting for transfers between devices  51.2 us (21%)
  starting transfers between devices  29.5 us (12%)
  matrix products  27.9 us (12%)
    pallas_call x2, Pallas kernels, second_stage(): pl.pallas_call(functools.partial(second_kernel, rows=rows, carry=prev is...  72 us
    all_to_all x2, waiting for transfers between devices, local(): lax.all_to_all(local_hidden.reshape(tiles, owned, half_rows, width // 2,...  34.5 us
    dot_general x6, matrix products, first_conv(): jnp.dot(sources[tap_row], wide_kernel, preferred_element_type=jnp.float32)  18.3 us
    ppermute x10, waiting for transfers between devices, halving_reduce_scatter(): buf = keep + lax.ppermute(send, axes, pairs)  16.7 us
    ppermute x10, starting transfers between devices, halving_reduce_scatter(): buf = keep + lax.ppermute(send, axes, pairs)  15.1 us
    reshape x1, local copies, waits for them, and re-layouts, first_conv(): paired = source.reshape(images, rows // 2, 2, width // 2, 2 * inputs)  12.9 us
    dot_general x2, matrix products, first_conv(): jnp.dot(shift_cols_right(halves), narrow_kernel, preferred_element_type=j...  9.62 us
    all_to_all x2, starting transfers between devices, local(): lax.all_to_all(local_hidden.reshape(tiles, owned, half_rows, width // 2,...  9.39 us
  transfers between devices with their start and end apart: 13, of which 7 were waited for; matrix products, arithmetic and copies ran while one was open for 24% of the time, Pallas kernels for 15%

profile of v2, /device:TPU:0, one launch (start us, length us, event | category | flops | bytes accessed | tf_op | source)
XLA Modules:
  0.0 238.6 jit_solution(4654854636835769043)
XLA Ops:
  0.6 1.0 slice.83
  1.6 5.0 %collective-permute-start = (bf16[8,1,128,128]{3,2,1,0:T(8,128)(2,1)S(1)}, bf16[8,1,128,128]{3,2,1,0:T(8,128)(2,1)S(1)}, u32[]{:S(2)}, u32[]{:S(2)}) collective-permute-start(bf16[8,1,128,128]{3,2,1,0:T(8,128)(2,1)S(1)} %slice.83), channel_id=1, source_target_pairs={{0,1},{1,2},{2,3},{3,4},{4,5},{5,6},{6,7},{8,9},{9,10},{10,11},{11... | collective-permute-start | bytes 786440 | tf_op jit(solution)/shard_map/ppermute | solution.py:14
  6.6 12.9 %reshape.52 = bf16[8,16,2,64,256]{4,3,2,1,0:T(8,128)(2,1)} reshape(bf16[8,32,128,128]{3,2,1,0:T(8,128)(2,1)} %param.4) | data formatting | bytes 16777216 | tf_op jit(solution)/shard_map/reshape | solution.py:30
  19.5 0.7 fusion.20
  20.3 4.2 %slice_bitcast_fusion = (bf16[8,16,64,256]{3,2,1,0:T(8,128)(2,1)S(1)}, bf16[8,16,64,256]{3,2,1,0:T(8,128)(2,1)S(1)}) fusion(bf16[8,16,2,64,256]{4,3,2,1,0:T(8,128)(2,1)} %reshape.52), kind=kLoop, calls=%fused_computation.8 | loop fusion | bytes 16777216 | tf_op jit(solution)/shard_map/squeeze | solution.py:31
  24.5 1.2 slice-done.1
  25.7 3.3 %fusion.13 = f32[8,16,64,128]{3,2,1,0:T(8,128)} fusion(bf16[256,128,1,1]{1,0,3,2:T(8,128)(2,1)S(1)} %bitcast.135, bf16[8,16,2,64,256]{4,3,2,1,0:T(8,128)(2,1)S(1)} %bitcast.122), kind=kOutput, calls=%fused_computation.44 | convolution fusion | flops 536870912 | bytes 8454144 | tf_op jit(solution)/shard_map/dot_general | solution.py:39
  29.0 3.3 %fusion.15 = f32[8,16,64,128]{3,2,1,0:T(8,128)} fusion(bf16[256,128,1,1]{1,0,3,2:T(8,128)(2,1)S(1)} %bitcast.134, bf16[8,16,2,64,256]{4,3,2,1,0:T(8,128)(2,1)S(1)} %bitcast.122), kind=kOutput, calls=%fused_computation.46 | convolution fusion | flops 536870912 | bytes 8454144 | tf_op jit(solution)/shard_map/dot_general | solution.py:39
  32.2 2.1 slice.106
  34.8 1.9 slice.108
  36.9 3.5 %fusion.7 = f32[8,16,64,128]{3,2,1,0:T(8,128)S(1)} fusion(bf16[256,128,1,1]{1,0,3,2:T(8,128)(2,1)} %bitcast.141, bf16[8,15,64,256]{3,2,1,0:T(8,128)(2,1)} %slice.106, bf16[8,1,64,256]{3,2,1,0:T(8,128)(2,1)S(1)} %reshape.51), kind=kOutput, calls=%fused_computation.13 | convolution fusion | flops 538968064 | bytes 8454144 | tf_op jit(solution)/shard_map/dot_general | solution.py:39
  40.5 1.1 copy-done.1
  41.6 1.1 copy-done.2
  42.7 5.5 %fusion.10 = bf16[8,1,16,64,128]{4,3,2,1,0:T(8,128)(2,1)} fusion(bf16[384,128,1,1]{1,0,3,2:T(8,128)(2,1)S(1)} %bitcast.139, f32[8,16,64,128]{3,2,1,0:T(8,128)S(1)} %copy-done, f32[8,16,64,128]{3,2,1,0:T(8,128)S(1)} %fusion.7, f32[8,16,64,128]{3,2,1,0:T(8,128)S(1)} %copy-done.1, bf16[8,16,64,128]{3,2,1,0:T(8,128)(2,1)S(1)} %slice.109, ...), kind=kOutput, calls=%fused_computation.16 | convolution fusion | flops 851443712 | bytes 23166976 | tf_op jit(solution)/shard_map/dot_general | solution.py:42
  48.2 4.9 %all-to-all-start.1 = ((bf16[8,1,16,64,128]{4,3,2,1,0:T(8,128)(2,1)}), bf16[8,1,16,64,128]{4,3,2,1,0:T(8,128)(2,1)S(1)}, u32[]{:S(2)}, u32[]{:S(2)}) async-start(bf16[8,1,16,64,128]{4,3,2,1,0:T(8,128)(2,1)} %fusion.10), calls=%async_computation.1 | async-start | bytes 4194304 | tf_op jit(solution)/shard_map/all_to_all | solution.py:156
  53.1 3.4 %fusion.14 = f32[8,16,64,128]{3,2,1,0:T(8,128)S(1)} fusion(bf16[256,128,1,1]{1,0,3,2:T(8,128)(2,1)S(1)} %bitcast.133, bf16[8,16,2,64,256]{4,3,2,1,0:T(8,128)(2,1)} %reshape.52), kind=kOutput, calls=%fused_computation.45 | convolution fusion | flops 536870912 | bytes 8454144 | tf_op jit(solution)/shard_map/dot_general | solution.py:39
  56.5 3.6 %fusion.16 = f32[8,16,64,128]{3,2,1,0:T(8,128)S(1)} fusion(bf16[256,128,1,1]{1,0,3,2:T(8,128)(2,1)S(1)} %bitcast.132, bf16[8,16,2,64,256]{4,3,2,1,0:T(8,128)(2,1)} %reshape.52), kind=kOutput, calls=%fused_computation.47 | convolution fusion | flops 536870912 | bytes 8454144 | tf_op jit(solution)/shard_map/dot_general | solution.py:39
  60.2 1.2 fusion.8
  62.4 4.1 %fusion.9 = bf16[8,1,16,64,128]{4,3,2,1,0:T(8,128)(2,1)} fusion(bf16[384,128,1,1]{1,0,3,2:T(8,128)(2,1)S(1)} %bitcast.138, f32[8,16,64,128]{3,2,1,0:T(8,128)S(1)} %fusion.14, f32[8,16,64,128]{3,2,1,0:T(8,128)S(1)} %fusion.8, f32[8,16,64,128]{3,2,1,0:T(8,128)S(1)} %fusion.16, bf16[8,16,64,128]{3,2,1,0:T(8,128)(2,1)S(1)} %copy-done.5, ...), kind=kOutput, calls=%fused_computation.15 | convolution fusion | flops 851443712 | bytes 23166976 | tf_op jit(solution)/shard_map/dot_general | solution.py:42
  66.5 34.5 %all-to-all-done.1 = bf16[8,1,16,64,128]{4,3,2,1,0:T(8,128)(2,1)S(1)} async-done(((bf16[8,1,16,64,128]{4,3,2,1,0:T(8,128)(2,1)}), bf16[8,1,16,64,128]{4,3,2,1,0:T(8,128)(2,1)S(1)}, u32[]{:S(2)}, u32[]{:S(2)}) %all-to-all-start.1) | async-done | bytes 2097184 | tf_op jit(solution)/shard_map/all_to_all | solution.py:156
  101.0 4.5 %all-to-all-start = ((bf16[8,1,16,64,128]{4,3,2,1,0:T(8,128)(2,1)}), bf16[8,1,16,64,128]{4,3,2,1,0:T(8,128)(2,1)}, u32[]{:S(2)}, u32[]{:S(2)}) async-start(bf16[8,1,16,64,128]{4,3,2,1,0:T(8,128)(2,1)} %fusion.9), calls=%async_computation | async-start | bytes 4194304 | tf_op jit(solution)/shard_map/all_to_all | solution.py:156
  105.6 6.5 %copy.14 = bf16[1,8192,256]{1,2,0:T(8,128)(2,1)} copy(bf16[1,8192,256]{2,1,0:T(8,128)(2,1)} %bitcast.125) | data formatting | bytes 8388608 | tf_op jit(solution)/shard_map/reshape | solution.py:150
  112.0 1.1 fusion.19
  113.2 1.7 pad.12.refs_1_
  114.9 1.2 pad_slice_fusion.2
  116.1 2.5 %concatenate.35.refs_0_ = bf16[1,130,64,128]{3,2,1,0:T(8,128)(2,1)} pad(bf16[1,130,63,128]{3,2,1,0:T(8,128)(2,1)S(1)} %get-tuple-element.19, bf16[]{:T(256)} %constant.72.clone.1), padding=0_0x0_0x1_0x0_0 | pad | bytes 4226562 | tf_op jit(solution)/shard_map/concatenate | solution.py:19
  118.6 1.8 concatenate.36.refs_2_
  120.4 36.0 %shard_map.59 = (f32[1,128,64,256]{3,2,1,0:T(8,128)}, f32[1,256,1152]{2,1,0:T(8,128)}) custom-call(bf16[1,130,64,128]{3,2,1,0:T(8,128)(2,1)} %concatenate.35.refs_0_, bf16[1,130,64,128]{3,2,1,0:T(8,128)(2,1)} %pad.12.refs_1_, bf16[1,130,64,128]{3,2,1,0:T(8,128)(2,1)} %concatenate.36.refs_2_, bf16[3,3,128,256]{3,2,1,0:T(8,128)(2,1)} %get-tuple-element.21.refs_3_, ...), custom_call_target="tpu_custom_call" | custom-call | flops 9663676416 | bytes 26345472 | tf_op jit(solution)/shard_map/pallas_call | solution.py:99
  156.4 3.4 %pad_slice_fusion = (bf16[1,130,63,128]{3,2,1,0:T(8,128)(2,1)S(1)}, bf16[1,130,63,128]{3,2,1,0:T(8,128)(2,1)S(1)}) fusion(bf16[1,128,64,128]{3,2,1,0:T(8,128)(2,1)} %bitcast.34), kind=kLoop, calls=%fused_computation.40 | loop fusion | bytes 6290432 | tf_op jit(solution)/shard_map/slice | solution.py:24
  159.9 3.3 %pad.13.refs_1_ = bf16[1,130,64,128]{3,2,1,0:T(8,128)(2,1)} pad(bf16[1,128,64,128]{3,2,1,0:T(8,128)(2,1)} %bitcast.34, bf16[]{:T(256)} %constant.72.clone.1), padding=0_0x1_1x0_0x0_0 | pad | bytes 4227074 | tf_op jit(solution)/shard_map/jit(_pad)/pad | solution.py:83
  163.2 2.5 %concatenate.37.refs_0_ = bf16[1,130,64,128]{3,2,1,0:T(8,128)(2,1)} pad(bf16[1,130,63,128]{3,2,1,0:T(8,128)(2,1)S(1)} %get-tuple-element.17, bf16[]{:T(256)} %constant.72.clone.1), padding=0_0x0_0x1_0x0_0 | pad | bytes 4226562 | tf_op jit(solution)/shard_map/concatenate | solution.py:19
  165.7 1.8 concatenate.38.refs_2_
  167.5 35.9 %shard_map.60 = (bf16[1,128,64,256]{3,2,1,0:T(8,128)(2,1)}, f32[1,256,1152]{2,1,0:T(8,128)}) custom-call(bf16[1,130,64,128]{3,2,1,0:T(8,128)(2,1)} %concatenate.37.refs_0_, bf16[1,130,64,128]{3,2,1,0:T(8,128)(2,1)} %pad.13.refs_1_, bf16[1,130,64,128]{3,2,1,0:T(8,128)(2,1)} %concatenate.38.refs_2_, bf16[3,3,128,256]{3,2,1,0:T(8,128)(2,1)} %get-tuple-element.20.refs_3_, ...), custom_call_target="tpu_custom_call" | custom-call | flops 9663676416 | bytes 26345472 | tf_op jit(solution)/shard_map/pallas_call | solution.py:99
  203.4 1.1 dynamic-slice_bitcast_fusion
  205.2 1.4 collective-permute-done.6
  206.6 1.1 bitcast_add_fusion
  207.8 1.6 collective-permute-start.7
  210.1 7.7 %collective-permute-done.7 = f32[2,2,2,8,1152]{4,3,2,1,0:T(8,128)S(1)} collective-permute-done((f32[2,2,2,8,1152]{4,3,2,1,0:T(8,128)S(1)}, f32[2,2,2,8,1152]{4,3,2,1,0:T(8,128)S(1)}, u32[]{:S(2)}, u32[]{:S(2)}) %collective-permute-start.7) | collective-permute-done | bytes 294944 | tf_op jit(solution)/shard_map/ppermute | solution.py:136
  217.8 1.8 collective-permute-start.8
  219.5 3.7 %collective-permute-done.2 = f32[2,2,2,8,1152]{4,3,2,1,0:T(8,128)S(1)} collective-permute-done((f32[2,2,2,8,1152]{4,3,2,1,0:T(8,128)S(1)}, f32[2,2,2,8,1152]{4,3,2,1,0:T(8,128)S(1)}, u32[]{:S(2)}, u32[]{:S(2)}) %collective-permute-start.2) | collective-permute-done | bytes 294944 | tf_op jit(solution)/shard_map/ppermute | solution.py:136
  223.3 1.8 collective-permute-start.3
  225.1 1.5 collective-permute-start.9
  226.6 1.9 collective-permute-done.3
  228.5 1.8 collective-permute-start.4
  230.3 2.5 %collective-permute-start.10 = (f32[8,1152]{1,0:T(8,128)S(1)}, f32[8,1152]{1,0:T(8,128)S(1)}, u32[]{:S(2)}, u32[]{:S(2)}) collective-permute-start(f32[8,1152]{1,0:T(8,128)S(1)} %dynamic-slice_bitcast_fusion.8), channel_id=1, source_target_pairs={{0,4},{1,5},{2,6},{3,7},{4,0},{5,1},{6,2},{7,3},{8,12},{9,13},{10,... | collective-permute-start | bytes 110600 | tf_op jit(solution)/shard_map/ppermute | solution.py:136
  233.0 3.1 %collective-permute-start.5 = (f32[8,1152]{1,0:T(8,128)S(1)}, f32[8,1152]{1,0:T(8,128)S(1)}, u32[]{:S(2)}, u32[]{:S(2)}) collective-permute-start(f32[8,1152]{1,0:T(8,128)S(1)} %dynamic-slice_bitcast_fusion.9), channel_id=1, source_target_pairs={{0,4},{1,5},{2,6},{3,7},{4,0},{5,1},{6,2},{7,3},{8,12},{9,13},{10,... | collective-permute-start | bytes 110600 | tf_op jit(solution)/shard_map/ppermute | solution.py:136
  236.1 1.9 collective-permute-done.5
  238.0 0.6 pad_maximum_fusion.3
  (55 shorter events, 3.3 us)
Async XLA Ops:
  1.6 17.9 %copy-start.9 = (bf16[3,3,128,256]{3,2,1,0:T(8,128)(2,1)S(1)}, bf16[3,3,128,256]{3,2,1,0:T(8,128)(2,1)}, u32[]{:S(2)}) copy-start(bf16[3,3,128,256]{3,2,1,0:T(8,128)(2,1)} %param.5) | copy-start | bytes 1769476
  1.6 35.2 %collective-permute-start = (bf16[8,1,128,128]{3,2,1,0:T(8,128)(2,1)S(1)}, bf16[8,1,128,128]{3,2,1,0:T(8,128)(2,1)S(1)}, u32[]{:S(2)}, u32[]{:S(2)}) collective-permute-start(bf16[8,1,128,128]{3,2,1,0:T(8,128)(2,1)S(1)} %slice.83), channel_id=1, source_target_pairs={{0,1},{1,2},{2,3},{3,4},{4,5},{5,6},{6,7},{8,9},{9,10},{10,11},{11... | collective-permute-start | bytes 786440 | tf_op jit(solution)/shard_map/ppermute | solution.py:14
  19.5 4.9 %slice-start = ((s8[8388608]{0:T(1024)(128)(4,1)}), s8[4194304]{0:T(1024)(128)(4,1)S(1)}, s32[]{:S(2)}) async-start(s8[8388608]{0:T(1024)(128)(4,1)} %bitcast.121), calls=%async_computation.2 | async-start | bytes 8388608
  20.3 5.4 %slice-start.1 = ((s8[8388608]{0:T(1024)(128)(4,1)}), s8[4194304]{0:T(1024)(128)(4,1)S(1)}, s32[]{:S(2)}) async-start(s8[8388608]{0:T(1024)(128)(4,1)} %bitcast.121), calls=%async_computation.3 | async-start | bytes 8388608
  34.8 5.6 %copy-start.4 = (bf16[8,16,64,128]{3,2,1,0:T(8,128)(2,1)}, bf16[8,16,64,128]{3,2,1,0:T(8,128)(2,1)S(1)}, u32[]{:S(2)}) copy-start(bf16[8,16,64,128]{3,2,1,0:T(8,128)(2,1)S(1)} %slice.109) | copy-start | bytes 6291460
  36.9 3.6 %copy-start = (f32[8,16,64,128]{3,2,1,0:T(8,128)S(1)}, f32[8,16,64,128]{3,2,1,0:T(8,128)}, u32[]{:S(2)}) copy-start(f32[8,16,64,128]{3,2,1,0:T(8,128)} %fusion.13) | copy-start | bytes 12582916
  36.9 4.7 %copy-start.1 = (f32[8,16,64,128]{3,2,1,0:T(8,128)S(1)}, f32[8,16,64,128]{3,2,1,0:T(8,128)}, u32[]{:S(2)}) copy-start(f32[8,16,64,128]{3,2,1,0:T(8,128)} %fusion.15) | copy-start | bytes 12582916
  36.9 5.8 %copy-start.2 = (bf16[8,15,64,256]{3,2,1,0:T(8,128)(2,1)S(1)}, bf16[8,15,64,256]{3,2,1,0:T(8,128)(2,1)}, u32[]{:S(2)}) copy-start(bf16[8,15,64,256]{3,2,1,0:T(8,128)(2,1)} %slice.106) | copy-start | bytes 11796484
  48.2 52.8 %all-to-all-start.1 = ((bf16[8,1,16,64,128]{4,3,2,1,0:T(8,128)(2,1)}), bf16[8,1,16,64,128]{4,3,2,1,0:T(8,128)(2,1)S(1)}, u32[]{:S(2)}, u32[]{:S(2)}) async-start(bf16[8,1,16,64,128]{4,3,2,1,0:T(8,128)(2,1)} %fusion.10), calls=%async_computation.1 | async-start | bytes 4194304 | tf_op jit(solution)/shard_map/all_to_all | solution.py:156
  56.5 3.6 %copy-start.3 = (bf16[8,15,64,256]{3,2,1,0:T(8,128)(2,1)S(1)}, bf16[8,15,64,256]{3,2,1,0:T(8,128)(2,1)}, u32[]{:S(2)}) copy-start(bf16[8,15,64,256]{3,2,1,0:T(8,128)(2,1)} %slice.106) | copy-start | bytes 11796484
  56.5 3.6 %copy-start.10 = (bf16[1,2,128,128]{3,2,1,0:T(8,128)(2,1)S(1)}, bf16[1,2,128,128]{3,2,1,0:T(8,128)(2,1)}, u32[]{:S(2)}) copy-start(bf16[1,2,128,128]{3,2,1,0:T(8,128)(2,1)} %get-tuple-element.26) | copy-start | bytes 196612
  60.1 1.6 copy-start.5
  60.2 2.2 copy-start.6
  101.0 55.4 %all-to-all-start = ((bf16[8,1,16,64,128]{4,3,2,1,0:T(8,128)(2,1)}), bf16[8,1,16,64,128]{4,3,2,1,0:T(8,128)(2,1)}, u32[]{:S(2)}, u32[]{:S(2)}) async-start(bf16[8,1,16,64,128]{4,3,2,1,0:T(8,128)(2,1)} %fusion.9), calls=%async_computation | async-start | bytes 4194304 | tf_op jit(solution)/shard_map/all_to_all | solution.py:156
  105.6 6.5 %copy-start.7 = (bf16[3,3,256,256]{3,2,1,0:T(8,128)(2,1)S(1)}, bf16[3,3,256,256]{3,2,1,0:T(8,128)(2,1)}, u32[]{:S(2)}) copy-start(bf16[3,3,256,256]{3,2,1,0:T(8,128)(2,1)} %param.6) | copy-start | bytes 3538948
  167.5 37.1 %copy-start.8 = (f32[1,256,1152]{2,1,0:T(8,128)S(1)}, f32[1,256,1152]{2,1,0:T(8,128)}, u32[]{:S(2)}) copy-start(f32[1,256,1152]{2,1,0:T(8,128)} %get-tuple-element.12) | copy-start | bytes 3538948
  204.6 2.1 collective-permute-start.6
  204.7 4.7 %collective-permute-start.1 = (f32[2,2,2,2,8,1152]{5,4,3,2,1,0:T(8,128)S(1)}, f32[2,2,2,2,8,1152]{5,4,3,2,1,0:T(8,128)S(1)}, u32[]{:S(2)}, u32[]{:S(2)}) collective-permute-start(f32[2,2,2,2,8,1152]{5,4,3,2,1,0:T(8,128)S(1)} %dynamic-slice_bitcast_fusion.1), channel_id=1, source_target_pairs={{0,8},{1,9},{2,10},{3,11},{4,12},{5,13},{6,14},{7,15},{8,0},{9,1},... | collective-permute-start | bytes 1769480 | tf_op jit(solution)/shard_map/ppermute | solution.py:136
  207.8 9.9 %collective-permute-start.7 = (f32[2,2,2,8,1152]{4,3,2,1,0:T(8,128)S(1)}, f32[2,2,2,8,1152]{4,3,2,1,0:T(8,128)S(1)}, u32[]{:S(2)}, u32[]{:S(2)}) collective-permute-start(f32[2,2,2,8,1152]{4,3,2,1,0:T(8,128)S(1)} %dynamic-slice_bitcast_fusion.2), channel_id=1, source_target_pairs={{0,16},{1,17},{2,18},{3,19},{4,20},{5,21},{6,22},{7,23},{8,24},{9,... | collective-permute-start | bytes 884744 | tf_op jit(solution)/shard_map/ppermute | solution.py:136
  209.5 13.7 %collective-permute-start.2 = (f32[2,2,2,8,1152]{4,3,2,1,0:T(8,128)S(1)}, f32[2,2,2,8,1152]{4,3,2,1,0:T(8,128)S(1)}, u32[]{:S(2)}, u32[]{:S(2)}) collective-permute-start(f32[2,2,2,8,1152]{4,3,2,1,0:T(8,128)S(1)} %dynamic-slice_bitcast_fusion.3), channel_id=1, source_target_pairs={{0,16},{1,17},{2,18},{3,19},{4,20},{5,21},{6,22},{7,23},{8,24},{9,... | collective-permute-start | bytes 884744 | tf_op jit(solution)/shard_map/ppermute | solution.py:136
  217.8 7.3 %collective-permute-start.8 = (f32[2,2,8,1152]{3,2,1,0:T(8,128)S(1)}, f32[2,2,8,1152]{3,2,1,0:T(8,128)S(1)}, u32[]{:S(2)}, u32[]{:S(2)}) collective-permute-start(f32[2,2,8,1152]{3,2,1,0:T(8,128)S(1)} %dynamic-slice_bitcast_fusion.4), channel_id=1, source_target_pairs={{0,1},{1,0},{2,3},{3,2},{4,5},{5,4},{6,7},{7,6},{8,9},{9,8},{10,11... | collective-permute-start | bytes 442376 | tf_op jit(solution)/shard_map/ppermute | solution.py:136
  223.3 5.2 %collective-permute-start.3 = (f32[2,2,8,1152]{3,2,1,0:T(8,128)S(1)}, f32[2,2,8,1152]{3,2,1,0:T(8,128)S(1)}, u32[]{:S(2)}, u32[]{:S(2)}) collective-permute-start(f32[2,2,8,1152]{3,2,1,0:T(8,128)S(1)} %dynamic-slice_bitcast_fusion.5), channel_id=1, source_target_pairs={{0,1},{1,0},{2,3},{3,2},{4,5},{5,4},{6,7},{7,6},{8,9},{9,8},{10,11... | collective-permute-start | bytes 442376 | tf_op jit(solution)/shard_map/ppermute | solution.py:136
  225.1 5.2 %collective-permute-start.9 = (f32[2,8,1152]{2,1,0:T(8,128)S(1)}, f32[2,8,1152]{2,1,0:T(8,128)S(1)}, u32[]{:S(2)}, u32[]{:S(2)}) collective-permute-start(f32[2,8,1152]{2,1,0:T(8,128)S(1)} %dynamic-slice_bitcast_fusion.6), channel_id=1, source_target_pairs={{0,2},{1,3},{2,0},{3,1},{4,6},{5,7},{6,4},{7,5},{8,10},{9,11},{10,... | collective-permute-start | bytes 221192 | tf_op jit(solution)/shard_map/ppermute | solution.py:136
  228.5 4.4 %collective-permute-start.4 = (f32[2,8,1152]{2,1,0:T(8,128)S(1)}, f32[2,8,1152]{2,1,0:T(8,128)S(1)}, u32[]{:S(2)}, u32[]{:S(2)}) collective-permute-start(f32[2,8,1152]{2,1,0:T(8,128)S(1)} %dynamic-slice_bitcast_fusion.7), channel_id=1, source_target_pairs={{0,2},{1,3},{2,0},{3,1},{4,6},{5,7},{6,4},{7,5},{8,10},{9,11},{10,... | collective-permute-start | bytes 221192 | tf_op jit(solution)/shard_map/ppermute | solution.py:136
  230.3 5.7 %collective-permute-start.10 = (f32[8,1152]{1,0:T(8,128)S(1)}, f32[8,1152]{1,0:T(8,128)S(1)}, u32[]{:S(2)}, u32[]{:S(2)}) collective-permute-start(f32[8,1152]{1,0:T(8,128)S(1)} %dynamic-slice_bitcast_fusion.8), channel_id=1, source_target_pairs={{0,4},{1,5},{2,6},{3,7},{4,0},{5,1},{6,2},{7,3},{8,12},{9,13},{10,... | collective-permute-start | bytes 110600 | tf_op jit(solution)/shard_map/ppermute | solution.py:136
  233.0 5.0 %collective-permute-start.5 = (f32[8,1152]{1,0:T(8,128)S(1)}, f32[8,1152]{1,0:T(8,128)S(1)}, u32[]{:S(2)}, u32[]{:S(2)}) collective-permute-start(f32[8,1152]{1,0:T(8,128)S(1)} %dynamic-slice_bitcast_fusion.9), channel_id=1, source_target_pairs={{0,4},{1,5},{2,6},{3,7},{4,0},{5,1},{6,2},{7,3},{8,12},{9,13},{10,... | collective-permute-start | bytes 110600 | tf_op jit(solution)/shard_map/ppermute | solution.py:136

commit v3 on v2

--- a/solution.py
+++ b/solution.py
@@ -45,7 +45,7 @@
     return jnp.maximum(total, 0.0).astype(jnp.bfloat16)
 
 
-def second_kernel(*refs, rows, carry):
+def second_kernel(*refs, rows, carry, group):
     if carry:
         left_ref, mid_ref, right_ref, weight_ref, grad_ref, prev_ref, out_ref, wgrad_ref = refs
     else:
@@ -53,25 +53,30 @@
     step = pl.program_id(1)
     _, width, outputs = out_ref.shape
     inputs = mid_ref.shape[-1]
+    sources = (left_ref, mid_ref, right_ref)
     grad_t = grad_ref[...]
     if carry:
         acc = prev_ref[...].reshape(rows * width, outputs)
     else:
         acc = jnp.zeros((rows * width, outputs), jnp.float32)
-    for tap_row in range(3):
-        for tap_col, src in enumerate((left_ref, mid_ref, right_ref)):
-            window = src[pl.ds(step * rows + tap_row, rows)].reshape(rows * width, inputs)
-            acc = acc + jnp.dot(window, weight_ref[tap_row, tap_col], preferred_element_type=jnp.float32)
-            term = jnp.dot(grad_t, window, preferred_element_type=jnp.float32)
-            tap = tap_row * 3 + tap_col
+    for first in range(0, 9, group):
+        taps = range(first, min(first + group, 9))
+        windows = [
+            sources[tap % 3][pl.ds(step * rows + tap // 3, rows)].reshape(rows * width, inputs)
+            for tap in taps
+        ]
+        window = windows[0] if len(windows) == 1 else jnp.concatenate(windows, axis=-1)
+        lanes = slice(first * inputs, (first + len(windows)) * inputs)
+        acc = acc + jnp.dot(window, weight_ref[lanes, :], preferred_element_type=jnp.float32)
+        term = jnp.dot(grad_t, window, preferred_element_type=jnp.float32)
 
-            @pl.when(step == 0)
-            def _():
-                wgrad_ref[:, tap * inputs:(tap + 1) * inputs] = term
+        @pl.when(step == 0)
+        def _():
+            wgrad_ref[:, lanes] = term
 
-            @pl.when(step > 0)
-            def _():
-                wgrad_ref[:, tap * inputs:(tap + 1) * inputs] += term
+        @pl.when(step > 0)
+        def _():
+            wgrad_ref[:, lanes] += term
 
     out_ref[...] = acc.astype(out_ref.dtype).reshape(rows, width, outputs)
 
@@ -88,16 +93,16 @@
         full,
         full,
         full,
-        pl.BlockSpec((3, 3, inputs, outputs), lambda n, i: (0, 0, 0, 0)),
+        pl.BlockSpec((9 * inputs, outputs), lambda n, i: (0, 0)),
         pl.BlockSpec((None, outputs, rows * out_cols), lambda n, i: (n, 0, i)),
     ]
-    operands = [*shifted, weight, grad_t]
+    operands = [*shifted, weight.reshape(9 * inputs, outputs), grad_t]
     if prev is not None:
         in_specs.append(block)
         operands.append(prev)
     flops = 4 * owned * out_rows * out_cols * 9 * inputs * outputs
     return pl.pallas_call(
-        functools.partial(second_kernel, rows=rows, carry=prev is not None),
+        functools.partial(second_kernel, rows=rows, carry=prev is not None, group=max(1, 256 // inputs)),
         grid=(owned, out_rows // rows),
         in_specs=in_specs,
         out_specs=[block, pl.BlockSpec((None, outputs, 9 * inputs), lambda n, i: (n, 0, 0))],

time: 240 us -> 224 us (0.933)
  Pallas kernels: 72 us -> 47.6 us
  waiting for transfers between devices: 51.2 us -> 66.6 us
  starting transfers between devices: 29.5 us -> 22.5 us
    pallas_call x2, Pallas kernels: 72 us -> 47.6 us  [second_stage(): pl.pallas_call(functools.partial(second_kernel, rows=rows, carry=prev is...]
    all_to_all x2, waiting for transfers between devices: 34.5 us -> 43.1 us  [local(): lax.all_to_all(local_hidden.reshape(tiles, owned, half_rows, width // 2,...]
    ppermute x10, starting transfers between devices: 15.1 us -> 8.15 us  [halving_reduce_scatter(): buf = keep + lax.ppermute(send, axes, pairs)]
    ppermute x10, waiting for transfers between devices: 16.7 us -> 23.5 us  [halving_reduce_scatter(): buf = keep + lax.ppermute(send, axes, pairs)]
  transfers between devices with their start and end apart: 13 -> 13, of which waited for: 7 -> 10; matrix products, arithmetic and copies ran while one was open for 24% -> 26% of each run, Pallas kernels for 15% -> 11%
where the time goes in v3:
time: 224 us; the launch traced here: 223 us
  waiting for transfers between devices  66.6 us (30%)
  local copies, waits for them, and re-layouts  55.1 us (25%)
  Pallas kernels  47.6 us (21%)
  matrix products  27.9 us (12%)
  starting transfers between devices  22.5 us (10%)
    pallas_call x2, Pallas kernels, second_stage(): pl.pallas_call(functools.partial(second_kernel, rows=rows, carry=prev is...  47.6 us
    all_to_all x2, waiting for transfers between devices, local(): lax.all_to_all(local_hidden.reshape(tiles, owned, half_rows, width // 2,...  43.1 us
    ppermute x10, waiting for transfers between devices, halving_reduce_scatter(): buf = keep + lax.ppermute(send, axes, pairs)  23.5 us
    dot_general x6, matrix products, first_conv(): jnp.dot(sources[tap_row], wide_kernel, preferred_element_type=jnp.float32)  18.3 us
    reshape x1, local copies, waits for them, and re-layouts, first_conv(): paired = source.reshape(images, rows // 2, 2, width // 2, 2 * inputs)  12.9 us
    dot_general x2, matrix products, first_conv(): jnp.dot(shift_cols_right(halves), narrow_kernel, preferred_element_type=j...  9.62 us
    all_to_all x2, starting transfers between devices, local(): lax.all_to_all(local_hidden.reshape(tiles, owned, half_rows, width // 2,...  9.39 us
    ppermute x10, starting transfers between devices, halving_reduce_scatter(): buf = keep + lax.ppermute(send, axes, pairs)  8.15 us
  transfers between devices with their start and end apart: 13, of which 10 were waited for; matrix products, arithmetic and copies ran while one was open for 26% of the time, Pallas kernels for 11%

profile of v3, /device:TPU:0, one launch (start us, length us, event | category | flops | bytes accessed | tf_op | source)
XLA Modules:
  0.0 222.8 jit_solution(3954804549495708742)
XLA Ops:
  0.6 1.0 slice.83
  1.6 5.0 %collective-permute-start = (bf16[8,1,128,128]{3,2,1,0:T(8,128)(2,1)S(1)}, bf16[8,1,128,128]{3,2,1,0:T(8,128)(2,1)S(1)}, u32[]{:S(2)}, u32[]{:S(2)}) collective-permute-start(bf16[8,1,128,128]{3,2,1,0:T(8,128)(2,1)S(1)} %slice.83), channel_id=1, source_target_pairs={{0,1},{1,2},{2,3},{3,4},{4,5},{5,6},{6,7},{8,9},{9,10},{10,11},{11... | collective-permute-start | bytes 786440 | tf_op jit(solution)/shard_map/ppermute | solution.py:14
  6.6 12.9 %reshape.58 = bf16[8,16,2,64,256]{4,3,2,1,0:T(8,128)(2,1)} reshape(bf16[8,32,128,128]{3,2,1,0:T(8,128)(2,1)} %param.4) | data formatting | bytes 16777216 | tf_op jit(solution)/shard_map/reshape | solution.py:30
  19.5 0.7 fusion.20
  20.3 4.2 %slice_bitcast_fusion = (bf16[8,16,64,256]{3,2,1,0:T(8,128)(2,1)S(1)}, bf16[8,16,64,256]{3,2,1,0:T(8,128)(2,1)S(1)}) fusion(bf16[8,16,2,64,256]{4,3,2,1,0:T(8,128)(2,1)} %reshape.58), kind=kLoop, calls=%fused_computation.8 | loop fusion | bytes 16777216 | tf_op jit(solution)/shard_map/squeeze | solution.py:31
  24.5 1.2 slice-done.1
  25.7 3.3 %fusion.13 = f32[8,16,64,128]{3,2,1,0:T(8,128)} fusion(bf16[256,128,1,1]{1,0,3,2:T(8,128)(2,1)S(1)} %bitcast.139, bf16[8,16,2,64,256]{4,3,2,1,0:T(8,128)(2,1)S(1)} %bitcast.124), kind=kOutput, calls=%fused_computation.44 | convolution fusion | flops 536870912 | bytes 8454144 | tf_op jit(solution)/shard_map/dot_general | solution.py:39
  29.0 3.3 %fusion.15 = f32[8,16,64,128]{3,2,1,0:T(8,128)} fusion(bf16[256,128,1,1]{1,0,3,2:T(8,128)(2,1)S(1)} %bitcast.138, bf16[8,16,2,64,256]{4,3,2,1,0:T(8,128)(2,1)S(1)} %bitcast.124), kind=kOutput, calls=%fused_computation.46 | convolution fusion | flops 536870912 | bytes 8454144 | tf_op jit(solution)/shard_map/dot_general | solution.py:39
  32.2 2.1 slice.106
  34.8 1.9 slice.108
  36.9 3.5 %fusion.7 = f32[8,16,64,128]{3,2,1,0:T(8,128)S(1)} fusion(bf16[256,128,1,1]{1,0,3,2:T(8,128)(2,1)} %bitcast.145, bf16[8,15,64,256]{3,2,1,0:T(8,128)(2,1)} %slice.106, bf16[8,1,64,256]{3,2,1,0:T(8,128)(2,1)S(1)} %reshape.57), kind=kOutput, calls=%fused_computation.13 | convolution fusion | flops 538968064 | bytes 8454144 | tf_op jit(solution)/shard_map/dot_general | solution.py:39
  40.5 1.1 copy-done.1
  41.6 1.1 copy-done.2
  42.7 5.5 %fusion.10 = bf16[8,1,16,64,128]{4,3,2,1,0:T(8,128)(2,1)} fusion(bf16[384,128,1,1]{1,0,3,2:T(8,128)(2,1)S(1)} %bitcast.143, f32[8,16,64,128]{3,2,1,0:T(8,128)S(1)} %copy-done, f32[8,16,64,128]{3,2,1,0:T(8,128)S(1)} %fusion.7, f32[8,16,64,128]{3,2,1,0:T(8,128)S(1)} %copy-done.1, bf16[8,16,64,128]{3,2,1,0:T(8,128)(2,1)S(1)} %slice.109, ...), kind=kOutput, calls=%fused_computation.16 | convolution fusion | flops 851443712 | bytes 23166976 | tf_op jit(solution)/shard_map/dot_general | solution.py:42
  48.2 4.9 %all-to-all-start.1 = ((bf16[8,1,16,64,128]{4,3,2,1,0:T(8,128)(2,1)}), bf16[8,1,16,64,128]{4,3,2,1,0:T(8,128)(2,1)S(1)}, u32[]{:S(2)}, u32[]{:S(2)}) async-start(bf16[8,1,16,64,128]{4,3,2,1,0:T(8,128)(2,1)} %fusion.10), calls=%async_computation.1 | async-start | bytes 4194304 | tf_op jit(solution)/shard_map/all_to_all | solution.py:161
  53.1 3.4 %fusion.14 = f32[8,16,64,128]{3,2,1,0:T(8,128)S(1)} fusion(bf16[256,128,1,1]{1,0,3,2:T(8,128)(2,1)S(1)} %bitcast.137, bf16[8,16,2,64,256]{4,3,2,1,0:T(8,128)(2,1)} %reshape.58), kind=kOutput, calls=%fused_computation.45 | convolution fusion | flops 536870912 | bytes 8454144 | tf_op jit(solution)/shard_map/dot_general | solution.py:39
  56.5 3.6 %fusion.16 = f32[8,16,64,128]{3,2,1,0:T(8,128)S(1)} fusion(bf16[256,128,1,1]{1,0,3,2:T(8,128)(2,1)S(1)} %bitcast.136, bf16[8,16,2,64,256]{4,3,2,1,0:T(8,128)(2,1)} %reshape.58), kind=kOutput, calls=%fused_computation.47 | convolution fusion | flops 536870912 | bytes 8454144 | tf_op jit(solution)/shard_map/dot_general | solution.py:39
  60.2 1.2 fusion.8
  62.4 4.1 %fusion.9 = bf16[8,1,16,64,128]{4,3,2,1,0:T(8,128)(2,1)} fusion(bf16[384,128,1,1]{1,0,3,2:T(8,128)(2,1)S(1)} %bitcast.142, f32[8,16,64,128]{3,2,1,0:T(8,128)S(1)} %fusion.14, f32[8,16,64,128]{3,2,1,0:T(8,128)S(1)} %fusion.8, f32[8,16,64,128]{3,2,1,0:T(8,128)S(1)} %fusion.16, bf16[8,16,64,128]{3,2,1,0:T(8,128)(2,1)S(1)} %copy-done.5, ...), kind=kOutput, calls=%fused_computation.15 | convolution fusion | flops 851443712 | bytes 23166976 | tf_op jit(solution)/shard_map/dot_general | solution.py:42
  66.5 34.5 %all-to-all-done.1 = bf16[8,1,16,64,128]{4,3,2,1,0:T(8,128)(2,1)S(1)} async-done(((bf16[8,1,16,64,128]{4,3,2,1,0:T(8,128)(2,1)}), bf16[8,1,16,64,128]{4,3,2,1,0:T(8,128)(2,1)S(1)}, u32[]{:S(2)}, u32[]{:S(2)}) %all-to-all-start.1) | async-done | bytes 2097184 | tf_op jit(solution)/shard_map/all_to_all | solution.py:161
  101.0 4.5 %all-to-all-start = ((bf16[8,1,16,64,128]{4,3,2,1,0:T(8,128)(2,1)}), bf16[8,1,16,64,128]{4,3,2,1,0:T(8,128)(2,1)}, u32[]{:S(2)}, u32[]{:S(2)}) async-start(bf16[8,1,16,64,128]{4,3,2,1,0:T(8,128)(2,1)} %fusion.9), calls=%async_computation | async-start | bytes 4194304 | tf_op jit(solution)/shard_map/all_to_all | solution.py:161
  105.6 6.5 %copy.14 = bf16[1,8192,256]{1,2,0:T(8,128)(2,1)} copy(bf16[1,8192,256]{2,1,0:T(8,128)(2,1)} %bitcast.127) | data formatting | bytes 8388608 | tf_op jit(solution)/shard_map/reshape | solution.py:155
  112.0 1.1 fusion.19
  113.2 1.7 pad.12.refs_1_
  114.9 1.2 pad_slice_fusion.2
  116.1 2.5 %concatenate.35.refs_0_ = bf16[1,130,64,128]{3,2,1,0:T(8,128)(2,1)} pad(bf16[1,130,63,128]{3,2,1,0:T(8,128)(2,1)S(1)} %get-tuple-element.19, bf16[]{:T(256)} %constant.72.clone.1), padding=0_0x0_0x1_0x0_0 | pad | bytes 4226562 | tf_op jit(solution)/shard_map/concatenate | solution.py:19
  118.6 1.8 concatenate.36.refs_2_
  120.4 24.3 %shard_map.59 = (f32[1,128,64,256]{3,2,1,0:T(8,128)}, f32[1,256,1152]{2,1,0:T(8,128)}) custom-call(bf16[1,130,64,128]{3,2,1,0:T(8,128)(2,1)} %concatenate.35.refs_0_, bf16[1,130,64,128]{3,2,1,0:T(8,128)(2,1)} %pad.12.refs_1_, bf16[1,130,64,128]{3,2,1,0:T(8,128)(2,1)} %concatenate.36.refs_2_, bf16[1152,256]{1,0:T(8,128)(2,1)} %bitcast.135, ...), custom_call_target="tpu_custom_call" | custom-call | flops 9663676416 | bytes 26345472 | tf_op jit(solution)/shard_map/pallas_call | solution.py:104
  144.7 8.6 %all-to-all-done = bf16[8,1,16,64,128]{4,3,2,1,0:T(8,128)(2,1)} async-done(((bf16[8,1,16,64,128]{4,3,2,1,0:T(8,128)(2,1)}), bf16[8,1,16,64,128]{4,3,2,1,0:T(8,128)(2,1)}, u32[]{:S(2)}, u32[]{:S(2)}) %all-to-all-start) | async-done | bytes 2097184 | tf_op jit(solution)/shard_map/all_to_all | solution.py:161
  153.3 3.4 %pad_slice_fusion = (bf16[1,130,63,128]{3,2,1,0:T(8,128)(2,1)S(1)}, bf16[1,130,63,128]{3,2,1,0:T(8,128)(2,1)S(1)}) fusion(bf16[1,128,64,128]{3,2,1,0:T(8,128)(2,1)} %bitcast.35), kind=kLoop, calls=%fused_computation.40 | loop fusion | bytes 6290432 | tf_op jit(solution)/shard_map/slice | solution.py:24
  156.7 3.3 %pad.13.refs_1_ = bf16[1,130,64,128]{3,2,1,0:T(8,128)(2,1)} pad(bf16[1,128,64,128]{3,2,1,0:T(8,128)(2,1)} %bitcast.35, bf16[]{:T(256)} %constant.72.clone.1), padding=0_0x1_1x0_0x0_0 | pad | bytes 4227074 | tf_op jit(solution)/shard_map/jit(_pad)/pad | solution.py:88
  160.1 2.5 %concatenate.37.refs_0_ = bf16[1,130,64,128]{3,2,1,0:T(8,128)(2,1)} pad(bf16[1,130,63,128]{3,2,1,0:T(8,128)(2,1)S(1)} %get-tuple-element.17, bf16[]{:T(256)} %constant.72.clone.1), padding=0_0x0_0x1_0x0_0 | pad | bytes 4226562 | tf_op jit(solution)/shard_map/concatenate | solution.py:19
  162.5 1.8 concatenate.38.refs_2_
  164.4 23.4 %shard_map.60 = (bf16[1,128,64,256]{3,2,1,0:T(8,128)(2,1)}, f32[1,256,1152]{2,1,0:T(8,128)}) custom-call(bf16[1,130,64,128]{3,2,1,0:T(8,128)(2,1)} %concatenate.37.refs_0_, bf16[1,130,64,128]{3,2,1,0:T(8,128)(2,1)} %pad.13.refs_1_, bf16[1,130,64,128]{3,2,1,0:T(8,128)(2,1)} %concatenate.38.refs_2_, bf16[1152,256]{1,0:T(8,128)(2,1)} %bitcast.134, ...), custom_call_target="tpu_custom_call" | custom-call | flops 9663676416 | bytes 26345472 | tf_op jit(solution)/shard_map/pallas_call | solution.py:104
  187.7 1.1 dynamic-slice_bitcast_fusion
  189.5 1.4 collective-permute-done.6
  190.9 1.1 bitcast_add_fusion
  192.1 1.6 collective-permute-start.7
  194.3 7.7 %collective-permute-done.7 = f32[2,2,2,8,1152]{4,3,2,1,0:T(8,128)S(1)} collective-permute-done((f32[2,2,2,8,1152]{4,3,2,1,0:T(8,128)S(1)}, f32[2,2,2,8,1152]{4,3,2,1,0:T(8,128)S(1)}, u32[]{:S(2)}, u32[]{:S(2)}) %collective-permute-start.7) | collective-permute-done | bytes 294944 | tf_op jit(solution)/shard_map/ppermute | solution.py:141
  202.0 1.4 collective-permute-start.8
  203.5 4.0 %collective-permute-done.2 = f32[2,2,2,8,1152]{4,3,2,1,0:T(8,128)S(1)} collective-permute-done((f32[2,2,2,8,1152]{4,3,2,1,0:T(8,128)S(1)}, f32[2,2,2,8,1152]{4,3,2,1,0:T(8,128)S(1)}, u32[]{:S(2)}, u32[]{:S(2)}) %collective-permute-start.2) | collective-permute-done | bytes 294944 | tf_op jit(solution)/shard_map/ppermute | solution.py:141
  207.6 1.4 collective-permute-start.3
  209.1 3.7 %collective-permute-done.3 = f32[2,2,8,1152]{3,2,1,0:T(8,128)S(1)} collective-permute-done((f32[2,2,8,1152]{3,2,1,0:T(8,128)S(1)}, f32[2,2,8,1152]{3,2,1,0:T(8,128)S(1)}, u32[]{:S(2)}, u32[]{:S(2)}) %collective-permute-start.3) | collective-permute-done | bytes 147488 | tf_op jit(solution)/shard_map/ppermute | solution.py:141
  213.5 1.9 collective-permute-start.10
  215.4 1.8 collective-permute-done.4
  217.7 1.0 collective-permute-done.10
  218.7 3.4 %collective-permute-done.5 = f32[8,1152]{1,0:T(8,128)S(1)} collective-permute-done((f32[8,1152]{1,0:T(8,128)S(1)}, f32[8,1152]{1,0:T(8,128)S(1)}, u32[]{:S(2)}, u32[]{:S(2)}) %collective-permute-start.5) | collective-permute-done | bytes 36896 | tf_op jit(solution)/shard_map/ppermute | solution.py:141
  222.2 0.6 pad_maximum_fusion.3
  (55 shorter events, 4.4 us)
Async XLA Ops:
  1.6 17.9 %copy-start.9 = (bf16[3,3,128,256]{3,2,1,0:T(8,128)(2,1)S(1)}, bf16[3,3,128,256]{3,2,1,0:T(8,128)(2,1)}, u32[]{:S(2)}) copy-start(bf16[3,3,128,256]{3,2,1,0:T(8,128)(2,1)} %param.5) | copy-start | bytes 1769476
  1.6 35.2 %collective-permute-start = (bf16[8,1,128,128]{3,2,1,0:T(8,128)(2,1)S(1)}, bf16[8,1,128,128]{3,2,1,0:T(8,128)(2,1)S(1)}, u32[]{:S(2)}, u32[]{:S(2)}) collective-permute-start(bf16[8,1,128,128]{3,2,1,0:T(8,128)(2,1)S(1)} %slice.83), channel_id=1, source_target_pairs={{0,1},{1,2},{2,3},{3,4},{4,5},{5,6},{6,7},{8,9},{9,10},{10,11},{11... | collective-permute-start | bytes 786440 | tf_op jit(solution)/shard_map/ppermute | solution.py:14
  19.5 4.9 %slice-start = ((s8[8388608]{0:T(1024)(128)(4,1)}), s8[4194304]{0:T(1024)(128)(4,1)S(1)}, s32[]{:S(2)}) async-start(s8[8388608]{0:T(1024)(128)(4,1)} %bitcast.123), calls=%async_computation.2 | async-start | bytes 8388608
  20.3 5.4 %slice-start.1 = ((s8[8388608]{0:T(1024)(128)(4,1)}), s8[4194304]{0:T(1024)(128)(4,1)S(1)}, s32[]{:S(2)}) async-start(s8[8388608]{0:T(1024)(128)(4,1)} %bitcast.123), calls=%async_computation.3 | async-start | bytes 8388608
  34.8 5.6 %copy-start.4 = (bf16[8,16,64,128]{3,2,1,0:T(8,128)(2,1)}, bf16[8,16,64,128]{3,2,1,0:T(8,128)(2,1)S(1)}, u32[]{:S(2)}) copy-start(bf16[8,16,64,128]{3,2,1,0:T(8,128)(2,1)S(1)} %slice.109) | copy-start | bytes 6291460
  36.9 3.6 %copy-start = (f32[8,16,64,128]{3,2,1,0:T(8,128)S(1)}, f32[8,16,64,128]{3,2,1,0:T(8,128)}, u32[]{:S(2)}) copy-start(f32[8,16,64,128]{3,2,1,0:T(8,128)} %fusion.13) | copy-start | bytes 12582916
  36.9 4.7 %copy-start.1 = (f32[8,16,64,128]{3,2,1,0:T(8,128)S(1)}, f32[8,16,64,128]{3,2,1,0:T(8,128)}, u32[]{:S(2)}) copy-start(f32[8,16,64,128]{3,2,1,0:T(8,128)} %fusion.15) | copy-start | bytes 12582916
  36.9 5.8 %copy-start.2 = (bf16[8,15,64,256]{3,2,1,0:T(8,128)(2,1)S(1)}, bf16[8,15,64,256]{3,2,1,0:T(8,128)(2,1)}, u32[]{:S(2)}) copy-start(bf16[8,15,64,256]{3,2,1,0:T(8,128)(2,1)} %slice.106) | copy-start | bytes 11796484
  48.2 52.8 %all-to-all-start.1 = ((bf16[8,1,16,64,128]{4,3,2,1,0:T(8,128)(2,1)}), bf16[8,1,16,64,128]{4,3,2,1,0:T(8,128)(2,1)S(1)}, u32[]{:S(2)}, u32[]{:S(2)}) async-start(bf16[8,1,16,64,128]{4,3,2,1,0:T(8,128)(2,1)} %fusion.10), calls=%async_computation.1 | async-start | bytes 4194304 | tf_op jit(solution)/shard_map/all_to_all | solution.py:161
  56.5 3.6 %copy-start.3 = (bf16[8,15,64,256]{3,2,1,0:T(8,128)(2,1)S(1)}, bf16[8,15,64,256]{3,2,1,0:T(8,128)(2,1)}, u32[]{:S(2)}) copy-start(bf16[8,15,64,256]{3,2,1,0:T(8,128)(2,1)} %slice.106) | copy-start | bytes 11796484
  56.5 3.6 %copy-start.10 = (bf16[1,2,128,128]{3,2,1,0:T(8,128)(2,1)S(1)}, bf16[1,2,128,128]{3,2,1,0:T(8,128)(2,1)}, u32[]{:S(2)}) copy-start(bf16[1,2,128,128]{3,2,1,0:T(8,128)(2,1)} %get-tuple-element.26) | copy-start | bytes 196612
  60.1 1.6 copy-start.5
  60.2 2.2 copy-start.6
  101.0 52.3 %all-to-all-start = ((bf16[8,1,16,64,128]{4,3,2,1,0:T(8,128)(2,1)}), bf16[8,1,16,64,128]{4,3,2,1,0:T(8,128)(2,1)}, u32[]{:S(2)}, u32[]{:S(2)}) async-start(bf16[8,1,16,64,128]{4,3,2,1,0:T(8,128)(2,1)} %fusion.9), calls=%async_computation | async-start | bytes 4194304 | tf_op jit(solution)/shard_map/all_to_all | solution.py:161
  105.6 6.5 %copy-start.7 = (bf16[3,3,256,256]{3,2,1,0:T(8,128)(2,1)S(1)}, bf16[3,3,256,256]{3,2,1,0:T(8,128)(2,1)}, u32[]{:S(2)}) copy-start(bf16[3,3,256,256]{3,2,1,0:T(8,128)(2,1)} %param.6) | copy-start | bytes 3538948
  164.4 24.6 %copy-start.8 = (f32[1,256,1152]{2,1,0:T(8,128)S(1)}, f32[1,256,1152]{2,1,0:T(8,128)}, u32[]{:S(2)}) copy-start(f32[1,256,1152]{2,1,0:T(8,128)} %get-tuple-element.12) | copy-start | bytes 3538948
  188.8 2.1 collective-permute-start.6
  189.0 4.7 %collective-permute-start.1 = (f32[2,2,2,2,8,1152]{5,4,3,2,1,0:T(8,128)S(1)}, f32[2,2,2,2,8,1152]{5,4,3,2,1,0:T(8,128)S(1)}, u32[]{:S(2)}, u32[]{:S(2)}) collective-permute-start(f32[2,2,2,2,8,1152]{5,4,3,2,1,0:T(8,128)S(1)} %dynamic-slice_bitcast_fusion.1), channel_id=1, source_target_pairs={{0,8},{1,9},{2,10},{3,11},{4,12},{5,13},{6,14},{7,15},{8,0},{9,1},... | collective-permute-start | bytes 1769480 | tf_op jit(solution)/shard_map/ppermute | solution.py:141
  192.1 9.9 %collective-permute-start.7 = (f32[2,2,2,8,1152]{4,3,2,1,0:T(8,128)S(1)}, f32[2,2,2,8,1152]{4,3,2,1,0:T(8,128)S(1)}, u32[]{:S(2)}, u32[]{:S(2)}) collective-permute-start(f32[2,2,2,8,1152]{4,3,2,1,0:T(8,128)S(1)} %dynamic-slice_bitcast_fusion.2), channel_id=1, source_target_pairs={{0,16},{1,17},{2,18},{3,19},{4,20},{5,21},{6,22},{7,23},{8,24},{9,... | collective-permute-start | bytes 884744 | tf_op jit(solution)/shard_map/ppermute | solution.py:141
  193.7 13.8 %collective-permute-start.2 = (f32[2,2,2,8,1152]{4,3,2,1,0:T(8,128)S(1)}, f32[2,2,2,8,1152]{4,3,2,1,0:T(8,128)S(1)}, u32[]{:S(2)}, u32[]{:S(2)}) collective-permute-start(f32[2,2,2,8,1152]{4,3,2,1,0:T(8,128)S(1)} %dynamic-slice_bitcast_fusion.3), channel_id=1, source_target_pairs={{0,16},{1,17},{2,18},{3,19},{4,20},{5,21},{6,22},{7,23},{8,24},{9,... | collective-permute-start | bytes 884744 | tf_op jit(solution)/shard_map/ppermute | solution.py:141
  202.0 6.9 %collective-permute-start.8 = (f32[2,2,8,1152]{3,2,1,0:T(8,128)S(1)}, f32[2,2,8,1152]{3,2,1,0:T(8,128)S(1)}, u32[]{:S(2)}, u32[]{:S(2)}) collective-permute-start(f32[2,2,8,1152]{3,2,1,0:T(8,128)S(1)} %dynamic-slice_bitcast_fusion.4), channel_id=1, source_target_pairs={{0,1},{1,0},{2,3},{3,2},{4,5},{5,4},{6,7},{7,6},{8,9},{9,8},{10,11... | collective-permute-start | bytes 442376 | tf_op jit(solution)/shard_map/ppermute | solution.py:141
  207.6 5.2 %collective-permute-start.3 = (f32[2,2,8,1152]{3,2,1,0:T(8,128)S(1)}, f32[2,2,8,1152]{3,2,1,0:T(8,128)S(1)}, u32[]{:S(2)}, u32[]{:S(2)}) collective-permute-start(f32[2,2,8,1152]{3,2,1,0:T(8,128)S(1)} %dynamic-slice_bitcast_fusion.5), channel_id=1, source_target_pairs={{0,1},{1,0},{2,3},{3,2},{4,5},{5,4},{6,7},{7,6},{8,9},{9,8},{10,11... | collective-permute-start | bytes 442376 | tf_op jit(solution)/shard_map/ppermute | solution.py:141
  209.0 4.4 %collective-permute-start.9 = (f32[2,8,1152]{2,1,0:T(8,128)S(1)}, f32[2,8,1152]{2,1,0:T(8,128)S(1)}, u32[]{:S(2)}, u32[]{:S(2)}) collective-permute-start(f32[2,8,1152]{2,1,0:T(8,128)S(1)} %dynamic-slice_bitcast_fusion.6), channel_id=1, source_target_pairs={{0,2},{1,3},{2,0},{3,1},{4,6},{5,7},{6,4},{7,5},{8,10},{9,11},{10,... | collective-permute-start | bytes 221192 | tf_op jit(solution)/shard_map/ppermute | solution.py:141
  212.8 4.4 %collective-permute-start.4 = (f32[2,8,1152]{2,1,0:T(8,128)S(1)}, f32[2,8,1152]{2,1,0:T(8,128)S(1)}, u32[]{:S(2)}, u32[]{:S(2)}) collective-permute-start(f32[2,8,1152]{2,1,0:T(8,128)S(1)} %dynamic-slice_bitcast_fusion.7), channel_id=1, source_target_pairs={{0,2},{1,3},{2,0},{3,1},{4,6},{5,7},{6,4},{7,5},{8,10},{9,11},{10,... | collective-permute-start | bytes 221192 | tf_op jit(solution)/shard_map/ppermute | solution.py:141
  213.5 5.3 %collective-permute-start.10 = (f32[8,1152]{1,0:T(8,128)S(1)}, f32[8,1152]{1,0:T(8,128)S(1)}, u32[]{:S(2)}, u32[]{:S(2)}) collective-permute-start(f32[8,1152]{1,0:T(8,128)S(1)} %dynamic-slice_bitcast_fusion.8), channel_id=1, source_target_pairs={{0,4},{1,5},{2,6},{3,7},{4,0},{5,1},{6,2},{7,3},{8,12},{9,13},{10,... | collective-permute-start | bytes 110600 | tf_op jit(solution)/shard_map/ppermute | solution.py:141
  217.3 4.9 %collective-permute-start.5 = (f32[8,1152]{1,0:T(8,128)S(1)}, f32[8,1152]{1,0:T(8,128)S(1)}, u32[]{:S(2)}, u32[]{:S(2)}) collective-permute-start(f32[8,1152]{1,0:T(8,128)S(1)} %dynamic-slice_bitcast_fusion.9), channel_id=1, source_target_pairs={{0,4},{1,5},{2,6},{3,7},{4,0},{5,1},{6,2},{7,3},{8,12},{9,13},{10,... | collective-permute-start | bytes 110600 | tf_op jit(solution)/shard_map/ppermute | solution.py:141

commit v4 on v3

--- a/solution.py
+++ b/solution.py
@@ -43,6 +43,56 @@
         shift_cols_right(halves), narrow_kernel, preferred_element_type=jnp.float32
     )
     return jnp.maximum(total, 0.0).astype(jnp.bfloat16)
+
+
+def first_kernel(x_ref, up_ref, w_ref, low_ref, high_ref, scratch):
+    rows, width, inputs = x_ref.shape
+    out_rows, out_cols = rows // 2, width // 2
+    scratch[0] = up_ref[0].astype(jnp.float32)
+    scratch[1:] = x_ref[...].astype(jnp.float32)
+    first_col = lax.broadcasted_iota(jnp.int32, (out_rows, out_cols, inputs), 1) == 0
+    pieces = []
+    for tap_row in range(3):
+        even = scratch[pl.ds(tap_row, out_rows, stride=2), pl.ds(0, out_cols, stride=2), :]
+        odd = scratch[pl.ds(tap_row, out_rows, stride=2), pl.ds(1, out_cols, stride=2), :]
+        left = jnp.where(first_col, 0.0, pltpu.roll(odd, 1, 1))
+        pieces += [even, odd, left]
+    patches = jnp.concatenate(
+        [p.astype(jnp.bfloat16).reshape(out_rows * out_cols, inputs) for p in pieces], axis=-1
+    )
+    total = jnp.dot(patches, w_ref[...], preferred_element_type=jnp.float32)
+    hidden = jnp.maximum(total, 0.0).astype(jnp.bfloat16).reshape(out_rows, out_cols, -1)
+    half = low_ref.shape[-1]
+    low_ref[...] = hidden[..., :half]
+    high_ref[...] = hidden[..., half:]
+
+
+def first_stage(maps, upper_row, first_weight, part):
+    images, rows, width, inputs = maps.shape
+    outputs = first_weight.shape[3]
+    weight = first_weight[:, jnp.array([1, 2, 0])].reshape(9 * inputs, outputs)
+    out_block = pl.BlockSpec((None, rows // 2, width // 2, part), lambda n: (n, 0, 0, 0))
+    shape = jax.ShapeDtypeStruct((images, rows // 2, width // 2, part), jnp.bfloat16)
+    return pl.pallas_call(
+        first_kernel,
+        grid=(images,),
+        in_specs=[
+            pl.BlockSpec((None, rows, width, inputs), lambda n: (n, 0, 0, 0)),
+            pl.BlockSpec((None, 1, width, inputs), lambda n: (n, 0, 0, 0)),
+            pl.BlockSpec((9 * inputs, outputs), lambda n: (0, 0)),
+        ],
+        out_specs=[out_block, out_block],
+        out_shape=[shape, shape],
+        scratch_shapes=[pltpu.VMEM((rows + 1, width, inputs), jnp.float32)],
+        compiler_params=pltpu.CompilerParams(
+            dimension_semantics=("arbitrary",), vmem_limit_bytes=60 * 1024 * 1024
+        ),
+        cost_estimate=pl.CostEstimate(
+            flops=2 * images * (rows // 2) * (width // 2) * 9 * inputs * outputs,
+            transcendentals=0,
+            bytes_accessed=maps.size * 2 + images * (rows // 2) * (width // 2) * outputs * 2,
+        ),
+    )(maps, upper_row, weight)
 
 
 def second_kernel(*refs, rows, carry, group):
@@ -149,15 +199,16 @@
     outputs = first_weight.shape[3]
     owned = images // tiles
     half_rows = height // 2
-    chunks = 2 if outputs % 256 == 0 else 1
+    chunks = 2
     part = outputs // chunks
     upper_row = shifted_2(maps[:, height - 1 : height], "tile", 1)
     grad_t = out_grad.reshape(owned, -1, outputs).transpose(0, 2, 1)
     conv = None
     pieces = []
+    halves = first_stage(maps, upper_row, first_weight, part)
     for chunk in range(chunks):
         channels = slice(chunk * part, (chunk + 1) * part)
-        local_hidden = first_conv(maps, upper_row, first_weight[..., channels])
+        local_hidden = halves[chunk]
         arrived = lax.all_to_all(
             local_hidden.reshape(tiles, owned, half_rows, width // 2, part),
             "tile",

time: 224 us -> 194 us (0.87)
  blocking collectives: 0 us -> 54.4 us
  waiting for transfers between devices: 66.6 us -> 31.3 us
  matrix products: 27.9 us -> 0 us
  local copies, waits for them, and re-layouts: 55.1 us -> 28.1 us
  Pallas kernels: 47.6 us -> 58.7 us
  starting transfers between devices: 22.5 us -> 17.9 us
    all_to_all x0 -> x1, blocking collectives: none -> 54.4 us  [local(): lax.all_to_all(local_hidden.reshape(tiles, owned, half_rows, width // 2,...]
    all_to_all x2 -> x1, waiting for transfers between devices: 43.1 us -> 7.14 us  [local(): lax.all_to_all(local_hidden.reshape(tiles, owned, half_rows, width // 2,...]
    dot_general x8 -> x0, matrix products: 27.9 us -> none  [the longest x6 18.3 us: first_conv(): jnp.dot(sources[tap_row], wide_kernel, preferred_element_type=jnp.float32)]
    reshape x2 -> x0, local copies, waits for them, and re-layouts: 13 us -> none  [the longest x1 12.9 us: first_conv(): paired = source.reshape(images, rows // 2, 2, width // 2, 2 * inputs)]
    pallas_call x0 -> x1, Pallas kernels: none -> 11.1 us  [first_stage(): pl.pallas_call(first_kernel, grid=(images,), in_specs=[pl.BlockSpec((None...]
    all_to_all x2 -> x1, starting transfers between devices: 9.39 us -> 3.6 us  [local(): lax.all_to_all(local_hidden.reshape(tiles, owned, half_rows, width // 2,...]
    slice x5 -> x0, local copies, waits for them, and re-layouts: 5.28 us -> none  [the longest x2 2.38 us: first_conv(): piece[..., inputs:]]
    squeeze x1 -> x0, local copies, waits for them, and re-layouts: 4.22 us -> none  [first_conv(): even_rows = paired[:, :, 0]]
  transfers between devices with their start and end apart: 13 -> 12, of which waited for: 10 -> 9; matrix products, arithmetic and copies ran while one was open for 26% -> 13% of each run, Pallas kernels for 11% -> 25%
where the time goes in v4:
time: 194 us; the launch traced here: 193 us
  Pallas kernels  58.7 us (30%)
  blocking collectives  54.4 us (28%)
  waiting for transfers between devices  31.3 us (16%)
  local copies, waits for them, and re-layouts  28.1 us (14%)
  starting transfers between devices  17.9 us (9%)
    all_to_all x1, blocking collectives, local(): lax.all_to_all(local_hidden.reshape(tiles, owned, half_rows, width // 2,...  54.4 us
    pallas_call x2, Pallas kernels, second_stage(): pl.pallas_call(functools.partial(second_kernel, rows=rows, carry=prev is...  47.6 us
    ppermute x10, waiting for transfers between devices, halving_reduce_scatter(): buf = keep + lax.ppermute(send, axes, pairs)  20.8 us
    pallas_call x1, Pallas kernels, first_stage(): pl.pallas_call(first_kernel, grid=(images,), in_specs=[pl.BlockSpec((None...  11.1 us
    ppermute x10, starting transfers between devices, halving_reduce_scatter(): buf = keep + lax.ppermute(send, axes, pairs)  9.43 us
    all_to_all x1, waiting for transfers between devices, local(): lax.all_to_all(local_hidden.reshape(tiles, owned, half_rows, width // 2,...  7.14 us
    reshape x1, local copies, waits for them, and re-layouts, local(): grad_t = out_grad.reshape(owned, -1, outputs).transpose(0, 2, 1)  6.37 us
    concatenate x2, local copies, waits for them, and re-layouts, shift_cols_right(): return jnp.concatenate([zero_col, slab[:, :, :-1]], axis=2)  4.97 us
  transfers between devices with their start and end apart: 12, of which 9 were waited for; matrix products, arithmetic and copies ran while one was open for 13% of the time, Pallas kernels for 25%

profile of v4, /device:TPU:0, one launch (start us, length us, event | category | flops | bytes accessed | tf_op | source)
XLA Modules:
  0.0 192.9 jit_solution(1671772338445649443)
XLA Ops:
  0.6 0.0 copy-start
  0.6 1.0 slice.21
  1.7 4.9 %collective-permute-start = (bf16[8,1,128,128]{3,2,1,0:T(8,128)(2,1)S(1)}, bf16[8,1,128,128]{3,2,1,0:T(8,128)(2,1)S(1)}, u32[]{:S(2)}, u32[]{:S(2)}) collective-permute-start(bf16[8,1,128,128]{3,2,1,0:T(8,128)(2,1)S(1)} %slice.21), channel_id=1, source_target_pairs={{0,1},{1,2},{2,3},{3,4},{4,5},{5,6},{6,7},{8,9},{9,10},{10,11},{11... | collective-permute-start | bytes 786440 | tf_op jit(solution)/shard_map/ppermute | solution.py:14
  6.6 0.7 pad_clamp_fusion
  7.2 0.6 gather_fusion
  7.8 0.9 copy.11
  8.7 3.4 %collective-permute-done.up_ref = bf16[8,1,128,128]{3,2,1,0:T(8,128)(2,1)S(1)} collective-permute-done((bf16[8,1,128,128]{3,2,1,0:T(8,128)(2,1)S(1)}, bf16[8,1,128,128]{3,2,1,0:T(8,128)(2,1)S(1)}, u32[]{:S(2)}, u32[]{:S(2)}) %collective-permute-start) | collective-permute-done | bytes 262176 | tf_op jit(solution)/shard_map/ppermute | solution.py:14
  12.1 0.7 copy-done.6
  12.8 11.1 %shard_map.68 = (bf16[8,16,64,128]{3,2,1,0:T(8,128)(2,1)}, bf16[8,16,64,128]{3,2,1,0:T(8,128)(2,1)}) custom-call(bf16[8,32,128,128]{3,2,1,0:T(8,128)(2,1)} %x_ref.1, bf16[8,1,128,128]{3,2,1,0:T(8,128)(2,1)} %copy-done.6, bf16[1152,256]{1,0:T(8,128)(2,1)} %bitcast.73), custom_call_target="tpu_custom_call" | custom-call | flops 4831838208 | bytes 12582912 | tf_op jit(solution)/shard_map/pallas_call | solution.py:76
  23.9 54.4 %all_to_all.21 = bf16[8,1,16,64,128]{4,3,2,1,0:T(8,128)(2,1)} all-to-all(bf16[8,1,16,64,128]{4,3,2,1,0:T(8,128)(2,1)} %bitcast.68), channel_id=1, replica_groups=mesh['group'=4,'tile'=8] {'tile'}, dimensions={0} | all-to-all | bytes 4194304 | tf_op jit(solution)/shard_map/all_to_all | solution.py:212
  78.2 3.6 %all-to-all-start = ((bf16[8,1,16,64,128]{4,3,2,1,0:T(8,128)(2,1)}), bf16[8,1,16,64,128]{4,3,2,1,0:T(8,128)(2,1)S(1)}, u32[]{:S(2)}, u32[]{:S(2)}) async-start(bf16[8,1,16,64,128]{4,3,2,1,0:T(8,128)(2,1)} %bitcast.67), calls=%async_computation | async-start | bytes 4194304 | tf_op jit(solution)/shard_map/all_to_all | solution.py:212
  81.9 6.4 %copy.14 = bf16[1,8192,256]{1,2,0:T(8,128)(2,1)} copy(bf16[1,8192,256]{2,1,0:T(8,128)(2,1)} %bitcast.63) | data formatting | bytes 8388608 | tf_op jit(solution)/shard_map/reshape | solution.py:205
  88.2 2.5 %fusion = (bf16[3,3,128,256]{3,2,1,0:T(8,128)(2,1)}, bf16[3,3,128,256]{3,2,1,0:T(8,128)(2,1)}) fusion(bf16[3,3,256,256]{3,2,1,0:T(8,128)(2,1)} %param.7), kind=kLoop, calls=%fused_computation.27 | loop fusion | bytes 2359296 | tf_op jit(solution)/shard_map/slice | solution.py:224
  90.8 1.7 pad.11.refs_1_
  92.5 1.3 pad_slice_fusion.2
  93.8 1.8 concatenate.21.refs_2_
  95.6 2.5 %concatenate.20.refs_0_ = bf16[1,130,64,128]{3,2,1,0:T(8,128)(2,1)} pad(bf16[1,130,63,128]{3,2,1,0:T(8,128)(2,1)S(1)} %get-tuple-element.21, bf16[]{:T(256)} %constant.76.clone.1), padding=0_0x0_0x1_0x0_0 | pad | bytes 4226562 | tf_op jit(solution)/shard_map/concatenate | solution.py:19
  98.1 24.3 %shard_map.69 = (f32[1,128,64,256]{3,2,1,0:T(8,128)}, f32[1,256,1152]{2,1,0:T(8,128)}) custom-call(bf16[1,130,64,128]{3,2,1,0:T(8,128)(2,1)} %concatenate.20.refs_0_, bf16[1,130,64,128]{3,2,1,0:T(8,128)(2,1)} %pad.11.refs_1_, bf16[1,130,64,128]{3,2,1,0:T(8,128)(2,1)} %concatenate.21.refs_2_, bf16[1152,256]{1,0:T(8,128)(2,1)} %bitcast.75, ...), custom_call_target="tpu_custom_call" | custom-call | flops 9663676416 | bytes 26345472 | tf_op jit(solution)/shard_map/pallas_call | solution.py:154
  122.4 7.1 %all-to-all-done = bf16[8,1,16,64,128]{4,3,2,1,0:T(8,128)(2,1)S(1)} async-done(((bf16[8,1,16,64,128]{4,3,2,1,0:T(8,128)(2,1)}), bf16[8,1,16,64,128]{4,3,2,1,0:T(8,128)(2,1)S(1)}, u32[]{:S(2)}, u32[]{:S(2)}) %all-to-all-start) | async-done | bytes 2097184 | tf_op jit(solution)/shard_map/all_to_all | solution.py:212
  129.5 1.7 pad.12.refs_1_
  131.3 1.2 pad_slice_fusion
  132.5 0.0 copy-done.3
  132.6 0.1 collective-permute-start.1
  132.7 1.8 concatenate.23.refs_2_
  134.5 2.5 %concatenate.22.refs_0_ = bf16[1,130,64,128]{3,2,1,0:T(8,128)(2,1)} pad(bf16[1,130,63,128]{3,2,1,0:T(8,128)(2,1)S(1)} %get-tuple-element.19, bf16[]{:T(256)} %constant.76.clone.1), padding=0_0x0_0x1_0x0_0 | pad | bytes 4226562 | tf_op jit(solution)/shard_map/concatenate | solution.py:19
  136.9 23.4 %shard_map.70 = (bf16[1,128,64,256]{3,2,1,0:T(8,128)(2,1)}, f32[1,256,1152]{2,1,0:T(8,128)}) custom-call(bf16[1,130,64,128]{3,2,1,0:T(8,128)(2,1)} %concatenate.22.refs_0_, bf16[1,130,64,128]{3,2,1,0:T(8,128)(2,1)} %pad.12.refs_1_, bf16[1,130,64,128]{3,2,1,0:T(8,128)(2,1)} %concatenate.23.refs_2_, bf16[1152,256]{1,0:T(8,128)(2,1)} %bitcast.74, ...), custom_call_target="tpu_custom_call" | custom-call | flops 9663676416 | bytes 26345472 | tf_op jit(solution)/shard_map/pallas_call | solution.py:154
  160.3 1.2 dynamic-slice_bitcast_fusion
  161.5 0.6 collective-permute-start.6
  162.1 0.0 collective-permute-done.1
  162.1 0.1 bitcast_add_fusion.1
  162.2 1.6 collective-permute-start.2
  163.8 0.1 bitcast_add_fusion
  163.8 0.0 copy-start.1
  163.9 1.5 collective-permute-start.7
  165.4 6.7 %collective-permute-done.2 = f32[2,2,2,8,1152]{4,3,2,1,0:T(8,128)S(1)} collective-permute-done((f32[2,2,2,8,1152]{4,3,2,1,0:T(8,128)S(1)}, f32[2,2,2,8,1152]{4,3,2,1,0:T(8,128)S(1)}, u32[]{:S(2)}, u32[]{:S(2)}) %collective-permute-start.2) | collective-permute-done | bytes 294944 | tf_op jit(solution)/shard_map/ppermute | solution.py:191
  172.2 1.5 collective-permute-start.3
  173.7 3.8 %collective-permute-done.7 = f32[2,2,2,8,1152]{4,3,2,1,0:T(8,128)S(1)} collective-permute-done((f32[2,2,2,8,1152]{4,3,2,1,0:T(8,128)S(1)}, f32[2,2,2,8,1152]{4,3,2,1,0:T(8,128)S(1)}, u32[]{:S(2)}, u32[]{:S(2)}) %collective-permute-start.7) | collective-permute-done | bytes 294944 | tf_op jit(solution)/shard_map/ppermute | solution.py:191
  177.6 1.5 collective-permute-start.8
  179.1 0.1 collective-permute-start.4
  179.2 3.6 %collective-permute-done.8 = f32[2,2,8,1152]{3,2,1,0:T(8,128)S(1)} collective-permute-done((f32[2,2,8,1152]{3,2,1,0:T(8,128)S(1)}, f32[2,2,8,1152]{3,2,1,0:T(8,128)S(1)}, u32[]{:S(2)}, u32[]{:S(2)}) %collective-permute-start.8) | collective-permute-done | bytes 147488 | tf_op jit(solution)/shard_map/ppermute | solution.py:191
  182.8 0.1 collective-permute-start.9
  182.9 0.7 collective-permute-done.4
  183.7 1.9 collective-permute-start.5
  185.6 1.7 collective-permute-done.9
  187.3 0.6 collective-permute-start.10
  187.9 0.7 collective-permute-done.5
  188.6 3.6 %collective-permute-done.10 = f32[8,1152]{1,0:T(8,128)S(1)} collective-permute-done((f32[8,1152]{1,0:T(8,128)S(1)}, f32[8,1152]{1,0:T(8,128)S(1)}, u32[]{:S(2)}, u32[]{:S(2)}) %collective-permute-start.10) | collective-permute-done | bytes 36896 | tf_op jit(solution)/shard_map/ppermute | solution.py:191
  192.2 0.6 pad_maximum_fusion
  (29 shorter events, 0.4 us)
Async XLA Ops:
  0.6 6.6 %copy-start = (bf16[3,3,128,256]{3,2,1,0:T(8,128)(2,1)S(1)}, bf16[3,3,128,256]{3,2,1,0:T(8,128)(2,1)}, u32[]{:S(2)}) copy-start(bf16[3,3,128,256]{3,2,1,0:T(8,128)(2,1)} %param.6) | copy-start | bytes 1769476
  1.7 10.4 %collective-permute-start = (bf16[8,1,128,128]{3,2,1,0:T(8,128)(2,1)S(1)}, bf16[8,1,128,128]{3,2,1,0:T(8,128)(2,1)S(1)}, u32[]{:S(2)}, u32[]{:S(2)}) collective-permute-start(bf16[8,1,128,128]{3,2,1,0:T(8,128)(2,1)S(1)} %slice.21), channel_id=1, source_target_pairs={{0,1},{1,2},{2,3},{3,4},{4,5},{5,6},{6,7},{8,9},{9,10},{10,11},{11... | collective-permute-start | bytes 786440 | tf_op jit(solution)/shard_map/ppermute | solution.py:14
  12.1 0.7 copy-start.6
  78.2 51.3 %all-to-all-start = ((bf16[8,1,16,64,128]{4,3,2,1,0:T(8,128)(2,1)}), bf16[8,1,16,64,128]{4,3,2,1,0:T(8,128)(2,1)S(1)}, u32[]{:S(2)}, u32[]{:S(2)}) async-start(bf16[8,1,16,64,128]{4,3,2,1,0:T(8,128)(2,1)} %bitcast.67), calls=%async_computation | async-start | bytes 4194304 | tf_op jit(solution)/shard_map/all_to_all | solution.py:212
  88.2 2.5 %copy-start.2 = (bf16[8,1,16,64,128]{4,3,2,1,0:T(8,128)(2,1)S(1)}, bf16[8,1,16,64,128]{4,3,2,1,0:T(8,128)(2,1)}, u32[]{:S(2)}) copy-start(bf16[8,1,16,64,128]{4,3,2,1,0:T(8,128)(2,1)} %all_to_all.21) | copy-start | bytes 6291460
  131.3 1.3 copy-start.3
  132.6 29.5 %collective-permute-start.1 = (f32[2,2,2,2,8,1152]{5,4,3,2,1,0:T(8,128)S(1)}, f32[2,2,2,2,8,1152]{5,4,3,2,1,0:T(8,128)S(1)}, u32[]{:S(2)}, u32[]{:S(2)}) collective-permute-start(f32[2,2,2,2,8,1152]{5,4,3,2,1,0:T(8,128)S(1)} %dynamic-slice_bitcast_fusion.1), channel_id=1, source_target_pairs={{0,8},{1,9},{2,10},{3,11},{4,12},{5,13},{6,14},{7,15},{8,0},{9,1},... | collective-permute-start | bytes 1769480 | tf_op jit(solution)/shard_map/ppermute | solution.py:191
  136.9 25.1 %copy-start.4 = (f32[1,256,1152]{2,1,0:T(8,128)S(1)}, f32[1,256,1152]{2,1,0:T(8,128)}, u32[]{:S(2)}) copy-start(f32[1,256,1152]{2,1,0:T(8,128)} %get-tuple-element.16) | copy-start | bytes 3538948
  160.3 3.5 %copy-start.5 = (f32[1,256,1152]{2,1,0:T(8,128)S(1)}, f32[1,256,1152]{2,1,0:T(8,128)}, u32[]{:S(2)}) copy-start(f32[1,256,1152]{2,1,0:T(8,128)} %get-tuple-element.17) | copy-start | bytes 3538948
  161.5 2.3 %collective-permute-start.6 = (f32[2,2,2,2,8,1152]{5,4,3,2,1,0:T(8,128)S(1)}, f32[2,2,2,2,8,1152]{5,4,3,2,1,0:T(8,128)S(1)}, u32[]{:S(2)}, u32[]{:S(2)}) collective-permute-start(f32[2,2,2,2,8,1152]{5,4,3,2,1,0:T(8,128)S(1)} %dynamic-slice_bitcast_fusion), channel_id=1, source_target_pairs={{0,8},{1,9},{2,10},{3,11},{4,12},{5,13},{6,14},{7,15},{8,0},{9,1},... | collective-permute-start | bytes 1769480 | tf_op jit(solution)/shard_map/ppermute | solution.py:191
  162.2 9.9 %collective-permute-start.2 = (f32[2,2,2,8,1152]{4,3,2,1,0:T(8,128)S(1)}, f32[2,2,2,8,1152]{4,3,2,1,0:T(8,128)S(1)}, u32[]{:S(2)}, u32[]{:S(2)}) collective-permute-start(f32[2,2,2,8,1152]{4,3,2,1,0:T(8,128)S(1)} %dynamic-slice_bitcast_fusion.3), channel_id=1, source_target_pairs={{0,16},{1,17},{2,18},{3,19},{4,20},{5,21},{6,22},{7,23},{8,24},{9,... | collective-permute-start | bytes 884744 | tf_op jit(solution)/shard_map/ppermute | solution.py:191
  163.8 29.0 %copy-start.1 = (bf16[3,3,128,256]{3,2,1,0:T(8,128)(2,1)S(1)}, bf16[3,3,128,256]{3,2,1,0:T(8,128)(2,1)}, u32[]{:S(2)}) copy-start(bf16[3,3,128,256]{3,2,1,0:T(8,128)(2,1)} %param.6) | copy-start | bytes 1769476
  163.9 13.6 %collective-permute-start.7 = (f32[2,2,2,8,1152]{4,3,2,1,0:T(8,128)S(1)}, f32[2,2,2,8,1152]{4,3,2,1,0:T(8,128)S(1)}, u32[]{:S(2)}, u32[]{:S(2)}) collective-permute-start(f32[2,2,2,8,1152]{4,3,2,1,0:T(8,128)S(1)} %dynamic-slice_bitcast_fusion.2), channel_id=1, source_target_pairs={{0,16},{1,17},{2,18},{3,19},{4,20},{5,21},{6,22},{7,23},{8,24},{9,... | collective-permute-start | bytes 884744 | tf_op jit(solution)/shard_map/ppermute | solution.py:191
  172.2 6.9 %collective-permute-start.3 = (f32[2,2,8,1152]{3,2,1,0:T(8,128)S(1)}, f32[2,2,8,1152]{3,2,1,0:T(8,128)S(1)}, u32[]{:S(2)}, u32[]{:S(2)}) collective-permute-start(f32[2,2,8,1152]{3,2,1,0:T(8,128)S(1)} %dynamic-slice_bitcast_fusion.5), channel_id=1, source_target_pairs={{0,1},{1,0},{2,3},{3,2},{4,5},{5,4},{6,7},{7,6},{8,9},{9,8},{10,11... | collective-permute-start | bytes 442376 | tf_op jit(solution)/shard_map/ppermute | solution.py:191
  177.6 5.2 %collective-permute-start.8 = (f32[2,2,8,1152]{3,2,1,0:T(8,128)S(1)}, f32[2,2,8,1152]{3,2,1,0:T(8,128)S(1)}, u32[]{:S(2)}, u32[]{:S(2)}) collective-permute-start(f32[2,2,8,1152]{3,2,1,0:T(8,128)S(1)} %dynamic-slice_bitcast_fusion.4), channel_id=1, source_target_pairs={{0,1},{1,0},{2,3},{3,2},{4,5},{5,4},{6,7},{7,6},{8,9},{9,8},{10,11... | collective-permute-start | bytes 442376 | tf_op jit(solution)/shard_map/ppermute | solution.py:191
  179.1 4.5 %collective-permute-start.4 = (f32[2,8,1152]{2,1,0:T(8,128)S(1)}, f32[2,8,1152]{2,1,0:T(8,128)S(1)}, u32[]{:S(2)}, u32[]{:S(2)}) collective-permute-start(f32[2,8,1152]{2,1,0:T(8,128)S(1)} %dynamic-slice_bitcast_fusion.7), channel_id=1, source_target_pairs={{0,2},{1,3},{2,0},{3,1},{4,6},{5,7},{6,4},{7,5},{8,10},{9,11},{10,... | collective-permute-start | bytes 221192 | tf_op jit(solution)/shard_map/ppermute | solution.py:191
  182.8 4.4 %collective-permute-start.9 = (f32[2,8,1152]{2,1,0:T(8,128)S(1)}, f32[2,8,1152]{2,1,0:T(8,128)S(1)}, u32[]{:S(2)}, u32[]{:S(2)}) collective-permute-start(f32[2,8,1152]{2,1,0:T(8,128)S(1)} %dynamic-slice_bitcast_fusion.6), channel_id=1, source_target_pairs={{0,2},{1,3},{2,0},{3,1},{4,6},{5,7},{6,4},{7,5},{8,10},{9,11},{10,... | collective-permute-start | bytes 221192 | tf_op jit(solution)/shard_map/ppermute | solution.py:191
  183.7 5.0 %collective-permute-start.5 = (f32[8,1152]{1,0:T(8,128)S(1)}, f32[8,1152]{1,0:T(8,128)S(1)}, u32[]{:S(2)}, u32[]{:S(2)}) collective-permute-start(f32[8,1152]{1,0:T(8,128)S(1)} %dynamic-slice_bitcast_fusion.9), channel_id=1, source_target_pairs={{0,4},{1,5},{2,6},{3,7},{4,0},{5,1},{6,2},{7,3},{8,12},{9,13},{10,... | collective-permute-start | bytes 110600 | tf_op jit(solution)/shard_map/ppermute | solution.py:191
  187.3 4.9 %collective-permute-start.10 = (f32[8,1152]{1,0:T(8,128)S(1)}, f32[8,1152]{1,0:T(8,128)S(1)}, u32[]{:S(2)}, u32[]{:S(2)}) collective-permute-start(f32[8,1152]{1,0:T(8,128)S(1)} %dynamic-slice_bitcast_fusion.8), channel_id=1, source_target_pairs={{0,4},{1,5},{2,6},{3,7},{4,0},{5,1},{6,2},{7,3},{8,12},{9,13},{10,... | collective-permute-start | bytes 110600 | tf_op jit(solution)/shard_map/ppermute | solution.py:191

commit v5 on v4

--- a/solution.py
+++ b/solution.py
@@ -45,10 +45,17 @@
     return jnp.maximum(total, 0.0).astype(jnp.bfloat16)
 
 
-def first_kernel(x_ref, up_ref, w_ref, low_ref, high_ref, scratch):
+def first_kernel(*refs, with_up):
+    if with_up:
+        x_ref, up_ref, w_ref, _, _, low_ref, high_ref, scratch = refs
+    else:
+        x_ref, w_ref, low_ref, high_ref, scratch = refs
     rows, width, inputs = x_ref.shape
     out_rows, out_cols = rows // 2, width // 2
-    scratch[0] = up_ref[0].astype(jnp.float32)
+    if with_up:
+        scratch[0] = up_ref[0].astype(jnp.float32)
+    else:
+        scratch[0] = jnp.zeros(scratch.shape[1:], jnp.float32)
     scratch[1:] = x_ref[...].astype(jnp.float32)
     first_col = lax.broadcasted_iota(jnp.int32, (out_rows, out_cols, inputs), 1) == 0
     pieces = []
@@ -71,28 +78,47 @@
     images, rows, width, inputs = maps.shape
     outputs = first_weight.shape[3]
     weight = first_weight[:, jnp.array([1, 2, 0])].reshape(9 * inputs, outputs)
+    shape = jax.ShapeDtypeStruct((images, rows // 2, width // 2, part), jnp.bfloat16)
+    params = pltpu.CompilerParams(dimension_semantics=("arbitrary",), vmem_limit_bytes=60 * 1024 * 1024)
+    weight_spec = pl.BlockSpec((9 * inputs, outputs), lambda n: (0, 0))
+
+    def cost(out_rows):
+        return pl.CostEstimate(
+            flops=2 * images * out_rows * (width // 2) * 9 * inputs * outputs,
+            transcendentals=0,
+            bytes_accessed=images * out_rows * 2 * width * inputs * 2 + images * out_rows * (width // 2) * outputs * 2,
+        )
+
     out_block = pl.BlockSpec((None, rows // 2, width // 2, part), lambda n: (n, 0, 0, 0))
-    shape = jax.ShapeDtypeStruct((images, rows // 2, width // 2, part), jnp.bfloat16)
-    return pl.pallas_call(
-        first_kernel,
+    low, high = pl.pallas_call(
+        functools.partial(first_kernel, with_up=False),
         grid=(images,),
-        in_specs=[
-            pl.BlockSpec((None, rows, width, inputs), lambda n: (n, 0, 0, 0)),
-            pl.BlockSpec((None, 1, width, inputs), lambda n: (n, 0, 0, 0)),
-            pl.BlockSpec((9 * inputs, outputs), lambda n: (0, 0)),
-        ],
+        in_specs=[pl.BlockSpec((None, rows, width, inputs), lambda n: (n, 0, 0, 0)), weight_spec],
         out_specs=[out_block, out_block],
         out_shape=[shape, shape],
         scratch_shapes=[pltpu.VMEM((rows + 1, width, inputs), jnp.float32)],
-        compiler_params=pltpu.CompilerParams(
-            dimension_semantics=("arbitrary",), vmem_limit_bytes=60 * 1024 * 1024
-        ),
-        cost_estimate=pl.CostEstimate(
-            flops=2 * images * (rows // 2) * (width // 2) * 9 * inputs * outputs,
-            transcendentals=0,
-            bytes_accessed=maps.size * 2 + images * (rows // 2) * (width // 2) * outputs * 2,
-        ),
-    )(maps, upper_row, weight)
+        compiler_params=params,
+        cost_estimate=cost(rows // 2),
+    )(maps, weight)
+    row_block = pl.BlockSpec((None, 1, width // 2, part), lambda n: (n, 0, 0, 0))
+    anywhere = pl.BlockSpec(memory_space=pl.ANY)
+    return pl.pallas_call(
+        functools.partial(first_kernel, with_up=True),
+        grid=(images,),
+        in_specs=[
+            pl.BlockSpec((None, 2, width, inputs), lambda n: (n, 0, 0, 0)),
+            pl.BlockSpec((None, 1, width, inputs), lambda n: (n, 0, 0, 0)),
+            weight_spec,
+            anywhere,
+            anywhere,
+        ],
+        out_specs=[row_block, row_block],
+        out_shape=[shape, shape],
+        scratch_shapes=[pltpu.VMEM((3, width, inputs), jnp.float32)],
+        input_output_aliases={3: 0, 4: 1},
+        compiler_params=params,
+        cost_estimate=cost(1),
+    )(maps, upper_row, weight, low, high)
 
 
 def second_kernel(*refs, rows, carry, group):

time: 194 us -> 195 us (level)
  Pallas kernels: 58.7 us -> 64.6 us
  waiting for transfers between devices: 31.3 us -> 27.8 us
    pallas_call x1 -> x2, Pallas kernels: 11.1 us -> 16.9 us  [the longest x1 11 us: first_stage(): pl.pallas_call(functools.partial(first_kernel, with_up=False), grid=(imag...]
    ppermute x1, waiting for transfers between devices: 3.39 us -> 0.01 us  [shifted_2(): return lax.ppermute(shard, axis, pairs)]
  transfers between devices with their start and end apart: 12 -> 12, of which waited for: 9 -> 8; matrix products, arithmetic and copies ran while one was open for 13% -> 13% of each run, Pallas kernels for 25% -> 30%
where the time goes in v5:
time: 195 us; the launch traced here: 194 us
  Pallas kernels  64.6 us (33%)
  blocking collectives  53 us (27%)
  local copies, waits for them, and re-layouts  28.2 us (14%)
  waiting for transfers between devices  27.8 us (14%)
  starting transfers between devices  18.1 us (9%)
    all_to_all x1, blocking collectives, local(): lax.all_to_all(local_hidden.reshape(tiles, owned, half_rows, width // 2,...  53 us
    pallas_call x2, Pallas kernels, second_stage(): pl.pallas_call(functools.partial(second_kernel, rows=rows, carry=prev is...  47.6 us
    ppermute x10, waiting for transfers between devices, halving_reduce_scatter(): buf = keep + lax.ppermute(send, axes, pairs)  20.6 us
    pallas_call x1, Pallas kernels, first_stage(): pl.pallas_call(functools.partial(first_kernel, with_up=False), grid=(imag...  11 us
    ppermute x10, starting transfers between devices, halving_reduce_scatter(): buf = keep + lax.ppermute(send, axes, pairs)  9.64 us
    all_to_all x1, waiting for transfers between devices, local(): lax.all_to_all(local_hidden.reshape(tiles, owned, half_rows, width // 2,...  7.16 us
    reshape x1, local copies, waits for them, and re-layouts, local(): grad_t = out_grad.reshape(owned, -1, outputs).transpose(0, 2, 1)  6.41 us
    pallas_call x1, Pallas kernels, first_stage(): pl.pallas_call(functools.partial(first_kernel, with_up=True), grid=(image...  5.91 us
  transfers between devices with their start and end apart: 12, of which 8 were waited for; matrix products, arithmetic and copies ran while one was open for 13% of the time, Pallas kernels for 30%

profile of v5, /device:TPU:0, one launch (start us, length us, event | category | flops | bytes accessed | tf_op | source)
XLA Modules:
  0.0 194.1 jit_solution(14429185501781596035)
XLA Ops:
  0.6 0.0 copy-start
  0.6 1.0 slice.21
  1.7 4.9 %collective-permute-start = (bf16[8,1,128,128]{3,2,1,0:T(8,128)(2,1)S(1)}, bf16[8,1,128,128]{3,2,1,0:T(8,128)(2,1)S(1)}, u32[]{:S(2)}, u32[]{:S(2)}) collective-permute-start(bf16[8,1,128,128]{3,2,1,0:T(8,128)(2,1)S(1)} %slice.21), channel_id=1, source_target_pairs={{0,1},{1,2},{2,3},{3,4},{4,5},{5,6},{6,7},{8,9},{9,10},{10,11},{11... | collective-permute-start | bytes 786440 | tf_op jit(solution)/shard_map/ppermute | solution.py:14
  6.6 0.7 pad_clamp_fusion
  7.2 0.6 gather_fusion
  7.8 0.9 copy.13
  8.7 11.0 %shard_map.68 = (bf16[8,16,64,128]{3,2,1,0:T(8,128)(2,1)}, bf16[8,16,64,128]{3,2,1,0:T(8,128)(2,1)}) custom-call(bf16[8,32,128,128]{3,2,1,0:T(8,128)(2,1)} %refs_0_.3, bf16[1152,256]{1,0:T(8,128)(2,1)} %bitcast.68), custom_call_target="tpu_custom_call" | custom-call | flops 4831838208 | bytes 12582912 | tf_op jit(solution)/shard_map/pallas_call | solution.py:93
  19.7 0.0 collective-permute-done.refs_1_
  19.7 0.7 copy-done.6
  20.5 5.9 %shard_map.69 = (bf16[8,16,64,128]{3,2,1,0:T(8,128)(2,1)}, bf16[8,16,64,128]{3,2,1,0:T(8,128)(2,1)}) custom-call(bf16[8,32,128,128]{3,2,1,0:T(8,128)(2,1)} %refs_0_.3, bf16[8,1,128,128]{3,2,1,0:T(8,128)(2,1)} %copy-done.6, bf16[1152,256]{1,0:T(8,128)(2,1)} %bitcast.69, ...), custom_call_target="tpu_custom_call", output_to_operand_aliasing={{0}: (3, {}), {1}: (4, {})} | custom-call | flops 301989888 | bytes 786432 | tf_op jit(solution)/shard_map/pallas_call | solution.py:105
  26.4 53.0 %all_to_all.21 = bf16[8,1,16,64,128]{4,3,2,1,0:T(8,128)(2,1)} all-to-all(bf16[8,1,16,64,128]{4,3,2,1,0:T(8,128)(2,1)} %bitcast.63), channel_id=1, replica_groups=mesh['group'=4,'tile'=8] {'tile'}, dimensions={0} | all-to-all | bytes 4194304 | tf_op jit(solution)/shard_map/all_to_all | solution.py:238
  79.4 3.6 %all-to-all-start = ((bf16[8,1,16,64,128]{4,3,2,1,0:T(8,128)(2,1)}), bf16[8,1,16,64,128]{4,3,2,1,0:T(8,128)(2,1)S(1)}, u32[]{:S(2)}, u32[]{:S(2)}) async-start(bf16[8,1,16,64,128]{4,3,2,1,0:T(8,128)(2,1)} %bitcast.64), calls=%async_computation | async-start | bytes 4194304 | tf_op jit(solution)/shard_map/all_to_all | solution.py:238
  83.0 6.4 %copy.16 = bf16[1,8192,256]{1,2,0:T(8,128)(2,1)} copy(bf16[1,8192,256]{2,1,0:T(8,128)(2,1)} %bitcast.65) | data formatting | bytes 8388608 | tf_op jit(solution)/shard_map/reshape | solution.py:231
  89.4 2.5 %fusion = (bf16[3,3,128,256]{3,2,1,0:T(8,128)(2,1)}, bf16[3,3,128,256]{3,2,1,0:T(8,128)(2,1)}) fusion(bf16[3,3,256,256]{3,2,1,0:T(8,128)(2,1)} %param.7), kind=kLoop, calls=%fused_computation.27 | loop fusion | bytes 2359296 | tf_op jit(solution)/shard_map/slice | solution.py:250
  91.9 1.7 pad.11.refs_1_
  93.7 1.3 pad_slice_fusion.2
  95.0 1.8 concatenate.21.refs_2_
  96.7 2.5 %concatenate.20.refs_0_ = bf16[1,130,64,128]{3,2,1,0:T(8,128)(2,1)} pad(bf16[1,130,63,128]{3,2,1,0:T(8,128)(2,1)S(1)} %get-tuple-element.25, bf16[]{:T(256)} %constant.76.clone.1), padding=0_0x0_0x1_0x0_0 | pad | bytes 4226562 | tf_op jit(solution)/shard_map/concatenate | solution.py:19
  99.2 24.3 %shard_map.70 = (f32[1,128,64,256]{3,2,1,0:T(8,128)}, f32[1,256,1152]{2,1,0:T(8,128)}) custom-call(bf16[1,130,64,128]{3,2,1,0:T(8,128)(2,1)} %concatenate.20.refs_0_, bf16[1,130,64,128]{3,2,1,0:T(8,128)(2,1)} %pad.11.refs_1_, bf16[1,130,64,128]{3,2,1,0:T(8,128)(2,1)} %concatenate.21.refs_2_, bf16[1152,256]{1,0:T(8,128)(2,1)} %bitcast.76, ...), custom_call_target="tpu_custom_call" | custom-call | flops 9663676416 | bytes 26345472 | tf_op jit(solution)/shard_map/pallas_call | solution.py:180
  123.5 7.2 %all-to-all-done = bf16[8,1,16,64,128]{4,3,2,1,0:T(8,128)(2,1)S(1)} async-done(((bf16[8,1,16,64,128]{4,3,2,1,0:T(8,128)(2,1)}), bf16[8,1,16,64,128]{4,3,2,1,0:T(8,128)(2,1)S(1)}, u32[]{:S(2)}, u32[]{:S(2)}) %all-to-all-start) | async-done | bytes 2097184 | tf_op jit(solution)/shard_map/all_to_all | solution.py:238
  130.7 1.8 pad.12.refs_1_
  132.5 1.2 pad_slice_fusion
  133.7 0.0 copy-done.3
  133.8 0.1 collective-permute-start.1
  133.9 1.8 concatenate.23.refs_2_
  135.7 2.5 %concatenate.22.refs_0_ = bf16[1,130,64,128]{3,2,1,0:T(8,128)(2,1)} pad(bf16[1,130,63,128]{3,2,1,0:T(8,128)(2,1)S(1)} %get-tuple-element.23, bf16[]{:T(256)} %constant.76.clone.1), padding=0_0x0_0x1_0x0_0 | pad | bytes 4226562 | tf_op jit(solution)/shard_map/concatenate | solution.py:19
  138.1 23.3 %shard_map.71 = (bf16[1,128,64,256]{3,2,1,0:T(8,128)(2,1)}, f32[1,256,1152]{2,1,0:T(8,128)}) custom-call(bf16[1,130,64,128]{3,2,1,0:T(8,128)(2,1)} %concatenate.22.refs_0_, bf16[1,130,64,128]{3,2,1,0:T(8,128)(2,1)} %pad.12.refs_1_, bf16[1,130,64,128]{3,2,1,0:T(8,128)(2,1)} %concatenate.23.refs_2_, bf16[1152,256]{1,0:T(8,128)(2,1)} %bitcast.75, ...), custom_call_target="tpu_custom_call" | custom-call | flops 9663676416 | bytes 26345472 | tf_op jit(solution)/shard_map/pallas_call | solution.py:180
  161.5 1.2 dynamic-slice_bitcast_fusion
  162.7 0.6 collective-permute-start.6
  163.3 0.1 bitcast_add_fusion.1
  163.4 1.6 collective-permute-start.2
  165.0 0.1 bitcast_add_fusion
  165.0 0.0 copy-start.1
  165.1 1.5 collective-permute-start.7
  166.6 6.7 %collective-permute-done.2 = f32[2,2,2,8,1152]{4,3,2,1,0:T(8,128)S(1)} collective-permute-done((f32[2,2,2,8,1152]{4,3,2,1,0:T(8,128)S(1)}, f32[2,2,2,8,1152]{4,3,2,1,0:T(8,128)S(1)}, u32[]{:S(2)}, u32[]{:S(2)}) %collective-permute-start.2) | collective-permute-done | bytes 294944 | tf_op jit(solution)/shard_map/ppermute | solution.py:217
  173.4 1.5 collective-permute-start.3
  174.9 3.8 %collective-permute-done.7 = f32[2,2,2,8,1152]{4,3,2,1,0:T(8,128)S(1)} collective-permute-done((f32[2,2,2,8,1152]{4,3,2,1,0:T(8,128)S(1)}, f32[2,2,2,8,1152]{4,3,2,1,0:T(8,128)S(1)}, u32[]{:S(2)}, u32[]{:S(2)}) %collective-permute-start.7) | collective-permute-done | bytes 294944 | tf_op jit(solution)/shard_map/ppermute | solution.py:217
  178.8 1.5 collective-permute-start.8
  180.3 0.1 collective-permute-start.4
  180.4 3.6 %collective-permute-done.8 = f32[2,2,8,1152]{3,2,1,0:T(8,128)S(1)} collective-permute-done((f32[2,2,8,1152]{3,2,1,0:T(8,128)S(1)}, f32[2,2,8,1152]{3,2,1,0:T(8,128)S(1)}, u32[]{:S(2)}, u32[]{:S(2)}) %collective-permute-start.8) | collective-permute-done | bytes 147488 | tf_op jit(solution)/shard_map/ppermute | solution.py:217
  184.0 0.1 collective-permute-start.9
  184.1 0.7 collective-permute-done.4
  184.9 2.0 %collective-permute-start.5 = (f32[8,1152]{1,0:T(8,128)S(1)}, f32[8,1152]{1,0:T(8,128)S(1)}, u32[]{:S(2)}, u32[]{:S(2)}) collective-permute-start(f32[8,1152]{1,0:T(8,128)S(1)} %dynamic-slice_bitcast_fusion.9), channel_id=1, source_target_pairs={{0,4},{1,5},{2,6},{3,7},{4,0},{5,1},{6,2},{7,3},{8,12},{9,13},{10,... | collective-permute-start | bytes 110600 | tf_op jit(solution)/shard_map/ppermute | solution.py:217
  186.9 1.6 collective-permute-done.9
  188.5 0.7 collective-permute-start.10
  189.2 0.6 collective-permute-done.5
  189.9 3.6 %collective-permute-done.10 = f32[8,1152]{1,0:T(8,128)S(1)} collective-permute-done((f32[8,1152]{1,0:T(8,128)S(1)}, f32[8,1152]{1,0:T(8,128)S(1)}, u32[]{:S(2)}, u32[]{:S(2)}) %collective-permute-start.10) | collective-permute-done | bytes 36896 | tf_op jit(solution)/shard_map/ppermute | solution.py:217
  193.4 0.6 pad_maximum_fusion
  (30 shorter events, 0.4 us)
Async XLA Ops:
  0.6 6.6 %copy-start = (bf16[3,3,128,256]{3,2,1,0:T(8,128)(2,1)S(1)}, bf16[3,3,128,256]{3,2,1,0:T(8,128)(2,1)}, u32[]{:S(2)}) copy-start(bf16[3,3,128,256]{3,2,1,0:T(8,128)(2,1)} %param.6) | copy-start | bytes 1769476
  1.7 18.1 %collective-permute-start = (bf16[8,1,128,128]{3,2,1,0:T(8,128)(2,1)S(1)}, bf16[8,1,128,128]{3,2,1,0:T(8,128)(2,1)S(1)}, u32[]{:S(2)}, u32[]{:S(2)}) collective-permute-start(bf16[8,1,128,128]{3,2,1,0:T(8,128)(2,1)S(1)} %slice.21), channel_id=1, source_target_pairs={{0,1},{1,2},{2,3},{3,4},{4,5},{5,6},{6,7},{8,9},{9,10},{10,11},{11... | collective-permute-start | bytes 786440 | tf_op jit(solution)/shard_map/ppermute | solution.py:14
  19.7 0.7 copy-start.6
  79.4 51.3 %all-to-all-start = ((bf16[8,1,16,64,128]{4,3,2,1,0:T(8,128)(2,1)}), bf16[8,1,16,64,128]{4,3,2,1,0:T(8,128)(2,1)S(1)}, u32[]{:S(2)}, u32[]{:S(2)}) async-start(bf16[8,1,16,64,128]{4,3,2,1,0:T(8,128)(2,1)} %bitcast.64), calls=%async_computation | async-start | bytes 4194304 | tf_op jit(solution)/shard_map/all_to_all | solution.py:238
  89.4 2.5 %copy-start.2 = (bf16[8,1,16,64,128]{4,3,2,1,0:T(8,128)(2,1)S(1)}, bf16[8,1,16,64,128]{4,3,2,1,0:T(8,128)(2,1)}, u32[]{:S(2)}) copy-start(bf16[8,1,16,64,128]{4,3,2,1,0:T(8,128)(2,1)} %all_to_all.21) | copy-start | bytes 6291460
  132.5 1.3 copy-start.3
  133.8 29.5 %collective-permute-start.1 = (f32[2,2,2,2,8,1152]{5,4,3,2,1,0:T(8,128)S(1)}, f32[2,2,2,2,8,1152]{5,4,3,2,1,0:T(8,128)S(1)}, u32[]{:S(2)}, u32[]{:S(2)}) collective-permute-start(f32[2,2,2,2,8,1152]{5,4,3,2,1,0:T(8,128)S(1)} %dynamic-slice_bitcast_fusion.1), channel_id=1, source_target_pairs={{0,8},{1,9},{2,10},{3,11},{4,12},{5,13},{6,14},{7,15},{8,0},{9,1},... | collective-permute-start | bytes 1769480 | tf_op jit(solution)/shard_map/ppermute | solution.py:217
  138.1 25.1 %copy-start.4 = (f32[1,256,1152]{2,1,0:T(8,128)S(1)}, f32[1,256,1152]{2,1,0:T(8,128)}, u32[]{:S(2)}) copy-start(f32[1,256,1152]{2,1,0:T(8,128)} %get-tuple-element.20) | copy-start | bytes 3538948
  161.5 3.5 %copy-start.5 = (f32[1,256,1152]{2,1,0:T(8,128)S(1)}, f32[1,256,1152]{2,1,0:T(8,128)}, u32[]{:S(2)}) copy-start(f32[1,256,1152]{2,1,0:T(8,128)} %get-tuple-element.21) | copy-start | bytes 3538948
  162.7 2.3 %collective-permute-start.6 = (f32[2,2,2,2,8,1152]{5,4,3,2,1,0:T(8,128)S(1)}, f32[2,2,2,2,8,1152]{5,4,3,2,1,0:T(8,128)S(1)}, u32[]{:S(2)}, u32[]{:S(2)}) collective-permute-start(f32[2,2,2,2,8,1152]{5,4,3,2,1,0:T(8,128)S(1)} %dynamic-slice_bitcast_fusion), channel_id=1, source_target_pairs={{0,8},{1,9},{2,10},{3,11},{4,12},{5,13},{6,14},{7,15},{8,0},{9,1},... | collective-permute-start | bytes 1769480 | tf_op jit(solution)/shard_map/ppermute | solution.py:217
  163.4 9.9 %collective-permute-start.2 = (f32[2,2,2,8,1152]{4,3,2,1,0:T(8,128)S(1)}, f32[2,2,2,8,1152]{4,3,2,1,0:T(8,128)S(1)}, u32[]{:S(2)}, u32[]{:S(2)}) collective-permute-start(f32[2,2,2,8,1152]{4,3,2,1,0:T(8,128)S(1)} %dynamic-slice_bitcast_fusion.3), channel_id=1, source_target_pairs={{0,16},{1,17},{2,18},{3,19},{4,20},{5,21},{6,22},{7,23},{8,24},{9,... | collective-permute-start | bytes 884744 | tf_op jit(solution)/shard_map/ppermute | solution.py:217
  165.0 29.0 %copy-start.1 = (bf16[3,3,128,256]{3,2,1,0:T(8,128)(2,1)S(1)}, bf16[3,3,128,256]{3,2,1,0:T(8,128)(2,1)}, u32[]{:S(2)}) copy-start(bf16[3,3,128,256]{3,2,1,0:T(8,128)(2,1)} %param.6) | copy-start | bytes 1769476
  165.1 13.6 %collective-permute-start.7 = (f32[2,2,2,8,1152]{4,3,2,1,0:T(8,128)S(1)}, f32[2,2,2,8,1152]{4,3,2,1,0:T(8,128)S(1)}, u32[]{:S(2)}, u32[]{:S(2)}) collective-permute-start(f32[2,2,2,8,1152]{4,3,2,1,0:T(8,128)S(1)} %dynamic-slice_bitcast_fusion.2), channel_id=1, source_target_pairs={{0,16},{1,17},{2,18},{3,19},{4,20},{5,21},{6,22},{7,23},{8,24},{9,... | collective-permute-start | bytes 884744 | tf_op jit(solution)/shard_map/ppermute | solution.py:217
  173.4 6.9 %collective-permute-start.3 = (f32[2,2,8,1152]{3,2,1,0:T(8,128)S(1)}, f32[2,2,8,1152]{3,2,1,0:T(8,128)S(1)}, u32[]{:S(2)}, u32[]{:S(2)}) collective-permute-start(f32[2,2,8,1152]{3,2,1,0:T(8,128)S(1)} %dynamic-slice_bitcast_fusion.5), channel_id=1, source_target_pairs={{0,1},{1,0},{2,3},{3,2},{4,5},{5,4},{6,7},{7,6},{8,9},{9,8},{10,11... | collective-permute-start | bytes 442376 | tf_op jit(solution)/shard_map/ppermute | solution.py:217
  178.8 5.2 %collective-permute-start.8 = (f32[2,2,8,1152]{3,2,1,0:T(8,128)S(1)}, f32[2,2,8,1152]{3,2,1,0:T(8,128)S(1)}, u32[]{:S(2)}, u32[]{:S(2)}) collective-permute-start(f32[2,2,8,1152]{3,2,1,0:T(8,128)S(1)} %dynamic-slice_bitcast_fusion.4), channel_id=1, source_target_pairs={{0,1},{1,0},{2,3},{3,2},{4,5},{5,4},{6,7},{7,6},{8,9},{9,8},{10,11... | collective-permute-start | bytes 442376 | tf_op jit(solution)/shard_map/ppermute | solution.py:217
  180.3 4.5 %collective-permute-start.4 = (f32[2,8,1152]{2,1,0:T(8,128)S(1)}, f32[2,8,1152]{2,1,0:T(8,128)S(1)}, u32[]{:S(2)}, u32[]{:S(2)}) collective-permute-start(f32[2,8,1152]{2,1,0:T(8,128)S(1)} %dynamic-slice_bitcast_fusion.7), channel_id=1, source_target_pairs={{0,2},{1,3},{2,0},{3,1},{4,6},{5,7},{6,4},{7,5},{8,10},{9,11},{10,... | collective-permute-start | bytes 221192 | tf_op jit(solution)/shard_map/ppermute | solution.py:217
  184.0 4.4 %collective-permute-start.9 = (f32[2,8,1152]{2,1,0:T(8,128)S(1)}, f32[2,8,1152]{2,1,0:T(8,128)S(1)}, u32[]{:S(2)}, u32[]{:S(2)}) collective-permute-start(f32[2,8,1152]{2,1,0:T(8,128)S(1)} %dynamic-slice_bitcast_fusion.6), channel_id=1, source_target_pairs={{0,2},{1,3},{2,0},{3,1},{4,6},{5,7},{6,4},{7,5},{8,10},{9,11},{10,... | collective-permute-start | bytes 221192 | tf_op jit(solution)/shard_map/ppermute | solution.py:217
  184.9 5.0 %collective-permute-start.5 = (f32[8,1152]{1,0:T(8,128)S(1)}, f32[8,1152]{1,0:T(8,128)S(1)}, u32[]{:S(2)}, u32[]{:S(2)}) collective-permute-start(f32[8,1152]{1,0:T(8,128)S(1)} %dynamic-slice_bitcast_fusion.9), channel_id=1, source_target_pairs={{0,4},{1,5},{2,6},{3,7},{4,0},{5,1},{6,2},{7,3},{8,12},{9,13},{10,... | collective-permute-start | bytes 110600 | tf_op jit(solution)/shard_map/ppermute | solution.py:217
  188.5 4.9 %collective-permute-start.10 = (f32[8,1152]{1,0:T(8,128)S(1)}, f32[8,1152]{1,0:T(8,128)S(1)}, u32[]{:S(2)}, u32[]{:S(2)}) collective-permute-start(f32[8,1152]{1,0:T(8,128)S(1)} %dynamic-slice_bitcast_fusion.8), channel_id=1, source_target_pairs={{0,4},{1,5},{2,6},{3,7},{4,0},{5,1},{6,2},{7,3},{8,12},{9,13},{10,... | collective-permute-start | bytes 110600 | tf_op jit(solution)/shard_map/ppermute | solution.py:217

commit v6 on v4

--- a/solution.py
+++ b/solution.py
@@ -95,84 +95,115 @@
     )(maps, upper_row, weight)
 
 
-def second_kernel(*refs, rows, carry, group):
-    if carry:
-        left_ref, mid_ref, right_ref, weight_ref, grad_ref, prev_ref, out_ref, wgrad_ref = refs
-    else:
-        left_ref, mid_ref, right_ref, weight_ref, grad_ref, out_ref, wgrad_ref = refs
+def second_kernel(*refs, rows, carry, group, base, conv, wgrad, alias):
+    refs = list(refs)
+    left_ref, mid_ref, right_ref, weight_ref, grad_ref = refs[:5]
+    rest = refs[5:]
+    prev_ref = rest.pop(0) if carry else None
+    if alias:
+        rest.pop(0)
+    out_ref = rest.pop(0) if conv else None
+    wgrad_ref = rest.pop(0) if wgrad else None
     step = pl.program_id(1)
-    _, width, outputs = out_ref.shape
+    block = base + step
+    width = mid_ref.shape[1]
     inputs = mid_ref.shape[-1]
+    outputs = weight_ref.shape[-1]
     sources = (left_ref, mid_ref, right_ref)
-    grad_t = grad_ref[...]
-    if carry:
-        acc = prev_ref[...].reshape(rows * width, outputs)
-    else:
-        acc = jnp.zeros((rows * width, outputs), jnp.float32)
+    if wgrad:
+        grad_t = grad_ref[...]
+    if conv:
+        if carry:
+            acc = prev_ref[...].reshape(rows * width, outputs)
+        else:
+            acc = jnp.zeros((rows * width, outputs), jnp.float32)
     for first in range(0, 9, group):
         taps = range(first, min(first + group, 9))
         windows = [
-            sources[tap % 3][pl.ds(step * rows + tap // 3, rows)].reshape(rows * width, inputs)
+            sources[tap % 3][pl.ds(block * rows + tap // 3, rows)].reshape(rows * width, inputs)
             for tap in taps
         ]
         window = windows[0] if len(windows) == 1 else jnp.concatenate(windows, axis=-1)
         lanes = slice(first * inputs, (first + len(windows)) * inputs)
-        acc = acc + jnp.dot(window, weight_ref[lanes, :], preferred_element_type=jnp.float32)
-        term = jnp.dot(grad_t, window, preferred_element_type=jnp.float32)
-
-        @pl.when(step == 0)
-        def _():
-            wgrad_ref[:, lanes] = term
-
-        @pl.when(step > 0)
-        def _():
-            wgrad_ref[:, lanes] += term
-
-    out_ref[...] = acc.astype(out_ref.dtype).reshape(rows, width, outputs)
-
-
-def second_stage(hidden, weight, grad_t, prev, out_dtype):
-    owned, out_rows, out_cols, inputs = hidden.shape
+        if conv:
+            acc = acc + jnp.dot(window, weight_ref[lanes, :], preferred_element_type=jnp.float32)
+        if wgrad:
+            term = jnp.dot(grad_t, window, preferred_element_type=jnp.float32)
+
+            @pl.when(step == 0)
+            def _():
+                wgrad_ref[:, lanes] = term
+
+            @pl.when(step > 0)
+            def _():
+                wgrad_ref[:, lanes] += term
+
+    if conv:
+        out_ref[...] = acc.astype(out_ref.dtype).reshape(rows, width, outputs)
+
+
+def second_stage(shifted, weight, grad_t, prev, out_dtype, conv=True, wgrad=True, span=None, into=None):
+    owned, padded_rows, out_cols, inputs = shifted[0].shape
+    out_rows = padded_rows - 2
     outputs = weight.shape[-1]
     rows = min(16, out_rows)
-    row_padded = jnp.pad(hidden, ((0, 0), (1, 1), (0, 0), (0, 0)))
-    shifted = [shift_cols_right(row_padded), row_padded, shift_cols_left(row_padded)]
+    first_row, last_row = span if span is not None else (0, out_rows)
+    base = first_row // rows
     full = pl.BlockSpec((None, out_rows + 2, out_cols, inputs), lambda n, i: (n, 0, 0, 0))
-    block = pl.BlockSpec((None, rows, out_cols, outputs), lambda n, i: (n, i, 0, 0))
+    block = pl.BlockSpec((None, rows, out_cols, outputs), lambda n, i: (n, base + i, 0, 0))
     in_specs = [
         full,
         full,
         full,
         pl.BlockSpec((9 * inputs, outputs), lambda n, i: (0, 0)),
-        pl.BlockSpec((None, outputs, rows * out_cols), lambda n, i: (n, 0, i)),
+        pl.BlockSpec((None, outputs, rows * out_cols), lambda n, i: (n, 0, base + i)),
     ]
     operands = [*shifted, weight.reshape(9 * inputs, outputs), grad_t]
     if prev is not None:
         in_specs.append(block)
         operands.append(prev)
-    flops = 4 * owned * out_rows * out_cols * 9 * inputs * outputs
+    aliases = {}
+    if into is not None:
+        aliases = {len(operands): 0}
+        in_specs.append(pl.BlockSpec(memory_space=pl.ANY))
+        operands.append(into)
+    out_specs, out_shape = [], []
+    if conv:
+        out_specs.append(block)
+        out_shape.append(jax.ShapeDtypeStruct((owned, out_rows, out_cols, outputs), out_dtype))
+    if wgrad:
+        out_specs.append(pl.BlockSpec((None, outputs, 9 * inputs), lambda n, i: (n, 0, 0)))
+        out_shape.append(jax.ShapeDtypeStruct((owned, outputs, 9 * inputs), jnp.float32))
+    span_rows = last_row - first_row
+    flops = 2 * owned * span_rows * out_cols * 9 * inputs * outputs * (int(conv) + int(wgrad))
     return pl.pallas_call(
-        functools.partial(second_kernel, rows=rows, carry=prev is not None, group=max(1, 256 // inputs)),
-        grid=(owned, out_rows // rows),
+        functools.partial(
+            second_kernel, rows=rows, carry=prev is not None, group=max(1, 256 // inputs),
+            base=base, conv=conv, wgrad=wgrad, alias=into is not None,
+        ),
+        grid=(owned, span_rows // rows),
         in_specs=in_specs,
-        out_specs=[block, pl.BlockSpec((None, outputs, 9 * inputs), lambda n, i: (n, 0, 0))],
-        out_shape=[
-            jax.ShapeDtypeStruct((owned, out_rows, out_cols, outputs), out_dtype),
-            jax.ShapeDtypeStruct((owned, outputs, 9 * inputs), jnp.float32),
-        ],
+        out_specs=out_specs,
+        out_shape=out_shape,
+        input_output_aliases=aliases,
         compiler_params=pltpu.CompilerParams(
             dimension_semantics=("arbitrary", "arbitrary"), vmem_limit_bytes=60 * 1024 * 1024
         ),
         cost_estimate=pl.CostEstimate(
             flops=flops,
             transcendentals=0,
-            bytes_accessed=hidden.size * 2 * 4 + owned * out_rows * out_cols * outputs * 8
-            + owned * outputs * 9 * inputs * 4,
+            bytes_accessed=owned * (out_rows + 2) * out_cols * inputs * 6
+            + owned * span_rows * out_cols * outputs * 8,
         ),
     )(*operands)
 
 
-def halving_reduce_scatter(partial, axes):
+def shift_copies(hidden):
+    row_padded = jnp.pad(hidden, ((0, 0), (1, 1), (0, 0), (0, 0)))
+    return [shift_cols_right(row_padded), row_padded, shift_cols_left(row_padded)]
+
+
+def halving_plan(partial, axes):
     devices = lax.axis_size(axes)
     tiles = lax.axis_size(axes[-1])
     bits = devices.bit_length() - 1
@@ -181,16 +212,24 @@
     order = [core] + [b for b in range(bits) if b > core] + [b for b in range(core)]
     rows = partial.shape[0] // devices
     buf = partial.reshape((2,) * bits + (rows,) + partial.shape[1:])
+
+    def make(bit, axis):
+        def step(buf):
+            mine = (me >> bit) & 1
+            keep = lax.dynamic_index_in_dim(buf, mine, axis=axis, keepdims=False)
+            send = lax.dynamic_index_in_dim(buf, 1 - mine, axis=axis, keepdims=False)
+            pairs = [(i, i ^ (1 << bit)) for i in range(devices)]
+            return keep + lax.ppermute(send, axes, pairs)
+
+        return step
+
     remaining = list(range(bits - 1, -1, -1))
+    steps = []
     for bit in order:
         axis = remaining.index(bit)
-        mine = (me >> bit) & 1
-        keep = lax.dynamic_index_in_dim(buf, mine, axis=axis, keepdims=False)
-        send = lax.dynamic_index_in_dim(buf, 1 - mine, axis=axis, keepdims=False)
-        pairs = [(i, i ^ (1 << bit)) for i in range(devices)]
-        buf = keep + lax.ppermute(send, axes, pairs)
+        steps.append(make(bit, axis))
         remaining.pop(axis)
-    return buf
+    return buf, steps
 
 
 def local(maps, first_weight, second_weight, out_grad):
@@ -204,7 +243,7 @@
     upper_row = shifted_2(maps[:, height - 1 : height], "tile", 1)
     grad_t = out_grad.reshape(owned, -1, outputs).transpose(0, 2, 1)
     conv = None
-    pieces = []
+    plans = []
     halves = first_stage(maps, upper_row, first_weight, part)
     for chunk in range(chunks):
         channels = slice(chunk * part, (chunk + 1) * part)
@@ -219,12 +258,28 @@
         if conv is not None:
             arrived, conv = lax.optimization_barrier((arrived, conv))
         hidden = arrived.reshape(owned, half_rows * tiles, width // 2, part)
-        last = chunk == chunks - 1
-        conv, partial = second_stage(
-            hidden, second_weight[:, :, channels], grad_t, conv, jnp.bfloat16 if last else jnp.float32
-        )
-        summed = halving_reduce_scatter(partial.sum(axis=0).reshape(outputs, 9 * part), ("group", "tile"))
-        pieces.append(summed.reshape(-1, 9, part))
+        shifted = shift_copies(hidden)
+        weight = second_weight[:, :, channels]
+        if chunk < chunks - 1:
+            conv, partial = second_stage(shifted, weight, grad_t, conv, jnp.float32)
+        else:
+            (partial,) = second_stage(shifted, weight, grad_t, None, jnp.float32, conv=False)
+        plans.append(halving_plan(partial.sum(axis=0).reshape(outputs, 9 * part), ("group", "tile")))
+    out_rows = half_rows * tiles
+    spans = 4 if out_rows % 64 == 0 else 1
+    span = out_rows // spans
+    bufs = [buf for buf, _ in plans]
+    result = None
+    for index in range(len(plans[0][1])):
+        bufs = [steps[index](buf) for buf, (_, steps) in zip(bufs, plans)]
+        if index < spans:
+            (result,) = second_stage(
+                shifted, weight, grad_t, conv, jnp.bfloat16, wgrad=False,
+                span=(index * span, (index + 1) * span), into=result,
+            )
+            result, bufs = lax.optimization_barrier((result, bufs))
+    pieces = [buf.reshape(-1, 9, part) for buf in bufs]
+    conv = result
     weight_grad = jnp.concatenate(pieces, axis=-1).reshape(-1, 3, 3, outputs)
     return (conv, weight_grad)
 

time: 194 us -> 207 us (1.067)
  Pallas kernels: 58.7 us -> 80 us
  waiting for transfers between devices: 31.3 us -> 20.5 us
  other arithmetic: 1.57 us -> 3.71 us
    pallas_call x2 -> x6, Pallas kernels: 47.6 us -> 68.9 us  [second_stage(): pl.pallas_call(functools.partial(second_kernel, rows=rows, carry=prev is...]
    ppermute x10, waiting for transfers between devices: 20.8 us -> 9.95 us  [step(): return keep + lax.ppermute(send, axes, pairs)]
    add x10, other arithmetic: 0.27 us -> 2.4 us  [step(): return keep + lax.ppermute(send, axes, pairs)]
  transfers between devices with their start and end apart: 12 -> 12, of which waited for: 9 -> 7; matrix products, arithmetic and copies ran while one was open for 13% -> 10% of each run, Pallas kernels for 25% -> 23%
where the time goes in v6:
time: 207 us; the launch traced here: 206 us
  Pallas kernels  80 us (39%)
  blocking collectives  54.4 us (26%)
  local copies, waits for them, and re-layouts  28 us (14%)
  waiting for transfers between devices  20.5 us (10%)
  starting transfers between devices  18.4 us (9%)
  other arithmetic  3.71 us (2%)
    pallas_call x6, Pallas kernels, second_stage(): pl.pallas_call(functools.partial(second_kernel, rows=rows, carry=prev is...  68.9 us
    all_to_all x1, blocking collectives, local(): lax.all_to_all(local_hidden.reshape(tiles, owned, half_rows, width // 2,...  54.4 us
    pallas_call x1, Pallas kernels, first_stage(): pl.pallas_call(first_kernel, grid=(images,), in_specs=[pl.BlockSpec((None...  11.1 us
    ppermute x10, starting transfers between devices, step(): return keep + lax.ppermute(send, axes, pairs)  9.97 us
    ppermute x10, waiting for transfers between devices, step(): return keep + lax.ppermute(send, axes, pairs)  9.95 us
    all_to_all x1, waiting for transfers between devices, local(): lax.all_to_all(local_hidden.reshape(tiles, owned, half_rows, width // 2,...  7.13 us
    reshape x1, local copies, waits for them, and re-layouts, local(): grad_t = out_grad.reshape(owned, -1, outputs).transpose(0, 2, 1)  6.38 us
    concatenate x2, local copies, waits for them, and re-layouts, shift_cols_right(): return jnp.concatenate([zero_col, slab[:, :, :-1]], axis=2)  4.99 us
  transfers between devices with their start and end apart: 12, of which 7 were waited for; matrix products, arithmetic and copies ran while one was open for 10% of the time, Pallas kernels for 23%

profile of v6, /device:TPU:0, one launch (start us, length us, event | category | flops | bytes accessed | tf_op | source)
XLA Modules:
  0.0 205.8 jit_solution(1808480606525095665)
XLA Ops:
  0.6 0.0 copy-start
  0.6 1.0 slice.21
  1.7 4.9 %collective-permute-start = (bf16[8,1,128,128]{3,2,1,0:T(8,128)(2,1)S(1)}, bf16[8,1,128,128]{3,2,1,0:T(8,128)(2,1)S(1)}, u32[]{:S(2)}, u32[]{:S(2)}) collective-permute-start(bf16[8,1,128,128]{3,2,1,0:T(8,128)(2,1)S(1)} %slice.21), channel_id=1, source_target_pairs={{0,1},{1,2},{2,3},{3,4},{4,5},{5,6},{6,7},{8,9},{9,10},{10,11},{11... | collective-permute-start | bytes 786440 | tf_op jit(solution)/shard_map/ppermute | solution.py:14
  6.6 0.7 pad_clamp_fusion
  7.2 0.6 gather_fusion
  7.8 0.9 copy.14
  8.7 3.4 %collective-permute-done.up_ref = bf16[8,1,128,128]{3,2,1,0:T(8,128)(2,1)S(1)} collective-permute-done((bf16[8,1,128,128]{3,2,1,0:T(8,128)(2,1)S(1)}, bf16[8,1,128,128]{3,2,1,0:T(8,128)(2,1)S(1)}, u32[]{:S(2)}, u32[]{:S(2)}) %collective-permute-start) | collective-permute-done | bytes 262176 | tf_op jit(solution)/shard_map/ppermute | solution.py:14
  12.1 0.7 copy-done.5
  12.8 11.1 %shard_map.68 = (bf16[8,16,64,128]{3,2,1,0:T(8,128)(2,1)}, bf16[8,16,64,128]{3,2,1,0:T(8,128)(2,1)}) custom-call(bf16[8,32,128,128]{3,2,1,0:T(8,128)(2,1)} %x_ref.1, bf16[8,1,128,128]{3,2,1,0:T(8,128)(2,1)} %copy-done.5, bf16[1152,256]{1,0:T(8,128)(2,1)} %bitcast.82), custom_call_target="tpu_custom_call" | custom-call | flops 4831838208 | bytes 12582912 | tf_op jit(solution)/shard_map/pallas_call | solution.py:76
  23.9 54.4 %all_to_all.21 = bf16[8,1,16,64,128]{4,3,2,1,0:T(8,128)(2,1)} all-to-all(bf16[8,1,16,64,128]{4,3,2,1,0:T(8,128)(2,1)} %bitcast.77), channel_id=1, replica_groups=mesh['group'=4,'tile'=8] {'tile'}, dimensions={0} | all-to-all | bytes 4194304 | tf_op jit(solution)/shard_map/all_to_all | solution.py:251
  78.2 3.6 %all-to-all-start = ((bf16[8,1,16,64,128]{4,3,2,1,0:T(8,128)(2,1)}), bf16[8,1,16,64,128]{4,3,2,1,0:T(8,128)(2,1)S(1)}, u32[]{:S(2)}, u32[]{:S(2)}) async-start(bf16[8,1,16,64,128]{4,3,2,1,0:T(8,128)(2,1)} %bitcast.76), calls=%async_computation | async-start | bytes 4194304 | tf_op jit(solution)/shard_map/all_to_all | solution.py:251
  81.9 6.4 %copy.17 = bf16[1,8192,256]{1,2,0:T(8,128)(2,1)} copy(bf16[1,8192,256]{2,1,0:T(8,128)(2,1)} %bitcast.74) | data formatting | bytes 8388608 | tf_op jit(solution)/shard_map/reshape | solution.py:244
  88.2 2.5 %fusion = (bf16[3,3,128,256]{3,2,1,0:T(8,128)(2,1)}, bf16[3,3,128,256]{3,2,1,0:T(8,128)(2,1)}) fusion(bf16[3,3,256,256]{3,2,1,0:T(8,128)(2,1)} %param.7), kind=kLoop, calls=%fused_computation.27 | loop fusion | bytes 2359296 | tf_op jit(solution)/shard_map/slice | solution.py:262
  90.8 1.7 pad.11.refs_1_
  92.5 1.3 pad_slice_fusion.2
  93.8 2.5 %concatenate.20.refs_0_ = bf16[1,130,64,128]{3,2,1,0:T(8,128)(2,1)} pad(bf16[1,130,63,128]{3,2,1,0:T(8,128)(2,1)S(1)} %get-tuple-element.41, bf16[]{:T(256)} %constant.76.clone.1), padding=0_0x0_0x1_0x0_0 | pad | bytes 4226562 | tf_op jit(solution)/shard_map/concatenate | solution.py:19
  96.3 1.8 concatenate.21.refs_2_
  98.1 24.3 %shard_map.69 = (f32[1,128,64,256]{3,2,1,0:T(8,128)}, f32[1,256,1152]{2,1,0:T(8,128)}) custom-call(bf16[1,130,64,128]{3,2,1,0:T(8,128)(2,1)} %concatenate.20.refs_0_, bf16[1,130,64,128]{3,2,1,0:T(8,128)(2,1)} %pad.11.refs_1_, bf16[1,130,64,128]{3,2,1,0:T(8,128)(2,1)} %concatenate.21.refs_2_, bf16[1152,256]{1,0:T(8,128)(2,1)} %bitcast.83, ...), custom_call_target="tpu_custom_call" | custom-call | flops 9663676416 | bytes 23166976 | tf_op jit(solution)/shard_map/pallas_call | solution.py:179
  122.4 7.1 %all-to-all-done = bf16[8,1,16,64,128]{4,3,2,1,0:T(8,128)(2,1)S(1)} async-done(((bf16[8,1,16,64,128]{4,3,2,1,0:T(8,128)(2,1)}), bf16[8,1,16,64,128]{4,3,2,1,0:T(8,128)(2,1)S(1)}, u32[]{:S(2)}, u32[]{:S(2)}) %all-to-all-start) | async-done | bytes 2097184 | tf_op jit(solution)/shard_map/all_to_all | solution.py:251
  129.5 1.2 pad_slice_fusion
  130.7 1.8 pad.12.refs_1_
  132.5 2.5 %concatenate.22.refs_0_ = bf16[1,130,64,128]{3,2,1,0:T(8,128)(2,1)} pad(bf16[1,130,63,128]{3,2,1,0:T(8,128)(2,1)S(1)} %get-tuple-element.39, bf16[]{:T(256)} %constant.76.clone.1), padding=0_0x0_0x1_0x0_0 | pad | bytes 4226562 | tf_op jit(solution)/shard_map/concatenate | solution.py:19
  135.0 1.8 concatenate.23.refs_2_
  136.8 20.7 %shard_map.71 = f32[1,256,1152]{2,1,0:T(8,128)} custom-call(bf16[1,130,64,128]{3,2,1,0:T(8,128)(2,1)} %concatenate.22.refs_0_, bf16[1,130,64,128]{3,2,1,0:T(8,128)(2,1)} %pad.12.refs_1_, bf16[1,130,64,128]{3,2,1,0:T(8,128)(2,1)} %concatenate.23.refs_2_, bf16[1152,256]{1,0:T(8,128)(2,1)} %bitcast.69, bf16[1,256,8192]{2,1,0:T(8,128)(2,1)} %bitcast.60), custom_call_target="tpu_custom_call" | custom-call | flops 4831838208 | bytes 23166976 | tf_op jit(solution)/shard_map/pallas_call | solution.py:179
  157.5 1.1 dynamic-slice_bitcast_fusion
  158.6 0.1 collective-permute-start.2
  158.8 0.5 collective-permute-start.1
  159.3 5.9 %shard_map.70.refs_6_ = bf16[1,128,64,256]{3,2,1,0:T(8,128)(2,1)} custom-call(bf16[1,130,64,128]{3,2,1,0:T(8,128)(2,1)} %concatenate.22.refs_0_, bf16[1,130,64,128]{3,2,1,0:T(8,128)(2,1)} %pad.12.refs_1_, bf16[1,130,64,128]{3,2,1,0:T(8,128)(2,1)} %concatenate.23.refs_2_, bf16[1152,256]{1,0:T(8,128)(2,1)} %bitcast.70, bf16[1,256,8192]{2,1,0:T(8,128)(2,1)} %bitcast.61, ...), custom_call_target="tpu_custom_call" | custom-call | flops 1207959552 | bytes 10584064 | tf_op jit(solution)/shard_map/pallas_call | solution.py:179
  165.3 0.0 collective-permute-done.2
  165.3 1.1 bitcast_add_fusion
  166.4 1.1 bitcast_add_fusion.1
  167.6 1.6 collective-permute-start.4
  169.2 0.6 collective-permute-start.3
  169.8 5.9 %shard_map.72.refs_6_ = bf16[1,128,64,256]{3,2,1,0:T(8,128)(2,1)} custom-call(bf16[1,130,64,128]{3,2,1,0:T(8,128)(2,1)} %concatenate.22.refs_0_, bf16[1,130,64,128]{3,2,1,0:T(8,128)(2,1)} %pad.12.refs_1_, bf16[1,130,64,128]{3,2,1,0:T(8,128)(2,1)} %concatenate.23.refs_2_, bf16[1152,256]{1,0:T(8,128)(2,1)} %bitcast.71, ...), custom_call_target="tpu_custom_call", output_to_operand_aliasing={{}: (6, {})} | custom-call | flops 1207959552 | bytes 10584064 | tf_op jit(solution)/shard_map/pallas_call | solution.py:179
  175.7 1.8 collective-permute-done.4
  177.5 5.5 %collective-permute-done.3 = f32[2,2,2,8,1152]{4,3,2,1,0:T(8,128)S(1)} collective-permute-done((f32[2,2,2,8,1152]{4,3,2,1,0:T(8,128)S(1)}, f32[2,2,2,8,1152]{4,3,2,1,0:T(8,128)S(1)}, u32[]{:S(2)}, u32[]{:S(2)}) %collective-permute-start.3) | collective-permute-done | bytes 294944 | tf_op jit(solution)/shard_map/ppermute | solution.py:222
  183.1 1.5 collective-permute-start.6
  184.6 0.6 collective-permute-start.5
  185.2 5.9 %shard_map.73.refs_6_ = bf16[1,128,64,256]{3,2,1,0:T(8,128)(2,1)} custom-call(bf16[1,130,64,128]{3,2,1,0:T(8,128)(2,1)} %concatenate.22.refs_0_, bf16[1,130,64,128]{3,2,1,0:T(8,128)(2,1)} %pad.12.refs_1_, bf16[1,130,64,128]{3,2,1,0:T(8,128)(2,1)} %concatenate.23.refs_2_, bf16[1152,256]{1,0:T(8,128)(2,1)} %bitcast.72, ...), custom_call_target="tpu_custom_call", output_to_operand_aliasing={{}: (6, {})} | custom-call | flops 1207959552 | bytes 10584064 | tf_op jit(solution)/shard_map/pallas_call | solution.py:179
  191.2 0.1 collective-permute-done.5
  191.4 0.1 collective-permute-start.8
  191.5 2.0 collective-permute-start.7
  193.5 6.0 %shard_map.74 = bf16[1,128,64,256]{3,2,1,0:T(8,128)(2,1)} custom-call(bf16[1,130,64,128]{3,2,1,0:T(8,128)(2,1)} %concatenate.22.refs_0_, bf16[1,130,64,128]{3,2,1,0:T(8,128)(2,1)} %pad.12.refs_1_, bf16[1,130,64,128]{3,2,1,0:T(8,128)(2,1)} %concatenate.23.refs_2_, bf16[1152,256]{1,0:T(8,128)(2,1)} %bitcast.73, ...), custom_call_target="tpu_custom_call", output_to_operand_aliasing={{}: (6, {})} | custom-call | flops 1207959552 | bytes 10584064 | tf_op jit(solution)/shard_map/pallas_call | solution.py:179
  199.6 0.7 collective-permute-start.9
  200.3 2.3 %collective-permute-start.10 = (f32[8,1152]{1,0:T(8,128)S(1)}, f32[8,1152]{1,0:T(8,128)S(1)}, u32[]{:S(2)}, u32[]{:S(2)}) collective-permute-start(f32[8,1152]{1,0:T(8,128)S(1)} %dynamic-slice_bitcast_fusion.8), channel_id=1, source_target_pairs={{0,4},{1,5},{2,6},{3,7},{4,0},{5,1},{6,2},{7,3},{8,12},{9,13},{10,... | collective-permute-start | bytes 110600 | tf_op jit(solution)/shard_map/ppermute | solution.py:222
  202.5 1.9 collective-permute-done.9
  204.5 0.6 collective-permute-done.10
  205.1 0.6 pad_maximum_fusion
  (31 shorter events, 0.3 us)
Async XLA Ops:
  0.6 6.6 %copy-start = (bf16[3,3,128,256]{3,2,1,0:T(8,128)(2,1)S(1)}, bf16[3,3,128,256]{3,2,1,0:T(8,128)(2,1)}, u32[]{:S(2)}) copy-start(bf16[3,3,128,256]{3,2,1,0:T(8,128)(2,1)} %param.6) | copy-start | bytes 1769476
  1.7 10.4 %collective-permute-start = (bf16[8,1,128,128]{3,2,1,0:T(8,128)(2,1)S(1)}, bf16[8,1,128,128]{3,2,1,0:T(8,128)(2,1)S(1)}, u32[]{:S(2)}, u32[]{:S(2)}) collective-permute-start(bf16[8,1,128,128]{3,2,1,0:T(8,128)(2,1)S(1)} %slice.21), channel_id=1, source_target_pairs={{0,1},{1,2},{2,3},{3,4},{4,5},{5,6},{6,7},{8,9},{9,10},{10,11},{11... | collective-permute-start | bytes 786440 | tf_op jit(solution)/shard_map/ppermute | solution.py:14
  12.1 0.7 copy-start.5
  78.2 51.3 %all-to-all-start = ((bf16[8,1,16,64,128]{4,3,2,1,0:T(8,128)(2,1)}), bf16[8,1,16,64,128]{4,3,2,1,0:T(8,128)(2,1)S(1)}, u32[]{:S(2)}, u32[]{:S(2)}) async-start(bf16[8,1,16,64,128]{4,3,2,1,0:T(8,128)(2,1)} %bitcast.76), calls=%async_computation | async-start | bytes 4194304 | tf_op jit(solution)/shard_map/all_to_all | solution.py:251
  88.2 2.5 %copy-start.2 = (bf16[8,1,16,64,128]{4,3,2,1,0:T(8,128)(2,1)S(1)}, bf16[8,1,16,64,128]{4,3,2,1,0:T(8,128)(2,1)}, u32[]{:S(2)}) copy-start(bf16[8,1,16,64,128]{4,3,2,1,0:T(8,128)(2,1)} %all_to_all.21) | copy-start | bytes 6291460
  136.8 22.0 %copy-start.3 = (f32[1,256,1152]{2,1,0:T(8,128)S(1)}, f32[1,256,1152]{2,1,0:T(8,128)}, u32[]{:S(2)}) copy-start(f32[1,256,1152]{2,1,0:T(8,128)} %get-tuple-element.25) | copy-start | bytes 3538948
  158.6 6.6 %collective-permute-start.2 = (f32[2,2,2,2,8,1152]{5,4,3,2,1,0:T(8,128)S(1)}, f32[2,2,2,2,8,1152]{5,4,3,2,1,0:T(8,128)}, u32[]{:S(2)}, u32[]{:S(2)}) collective-permute-start(f32[2,2,2,2,8,1152]{5,4,3,2,1,0:T(8,128)S(1)} %dynamic-slice_bitcast_fusion), channel_id=1, source_target_pairs={{0,8},{1,9},{2,10},{3,11},{4,12},{5,13},{6,14},{7,15},{8,0},{9,1},... | collective-permute-start | bytes 1769480 | tf_op jit(solution)/shard_map/ppermute | solution.py:222
  158.8 6.5 %copy-start.4 = (f32[1,256,1152]{2,1,0:T(8,128)S(1)}, f32[1,256,1152]{2,1,0:T(8,128)}, u32[]{:S(2)}) copy-start(f32[1,256,1152]{2,1,0:T(8,128)} %shard_map.71) | copy-start | bytes 3538948
  158.8 7.6 %collective-permute-start.1 = (f32[2,2,2,2,8,1152]{5,4,3,2,1,0:T(8,128)S(1)}, f32[2,2,2,2,8,1152]{5,4,3,2,1,0:T(8,128)}, u32[]{:S(2)}, u32[]{:S(2)}) collective-permute-start(f32[2,2,2,2,8,1152]{5,4,3,2,1,0:T(8,128)S(1)} %dynamic-slice_bitcast_fusion.1), channel_id=1, source_target_pairs={{0,8},{1,9},{2,10},{3,11},{4,12},{5,13},{6,14},{7,15},{8,0},{9,1},... | collective-permute-start | bytes 1769480 | tf_op jit(solution)/shard_map/ppermute | solution.py:222
  167.6 9.9 %collective-permute-start.4 = (f32[2,2,2,8,1152]{4,3,2,1,0:T(8,128)S(1)}, f32[2,2,2,8,1152]{4,3,2,1,0:T(8,128)S(1)}, u32[]{:S(2)}, u32[]{:S(2)}) collective-permute-start(f32[2,2,2,8,1152]{4,3,2,1,0:T(8,128)S(1)} %dynamic-slice_bitcast_fusion.2), channel_id=1, source_target_pairs={{0,16},{1,17},{2,18},{3,19},{4,20},{5,21},{6,22},{7,23},{8,24},{9,... | collective-permute-start | bytes 884744 | tf_op jit(solution)/shard_map/ppermute | solution.py:222
  169.2 13.8 %collective-permute-start.3 = (f32[2,2,2,8,1152]{4,3,2,1,0:T(8,128)S(1)}, f32[2,2,2,8,1152]{4,3,2,1,0:T(8,128)S(1)}, u32[]{:S(2)}, u32[]{:S(2)}) collective-permute-start(f32[2,2,2,8,1152]{4,3,2,1,0:T(8,128)S(1)} %dynamic-slice_bitcast_fusion.3), channel_id=1, source_target_pairs={{0,16},{1,17},{2,18},{3,19},{4,20},{5,21},{6,22},{7,23},{8,24},{9,... | collective-permute-start | bytes 884744 | tf_op jit(solution)/shard_map/ppermute | solution.py:222
  183.1 8.1 %collective-permute-start.6 = (f32[2,2,8,1152]{3,2,1,0:T(8,128)S(1)}, f32[2,2,8,1152]{3,2,1,0:T(8,128)S(1)}, u32[]{:S(2)}, u32[]{:S(2)}) collective-permute-start(f32[2,2,8,1152]{3,2,1,0:T(8,128)S(1)} %dynamic-slice_bitcast_fusion.4), channel_id=1, source_target_pairs={{0,1},{1,0},{2,3},{3,2},{4,5},{5,4},{6,7},{7,6},{8,9},{9,8},{10,11... | collective-permute-start | bytes 442376 | tf_op jit(solution)/shard_map/ppermute | solution.py:222
  184.6 6.7 %collective-permute-start.5 = (f32[2,2,8,1152]{3,2,1,0:T(8,128)S(1)}, f32[2,2,8,1152]{3,2,1,0:T(8,128)S(1)}, u32[]{:S(2)}, u32[]{:S(2)}) collective-permute-start(f32[2,2,8,1152]{3,2,1,0:T(8,128)S(1)} %dynamic-slice_bitcast_fusion.5), channel_id=1, source_target_pairs={{0,1},{1,0},{2,3},{3,2},{4,5},{5,4},{6,7},{7,6},{8,9},{9,8},{10,11... | collective-permute-start | bytes 442376 | tf_op jit(solution)/shard_map/ppermute | solution.py:222
  191.4 8.1 %collective-permute-start.8 = (f32[2,8,1152]{2,1,0:T(8,128)S(1)}, f32[2,8,1152]{2,1,0:T(8,128)S(1)}, u32[]{:S(2)}, u32[]{:S(2)}) collective-permute-start(f32[2,8,1152]{2,1,0:T(8,128)S(1)} %dynamic-slice_bitcast_fusion.6), channel_id=1, source_target_pairs={{0,2},{1,3},{2,0},{3,1},{4,6},{5,7},{6,4},{7,5},{8,10},{9,11},{10,... | collective-permute-start | bytes 221192 | tf_op jit(solution)/shard_map/ppermute | solution.py:222
  191.5 8.0 %collective-permute-start.7 = (f32[2,8,1152]{2,1,0:T(8,128)S(1)}, f32[2,8,1152]{2,1,0:T(8,128)S(1)}, u32[]{:S(2)}, u32[]{:S(2)}) collective-permute-start(f32[2,8,1152]{2,1,0:T(8,128)S(1)} %dynamic-slice_bitcast_fusion.7), channel_id=1, source_target_pairs={{0,2},{1,3},{2,0},{3,1},{4,6},{5,7},{6,4},{7,5},{8,10},{9,11},{10,... | collective-permute-start | bytes 221192 | tf_op jit(solution)/shard_map/ppermute | solution.py:222
  193.5 12.3 %copy-start.1 = (bf16[3,3,128,256]{3,2,1,0:T(8,128)(2,1)S(1)}, bf16[3,3,128,256]{3,2,1,0:T(8,128)(2,1)}, u32[]{:S(2)}) copy-start(bf16[3,3,128,256]{3,2,1,0:T(8,128)(2,1)} %param.6) | copy-start | bytes 1769476
  199.6 4.9 %collective-permute-start.9 = (f32[8,1152]{1,0:T(8,128)S(1)}, f32[8,1152]{1,0:T(8,128)S(1)}, u32[]{:S(2)}, u32[]{:S(2)}) collective-permute-start(f32[8,1152]{1,0:T(8,128)S(1)} %dynamic-slice_bitcast_fusion.9), channel_id=1, source_target_pairs={{0,4},{1,5},{2,6},{3,7},{4,0},{5,1},{6,2},{7,3},{8,12},{9,13},{10,... | collective-permute-start | bytes 110600 | tf_op jit(solution)/shard_map/ppermute | solution.py:222
  200.3 4.9 %collective-permute-start.10 = (f32[8,1152]{1,0:T(8,128)S(1)}, f32[8,1152]{1,0:T(8,128)S(1)}, u32[]{:S(2)}, u32[]{:S(2)}) collective-permute-start(f32[8,1152]{1,0:T(8,128)S(1)} %dynamic-slice_bitcast_fusion.8), channel_id=1, source_target_pairs={{0,4},{1,5},{2,6},{3,7},{4,0},{5,1},{6,2},{7,3},{8,12},{9,13},{10,... | collective-permute-start | bytes 110600 | tf_op jit(solution)/shard_map/ppermute | solution.py:222

commit v7 on v4

--- a/solution.py
+++ b/solution.py
@@ -95,7 +95,7 @@
     )(maps, upper_row, weight)
 
 
-def second_kernel(*refs, rows, carry, group):
+def second_kernel(*refs, rows, carry):
     if carry:
         left_ref, mid_ref, right_ref, weight_ref, grad_ref, prev_ref, out_ref, wgrad_ref = refs
     else:
@@ -104,34 +104,31 @@
     _, width, outputs = out_ref.shape
     inputs = mid_ref.shape[-1]
     sources = (left_ref, mid_ref, right_ref)
-    grad_t = grad_ref[...]
+    patches = jnp.concatenate(
+        [
+            sources[tap % 3][pl.ds(step * rows + tap // 3, rows)].reshape(rows * width, inputs)
+            for tap in range(9)
+        ],
+        axis=-1,
+    )
+    total = jnp.dot(patches, weight_ref[...], preferred_element_type=jnp.float32)
     if carry:
-        acc = prev_ref[...].reshape(rows * width, outputs)
-    else:
-        acc = jnp.zeros((rows * width, outputs), jnp.float32)
-    for first in range(0, 9, group):
-        taps = range(first, min(first + group, 9))
-        windows = [
-            sources[tap % 3][pl.ds(step * rows + tap // 3, rows)].reshape(rows * width, inputs)
-            for tap in taps
-        ]
-        window = windows[0] if len(windows) == 1 else jnp.concatenate(windows, axis=-1)
-        lanes = slice(first * inputs, (first + len(windows)) * inputs)
-        acc = acc + jnp.dot(window, weight_ref[lanes, :], preferred_element_type=jnp.float32)
-        term = jnp.dot(grad_t, window, preferred_element_type=jnp.float32)
-
-        @pl.when(step == 0)
-        def _():
-            wgrad_ref[:, lanes] = term
-
-        @pl.when(step > 0)
-        def _():
-            wgrad_ref[:, lanes] += term
-
-    out_ref[...] = acc.astype(out_ref.dtype).reshape(rows, width, outputs)
-
-
-def second_stage(hidden, weight, grad_t, prev, out_dtype):
+        total = total + prev_ref[...].reshape(rows * width, outputs)
+    out_ref[...] = total.astype(out_ref.dtype).reshape(rows, width, outputs)
+    term = lax.dot_general(
+        patches, grad_ref[...], (((0,), (0,)), ((), ())), preferred_element_type=jnp.float32
+    )
+
+    @pl.when(step == 0)
+    def _():
+        wgrad_ref[...] = term
+
+    @pl.when(step > 0)
+    def _():
+        wgrad_ref[...] += term
+
+
+def second_stage(hidden, weight, grad, prev, out_dtype):
     owned, out_rows, out_cols, inputs = hidden.shape
     outputs = weight.shape[-1]
     rows = min(16, out_rows)
@@ -144,21 +141,21 @@
         full,
         full,
         pl.BlockSpec((9 * inputs, outputs), lambda n, i: (0, 0)),
-        pl.BlockSpec((None, outputs, rows * out_cols), lambda n, i: (n, 0, i)),
+        pl.BlockSpec((None, rows * out_cols, outputs), lambda n, i: (n, i, 0)),
     ]
-    operands = [*shifted, weight.reshape(9 * inputs, outputs), grad_t]
+    operands = [*shifted, weight.reshape(9 * inputs, outputs), grad]
     if prev is not None:
         in_specs.append(block)
         operands.append(prev)
     flops = 4 * owned * out_rows * out_cols * 9 * inputs * outputs
-    return pl.pallas_call(
-        functools.partial(second_kernel, rows=rows, carry=prev is not None, group=max(1, 256 // inputs)),
+    conv, wgrad_t = pl.pallas_call(
+        functools.partial(second_kernel, rows=rows, carry=prev is not None),
         grid=(owned, out_rows // rows),
         in_specs=in_specs,
-        out_specs=[block, pl.BlockSpec((None, outputs, 9 * inputs), lambda n, i: (n, 0, 0))],
+        out_specs=[block, pl.BlockSpec((None, 9 * inputs, outputs), lambda n, i: (n, 0, 0))],
         out_shape=[
             jax.ShapeDtypeStruct((owned, out_rows, out_cols, outputs), out_dtype),
-            jax.ShapeDtypeStruct((owned, outputs, 9 * inputs), jnp.float32),
+            jax.ShapeDtypeStruct((owned, 9 * inputs, outputs), jnp.float32),
         ],
         compiler_params=pltpu.CompilerParams(
             dimension_semantics=("arbitrary", "arbitrary"), vmem_limit_bytes=60 * 1024 * 1024
@@ -170,6 +167,7 @@
             + owned * outputs * 9 * inputs * 4,
         ),
     )(*operands)
+    return conv, wgrad_t.sum(axis=0).T
 
 
 def halving_reduce_scatter(partial, axes):
@@ -202,7 +200,7 @@
     chunks = 2
     part = outputs // chunks
     upper_row = shifted_2(maps[:, height - 1 : height], "tile", 1)
-    grad_t = out_grad.reshape(owned, -1, outputs).transpose(0, 2, 1)
+    grad = out_grad.reshape(owned, -1, outputs)
     conv = None
     pieces = []
     halves = first_stage(maps, upper_row, first_weight, part)
@@ -221,9 +219,9 @@
         hidden = arrived.reshape(owned, half_rows * tiles, width // 2, part)
         last = chunk == chunks - 1
         conv, partial = second_stage(
-            hidden, second_weight[:, :, channels], grad_t, conv, jnp.bfloat16 if last else jnp.float32
+            hidden, second_weight[:, :, channels], grad, conv, jnp.bfloat16 if last else jnp.float32
         )
-        summed = halving_reduce_scatter(partial.sum(axis=0).reshape(outputs, 9 * part), ("group", "tile"))
+        summed = halving_reduce_scatter(partial.reshape(outputs, 9 * part), ("group", "tile"))
         pieces.append(summed.reshape(-1, 9, part))
     weight_grad = jnp.concatenate(pieces, axis=-1).reshape(-1, 3, 3, outputs)
     return (conv, weight_grad)

time: 194 us -> 198 us (1.021)
  waiting for transfers between devices: 31.3 us -> 47.2 us
  Pallas kernels: 58.7 us -> 45.8 us
  other arithmetic: 1.57 us -> 3.7 us
    all_to_all x1, waiting for transfers between devices: 7.14 us -> 20.9 us  [local(): lax.all_to_all(local_hidden.reshape(tiles, owned, half_rows, width // 2,...]
    pallas_call x2, Pallas kernels: 47.6 us -> 34.6 us  [second_stage(): pl.pallas_call(functools.partial(second_kernel, rows=rows, carry=prev is...]
    reshape x1 -> x0, local copies, waits for them, and re-layouts: 6.37 us -> none  [local(): grad_t = out_grad.reshape(owned, -1, outputs).transpose(0, 2, 1)]
    transpose x0 -> x2, local copies, waits for them, and re-layouts: none -> 3.42 us  [second_stage(): return (conv, wgrad_t.sum(axis=0).T)]
    add x10, other arithmetic: 0.27 us -> 2.4 us  [halving_reduce_scatter(): buf = keep + lax.ppermute(send, axes, pairs)]
    slice x2, local copies, waits for them, and re-layouts: 2.51 us -> 4.63 us  [shift_cols_left(): return jnp.concatenate([slab[:, :, 1:], zero_col], axis=2)]
    ppermute x10, waiting for transfers between devices: 20.8 us -> 22.9 us  [halving_reduce_scatter(): buf = keep + lax.ppermute(send, axes, pairs)]
  transfers between devices with their start and end apart: 12 -> 12, of which waited for: 9 -> 10; matrix products, arithmetic and copies ran while one was open for 13% -> 10% of each run, Pallas kernels for 25% -> 18%
where the time goes in v7:
time: 198 us; the launch traced here: 197 us
  blocking collectives  54.4 us (27%)
  waiting for transfers between devices  47.2 us (24%)
  Pallas kernels  45.8 us (23%)
  local copies, waits for them, and re-layouts  27.8 us (14%)
  starting transfers between devices  17.5 us (9%)
  other arithmetic  3.7 us (2%)
    all_to_all x1, blocking collectives, local(): lax.all_to_all(local_hidden.reshape(tiles, owned, half_rows, width // 2,...  54.4 us
    pallas_call x2, Pallas kernels, second_stage(): pl.pallas_call(functools.partial(second_kernel, rows=rows, carry=prev is...  34.6 us
    ppermute x10, waiting for transfers between devices, halving_reduce_scatter(): buf = keep + lax.ppermute(send, axes, pairs)  22.9 us
    all_to_all x1, waiting for transfers between devices, local(): lax.all_to_all(local_hidden.reshape(tiles, owned, half_rows, width // 2,...  20.9 us
    pallas_call x1, Pallas kernels, first_stage(): pl.pallas_call(first_kernel, grid=(images,), in_specs=[pl.BlockSpec((None...  11.1 us
    ppermute x10, starting transfers between devices, halving_reduce_scatter(): buf = keep + lax.ppermute(send, axes, pairs)  8.88 us
    concatenate x2, local copies, waits for them, and re-layouts, shift_cols_right(): return jnp.concatenate([zero_col, slab[:, :, :-1]], axis=2)  4.99 us
    ppermute x1, starting transfers between devices, shifted_2(): return lax.ppermute(shard, axis, pairs)  4.86 us
  transfers between devices with their start and end apart: 12, of which 10 were waited for; matrix products, arithmetic and copies ran while one was open for 10% of the time, Pallas kernels for 18%

profile of v7, /device:TPU:0, one launch (start us, length us, event | category | flops | bytes accessed | tf_op | source)
XLA Modules:
  0.0 197.1 jit_solution(15410109725730753484)
XLA Ops:
  0.6 1.0 slice.21
  1.7 4.9 %collective-permute-start = (bf16[8,1,128,128]{3,2,1,0:T(8,128)(2,1)S(1)}, bf16[8,1,128,128]{3,2,1,0:T(8,128)(2,1)S(1)}, u32[]{:S(2)}, u32[]{:S(2)}) collective-permute-start(bf16[8,1,128,128]{3,2,1,0:T(8,128)(2,1)S(1)} %slice.21), channel_id=1, source_target_pairs={{0,1},{1,2},{2,3},{3,4},{4,5},{5,6},{6,7},{8,9},{9,10},{10,11},{11... | collective-permute-start | bytes 786440 | tf_op jit(solution)/shard_map/ppermute | solution.py:14
  6.6 0.7 pad_clamp_fusion
  7.2 0.6 gather_fusion
  7.8 0.9 copy.18
  8.7 3.4 %collective-permute-done.up_ref = bf16[8,1,128,128]{3,2,1,0:T(8,128)(2,1)S(1)} collective-permute-done((bf16[8,1,128,128]{3,2,1,0:T(8,128)(2,1)S(1)}, bf16[8,1,128,128]{3,2,1,0:T(8,128)(2,1)S(1)}, u32[]{:S(2)}, u32[]{:S(2)}) %collective-permute-start) | collective-permute-done | bytes 262176 | tf_op jit(solution)/shard_map/ppermute | solution.py:14
  12.1 0.7 copy-done.6
  12.8 11.1 %shard_map.68 = (bf16[8,16,64,128]{3,2,1,0:T(8,128)(2,1)}, bf16[8,16,64,128]{3,2,1,0:T(8,128)(2,1)}) custom-call(bf16[8,32,128,128]{3,2,1,0:T(8,128)(2,1)} %x_ref.1, bf16[8,1,128,128]{3,2,1,0:T(8,128)(2,1)} %copy-done.6, bf16[1152,256]{1,0:T(8,128)(2,1)} %bitcast.79), custom_call_target="tpu_custom_call" | custom-call | flops 4831838208 | bytes 12582912 | tf_op jit(solution)/shard_map/pallas_call | solution.py:76
  23.9 54.4 %all_to_all.21 = bf16[8,1,16,64,128]{4,3,2,1,0:T(8,128)(2,1)} all-to-all(bf16[8,1,16,64,128]{4,3,2,1,0:T(8,128)(2,1)} %bitcast.76), channel_id=1, replica_groups=mesh['group'=4,'tile'=8] {'tile'}, dimensions={0} | all-to-all | bytes 4194304 | tf_op jit(solution)/shard_map/all_to_all | solution.py:210
  78.3 3.7 %all-to-all-start = ((bf16[8,1,16,64,128]{4,3,2,1,0:T(8,128)(2,1)}), bf16[8,1,16,64,128]{4,3,2,1,0:T(8,128)(2,1)S(1)}, u32[]{:S(2)}, u32[]{:S(2)}) async-start(bf16[8,1,16,64,128]{4,3,2,1,0:T(8,128)(2,1)} %bitcast.75), calls=%async_computation | async-start | bytes 4194304 | tf_op jit(solution)/shard_map/all_to_all | solution.py:210
  82.1 1.1 fusion
  83.2 0.9 copy-done.2
  84.1 1.8 pad.11.refs_1_
  85.9 1.3 pad_slice_fusion.2
  87.2 1.8 concatenate.21.refs_2_
  89.0 2.5 %concatenate.20.refs_0_ = bf16[1,130,64,128]{3,2,1,0:T(8,128)(2,1)} pad(bf16[1,130,63,128]{3,2,1,0:T(8,128)(2,1)S(1)} %get-tuple-element.21, bf16[]{:T(256)} %constant.76.clone.1), padding=0_0x0_0x1_0x0_0 | pad | bytes 4226562 | tf_op jit(solution)/shard_map/concatenate | solution.py:19
  91.5 17.3 %shard_map.69 = (f32[1,128,64,256]{3,2,1,0:T(8,128)}, f32[1,1152,256]{2,1,0:T(8,128)}) custom-call(bf16[1,130,64,128]{3,2,1,0:T(8,128)(2,1)} %concatenate.20.refs_0_, bf16[1,130,64,128]{3,2,1,0:T(8,128)(2,1)} %pad.11.refs_1_, bf16[1,130,64,128]{3,2,1,0:T(8,128)(2,1)} %concatenate.21.refs_2_, bf16[1152,256]{1,0:T(8,128)(2,1)} %bitcast.81, ...), custom_call_target="tpu_custom_call" | custom-call | flops 9663676416 | bytes 26345472 | tf_op jit(solution)/shard_map/pallas_call | solution.py:151
  108.8 20.9 %all-to-all-done = bf16[8,1,16,64,128]{4,3,2,1,0:T(8,128)(2,1)S(1)} async-done(((bf16[8,1,16,64,128]{4,3,2,1,0:T(8,128)(2,1)}), bf16[8,1,16,64,128]{4,3,2,1,0:T(8,128)(2,1)S(1)}, u32[]{:S(2)}, u32[]{:S(2)}) %all-to-all-start) | async-done | bytes 2097184 | tf_op jit(solution)/shard_map/all_to_all | solution.py:210
  129.7 1.8 pad.12.refs_1_
  131.5 3.3 %pad_slice_fusion = (bf16[1,130,63,128]{3,2,1,0:T(8,128)(2,1)}, bf16[1,130,63,128]{3,2,1,0:T(8,128)(2,1)}) fusion(bf16[1,128,64,128]{3,2,1,0:T(8,128)(2,1)S(1)} %bitcast.67), kind=kLoop, calls=%fused_computation.27 | loop fusion | bytes 6290432 | tf_op jit(solution)/shard_map/slice | solution.py:24
  134.8 1.8 copy.21
  136.6 0.9 dynamic-slice_bitcast_fusion.1
  137.5 1.8 concatenate.23.refs_2_
  139.3 0.2 copy-done.3
  139.6 2.5 %concatenate.22.refs_0_ = bf16[1,130,64,128]{3,2,1,0:T(8,128)(2,1)} pad(bf16[1,130,63,128]{3,2,1,0:T(8,128)(2,1)S(1)} %copy-done.3, bf16[]{:T(256)} %constant.76.clone.1), padding=0_0x0_0x1_0x0_0 | pad | bytes 4226562 | tf_op jit(solution)/shard_map/concatenate | solution.py:19
  142.1 17.3 %shard_map.70 = (bf16[1,128,64,256]{3,2,1,0:T(8,128)(2,1)}, f32[1,1152,256]{2,1,0:T(8,128)}) custom-call(bf16[1,130,64,128]{3,2,1,0:T(8,128)(2,1)} %concatenate.22.refs_0_, bf16[1,130,64,128]{3,2,1,0:T(8,128)(2,1)} %pad.12.refs_1_, bf16[1,130,64,128]{3,2,1,0:T(8,128)(2,1)} %concatenate.23.refs_2_, bf16[1152,256]{1,0:T(8,128)(2,1)} %bitcast.80, ...), custom_call_target="tpu_custom_call" | custom-call | flops 9663676416 | bytes 26345472 | tf_op jit(solution)/shard_map/pallas_call | solution.py:151
  159.4 1.6 copy.24
  161.0 0.9 dynamic-slice_bitcast_fusion
  161.9 0.5 collective-permute-start.6
  162.5 1.1 bitcast_add_fusion.1
  163.6 0.8 collective-permute-done.6
  164.4 1.1 bitcast_add_fusion
  165.5 0.1 constant_dynamic-slice_fusion.1
  165.7 1.6 collective-permute-start.2
  167.3 0.6 collective-permute-start.7
  167.9 7.7 %collective-permute-done.2 = f32[2,2,2,8,1152]{4,3,1,0,2:T(8,128)S(1)} collective-permute-done((f32[2,2,2,8,1152]{4,3,1,0,2:T(8,128)S(1)}, f32[2,2,2,8,1152]{4,3,1,0,2:T(8,128)S(1)}, u32[]{:S(2)}, u32[]{:S(2)}) %collective-permute-start.2) | collective-permute-done | bytes 294944 | tf_op jit(solution)/shard_map/ppermute | solution.py:189
  175.7 1.5 collective-permute-start.3
  177.2 4.2 %collective-permute-done.7 = f32[2,2,2,8,1152]{4,3,1,0,2:T(8,128)S(1)} collective-permute-done((f32[2,2,2,8,1152]{4,3,1,0,2:T(8,128)S(1)}, f32[2,2,2,8,1152]{4,3,1,0,2:T(8,128)S(1)}, u32[]{:S(2)}, u32[]{:S(2)}) %collective-permute-start.7) | collective-permute-done | bytes 294944 | tf_op jit(solution)/shard_map/ppermute | solution.py:189
  181.4 1.5 collective-permute-start.8
  183.1 3.7 %collective-permute-done.8 = f32[2,2,8,1152]{3,2,1,0:T(8,128)S(1)} collective-permute-done((f32[2,2,8,1152]{3,2,1,0:T(8,128)S(1)}, f32[2,2,8,1152]{3,2,1,0:T(8,128)S(1)}, u32[]{:S(2)}, u32[]{:S(2)}) %collective-permute-start.8) | collective-permute-done | bytes 147488 | tf_op jit(solution)/shard_map/ppermute | solution.py:189
  186.8 0.1 collective-permute-start.9
  186.9 0.5 collective-permute-done.4
  187.4 2.1 %collective-permute-start.5 = (f32[8,1152]{1,0:T(8,128)S(1)}, f32[8,1152]{1,0:T(8,128)S(1)}, u32[]{:S(2)}, u32[]{:S(2)}) collective-permute-start(f32[8,1152]{1,0:T(8,128)S(1)} %dynamic-slice_bitcast_fusion.7), channel_id=1, source_target_pairs={{0,4},{1,5},{2,6},{3,7},{4,0},{5,1},{6,2},{7,3},{8,12},{9,13},{10,... | collective-permute-start | bytes 110600 | tf_op jit(solution)/shard_map/ppermute | solution.py:189
  189.6 1.7 collective-permute-done.9
  191.3 0.9 collective-permute-start.10
  192.2 1.2 collective-permute-done.5
  193.4 3.1 %collective-permute-done.10 = f32[8,1152]{1,0:T(8,128)S(1)} collective-permute-done((f32[8,1152]{1,0:T(8,128)S(1)}, f32[8,1152]{1,0:T(8,128)S(1)}, u32[]{:S(2)}, u32[]{:S(2)}) %collective-permute-start.10) | collective-permute-done | bytes 36896 | tf_op jit(solution)/shard_map/ppermute | solution.py:189
  196.5 0.6 pad_maximum_fusion
  (31 shorter events, 0.4 us)
Async XLA Ops:
  0.6 6.6 %copy-start = (bf16[3,3,128,256]{3,2,1,0:T(8,128)(2,1)S(1)}, bf16[3,3,128,256]{3,2,1,0:T(8,128)(2,1)}, u32[]{:S(2)}) copy-start(bf16[3,3,128,256]{3,2,1,0:T(8,128)(2,1)} %param.6) | copy-start | bytes 1769476
  1.7 10.4 %collective-permute-start = (bf16[8,1,128,128]{3,2,1,0:T(8,128)(2,1)S(1)}, bf16[8,1,128,128]{3,2,1,0:T(8,128)(2,1)S(1)}, u32[]{:S(2)}, u32[]{:S(2)}) collective-permute-start(bf16[8,1,128,128]{3,2,1,0:T(8,128)(2,1)S(1)} %slice.21), channel_id=1, source_target_pairs={{0,1},{1,2},{2,3},{3,4},{4,5},{5,6},{6,7},{8,9},{9,10},{10,11},{11... | collective-permute-start | bytes 786440 | tf_op jit(solution)/shard_map/ppermute | solution.py:14
  12.1 0.7 copy-start.6
  78.3 3.8 %copy-start.5 = (bf16[3,3,256,256]{3,2,1,0:T(8,128)(2,1)S(1)}, bf16[3,3,256,256]{3,2,1,0:T(8,128)(2,1)}, u32[]{:S(2)}) copy-start(bf16[3,3,256,256]{3,2,1,0:T(8,128)(2,1)} %param.7) | copy-start | bytes 3538948
  78.3 51.4 %all-to-all-start = ((bf16[8,1,16,64,128]{4,3,2,1,0:T(8,128)(2,1)}), bf16[8,1,16,64,128]{4,3,2,1,0:T(8,128)(2,1)S(1)}, u32[]{:S(2)}, u32[]{:S(2)}) async-start(bf16[8,1,16,64,128]{4,3,2,1,0:T(8,128)(2,1)} %bitcast.75), calls=%async_computation | async-start | bytes 4194304 | tf_op jit(solution)/shard_map/all_to_all | solution.py:210
  82.0 2.0 %copy-start.2 = (bf16[8,1,16,64,128]{4,3,2,1,0:T(8,128)(2,1)S(1)}, bf16[8,1,16,64,128]{4,3,2,1,0:T(8,128)(2,1)}, u32[]{:S(2)}) copy-start(bf16[8,1,16,64,128]{4,3,2,1,0:T(8,128)(2,1)} %all_to_all.21) | copy-start | bytes 6291460
  134.8 2.7 %copy-start.4 = (bf16[1,130,63,128]{3,2,1,0:T(8,128)(2,1)S(1)}, bf16[1,130,63,128]{3,2,1,0:T(8,128)(2,1)}, u32[]{:S(2)}) copy-start(bf16[1,130,63,128]{3,2,1,0:T(8,128)(2,1)} %get-tuple-element.18) | copy-start | bytes 6289924
  137.5 24.9 %collective-permute-start.1 = (f32[2,2,2,2,8,1152]{5,4,3,2,1,0:T(8,128)}, f32[2,2,2,2,8,1152]{5,4,3,2,1,0:T(8,128)}, u32[]{:S(2)}, u32[]{:S(2)}) collective-permute-start(f32[2,2,2,2,8,1152]{5,4,3,2,1,0:T(8,128)} %dynamic-slice_bitcast_fusion.1), channel_id=1, source_target_pairs={{0,8},{1,9},{2,10},{3,11},{4,12},{5,13},{6,14},{7,15},{8,0},{9,1},... | collective-permute-start | bytes 1769480 | tf_op jit(solution)/shard_map/ppermute | solution.py:189
  137.5 2.0 %copy-start.3 = (bf16[1,130,63,128]{3,2,1,0:T(8,128)(2,1)S(1)}, bf16[1,130,63,128]{3,2,1,0:T(8,128)(2,1)}, u32[]{:S(2)}) copy-start(bf16[1,130,63,128]{3,2,1,0:T(8,128)(2,1)} %get-tuple-element.19) | copy-start | bytes 6289924
  161.9 2.5 %collective-permute-start.6 = (f32[2,2,2,2,8,1152]{5,4,3,2,1,0:T(8,128)}, f32[2,2,2,2,8,1152]{5,4,3,2,1,0:T(8,128)}, u32[]{:S(2)}, u32[]{:S(2)}) collective-permute-start(f32[2,2,2,2,8,1152]{5,4,3,2,1,0:T(8,128)} %dynamic-slice_bitcast_fusion), channel_id=1, source_target_pairs={{0,8},{1,9},{2,10},{3,11},{4,12},{5,13},{6,14},{7,15},{8,0},{9,1},... | collective-permute-start | bytes 1769480 | tf_op jit(solution)/shard_map/ppermute | solution.py:189
  165.7 9.9 %collective-permute-start.2 = (f32[2,2,2,8,1152]{4,3,1,0,2:T(8,128)S(1)}, f32[2,2,2,8,1152]{4,3,1,0,2:T(8,128)S(1)}, u32[]{:S(2)}, u32[]{:S(2)}) collective-permute-start(f32[2,2,2,8,1152]{4,3,1,0,2:T(8,128)S(1)} %bitcast.82), channel_id=1, source_target_pairs={{0,16},{1,17},{2,18},{3,19},{4,20},{5,21},{6,22},{7,23},{8,24},{9,... | collective-permute-start | bytes 884744 | tf_op jit(solution)/shard_map/ppermute | solution.py:189
  167.3 14.1 %collective-permute-start.7 = (f32[2,2,2,8,1152]{4,3,1,0,2:T(8,128)S(1)}, f32[2,2,2,8,1152]{4,3,1,0,2:T(8,128)S(1)}, u32[]{:S(2)}, u32[]{:S(2)}) collective-permute-start(f32[2,2,2,8,1152]{4,3,1,0,2:T(8,128)S(1)} %bitcast.83), channel_id=1, source_target_pairs={{0,16},{1,17},{2,18},{3,19},{4,20},{5,21},{6,22},{7,23},{8,24},{9,... | collective-permute-start | bytes 884744 | tf_op jit(solution)/shard_map/ppermute | solution.py:189
  175.6 21.5 %copy-start.1 = (bf16[3,3,128,256]{3,2,1,0:T(8,128)(2,1)S(1)}, bf16[3,3,128,256]{3,2,1,0:T(8,128)(2,1)}, u32[]{:S(2)}) copy-start(bf16[3,3,128,256]{3,2,1,0:T(8,128)(2,1)} %param.6) | copy-start | bytes 1769476
  175.7 7.3 %collective-permute-start.3 = (f32[2,2,8,1152]{3,2,1,0:T(8,128)S(1)}, f32[2,2,8,1152]{3,2,1,0:T(8,128)S(1)}, u32[]{:S(2)}, u32[]{:S(2)}) collective-permute-start(f32[2,2,8,1152]{3,2,1,0:T(8,128)S(1)} %dynamic-slice_bitcast_fusion.3), channel_id=1, source_target_pairs={{0,1},{1,0},{2,3},{3,2},{4,5},{5,4},{6,7},{7,6},{8,9},{9,8},{10,11... | collective-permute-start | bytes 442376 | tf_op jit(solution)/shard_map/ppermute | solution.py:189
  181.4 5.4 %collective-permute-start.8 = (f32[2,2,8,1152]{3,2,1,0:T(8,128)S(1)}, f32[2,2,8,1152]{3,2,1,0:T(8,128)S(1)}, u32[]{:S(2)}, u32[]{:S(2)}) collective-permute-start(f32[2,2,8,1152]{3,2,1,0:T(8,128)S(1)} %dynamic-slice_bitcast_fusion.2), channel_id=1, source_target_pairs={{0,1},{1,0},{2,3},{3,2},{4,5},{5,4},{6,7},{7,6},{8,9},{9,8},{10,11... | collective-permute-start | bytes 442376 | tf_op jit(solution)/shard_map/ppermute | solution.py:189
  183.0 4.4 %collective-permute-start.4 = (f32[2,8,1152]{2,1,0:T(8,128)S(1)}, f32[2,8,1152]{2,1,0:T(8,128)S(1)}, u32[]{:S(2)}, u32[]{:S(2)}) collective-permute-start(f32[2,8,1152]{2,1,0:T(8,128)S(1)} %dynamic-slice_bitcast_fusion.5), channel_id=1, source_target_pairs={{0,2},{1,3},{2,0},{3,1},{4,6},{5,7},{6,4},{7,5},{8,10},{9,11},{10,... | collective-permute-start | bytes 221192 | tf_op jit(solution)/shard_map/ppermute | solution.py:189
  186.8 4.4 %collective-permute-start.9 = (f32[2,8,1152]{2,1,0:T(8,128)S(1)}, f32[2,8,1152]{2,1,0:T(8,128)S(1)}, u32[]{:S(2)}, u32[]{:S(2)}) collective-permute-start(f32[2,8,1152]{2,1,0:T(8,128)S(1)} %dynamic-slice_bitcast_fusion.4), channel_id=1, source_target_pairs={{0,2},{1,3},{2,0},{3,1},{4,6},{5,7},{6,4},{7,5},{8,10},{9,11},{10,... | collective-permute-start | bytes 221192 | tf_op jit(solution)/shard_map/ppermute | solution.py:189
  187.4 5.9 %collective-permute-start.5 = (f32[8,1152]{1,0:T(8,128)S(1)}, f32[8,1152]{1,0:T(8,128)S(1)}, u32[]{:S(2)}, u32[]{:S(2)}) collective-permute-start(f32[8,1152]{1,0:T(8,128)S(1)} %dynamic-slice_bitcast_fusion.7), channel_id=1, source_target_pairs={{0,4},{1,5},{2,6},{3,7},{4,0},{5,1},{6,2},{7,3},{8,12},{9,13},{10,... | collective-permute-start | bytes 110600 | tf_op jit(solution)/shard_map/ppermute | solution.py:189
  191.3 5.2 %collective-permute-start.10 = (f32[8,1152]{1,0:T(8,128)S(1)}, f32[8,1152]{1,0:T(8,128)S(1)}, u32[]{:S(2)}, u32[]{:S(2)}) collective-permute-start(f32[8,1152]{1,0:T(8,128)S(1)} %dynamic-slice_bitcast_fusion.6), channel_id=1, source_target_pairs={{0,4},{1,5},{2,6},{3,7},{4,0},{5,1},{6,2},{7,3},{8,12},{9,13},{10,... | collective-permute-start | bytes 110600 | tf_op jit(solution)/shard_map/ppermute | solution.py:189

commit v8 on v4

--- a/solution.py
+++ b/solution.py
@@ -172,13 +172,15 @@
     )(*operands)
 
 
-def halving_reduce_scatter(partial, axes):
+def halving_reduce_scatter(partial, axes, swap=False):
     devices = lax.axis_size(axes)
     tiles = lax.axis_size(axes[-1])
     bits = devices.bit_length() - 1
     me = lax.axis_index(axes)
     core = tiles.bit_length() - 1
-    order = [core] + [b for b in range(bits) if b > core] + [b for b in range(core)]
+    high = [b for b in range(bits) if b > core]
+    low = [b for b in range(core)]
+    order = [core] + (low[:1] + high + low[1:] if swap else high + low)
     rows = partial.shape[0] // devices
     buf = partial.reshape((2,) * bits + (rows,) + partial.shape[1:])
     remaining = list(range(bits - 1, -1, -1))
@@ -223,7 +225,9 @@
         conv, partial = second_stage(
             hidden, second_weight[:, :, channels], grad_t, conv, jnp.bfloat16 if last else jnp.float32
         )
-        summed = halving_reduce_scatter(partial.sum(axis=0).reshape(outputs, 9 * part), ("group", "tile"))
+        summed = halving_reduce_scatter(
+            partial.sum(axis=0).reshape(outputs, 9 * part), ("group", "tile"), swap=chunk % 2 == 1
+        )
         pieces.append(summed.reshape(-1, 9, part))
     weight_grad = jnp.concatenate(pieces, axis=-1).reshape(-1, 3, 3, outputs)
     return (conv, weight_grad)

time: 194 us -> 189 us (0.974)
  waiting for transfers between devices: 31.3 us -> 27.2 us
    ppermute x10, waiting for transfers between devices: 20.8 us -> 16.7 us  [halving_reduce_scatter(): buf = keep + lax.ppermute(send, axes, pairs)]
  transfers between devices with their start and end apart: 12 -> 12, of which waited for: 9 -> 10; matrix products, arithmetic and copies ran while one was open for 13% -> 13% of each run, Pallas kernels for 25% -> 25%
where the time goes in v8:
time: 189 us
  Pallas kernels  58.7 us (31%)
  blocking collectives  54.4 us (29%)
  local copies, waits for them, and re-layouts  28.1 us (15%)
  waiting for transfers between devices  27.2 us (14%)
  starting transfers between devices  17.8 us (9%)
    all_to_all x1, blocking collectives, local(): lax.all_to_all(local_hidden.reshape(tiles, owned, half_rows, width // 2,...  54.4 us
    pallas_call x2, Pallas kernels, second_stage(): pl.pallas_call(functools.partial(second_kernel, rows=rows, carry=prev is...  47.6 us
    ppermute x10, waiting for transfers between devices, halving_reduce_scatter(): buf = keep + lax.ppermute(send, axes, pairs)  16.7 us
    pallas_call x1, Pallas kernels, first_stage(): pl.pallas_call(first_kernel, grid=(images,), in_specs=[pl.BlockSpec((None...  11.1 us
    ppermute x10, starting transfers between devices, halving_reduce_scatter(): buf = keep + lax.ppermute(send, axes, pairs)  9.33 us
    all_to_all x1, waiting for transfers between devices, local(): lax.all_to_all(local_hidden.reshape(tiles, owned, half_rows, width // 2,...  7.14 us
    reshape x1, local copies, waits for them, and re-layouts, local(): grad_t = out_grad.reshape(owned, -1, outputs).transpose(0, 2, 1)  6.37 us
    concatenate x2, local copies, waits for them, and re-layouts, shift_cols_right(): return jnp.concatenate([zero_col, slab[:, :, :-1]], axis=2)  4.97 us
  transfers between devices with their start and end apart: 12, of which 10 were waited for; matrix products, arithmetic and copies ran while one was open for 13% of the time, Pallas kernels for 25%

profile of v8, /device:TPU:0, one launch (start us, length us, event | category | flops | bytes accessed | tf_op | source)
XLA Modules:
  0.0 188.7 jit_solution(14884526151991640193)
XLA Ops:
  0.6 0.0 copy-start
  0.6 1.0 slice.21
  1.7 4.9 %collective-permute-start = (bf16[8,1,128,128]{3,2,1,0:T(8,128)(2,1)S(1)}, bf16[8,1,128,128]{3,2,1,0:T(8,128)(2,1)S(1)}, u32[]{:S(2)}, u32[]{:S(2)}) collective-permute-start(bf16[8,1,128,128]{3,2,1,0:T(8,128)(2,1)S(1)} %slice.21), channel_id=1, source_target_pairs={{0,1},{1,2},{2,3},{3,4},{4,5},{5,6},{6,7},{8,9},{9,10},{10,11},{11... | collective-permute-start | bytes 786440 | tf_op jit(solution)/shard_map/ppermute | solution.py:14
  6.6 0.7 pad_clamp_fusion
  7.2 0.6 gather_fusion
  7.8 0.9 copy.11
  8.7 3.4 %collective-permute-done.up_ref = bf16[8,1,128,128]{3,2,1,0:T(8,128)(2,1)S(1)} collective-permute-done((bf16[8,1,128,128]{3,2,1,0:T(8,128)(2,1)S(1)}, bf16[8,1,128,128]{3,2,1,0:T(8,128)(2,1)S(1)}, u32[]{:S(2)}, u32[]{:S(2)}) %collective-permute-start) | collective-permute-done | bytes 262176 | tf_op jit(solution)/shard_map/ppermute | solution.py:14
  12.1 0.7 copy-done.6
  12.8 11.1 %shard_map.68 = (bf16[8,16,64,128]{3,2,1,0:T(8,128)(2,1)}, bf16[8,16,64,128]{3,2,1,0:T(8,128)(2,1)}) custom-call(bf16[8,32,128,128]{3,2,1,0:T(8,128)(2,1)} %x_ref.1, bf16[8,1,128,128]{3,2,1,0:T(8,128)(2,1)} %copy-done.6, bf16[1152,256]{1,0:T(8,128)(2,1)} %bitcast.73), custom_call_target="tpu_custom_call" | custom-call | flops 4831838208 | bytes 12582912 | tf_op jit(solution)/shard_map/pallas_call | solution.py:76
  23.9 54.4 %all_to_all.21 = bf16[8,1,16,64,128]{4,3,2,1,0:T(8,128)(2,1)} all-to-all(bf16[8,1,16,64,128]{4,3,2,1,0:T(8,128)(2,1)} %bitcast.68), channel_id=1, replica_groups=mesh['group'=4,'tile'=8] {'tile'}, dimensions={0} | all-to-all | bytes 4194304 | tf_op jit(solution)/shard_map/all_to_all | solution.py:214
  78.2 3.6 %all-to-all-start = ((bf16[8,1,16,64,128]{4,3,2,1,0:T(8,128)(2,1)}), bf16[8,1,16,64,128]{4,3,2,1,0:T(8,128)(2,1)S(1)}, u32[]{:S(2)}, u32[]{:S(2)}) async-start(bf16[8,1,16,64,128]{4,3,2,1,0:T(8,128)(2,1)} %bitcast.67), calls=%async_computation | async-start | bytes 4194304 | tf_op jit(solution)/shard_map/all_to_all | solution.py:214
  81.9 6.4 %copy.14 = bf16[1,8192,256]{1,2,0:T(8,128)(2,1)} copy(bf16[1,8192,256]{2,1,0:T(8,128)(2,1)} %bitcast.63) | data formatting | bytes 8388608 | tf_op jit(solution)/shard_map/reshape | solution.py:207
  88.2 2.5 %fusion = (bf16[3,3,128,256]{3,2,1,0:T(8,128)(2,1)}, bf16[3,3,128,256]{3,2,1,0:T(8,128)(2,1)}) fusion(bf16[3,3,256,256]{3,2,1,0:T(8,128)(2,1)} %param.7), kind=kLoop, calls=%fused_computation.27 | loop fusion | bytes 2359296 | tf_op jit(solution)/shard_map/slice | solution.py:226
  90.8 1.7 pad.11.refs_1_
  92.5 1.3 pad_slice_fusion.2
  93.8 1.8 concatenate.21.refs_2_
  95.6 2.5 %concatenate.20.refs_0_ = bf16[1,130,64,128]{3,2,1,0:T(8,128)(2,1)} pad(bf16[1,130,63,128]{3,2,1,0:T(8,128)(2,1)S(1)} %get-tuple-element.21, bf16[]{:T(256)} %constant.80.clone.1), padding=0_0x0_0x1_0x0_0 | pad | bytes 4226562 | tf_op jit(solution)/shard_map/concatenate | solution.py:19
  98.1 24.3 %shard_map.69 = (f32[1,128,64,256]{3,2,1,0:T(8,128)}, f32[1,256,1152]{2,1,0:T(8,128)}) custom-call(bf16[1,130,64,128]{3,2,1,0:T(8,128)(2,1)} %concatenate.20.refs_0_, bf16[1,130,64,128]{3,2,1,0:T(8,128)(2,1)} %pad.11.refs_1_, bf16[1,130,64,128]{3,2,1,0:T(8,128)(2,1)} %concatenate.21.refs_2_, bf16[1152,256]{1,0:T(8,128)(2,1)} %bitcast.75, ...), custom_call_target="tpu_custom_call" | custom-call | flops 9663676416 | bytes 26345472 | tf_op jit(solution)/shard_map/pallas_call | solution.py:154
  122.4 7.1 %all-to-all-done = bf16[8,1,16,64,128]{4,3,2,1,0:T(8,128)(2,1)S(1)} async-done(((bf16[8,1,16,64,128]{4,3,2,1,0:T(8,128)(2,1)}), bf16[8,1,16,64,128]{4,3,2,1,0:T(8,128)(2,1)S(1)}, u32[]{:S(2)}, u32[]{:S(2)}) %all-to-all-start) | async-done | bytes 2097184 | tf_op jit(solution)/shard_map/all_to_all | solution.py:214
  129.5 1.7 pad.12.refs_1_
  131.3 1.2 pad_slice_fusion
  132.5 0.0 copy-done.3
  132.6 0.1 collective-permute-start.1
  132.7 1.8 concatenate.23.refs_2_
  134.5 2.5 %concatenate.22.refs_0_ = bf16[1,130,64,128]{3,2,1,0:T(8,128)(2,1)} pad(bf16[1,130,63,128]{3,2,1,0:T(8,128)(2,1)S(1)} %get-tuple-element.19, bf16[]{:T(256)} %constant.80.clone.1), padding=0_0x0_0x1_0x0_0 | pad | bytes 4226562 | tf_op jit(solution)/shard_map/concatenate | solution.py:19
  136.9 23.4 %shard_map.70 = (bf16[1,128,64,256]{3,2,1,0:T(8,128)(2,1)}, f32[1,256,1152]{2,1,0:T(8,128)}) custom-call(bf16[1,130,64,128]{3,2,1,0:T(8,128)(2,1)} %concatenate.22.refs_0_, bf16[1,130,64,128]{3,2,1,0:T(8,128)(2,1)} %pad.12.refs_1_, bf16[1,130,64,128]{3,2,1,0:T(8,128)(2,1)} %concatenate.23.refs_2_, bf16[1152,256]{1,0:T(8,128)(2,1)} %bitcast.74, ...), custom_call_target="tpu_custom_call" | custom-call | flops 9663676416 | bytes 26345472 | tf_op jit(solution)/shard_map/pallas_call | solution.py:154
  160.3 1.2 dynamic-slice_bitcast_fusion
  161.5 0.6 collective-permute-start.6
  162.1 0.1 bitcast_add_fusion.1
  162.2 1.6 collective-permute-start.2
  163.8 0.1 bitcast_add_fusion
  163.8 0.0 copy-start.1
  163.9 1.5 collective-permute-start.7
  165.4 5.8 %collective-permute-done.2 = f32[2,2,2,8,1152]{4,3,2,1,0:T(8,128)S(1)} collective-permute-done((f32[2,2,2,8,1152]{4,3,2,1,0:T(8,128)S(1)}, f32[2,2,2,8,1152]{4,3,2,1,0:T(8,128)S(1)}, u32[]{:S(2)}, u32[]{:S(2)}) %collective-permute-start.2) | collective-permute-done | bytes 294944 | tf_op jit(solution)/shard_map/ppermute | solution.py:193
  171.2 1.5 collective-permute-start.3
  172.8 0.4 collective-permute-done.7
  173.2 1.6 collective-permute-start.8
  174.8 1.6 collective-permute-done.3
  176.5 0.1 collective-permute-start.4
  176.6 2.0 %collective-permute-done.8 = f32[2,2,8,1152]{3,2,1,0:T(8,128)S(1)} collective-permute-done((f32[2,2,8,1152]{3,2,1,0:T(8,128)S(1)}, f32[2,2,8,1152]{3,2,1,0:T(8,128)S(1)}, u32[]{:S(2)}, u32[]{:S(2)}) %collective-permute-start.8) | collective-permute-done | bytes 147488 | tf_op jit(solution)/shard_map/ppermute | solution.py:193
  178.6 0.1 collective-permute-start.9
  178.7 2.7 %collective-permute-done.4 = f32[2,8,1152]{2,1,0:T(8,128)S(1)} collective-permute-done((f32[2,8,1152]{2,1,0:T(8,128)S(1)}, f32[2,8,1152]{2,1,0:T(8,128)S(1)}, u32[]{:S(2)}, u32[]{:S(2)}) %collective-permute-start.4) | collective-permute-done | bytes 73760 | tf_op jit(solution)/shard_map/ppermute | solution.py:193
  181.4 0.9 collective-permute-start.5
  182.3 0.7 collective-permute-done.9
  183.1 1.4 collective-permute-start.10
  184.5 1.9 %collective-permute-done.5 = f32[8,1152]{1,0:T(8,128)S(1)} collective-permute-done((f32[8,1152]{1,0:T(8,128)S(1)}, f32[8,1152]{1,0:T(8,128)S(1)}, u32[]{:S(2)}, u32[]{:S(2)}) %collective-permute-start.5) | collective-permute-done | bytes 36896 | tf_op jit(solution)/shard_map/ppermute | solution.py:193
  186.5 1.5 collective-permute-done.10
  188.0 0.6 pad_maximum_fusion
  (29 shorter events, 0.4 us)
Async XLA Ops:
  0.6 6.6 %copy-start = (bf16[3,3,128,256]{3,2,1,0:T(8,128)(2,1)S(1)}, bf16[3,3,128,256]{3,2,1,0:T(8,128)(2,1)}, u32[]{:S(2)}) copy-start(bf16[3,3,128,256]{3,2,1,0:T(8,128)(2,1)} %param.6) | copy-start | bytes 1769476
  1.7 10.4 %collective-permute-start = (bf16[8,1,128,128]{3,2,1,0:T(8,128)(2,1)S(1)}, bf16[8,1,128,128]{3,2,1,0:T(8,128)(2,1)S(1)}, u32[]{:S(2)}, u32[]{:S(2)}) collective-permute-start(bf16[8,1,128,128]{3,2,1,0:T(8,128)(2,1)S(1)} %slice.21), channel_id=1, source_target_pairs={{0,1},{1,2},{2,3},{3,4},{4,5},{5,6},{6,7},{8,9},{9,10},{10,11},{11... | collective-permute-start | bytes 786440 | tf_op jit(solution)/shard_map/ppermute | solution.py:14
  12.1 0.7 copy-start.6
  78.2 51.3 %all-to-all-start = ((bf16[8,1,16,64,128]{4,3,2,1,0:T(8,128)(2,1)}), bf16[8,1,16,64,128]{4,3,2,1,0:T(8,128)(2,1)S(1)}, u32[]{:S(2)}, u32[]{:S(2)}) async-start(bf16[8,1,16,64,128]{4,3,2,1,0:T(8,128)(2,1)} %bitcast.67), calls=%async_computation | async-start | bytes 4194304 | tf_op jit(solution)/shard_map/all_to_all | solution.py:214
  88.2 2.5 %copy-start.2 = (bf16[8,1,16,64,128]{4,3,2,1,0:T(8,128)(2,1)S(1)}, bf16[8,1,16,64,128]{4,3,2,1,0:T(8,128)(2,1)}, u32[]{:S(2)}) copy-start(bf16[8,1,16,64,128]{4,3,2,1,0:T(8,128)(2,1)} %all_to_all.21) | copy-start | bytes 6291460
  131.3 1.3 copy-start.3
  132.6 29.5 %collective-permute-start.1 = (f32[2,2,2,2,8,1152]{5,4,3,2,1,0:T(8,128)S(1)}, f32[2,2,2,2,8,1152]{5,4,3,2,1,0:T(8,128)S(1)}, u32[]{:S(2)}, u32[]{:S(2)}) collective-permute-start(f32[2,2,2,2,8,1152]{5,4,3,2,1,0:T(8,128)S(1)} %dynamic-slice_bitcast_fusion.1), channel_id=1, source_target_pairs={{0,8},{1,9},{2,10},{3,11},{4,12},{5,13},{6,14},{7,15},{8,0},{9,1},... | collective-permute-start | bytes 1769480 | tf_op jit(solution)/shard_map/ppermute | solution.py:193
  136.9 25.1 %copy-start.4 = (f32[1,256,1152]{2,1,0:T(8,128)S(1)}, f32[1,256,1152]{2,1,0:T(8,128)}, u32[]{:S(2)}) copy-start(f32[1,256,1152]{2,1,0:T(8,128)} %get-tuple-element.16) | copy-start | bytes 3538948
  160.3 3.5 %copy-start.5 = (f32[1,256,1152]{2,1,0:T(8,128)S(1)}, f32[1,256,1152]{2,1,0:T(8,128)}, u32[]{:S(2)}) copy-start(f32[1,256,1152]{2,1,0:T(8,128)} %get-tuple-element.17) | copy-start | bytes 3538948
  161.5 2.3 %collective-permute-start.6 = (f32[2,2,2,2,8,1152]{5,4,3,2,1,0:T(8,128)S(1)}, f32[2,2,2,2,8,1152]{5,4,3,2,1,0:T(8,128)S(1)}, u32[]{:S(2)}, u32[]{:S(2)}) collective-permute-start(f32[2,2,2,2,8,1152]{5,4,3,2,1,0:T(8,128)S(1)} %dynamic-slice_bitcast_fusion), channel_id=1, source_target_pairs={{0,8},{1,9},{2,10},{3,11},{4,12},{5,13},{6,14},{7,15},{8,0},{9,1},... | collective-permute-start | bytes 1769480 | tf_op jit(solution)/shard_map/ppermute | solution.py:193
  162.2 9.0 %collective-permute-start.2 = (f32[2,2,2,8,1152]{4,3,2,1,0:T(8,128)S(1)}, f32[2,2,2,8,1152]{4,3,2,1,0:T(8,128)S(1)}, u32[]{:S(2)}, u32[]{:S(2)}) collective-permute-start(f32[2,2,2,8,1152]{4,3,2,1,0:T(8,128)S(1)} %dynamic-slice_bitcast_fusion.3), channel_id=1, source_target_pairs={{0,16},{1,17},{2,18},{3,19},{4,20},{5,21},{6,22},{7,23},{8,24},{9,... | collective-permute-start | bytes 884744 | tf_op jit(solution)/shard_map/ppermute | solution.py:193
  163.8 24.8 %copy-start.1 = (bf16[3,3,128,256]{3,2,1,0:T(8,128)(2,1)S(1)}, bf16[3,3,128,256]{3,2,1,0:T(8,128)(2,1)}, u32[]{:S(2)}) copy-start(bf16[3,3,128,256]{3,2,1,0:T(8,128)(2,1)} %param.6) | copy-start | bytes 1769476
  163.9 9.3 %collective-permute-start.7 = (f32[2,2,2,8,1152]{4,3,2,1,0:T(8,128)S(1)}, f32[2,2,2,8,1152]{4,3,2,1,0:T(8,128)S(1)}, u32[]{:S(2)}, u32[]{:S(2)}) collective-permute-start(f32[2,2,2,8,1152]{4,3,2,1,0:T(8,128)S(1)} %dynamic-slice_bitcast_fusion.2), channel_id=1, source_target_pairs={{0,1},{1,0},{2,3},{3,2},{4,5},{5,4},{6,7},{7,6},{8,9},{9,8},{10,11... | collective-permute-start | bytes 884744 | tf_op jit(solution)/shard_map/ppermute | solution.py:193
  171.2 5.2 %collective-permute-start.3 = (f32[2,2,8,1152]{3,2,1,0:T(8,128)S(1)}, f32[2,2,8,1152]{3,2,1,0:T(8,128)S(1)}, u32[]{:S(2)}, u32[]{:S(2)}) collective-permute-start(f32[2,2,8,1152]{3,2,1,0:T(8,128)S(1)} %dynamic-slice_bitcast_fusion.5), channel_id=1, source_target_pairs={{0,1},{1,0},{2,3},{3,2},{4,5},{5,4},{6,7},{7,6},{8,9},{9,8},{10,11... | collective-permute-start | bytes 442376 | tf_op jit(solution)/shard_map/ppermute | solution.py:193
  173.2 5.3 %collective-permute-start.8 = (f32[2,2,8,1152]{3,2,1,0:T(8,128)S(1)}, f32[2,2,8,1152]{3,2,1,0:T(8,128)S(1)}, u32[]{:S(2)}, u32[]{:S(2)}) collective-permute-start(f32[2,2,8,1152]{3,2,1,0:T(8,128)S(1)} %dynamic-slice_bitcast_fusion.4), channel_id=1, source_target_pairs={{0,16},{1,17},{2,18},{3,19},{4,20},{5,21},{6,22},{7,23},{8,24},{9,... | collective-permute-start | bytes 442376 | tf_op jit(solution)/shard_map/ppermute | solution.py:193
  176.5 4.9 %collective-permute-start.4 = (f32[2,8,1152]{2,1,0:T(8,128)S(1)}, f32[2,8,1152]{2,1,0:T(8,128)S(1)}, u32[]{:S(2)}, u32[]{:S(2)}) collective-permute-start(f32[2,8,1152]{2,1,0:T(8,128)S(1)} %dynamic-slice_bitcast_fusion.7), channel_id=1, source_target_pairs={{0,2},{1,3},{2,0},{3,1},{4,6},{5,7},{6,4},{7,5},{8,10},{9,11},{10,... | collective-permute-start | bytes 221192 | tf_op jit(solution)/shard_map/ppermute | solution.py:193
  178.6 4.5 %collective-permute-start.9 = (f32[2,8,1152]{2,1,0:T(8,128)S(1)}, f32[2,8,1152]{2,1,0:T(8,128)S(1)}, u32[]{:S(2)}, u32[]{:S(2)}) collective-permute-start(f32[2,8,1152]{2,1,0:T(8,128)S(1)} %dynamic-slice_bitcast_fusion.6), channel_id=1, source_target_pairs={{0,2},{1,3},{2,0},{3,1},{4,6},{5,7},{6,4},{7,5},{8,10},{9,11},{10,... | collective-permute-start | bytes 221192 | tf_op jit(solution)/shard_map/ppermute | solution.py:193
  181.4 5.0 %collective-permute-start.5 = (f32[8,1152]{1,0:T(8,128)S(1)}, f32[8,1152]{1,0:T(8,128)S(1)}, u32[]{:S(2)}, u32[]{:S(2)}) collective-permute-start(f32[8,1152]{1,0:T(8,128)S(1)} %dynamic-slice_bitcast_fusion.9), channel_id=1, source_target_pairs={{0,4},{1,5},{2,6},{3,7},{4,0},{5,1},{6,2},{7,3},{8,12},{9,13},{10,... | collective-permute-start | bytes 110600 | tf_op jit(solution)/shard_map/ppermute | solution.py:193
  183.1 4.9 %collective-permute-start.10 = (f32[8,1152]{1,0:T(8,128)S(1)}, f32[8,1152]{1,0:T(8,128)S(1)}, u32[]{:S(2)}, u32[]{:S(2)}) collective-permute-start(f32[8,1152]{1,0:T(8,128)S(1)} %dynamic-slice_bitcast_fusion.8), channel_id=1, source_target_pairs={{0,4},{1,5},{2,6},{3,7},{4,0},{5,1},{6,2},{7,3},{8,12},{9,13},{10,... | collective-permute-start | bytes 110600 | tf_op jit(solution)/shard_map/ppermute | solution.py:193

commit v9 on v7

--- a/solution.py
+++ b/solution.py
@@ -97,9 +97,9 @@
 
 def second_kernel(*refs, rows, carry):
     if carry:
-        left_ref, mid_ref, right_ref, weight_ref, grad_ref, prev_ref, out_ref, wgrad_ref = refs
+        left_ref, mid_ref, right_ref, weight_ref, grad_ref, prev_ref, out_ref, wgrad_ref, acc_ref = refs
     else:
-        left_ref, mid_ref, right_ref, weight_ref, grad_ref, out_ref, wgrad_ref = refs
+        left_ref, mid_ref, right_ref, weight_ref, grad_ref, out_ref, wgrad_ref, acc_ref = refs
     step = pl.program_id(1)
     _, width, outputs = out_ref.shape
     inputs = mid_ref.shape[-1]
@@ -121,11 +121,15 @@
 
     @pl.when(step == 0)
     def _():
-        wgrad_ref[...] = term
+        acc_ref[...] = term
 
     @pl.when(step > 0)
     def _():
-        wgrad_ref[...] += term
+        acc_ref[...] += term
+
+    @pl.when(step == pl.num_programs(1) - 1)
+    def _():
+        wgrad_ref[...] = acc_ref[...].T
 
 
 def second_stage(hidden, weight, grad, prev, out_dtype):
@@ -148,15 +152,16 @@
         in_specs.append(block)
         operands.append(prev)
     flops = 4 * owned * out_rows * out_cols * 9 * inputs * outputs
-    conv, wgrad_t = pl.pallas_call(
+    return pl.pallas_call(
         functools.partial(second_kernel, rows=rows, carry=prev is not None),
         grid=(owned, out_rows // rows),
         in_specs=in_specs,
-        out_specs=[block, pl.BlockSpec((None, 9 * inputs, outputs), lambda n, i: (n, 0, 0))],
+        out_specs=[block, pl.BlockSpec((None, outputs, 9 * inputs), lambda n, i: (n, 0, 0))],
         out_shape=[
             jax.ShapeDtypeStruct((owned, out_rows, out_cols, outputs), out_dtype),
-            jax.ShapeDtypeStruct((owned, 9 * inputs, outputs), jnp.float32),
+            jax.ShapeDtypeStruct((owned, outputs, 9 * inputs), jnp.float32),
         ],
+        scratch_shapes=[pltpu.VMEM((9 * inputs, outputs), jnp.float32)],
         compiler_params=pltpu.CompilerParams(
             dimension_semantics=("arbitrary", "arbitrary"), vmem_limit_bytes=60 * 1024 * 1024
         ),
@@ -167,16 +172,17 @@
             + owned * outputs * 9 * inputs * 4,
         ),
     )(*operands)
-    return conv, wgrad_t.sum(axis=0).T
-
-
-def halving_reduce_scatter(partial, axes):
+
+
+def halving_reduce_scatter(partial, axes, swap=False):
     devices = lax.axis_size(axes)
     tiles = lax.axis_size(axes[-1])
     bits = devices.bit_length() - 1
     me = lax.axis_index(axes)
     core = tiles.bit_length() - 1
-    order = [core] + [b for b in range(bits) if b > core] + [b for b in range(core)]
+    high = [b for b in range(bits) if b > core]
+    low = [b for b in range(core)]
+    order = [core] + (low[:1] + high + low[1:] if swap else high + low)
     rows = partial.shape[0] // devices
     buf = partial.reshape((2,) * bits + (rows,) + partial.shape[1:])
     remaining = list(range(bits - 1, -1, -1))
@@ -221,7 +227,9 @@
         conv, partial = second_stage(
             hidden, second_weight[:, :, channels], grad, conv, jnp.bfloat16 if last else jnp.float32
         )
-        summed = halving_reduce_scatter(partial.reshape(outputs, 9 * part), ("group", "tile"))
+        summed = halving_reduce_scatter(
+            partial.sum(axis=0).reshape(outputs, 9 * part), ("group", "tile"), swap=chunk % 2 == 1
+        )
         pieces.append(summed.reshape(-1, 9, part))
     weight_grad = jnp.concatenate(pieces, axis=-1).reshape(-1, 3, 3, outputs)
     return (conv, weight_grad)

time: 198 us -> 184 us (0.929)
  waiting for transfers between devices: 47.2 us -> 40.1 us
  local copies, waits for them, and re-layouts: 27.8 us -> 21.9 us
  other arithmetic: 3.7 us -> 1.57 us
    ppermute x10, waiting for transfers between devices: 22.9 us -> 16.7 us  [halving_reduce_scatter(): buf = keep + lax.ppermute(send, axes, pairs)]
    transpose x2 -> x0, local copies, waits for them, and re-layouts: 3.42 us -> none  [second_stage(): return (conv, wgrad_t.sum(axis=0).T)]
    add x10, other arithmetic: 2.4 us -> 0.26 us  [halving_reduce_scatter(): buf = keep + lax.ppermute(send, axes, pairs)]
    slice x2, local copies, waits for them, and re-layouts: 4.63 us -> 2.51 us  [shift_cols_left(): return jnp.concatenate([slab[:, :, 1:], zero_col], axis=2)]
  transfers between devices with their start and end apart: 12 -> 12, of which waited for: 10 -> 10; matrix products, arithmetic and copies ran while one was open for 10% -> 10% of each run, Pallas kernels for 18% -> 19%
where the time goes in v9:
time: 184 us; the launch traced here: 183 us
  blocking collectives  54.4 us (30%)
  Pallas kernels  46.6 us (25%)
  waiting for transfers between devices  40.1 us (22%)
  local copies, waits for them, and re-layouts  21.9 us (12%)
  starting transfers between devices  17.8 us (10%)
    all_to_all x1, blocking collectives, local(): lax.all_to_all(local_hidden.reshape(tiles, owned, half_rows, width // 2,...  54.4 us
    pallas_call x2, Pallas kernels, second_stage(): pl.pallas_call(functools.partial(second_kernel, rows=rows, carry=prev is...  35.5 us
    all_to_all x1, waiting for transfers between devices, local(): lax.all_to_all(local_hidden.reshape(tiles, owned, half_rows, width // 2,...  20 us
    ppermute x10, waiting for transfers between devices, halving_reduce_scatter(): buf = keep + lax.ppermute(send, axes, pairs)  16.7 us
    pallas_call x1, Pallas kernels, first_stage(): pl.pallas_call(first_kernel, grid=(images,), in_specs=[pl.BlockSpec((None...  11.1 us
    ppermute x10, starting transfers between devices, halving_reduce_scatter(): buf = keep + lax.ppermute(send, axes, pairs)  9.37 us
    concatenate x2, local copies, waits for them, and re-layouts, shift_cols_right(): return jnp.concatenate([zero_col, slab[:, :, :-1]], axis=2)  5.06 us
    ppermute x1, starting transfers between devices, shifted_2(): return lax.ppermute(shard, axis, pairs)  4.86 us
  transfers between devices with their start and end apart: 12, of which 10 were waited for; matrix products, arithmetic and copies ran while one was open for 10% of the time, Pallas kernels for 19%

profile of v9, /device:TPU:0, one launch (start us, length us, event | category | flops | bytes accessed | tf_op | source)
XLA Modules:
  0.0 183.2 jit_solution(4190275799338606958)
XLA Ops:
  0.6 0.0 copy-start
  0.6 1.0 slice.21
  1.7 4.9 %collective-permute-start = (bf16[8,1,128,128]{3,2,1,0:T(8,128)(2,1)S(1)}, bf16[8,1,128,128]{3,2,1,0:T(8,128)(2,1)S(1)}, u32[]{:S(2)}, u32[]{:S(2)}) collective-permute-start(bf16[8,1,128,128]{3,2,1,0:T(8,128)(2,1)S(1)} %slice.21), channel_id=1, source_target_pairs={{0,1},{1,2},{2,3},{3,4},{4,5},{5,6},{6,7},{8,9},{9,10},{10,11},{11... | collective-permute-start | bytes 786440 | tf_op jit(solution)/shard_map/ppermute | solution.py:14
  6.6 0.7 pad_clamp_fusion
  7.2 0.6 gather_fusion
  7.8 0.9 copy.8
  8.7 3.4 %collective-permute-done.up_ref = bf16[8,1,128,128]{3,2,1,0:T(8,128)(2,1)S(1)} collective-permute-done((bf16[8,1,128,128]{3,2,1,0:T(8,128)(2,1)S(1)}, bf16[8,1,128,128]{3,2,1,0:T(8,128)(2,1)S(1)}, u32[]{:S(2)}, u32[]{:S(2)}) %collective-permute-start) | collective-permute-done | bytes 262176 | tf_op jit(solution)/shard_map/ppermute | solution.py:14
  12.1 0.7 copy-done.6
  12.8 11.1 %shard_map.68 = (bf16[8,16,64,128]{3,2,1,0:T(8,128)(2,1)}, bf16[8,16,64,128]{3,2,1,0:T(8,128)(2,1)}) custom-call(bf16[8,32,128,128]{3,2,1,0:T(8,128)(2,1)} %x_ref.1, bf16[8,1,128,128]{3,2,1,0:T(8,128)(2,1)} %copy-done.6, bf16[1152,256]{1,0:T(8,128)(2,1)} %bitcast.69), custom_call_target="tpu_custom_call" | custom-call | flops 4831838208 | bytes 12582912 | tf_op jit(solution)/shard_map/pallas_call | solution.py:76
  23.9 54.4 %all_to_all.21 = bf16[8,1,16,64,128]{4,3,2,1,0:T(8,128)(2,1)} all-to-all(bf16[8,1,16,64,128]{4,3,2,1,0:T(8,128)(2,1)} %bitcast.64), channel_id=1, replica_groups=mesh['group'=4,'tile'=8] {'tile'}, dimensions={0} | all-to-all | bytes 4194304 | tf_op jit(solution)/shard_map/all_to_all | solution.py:216
  78.3 3.6 %all-to-all-start = ((bf16[8,1,16,64,128]{4,3,2,1,0:T(8,128)(2,1)}), bf16[8,1,16,64,128]{4,3,2,1,0:T(8,128)(2,1)S(1)}, u32[]{:S(2)}, u32[]{:S(2)}) async-start(bf16[8,1,16,64,128]{4,3,2,1,0:T(8,128)(2,1)} %bitcast.63), calls=%async_computation | async-start | bytes 4194304 | tf_op jit(solution)/shard_map/all_to_all | solution.py:216
  81.9 2.5 %fusion = (bf16[3,3,128,256]{3,2,1,0:T(8,128)(2,1)}, bf16[3,3,128,256]{3,2,1,0:T(8,128)(2,1)}) fusion(bf16[3,3,256,256]{3,2,1,0:T(8,128)(2,1)} %param.7), kind=kLoop, calls=%fused_computation.27 | loop fusion | bytes 2359296 | tf_op jit(solution)/shard_map/slice | solution.py:228
  84.4 1.8 pad.11.refs_1_
  86.3 1.3 pad_slice_fusion.2
  87.6 1.8 concatenate.21.refs_2_
  89.4 2.5 %concatenate.20.refs_0_ = bf16[1,130,64,128]{3,2,1,0:T(8,128)(2,1)} pad(bf16[1,130,63,128]{3,2,1,0:T(8,128)(2,1)S(1)} %get-tuple-element.21, bf16[]{:T(256)} %constant.80.clone.1), padding=0_0x0_0x1_0x0_0 | pad | bytes 4226562 | tf_op jit(solution)/shard_map/concatenate | solution.py:19
  91.8 17.7 %shard_map.69 = (f32[1,128,64,256]{3,2,1,0:T(8,128)}, f32[1,256,1152]{2,1,0:T(8,128)}) custom-call(bf16[1,130,64,128]{3,2,1,0:T(8,128)(2,1)} %concatenate.20.refs_0_, bf16[1,130,64,128]{3,2,1,0:T(8,128)(2,1)} %pad.11.refs_1_, bf16[1,130,64,128]{3,2,1,0:T(8,128)(2,1)} %concatenate.21.refs_2_, bf16[1152,256]{1,0:T(8,128)(2,1)} %bitcast.71, ...), custom_call_target="tpu_custom_call" | custom-call | flops 9663676416 | bytes 26345472 | tf_op jit(solution)/shard_map/pallas_call | solution.py:155
  109.5 20.0 %all-to-all-done = bf16[8,1,16,64,128]{4,3,2,1,0:T(8,128)(2,1)S(1)} async-done(((bf16[8,1,16,64,128]{4,3,2,1,0:T(8,128)(2,1)}), bf16[8,1,16,64,128]{4,3,2,1,0:T(8,128)(2,1)S(1)}, u32[]{:S(2)}, u32[]{:S(2)}) %all-to-all-start) | async-done | bytes 2097184 | tf_op jit(solution)/shard_map/all_to_all | solution.py:216
  129.5 1.8 pad.12.refs_1_
  131.3 1.2 pad_slice_fusion
  132.5 0.0 copy-done.3
  132.6 0.1 collective-permute-start.1
  132.7 1.8 concatenate.23.refs_2_
  134.5 2.6 %concatenate.22.refs_0_ = bf16[1,130,64,128]{3,2,1,0:T(8,128)(2,1)} pad(bf16[1,130,63,128]{3,2,1,0:T(8,128)(2,1)S(1)} %get-tuple-element.19, bf16[]{:T(256)} %constant.80.clone.1), padding=0_0x0_0x1_0x0_0 | pad | bytes 4226562 | tf_op jit(solution)/shard_map/concatenate | solution.py:19
  137.0 17.8 %shard_map.70 = (bf16[1,128,64,256]{3,2,1,0:T(8,128)(2,1)}, f32[1,256,1152]{2,1,0:T(8,128)}) custom-call(bf16[1,130,64,128]{3,2,1,0:T(8,128)(2,1)} %concatenate.22.refs_0_, bf16[1,130,64,128]{3,2,1,0:T(8,128)(2,1)} %pad.12.refs_1_, bf16[1,130,64,128]{3,2,1,0:T(8,128)(2,1)} %concatenate.23.refs_2_, bf16[1152,256]{1,0:T(8,128)(2,1)} %bitcast.70, ...), custom_call_target="tpu_custom_call" | custom-call | flops 9663676416 | bytes 26345472 | tf_op jit(solution)/shard_map/pallas_call | solution.py:155
  154.9 1.2 dynamic-slice_bitcast_fusion
  156.1 0.6 collective-permute-start.6
  156.6 0.0 collective-permute-done.1
  156.6 0.1 bitcast_add_fusion.1
  156.7 1.6 collective-permute-start.2
  158.3 0.1 bitcast_add_fusion
  158.4 0.0 copy-start.1
  158.5 1.5 collective-permute-start.7
  160.0 5.8 %collective-permute-done.2 = f32[2,2,2,8,1152]{4,3,2,1,0:T(8,128)S(1)} collective-permute-done((f32[2,2,2,8,1152]{4,3,2,1,0:T(8,128)S(1)}, f32[2,2,2,8,1152]{4,3,2,1,0:T(8,128)S(1)}, u32[]{:S(2)}, u32[]{:S(2)}) %collective-permute-start.2) | collective-permute-done | bytes 294944 | tf_op jit(solution)/shard_map/ppermute | solution.py:195
  165.8 1.5 collective-permute-start.3
  167.3 0.4 collective-permute-done.7
  167.8 1.6 collective-permute-start.8
  169.4 1.6 collective-permute-done.3
  171.1 0.1 collective-permute-start.4
  171.2 2.0 %collective-permute-done.8 = f32[2,2,8,1152]{3,2,1,0:T(8,128)S(1)} collective-permute-done((f32[2,2,8,1152]{3,2,1,0:T(8,128)S(1)}, f32[2,2,8,1152]{3,2,1,0:T(8,128)S(1)}, u32[]{:S(2)}, u32[]{:S(2)}) %collective-permute-start.8) | collective-permute-done | bytes 147488 | tf_op jit(solution)/shard_map/ppermute | solution.py:195
  173.2 0.1 collective-permute-start.9
  173.3 2.7 %collective-permute-done.4 = f32[2,8,1152]{2,1,0:T(8,128)S(1)} collective-permute-done((f32[2,8,1152]{2,1,0:T(8,128)S(1)}, f32[2,8,1152]{2,1,0:T(8,128)S(1)}, u32[]{:S(2)}, u32[]{:S(2)}) %collective-permute-start.4) | collective-permute-done | bytes 73760 | tf_op jit(solution)/shard_map/ppermute | solution.py:195
  176.0 0.9 collective-permute-start.5
  176.9 0.7 collective-permute-done.9
  177.7 1.4 collective-permute-start.10
  179.1 1.9 %collective-permute-done.5 = f32[8,1152]{1,0:T(8,128)S(1)} collective-permute-done((f32[8,1152]{1,0:T(8,128)S(1)}, f32[8,1152]{1,0:T(8,128)S(1)}, u32[]{:S(2)}, u32[]{:S(2)}) %collective-permute-start.5) | collective-permute-done | bytes 36896 | tf_op jit(solution)/shard_map/ppermute | solution.py:195
  181.1 1.5 collective-permute-done.10
  182.6 0.6 pad_maximum_fusion
  (28 shorter events, 0.4 us)
Async XLA Ops:
  0.6 6.6 %copy-start = (bf16[3,3,128,256]{3,2,1,0:T(8,128)(2,1)S(1)}, bf16[3,3,128,256]{3,2,1,0:T(8,128)(2,1)}, u32[]{:S(2)}) copy-start(bf16[3,3,128,256]{3,2,1,0:T(8,128)(2,1)} %param.6) | copy-start | bytes 1769476
  1.7 10.4 %collective-permute-start = (bf16[8,1,128,128]{3,2,1,0:T(8,128)(2,1)S(1)}, bf16[8,1,128,128]{3,2,1,0:T(8,128)(2,1)S(1)}, u32[]{:S(2)}, u32[]{:S(2)}) collective-permute-start(bf16[8,1,128,128]{3,2,1,0:T(8,128)(2,1)S(1)} %slice.21), channel_id=1, source_target_pairs={{0,1},{1,2},{2,3},{3,4},{4,5},{5,6},{6,7},{8,9},{9,10},{10,11},{11... | collective-permute-start | bytes 786440 | tf_op jit(solution)/shard_map/ppermute | solution.py:14
  12.1 0.7 copy-start.6
  78.3 51.3 %all-to-all-start = ((bf16[8,1,16,64,128]{4,3,2,1,0:T(8,128)(2,1)}), bf16[8,1,16,64,128]{4,3,2,1,0:T(8,128)(2,1)S(1)}, u32[]{:S(2)}, u32[]{:S(2)}) async-start(bf16[8,1,16,64,128]{4,3,2,1,0:T(8,128)(2,1)} %bitcast.63), calls=%async_computation | async-start | bytes 4194304 | tf_op jit(solution)/shard_map/all_to_all | solution.py:216
  81.9 2.5 %copy-start.2 = (bf16[8,1,16,64,128]{4,3,2,1,0:T(8,128)(2,1)S(1)}, bf16[8,1,16,64,128]{4,3,2,1,0:T(8,128)(2,1)}, u32[]{:S(2)}) copy-start(bf16[8,1,16,64,128]{4,3,2,1,0:T(8,128)(2,1)} %all_to_all.21) | copy-start | bytes 6291460
  131.3 1.3 copy-start.3
  132.6 24.0 %collective-permute-start.1 = (f32[2,2,2,2,8,1152]{5,4,3,2,1,0:T(8,128)S(1)}, f32[2,2,2,2,8,1152]{5,4,3,2,1,0:T(8,128)S(1)}, u32[]{:S(2)}, u32[]{:S(2)}) collective-permute-start(f32[2,2,2,2,8,1152]{5,4,3,2,1,0:T(8,128)S(1)} %dynamic-slice_bitcast_fusion.1), channel_id=1, source_target_pairs={{0,8},{1,9},{2,10},{3,11},{4,12},{5,13},{6,14},{7,15},{8,0},{9,1},... | collective-permute-start | bytes 1769480 | tf_op jit(solution)/shard_map/ppermute | solution.py:195
  137.0 19.6 %copy-start.4 = (f32[1,256,1152]{2,1,0:T(8,128)S(1)}, f32[1,256,1152]{2,1,0:T(8,128)}, u32[]{:S(2)}) copy-start(f32[1,256,1152]{2,1,0:T(8,128)} %get-tuple-element.16) | copy-start | bytes 3538948
  154.9 3.5 %copy-start.5 = (f32[1,256,1152]{2,1,0:T(8,128)S(1)}, f32[1,256,1152]{2,1,0:T(8,128)}, u32[]{:S(2)}) copy-start(f32[1,256,1152]{2,1,0:T(8,128)} %get-tuple-element.17) | copy-start | bytes 3538948
  156.1 2.3 %collective-permute-start.6 = (f32[2,2,2,2,8,1152]{5,4,3,2,1,0:T(8,128)S(1)}, f32[2,2,2,2,8,1152]{5,4,3,2,1,0:T(8,128)S(1)}, u32[]{:S(2)}, u32[]{:S(2)}) collective-permute-start(f32[2,2,2,2,8,1152]{5,4,3,2,1,0:T(8,128)S(1)} %dynamic-slice_bitcast_fusion), channel_id=1, source_target_pairs={{0,8},{1,9},{2,10},{3,11},{4,12},{5,13},{6,14},{7,15},{8,0},{9,1},... | collective-permute-start | bytes 1769480 | tf_op jit(solution)/shard_map/ppermute | solution.py:195
  156.7 9.0 %collective-permute-start.2 = (f32[2,2,2,8,1152]{4,3,2,1,0:T(8,128)S(1)}, f32[2,2,2,8,1152]{4,3,2,1,0:T(8,128)S(1)}, u32[]{:S(2)}, u32[]{:S(2)}) collective-permute-start(f32[2,2,2,8,1152]{4,3,2,1,0:T(8,128)S(1)} %dynamic-slice_bitcast_fusion.3), channel_id=1, source_target_pairs={{0,16},{1,17},{2,18},{3,19},{4,20},{5,21},{6,22},{7,23},{8,24},{9,... | collective-permute-start | bytes 884744 | tf_op jit(solution)/shard_map/ppermute | solution.py:195
  158.4 24.8 %copy-start.1 = (bf16[3,3,128,256]{3,2,1,0:T(8,128)(2,1)S(1)}, bf16[3,3,128,256]{3,2,1,0:T(8,128)(2,1)}, u32[]{:S(2)}) copy-start(bf16[3,3,128,256]{3,2,1,0:T(8,128)(2,1)} %param.6) | copy-start | bytes 1769476
  158.5 9.3 %collective-permute-start.7 = (f32[2,2,2,8,1152]{4,3,2,1,0:T(8,128)S(1)}, f32[2,2,2,8,1152]{4,3,2,1,0:T(8,128)S(1)}, u32[]{:S(2)}, u32[]{:S(2)}) collective-permute-start(f32[2,2,2,8,1152]{4,3,2,1,0:T(8,128)S(1)} %dynamic-slice_bitcast_fusion.2), channel_id=1, source_target_pairs={{0,1},{1,0},{2,3},{3,2},{4,5},{5,4},{6,7},{7,6},{8,9},{9,8},{10,11... | collective-permute-start | bytes 884744 | tf_op jit(solution)/shard_map/ppermute | solution.py:195
  165.8 5.2 %collective-permute-start.3 = (f32[2,2,8,1152]{3,2,1,0:T(8,128)S(1)}, f32[2,2,8,1152]{3,2,1,0:T(8,128)S(1)}, u32[]{:S(2)}, u32[]{:S(2)}) collective-permute-start(f32[2,2,8,1152]{3,2,1,0:T(8,128)S(1)} %dynamic-slice_bitcast_fusion.5), channel_id=1, source_target_pairs={{0,1},{1,0},{2,3},{3,2},{4,5},{5,4},{6,7},{7,6},{8,9},{9,8},{10,11... | collective-permute-start | bytes 442376 | tf_op jit(solution)/shard_map/ppermute | solution.py:195
  167.8 5.3 %collective-permute-start.8 = (f32[2,2,8,1152]{3,2,1,0:T(8,128)S(1)}, f32[2,2,8,1152]{3,2,1,0:T(8,128)S(1)}, u32[]{:S(2)}, u32[]{:S(2)}) collective-permute-start(f32[2,2,8,1152]{3,2,1,0:T(8,128)S(1)} %dynamic-slice_bitcast_fusion.4), channel_id=1, source_target_pairs={{0,16},{1,17},{2,18},{3,19},{4,20},{5,21},{6,22},{7,23},{8,24},{9,... | collective-permute-start | bytes 442376 | tf_op jit(solution)/shard_map/ppermute | solution.py:195
  171.1 4.9 %collective-permute-start.4 = (f32[2,8,1152]{2,1,0:T(8,128)S(1)}, f32[2,8,1152]{2,1,0:T(8,128)S(1)}, u32[]{:S(2)}, u32[]{:S(2)}) collective-permute-start(f32[2,8,1152]{2,1,0:T(8,128)S(1)} %dynamic-slice_bitcast_fusion.7), channel_id=1, source_target_pairs={{0,2},{1,3},{2,0},{3,1},{4,6},{5,7},{6,4},{7,5},{8,10},{9,11},{10,... | collective-permute-start | bytes 221192 | tf_op jit(solution)/shard_map/ppermute | solution.py:195
  173.2 4.5 %collective-permute-start.9 = (f32[2,8,1152]{2,1,0:T(8,128)S(1)}, f32[2,8,1152]{2,1,0:T(8,128)S(1)}, u32[]{:S(2)}, u32[]{:S(2)}) collective-permute-start(f32[2,8,1152]{2,1,0:T(8,128)S(1)} %dynamic-slice_bitcast_fusion.6), channel_id=1, source_target_pairs={{0,2},{1,3},{2,0},{3,1},{4,6},{5,7},{6,4},{7,5},{8,10},{9,11},{10,... | collective-permute-start | bytes 221192 | tf_op jit(solution)/shard_map/ppermute | solution.py:195
  176.0 5.0 %collective-permute-start.5 = (f32[8,1152]{1,0:T(8,128)S(1)}, f32[8,1152]{1,0:T(8,128)S(1)}, u32[]{:S(2)}, u32[]{:S(2)}) collective-permute-start(f32[8,1152]{1,0:T(8,128)S(1)} %dynamic-slice_bitcast_fusion.9), channel_id=1, source_target_pairs={{0,4},{1,5},{2,6},{3,7},{4,0},{5,1},{6,2},{7,3},{8,12},{9,13},{10,... | collective-permute-start | bytes 110600 | tf_op jit(solution)/shard_map/ppermute | solution.py:195
  177.7 4.9 %collective-permute-start.10 = (f32[8,1152]{1,0:T(8,128)S(1)}, f32[8,1152]{1,0:T(8,128)S(1)}, u32[]{:S(2)}, u32[]{:S(2)}) collective-permute-start(f32[8,1152]{1,0:T(8,128)S(1)} %dynamic-slice_bitcast_fusion.8), channel_id=1, source_target_pairs={{0,4},{1,5},{2,6},{3,7},{4,0},{5,1},{6,2},{7,3},{8,12},{9,13},{10,... | collective-permute-start | bytes 110600 | tf_op jit(solution)/shard_map/ppermute | solution.py:195

commit v10 on v9

--- a/solution.py
+++ b/solution.py
@@ -174,7 +174,7 @@
     )(*operands)
 
 
-def halving_reduce_scatter(partial, axes, swap=False):
+def halving_reduce_scatter(partials, axes):
     devices = lax.axis_size(axes)
     tiles = lax.axis_size(axes[-1])
     bits = devices.bit_length() - 1
@@ -182,19 +182,35 @@
     core = tiles.bit_length() - 1
     high = [b for b in range(bits) if b > core]
     low = [b for b in range(core)]
-    order = [core] + (low[:1] + high + low[1:] if swap else high + low)
-    rows = partial.shape[0] // devices
-    buf = partial.reshape((2,) * bits + (rows,) + partial.shape[1:])
-    remaining = list(range(bits - 1, -1, -1))
-    for bit in order:
-        axis = remaining.index(bit)
-        mine = (me >> bit) & 1
-        keep = lax.dynamic_index_in_dim(buf, mine, axis=axis, keepdims=False)
-        send = lax.dynamic_index_in_dim(buf, 1 - mine, axis=axis, keepdims=False)
-        pairs = [(i, i ^ (1 << bit)) for i in range(devices)]
-        buf = keep + lax.ppermute(send, axes, pairs)
-        remaining.pop(axis)
-    return buf
+    orders = [[core] + (low[:1] + high + low[1:] if index % 2 else high + low) for index in range(len(partials))]
+    bufs = []
+    for partial in partials:
+        rows = partial.shape[0] // devices
+        bufs.append(partial.reshape((2,) * bits + (rows,) + partial.shape[1:]))
+    remaining = [list(range(bits - 1, -1, -1)) for _ in partials]
+    for step in range(bits):
+        keeps, sends = [], []
+        for index, buf in enumerate(bufs):
+            bit = orders[index][step]
+            axis = remaining[index].index(bit)
+            mine = (me >> bit) & 1
+            keeps.append(lax.dynamic_index_in_dim(buf, mine, axis=axis, keepdims=False))
+            sends.append(lax.dynamic_index_in_dim(buf, 1 - mine, axis=axis, keepdims=False))
+            remaining[index].pop(axis)
+        groups = {}
+        for index in range(len(bufs)):
+            groups.setdefault(orders[index][step], []).append(index)
+        arrived = [None] * len(bufs)
+        for bit, members in groups.items():
+            pairs = [(i, i ^ (1 << bit)) for i in range(devices)]
+            if len(members) == 1:
+                arrived[members[0]] = lax.ppermute(sends[members[0]], axes, pairs)
+            else:
+                moved = lax.ppermute(jnp.stack([sends[m] for m in members]), axes, pairs)
+                for position, m in enumerate(members):
+                    arrived[m] = moved[position]
+        bufs = [keep + got for keep, got in zip(keeps, arrived)]
+    return bufs
 
 
 def local(maps, first_weight, second_weight, out_grad):
@@ -208,7 +224,7 @@
     upper_row = shifted_2(maps[:, height - 1 : height], "tile", 1)
     grad = out_grad.reshape(owned, -1, outputs)
     conv = None
-    pieces = []
+    partials = []
     halves = first_stage(maps, upper_row, first_weight, part)
     for chunk in range(chunks):
         channels = slice(chunk * part, (chunk + 1) * part)
@@ -227,10 +243,8 @@
         conv, partial = second_stage(
             hidden, second_weight[:, :, channels], grad, conv, jnp.bfloat16 if last else jnp.float32
         )
-        summed = halving_reduce_scatter(
-            partial.sum(axis=0).reshape(outputs, 9 * part), ("group", "tile"), swap=chunk % 2 == 1
-        )
-        pieces.append(summed.reshape(-1, 9, part))
+        partials.append(partial.sum(axis=0).reshape(outputs, 9 * part))
+    pieces = [summed.reshape(-1, 9, part) for summed in halving_reduce_scatter(partials, ("group", "tile"))]
     weight_grad = jnp.concatenate(pieces, axis=-1).reshape(-1, 3, 3, outputs)
     return (conv, weight_grad)
 

time: 184 us -> 189 us (1.027)
  waiting for transfers between devices: 40.1 us -> 46.3 us
  starting transfers between devices: 17.8 us -> 15.2 us
    ppermute x10 -> x7, waiting for transfers between devices: 16.7 us -> 22.8 us  [the longest x3 13.3 us: halving_reduce_scatter(): moved = lax.ppermute(jnp.stack([sends[m] for m in members]), axes, pairs)]
    ppermute x10 -> x7, starting transfers between devices: 9.37 us -> 6.7 us  [the longest x4 6.2 us: halving_reduce_scatter(): arrived[members[0]] = lax.ppermute(sends[members[0]], axes, pairs)]
  transfers between devices with their start and end apart: 12 -> 9, of which waited for: 10 -> 8; matrix products, arithmetic and copies ran while one was open for 10% -> 6% of each run, Pallas kernels for 19% -> 9%
where the time goes in v10:
time: 189 us; the launch traced here: 188 us
  blocking collectives  54.4 us (29%)
  Pallas kernels  46.6 us (25%)
  waiting for transfers between devices  46.3 us (24%)
  local copies, waits for them, and re-layouts  21.8 us (12%)
  starting transfers between devices  15.2 us (8%)
  other arithmetic  3.08 us (2%)
    all_to_all x1, blocking collectives, local(): lax.all_to_all(local_hidden.reshape(tiles, owned, half_rows, width // 2,...  54.4 us
    pallas_call x2, Pallas kernels, second_stage(): pl.pallas_call(functools.partial(second_kernel, rows=rows, carry=prev is...  35.5 us
    all_to_all x1, waiting for transfers between devices, local(): lax.all_to_all(local_hidden.reshape(tiles, owned, half_rows, width // 2,...  20 us
    ppermute x3, waiting for transfers between devices, halving_reduce_scatter(): moved = lax.ppermute(jnp.stack([sends[m] for m in members]), axes, pairs)  13.3 us
    pallas_call x1, Pallas kernels, first_stage(): pl.pallas_call(first_kernel, grid=(images,), in_specs=[pl.BlockSpec((None...  11.1 us
    ppermute x4, waiting for transfers between devices, halving_reduce_scatter(): arrived[members[0]] = lax.ppermute(sends[members[0]], axes, pairs)  9.57 us
    ppermute x4, starting transfers between devices, halving_reduce_scatter(): arrived[members[0]] = lax.ppermute(sends[members[0]], axes, pairs)  6.2 us
    concatenate x2, local copies, waits for them, and re-layouts, shift_cols_right(): return jnp.concatenate([zero_col, slab[:, :, :-1]], axis=2)  5.07 us
  transfers between devices with their start and end apart: 9, of which 8 were waited for; matrix products, arithmetic and copies ran while one was open for 6% of the time, Pallas kernels for 9%

profile of v10, /device:TPU:0, one launch (start us, length us, event | category | flops | bytes accessed | tf_op | source)
XLA Modules:
  0.0 188.1 jit_solution(310304457324989050)
XLA Ops:
  0.6 0.0 copy-start
  0.6 1.0 slice.39
  1.7 4.9 %collective-permute-start = (bf16[8,1,128,128]{3,2,1,0:T(8,128)(2,1)S(1)}, bf16[8,1,128,128]{3,2,1,0:T(8,128)(2,1)S(1)}, u32[]{:S(2)}, u32[]{:S(2)}) collective-permute-start(bf16[8,1,128,128]{3,2,1,0:T(8,128)(2,1)S(1)} %slice.39), channel_id=1, source_target_pairs={{0,1},{1,2},{2,3},{3,4},{4,5},{5,6},{6,7},{8,9},{9,10},{10,11},{11... | collective-permute-start | bytes 786440 | tf_op jit(solution)/shard_map/ppermute | solution.py:14
  6.6 0.7 pad_clamp_fusion
  7.2 0.0 copy-done
  7.2 0.6 gather_fusion
  7.8 0.9 copy.8
  8.7 3.4 %collective-permute-done.up_ref = bf16[8,1,128,128]{3,2,1,0:T(8,128)(2,1)S(1)} collective-permute-done((bf16[8,1,128,128]{3,2,1,0:T(8,128)(2,1)S(1)}, bf16[8,1,128,128]{3,2,1,0:T(8,128)(2,1)S(1)}, u32[]{:S(2)}, u32[]{:S(2)}) %collective-permute-start) | collective-permute-done | bytes 262176 | tf_op jit(solution)/shard_map/ppermute | solution.py:14
  12.1 0.0 copy-start.4
  12.1 0.7 copy-done.4
  12.8 11.1 %shard_map.68 = (bf16[8,16,64,128]{3,2,1,0:T(8,128)(2,1)}, bf16[8,16,64,128]{3,2,1,0:T(8,128)(2,1)}) custom-call(bf16[8,32,128,128]{3,2,1,0:T(8,128)(2,1)} %x_ref.1, bf16[8,1,128,128]{3,2,1,0:T(8,128)(2,1)} %copy-done.4, bf16[1152,256]{1,0:T(8,128)(2,1)} %bitcast.77), custom_call_target="tpu_custom_call" | custom-call | flops 4831838208 | bytes 12582912 | tf_op jit(solution)/shard_map/pallas_call | solution.py:76
  23.9 54.4 %all_to_all.21 = bf16[8,1,16,64,128]{4,3,2,1,0:T(8,128)(2,1)} all-to-all(bf16[8,1,16,64,128]{4,3,2,1,0:T(8,128)(2,1)} %bitcast.72), channel_id=1, replica_groups=mesh['group'=4,'tile'=8] {'tile'}, dimensions={0} | all-to-all | bytes 4194304 | tf_op jit(solution)/shard_map/all_to_all | solution.py:232
  78.3 3.6 %all-to-all-start = ((bf16[8,1,16,64,128]{4,3,2,1,0:T(8,128)(2,1)}), bf16[8,1,16,64,128]{4,3,2,1,0:T(8,128)(2,1)S(1)}, u32[]{:S(2)}, u32[]{:S(2)}) async-start(bf16[8,1,16,64,128]{4,3,2,1,0:T(8,128)(2,1)} %bitcast.71), calls=%async_computation | async-start | bytes 4194304 | tf_op jit(solution)/shard_map/all_to_all | solution.py:232
  81.9 0.0 copy-start.2
  81.9 2.5 %fusion.4 = (bf16[3,3,128,256]{3,2,1,0:T(8,128)(2,1)}, bf16[3,3,128,256]{3,2,1,0:T(8,128)(2,1)}) fusion(bf16[3,3,256,256]{3,2,1,0:T(8,128)(2,1)} %param.7), kind=kLoop, calls=%fused_computation.34 | loop fusion | bytes 2359296 | tf_op jit(solution)/shard_map/slice | solution.py:244
  84.4 0.0 copy-done.2
  84.4 1.8 pad.11.refs_1_
  86.2 1.3 pad_slice_fusion.2
  87.5 2.5 %concatenate.16.refs_0_ = bf16[1,130,64,128]{3,2,1,0:T(8,128)(2,1)} pad(bf16[1,130,63,128]{3,2,1,0:T(8,128)(2,1)S(1)} %get-tuple-element.21, bf16[]{:T(256)} %constant.80.clone.1), padding=0_0x0_0x1_0x0_0 | pad | bytes 4226562 | tf_op jit(solution)/shard_map/concatenate | solution.py:19
  90.0 1.8 concatenate.17.refs_2_
  91.8 17.7 %shard_map.69 = (f32[1,128,64,256]{3,2,1,0:T(8,128)}, f32[1,256,1152]{2,1,0:T(8,128)}) custom-call(bf16[1,130,64,128]{3,2,1,0:T(8,128)(2,1)} %concatenate.16.refs_0_, bf16[1,130,64,128]{3,2,1,0:T(8,128)(2,1)} %pad.11.refs_1_, bf16[1,130,64,128]{3,2,1,0:T(8,128)(2,1)} %concatenate.17.refs_2_, bf16[1152,256]{1,0:T(8,128)(2,1)} %bitcast.79, ...), custom_call_target="tpu_custom_call" | custom-call | flops 9663676416 | bytes 26345472 | tf_op jit(solution)/shard_map/pallas_call | solution.py:155
  109.5 20.0 %all-to-all-done = bf16[8,1,16,64,128]{4,3,2,1,0:T(8,128)(2,1)S(1)} async-done(((bf16[8,1,16,64,128]{4,3,2,1,0:T(8,128)(2,1)}), bf16[8,1,16,64,128]{4,3,2,1,0:T(8,128)(2,1)S(1)}, u32[]{:S(2)}, u32[]{:S(2)}) %all-to-all-start) | async-done | bytes 2097184 | tf_op jit(solution)/shard_map/all_to_all | solution.py:232
  129.5 1.2 pad_slice_fusion
  130.8 1.8 pad.12.refs_1_
  132.5 2.6 %concatenate.18.refs_0_ = bf16[1,130,64,128]{3,2,1,0:T(8,128)(2,1)} pad(bf16[1,130,63,128]{3,2,1,0:T(8,128)(2,1)S(1)} %get-tuple-element.19, bf16[]{:T(256)} %constant.80.clone.1), padding=0_0x0_0x1_0x0_0 | pad | bytes 4226562 | tf_op jit(solution)/shard_map/concatenate | solution.py:19
  135.1 1.8 concatenate.19.refs_2_
  136.9 0.0 copy-start.3
  136.9 17.8 %shard_map.70 = (bf16[1,128,64,256]{3,2,1,0:T(8,128)(2,1)}, f32[1,256,1152]{2,1,0:T(8,128)}) custom-call(bf16[1,130,64,128]{3,2,1,0:T(8,128)(2,1)} %concatenate.18.refs_0_, bf16[1,130,64,128]{3,2,1,0:T(8,128)(2,1)} %pad.12.refs_1_, bf16[1,130,64,128]{3,2,1,0:T(8,128)(2,1)} %concatenate.19.refs_2_, bf16[1152,256]{1,0:T(8,128)(2,1)} %bitcast.78, ...), custom_call_target="tpu_custom_call" | custom-call | flops 9663676416 | bytes 26345472 | tf_op jit(solution)/shard_map/pallas_call | solution.py:155
  154.7 0.0 copy-done.3
  154.7 1.2 dynamic-slice_bitcast_fusion
  155.9 0.1 pad_maximum_fusion
  155.9 0.1 collective-permute-start.1
  156.0 3.0 %collective-permute-done.1 = f32[2,2,2,2,2,8,1152]{6,5,4,3,2,1,0:T(8,128)} collective-permute-done((f32[2,2,2,2,2,8,1152]{6,5,4,3,2,1,0:T(8,128)S(1)}, f32[2,2,2,2,2,8,1152]{6,5,4,3,2,1,0:T(8,128)}, u32[]{:S(2)}, u32[]{:S(2)}) %collective-permute-start.1) | collective-permute-done | bytes 1179680 | tf_op jit(solution)/shard_map/ppermute | solution.py:209
  159.0 1.5 fusion.1
  160.6 1.6 collective-permute-start.2
  162.2 1.5 collective-permute-start.4
  163.7 6.0 %collective-permute-done.2 = f32[2,2,2,8,1152]{4,3,2,1,0:T(8,128)S(1)} collective-permute-done((f32[2,2,2,8,1152]{4,3,2,1,0:T(8,128)S(1)}, f32[2,2,2,8,1152]{4,3,2,1,0:T(8,128)S(1)}, u32[]{:S(2)}, u32[]{:S(2)}) %collective-permute-start.2) | collective-permute-done | bytes 294944 | tf_op jit(solution)/shard_map/ppermute | solution.py:207
  169.8 1.5 collective-permute-start.3
  171.3 0.0 collective-permute-done.4
  171.3 1.6 collective-permute-start.5
  172.9 2.0 %collective-permute-done.3 = f32[2,2,8,1152]{3,2,1,0:T(8,128)S(1)} collective-permute-done((f32[2,2,8,1152]{3,2,1,0:T(8,128)S(1)}, f32[2,2,8,1152]{3,2,1,0:T(8,128)S(1)}, u32[]{:S(2)}, u32[]{:S(2)}) %collective-permute-start.3) | collective-permute-done | bytes 147488 | tf_op jit(solution)/shard_map/ppermute | solution.py:207
  175.0 1.5 collective-permute-done.5
  176.6 0.1 collective-permute-start.6
  176.7 5.1 %collective-permute-done.6 = f32[2,2,8,1152]{3,2,1,0:T(8,128)S(1)} collective-permute-done((f32[2,2,8,1152]{3,2,1,0:T(8,128)S(1)}, f32[2,2,8,1152]{3,2,1,0:T(8,128)S(1)}, u32[]{:S(2)}, u32[]{:S(2)}) %collective-permute-start.6) | collective-permute-done | bytes 147488 | tf_op jit(solution)/shard_map/ppermute | solution.py:209
  181.9 0.4 collective-permute-start.7
  182.3 5.2 %collective-permute-done.7 = f32[2,8,1152]{2,1,0:T(8,128)S(1)} collective-permute-done((f32[2,8,1152]{2,1,0:T(8,128)S(1)}, f32[2,8,1152]{2,1,0:T(8,128)S(1)}, u32[]{:S(2)}, u32[]{:S(2)}) %collective-permute-start.7) | collective-permute-done | bytes 73760 | tf_op jit(solution)/shard_map/ppermute | solution.py:209
  187.5 0.6 pad_maximum_fusion.3
  188.1 0.0 copy-done.1
  (17 shorter events, 0.3 us)
Async XLA Ops:
  0.6 6.6 %copy-start = (bf16[3,3,128,256]{3,2,1,0:T(8,128)(2,1)S(1)}, bf16[3,3,128,256]{3,2,1,0:T(8,128)(2,1)}, u32[]{:S(2)}) copy-start(bf16[3,3,128,256]{3,2,1,0:T(8,128)(2,1)} %param.6) | copy-start | bytes 1769476
  1.7 10.4 %collective-permute-start = (bf16[8,1,128,128]{3,2,1,0:T(8,128)(2,1)S(1)}, bf16[8,1,128,128]{3,2,1,0:T(8,128)(2,1)S(1)}, u32[]{:S(2)}, u32[]{:S(2)}) collective-permute-start(bf16[8,1,128,128]{3,2,1,0:T(8,128)(2,1)S(1)} %slice.39), channel_id=1, source_target_pairs={{0,1},{1,2},{2,3},{3,4},{4,5},{5,6},{6,7},{8,9},{9,10},{10,11},{11... | collective-permute-start | bytes 786440 | tf_op jit(solution)/shard_map/ppermute | solution.py:14
  12.1 0.7 copy-start.4
  78.3 51.3 %all-to-all-start = ((bf16[8,1,16,64,128]{4,3,2,1,0:T(8,128)(2,1)}), bf16[8,1,16,64,128]{4,3,2,1,0:T(8,128)(2,1)S(1)}, u32[]{:S(2)}, u32[]{:S(2)}) async-start(bf16[8,1,16,64,128]{4,3,2,1,0:T(8,128)(2,1)} %bitcast.71), calls=%async_computation | async-start | bytes 4194304 | tf_op jit(solution)/shard_map/all_to_all | solution.py:232
  81.9 2.5 %copy-start.2 = (bf16[8,1,16,64,128]{4,3,2,1,0:T(8,128)(2,1)S(1)}, bf16[8,1,16,64,128]{4,3,2,1,0:T(8,128)(2,1)}, u32[]{:S(2)}) copy-start(bf16[8,1,16,64,128]{4,3,2,1,0:T(8,128)(2,1)} %all_to_all.21) | copy-start | bytes 6291460
  136.9 17.8 %copy-start.3 = (f32[1,256,1152]{2,1,0:T(8,128)S(1)}, f32[1,256,1152]{2,1,0:T(8,128)}, u32[]{:S(2)}) copy-start(f32[1,256,1152]{2,1,0:T(8,128)} %get-tuple-element.16) | copy-start | bytes 3538948
  155.9 3.0 %collective-permute-start.1 = (f32[2,2,2,2,2,8,1152]{6,5,4,3,2,1,0:T(8,128)S(1)}, f32[2,2,2,2,2,8,1152]{6,5,4,3,2,1,0:T(8,128)}, u32[]{:S(2)}, u32[]{:S(2)}) collective-permute-start(f32[2,2,2,2,2,8,1152]{6,5,4,3,2,1,0:T(8,128)S(1)} %pad_maximum_fusion), channel_id=1, source_target_pairs={{0,8},{1,9},{2,10},{3,11},{4,12},{5,13},{6,14},{7,15},{8,0},{9,1},... | collective-permute-start | bytes 3538952 | tf_op jit(solution)/shard_map/ppermute | solution.py:209
  160.6 9.1 %collective-permute-start.2 = (f32[2,2,2,8,1152]{4,3,2,1,0:T(8,128)S(1)}, f32[2,2,2,8,1152]{4,3,2,1,0:T(8,128)S(1)}, u32[]{:S(2)}, u32[]{:S(2)}) collective-permute-start(f32[2,2,2,8,1152]{4,3,2,1,0:T(8,128)S(1)} %dynamic-slice_bitcast_fusion.3), channel_id=1, source_target_pairs={{0,16},{1,17},{2,18},{3,19},{4,20},{5,21},{6,22},{7,23},{8,24},{9,... | collective-permute-start | bytes 884744 | tf_op jit(solution)/shard_map/ppermute | solution.py:207
  162.2 9.1 %collective-permute-start.4 = (f32[2,2,2,8,1152]{4,3,2,1,0:T(8,128)S(1)}, f32[2,2,2,8,1152]{4,3,2,1,0:T(8,128)S(1)}, u32[]{:S(2)}, u32[]{:S(2)}) collective-permute-start(f32[2,2,2,8,1152]{4,3,2,1,0:T(8,128)S(1)} %dynamic-slice_bitcast_fusion.2), channel_id=1, source_target_pairs={{0,1},{1,0},{2,3},{3,2},{4,5},{5,4},{6,7},{7,6},{8,9},{9,8},{10,11... | collective-permute-start | bytes 884744 | tf_op jit(solution)/shard_map/ppermute | solution.py:207
  169.7 18.4 %copy-start.1 = (bf16[3,3,128,256]{3,2,1,0:T(8,128)(2,1)S(1)}, bf16[3,3,128,256]{3,2,1,0:T(8,128)(2,1)}, u32[]{:S(2)}) copy-start(bf16[3,3,128,256]{3,2,1,0:T(8,128)(2,1)} %param.6) | copy-start | bytes 1769476
  169.8 5.2 %collective-permute-start.3 = (f32[2,2,8,1152]{3,2,1,0:T(8,128)S(1)}, f32[2,2,8,1152]{3,2,1,0:T(8,128)S(1)}, u32[]{:S(2)}, u32[]{:S(2)}) collective-permute-start(f32[2,2,8,1152]{3,2,1,0:T(8,128)S(1)} %dynamic-slice_bitcast_fusion.5), channel_id=1, source_target_pairs={{0,1},{1,0},{2,3},{3,2},{4,5},{5,4},{6,7},{7,6},{8,9},{9,8},{10,11... | collective-permute-start | bytes 442376 | tf_op jit(solution)/shard_map/ppermute | solution.py:207
  171.3 5.2 %collective-permute-start.5 = (f32[2,2,8,1152]{3,2,1,0:T(8,128)S(1)}, f32[2,2,8,1152]{3,2,1,0:T(8,128)S(1)}, u32[]{:S(2)}, u32[]{:S(2)}) collective-permute-start(f32[2,2,8,1152]{3,2,1,0:T(8,128)S(1)} %dynamic-slice_bitcast_fusion.4), channel_id=1, source_target_pairs={{0,16},{1,17},{2,18},{3,19},{4,20},{5,21},{6,22},{7,23},{8,24},{9,... | collective-permute-start | bytes 442376 | tf_op jit(solution)/shard_map/ppermute | solution.py:207
  176.6 5.2 %collective-permute-start.6 = (f32[2,2,8,1152]{3,2,1,0:T(8,128)S(1)}, f32[2,2,8,1152]{3,2,1,0:T(8,128)S(1)}, u32[]{:S(2)}, u32[]{:S(2)}) collective-permute-start(f32[2,2,8,1152]{3,2,1,0:T(8,128)S(1)} %pad_maximum_fusion.1), channel_id=1, source_target_pairs={{0,2},{1,3},{2,0},{3,1},{4,6},{5,7},{6,4},{7,5},{8,10},{9,11},{10,... | collective-permute-start | bytes 442376 | tf_op jit(solution)/shard_map/ppermute | solution.py:209
  181.9 5.5 %collective-permute-start.7 = (f32[2,8,1152]{2,1,0:T(8,128)S(1)}, f32[2,8,1152]{2,1,0:T(8,128)S(1)}, u32[]{:S(2)}, u32[]{:S(2)}) collective-permute-start(f32[2,8,1152]{2,1,0:T(8,128)S(1)} %pad_maximum_fusion.2), channel_id=1, source_target_pairs={{0,4},{1,5},{2,6},{3,7},{4,0},{5,1},{6,2},{7,3},{8,12},{9,13},{10,... | collective-permute-start | bytes 221192 | tf_op jit(solution)/shard_map/ppermute | solution.py:209

commit v11 on v9

--- a/solution.py
+++ b/solution.py
@@ -224,9 +224,10 @@
             arrived, conv = lax.optimization_barrier((arrived, conv))
         hidden = arrived.reshape(owned, half_rows * tiles, width // 2, part)
         last = chunk == chunks - 1
-        conv, partial = second_stage(
-            hidden, second_weight[:, :, channels], grad, conv, jnp.bfloat16 if last else jnp.float32
-        )
+        weight = second_weight[:, :, channels]
+        if pieces:
+            weight, pieces = lax.optimization_barrier((weight, pieces))
+        conv, partial = second_stage(hidden, weight, grad, conv, jnp.bfloat16 if last else jnp.float32)
         summed = halving_reduce_scatter(
             partial.sum(axis=0).reshape(outputs, 9 * part), ("group", "tile"), swap=chunk % 2 == 1
         )

time: 184 us -> 192 us (1.043)
  blocking collectives: 54.4 us -> 0 us
  waiting for transfers between devices: 40.1 us -> 83.7 us
  starting transfers between devices: 17.8 us -> 29.5 us
  local copies, waits for them, and re-layouts: 21.9 us -> 26.4 us
  other arithmetic: 1.57 us -> 3.69 us
    all_to_all x1 -> x0, blocking collectives: 54.4 us -> none  [local(): lax.all_to_all(local_hidden.reshape(tiles, owned, half_rows, width // 2,...]
    all_to_all x1 -> x2, waiting for transfers between devices: 20 us -> 45.1 us  [local(): lax.all_to_all(local_hidden.reshape(tiles, owned, half_rows, width // 2,...]
    ppermute x10, waiting for transfers between devices: 16.7 us -> 35.3 us  [halving_reduce_scatter(): buf = keep + lax.ppermute(send, axes, pairs)]
    all_to_all x1 -> x2, starting transfers between devices: 3.6 us -> 10.4 us  [local(): lax.all_to_all(local_hidden.reshape(tiles, owned, half_rows, width // 2,...]
    ppermute x10, starting transfers between devices: 9.37 us -> 14.2 us  [halving_reduce_scatter(): buf = keep + lax.ppermute(send, axes, pairs)]
    slice x2, local copies, waits for them, and re-layouts: 2.51 us -> 4.81 us  [shift_cols_left(): return jnp.concatenate([slab[:, :, 1:], zero_col], axis=2)]
    add x10 -> x9, other arithmetic: 0.26 us -> 2.38 us  [halving_reduce_scatter(): buf = keep + lax.ppermute(send, axes, pairs)]
  transfers between devices with their start and end apart: 12 -> 13, of which waited for: 10 -> 12; matrix products, arithmetic and copies ran while one was open for 10% -> 13% of each run, Pallas kernels for 19% -> 9%
where the time goes in v11:
time: 192 us; the launch traced here: 191 us
  waiting for transfers between devices  83.7 us (44%)
  Pallas kernels  46.6 us (24%)
  starting transfers between devices  29.5 us (15%)
  local copies, waits for them, and re-layouts  26.4 us (14%)
  other arithmetic  3.69 us (2%)
    all_to_all x2, waiting for transfers between devices, local(): lax.all_to_all(local_hidden.reshape(tiles, owned, half_rows, width // 2,...  45.1 us
    pallas_call x2, Pallas kernels, second_stage(): pl.pallas_call(functools.partial(second_kernel, rows=rows, carry=prev is...  35.4 us
    ppermute x10, waiting for transfers between devices, halving_reduce_scatter(): buf = keep + lax.ppermute(send, axes, pairs)  35.3 us
    ppermute x10, starting transfers between devices, halving_reduce_scatter(): buf = keep + lax.ppermute(send, axes, pairs)  14.2 us
    pallas_call x1, Pallas kernels, first_stage(): pl.pallas_call(first_kernel, grid=(images,), in_specs=[pl.BlockSpec((None...  11.1 us
    all_to_all x2, starting transfers between devices, local(): lax.all_to_all(local_hidden.reshape(tiles, owned, half_rows, width // 2,...  10.4 us
    concatenate x2, local copies, waits for them, and re-layouts, shift_cols_right(): return jnp.concatenate([zero_col, slab[:, :, :-1]], axis=2)  5.06 us
    ppermute x1, starting transfers between devices, shifted_2(): return lax.ppermute(shard, axis, pairs)  4.86 us
  transfers between devices with their start and end apart: 13, of which 12 were waited for; matrix products, arithmetic and copies ran while one was open for 13% of the time, Pallas kernels for 9%

profile of v11, /device:TPU:0, one launch (start us, length us, event | category | flops | bytes accessed | tf_op | source)
XLA Modules:
  0.0 190.7 jit_solution(6001537291566657275)
XLA Ops:
  0.6 1.0 slice.21
  1.7 4.9 %collective-permute-start = (bf16[8,1,128,128]{3,2,1,0:T(8,128)(2,1)S(1)}, bf16[8,1,128,128]{3,2,1,0:T(8,128)(2,1)S(1)}, u32[]{:S(2)}, u32[]{:S(2)}) collective-permute-start(bf16[8,1,128,128]{3,2,1,0:T(8,128)(2,1)S(1)} %slice.21), channel_id=1, source_target_pairs={{0,1},{1,2},{2,3},{3,4},{4,5},{5,6},{6,7},{8,9},{9,10},{10,11},{11... | collective-permute-start | bytes 786440 | tf_op jit(solution)/shard_map/ppermute | solution.py:14
  6.6 0.7 pad_clamp_fusion
  7.2 0.6 gather_fusion
  7.8 0.9 copy.8
  8.7 3.4 %collective-permute-done.up_ref = bf16[8,1,128,128]{3,2,1,0:T(8,128)(2,1)S(1)} collective-permute-done((bf16[8,1,128,128]{3,2,1,0:T(8,128)(2,1)S(1)}, bf16[8,1,128,128]{3,2,1,0:T(8,128)(2,1)S(1)}, u32[]{:S(2)}, u32[]{:S(2)}) %collective-permute-start) | collective-permute-done | bytes 262176 | tf_op jit(solution)/shard_map/ppermute | solution.py:14
  12.1 0.7 copy-done.4
  12.8 11.1 %shard_map.68 = (bf16[8,16,64,128]{3,2,1,0:T(8,128)(2,1)}, bf16[8,16,64,128]{3,2,1,0:T(8,128)(2,1)}) custom-call(bf16[8,32,128,128]{3,2,1,0:T(8,128)(2,1)} %x_ref.1, bf16[8,1,128,128]{3,2,1,0:T(8,128)(2,1)} %copy-done.4, bf16[1152,256]{1,0:T(8,128)(2,1)} %bitcast.73), custom_call_target="tpu_custom_call" | custom-call | flops 4831838208 | bytes 12582912 | tf_op jit(solution)/shard_map/pallas_call | solution.py:76
  23.9 6.8 %all-to-all-start.1 = ((bf16[8,1,16,64,128]{4,3,2,1,0:T(8,128)(2,1)}), bf16[8,1,16,64,128]{4,3,2,1,0:T(8,128)(2,1)S(1)}, u32[]{:S(2)}, u32[]{:S(2)}) async-start(bf16[8,1,16,64,128]{4,3,2,1,0:T(8,128)(2,1)} %bitcast.68), calls=%async_computation.1 | async-start | bytes 4194304 | tf_op jit(solution)/shard_map/all_to_all | solution.py:216
  30.7 2.4 %fusion.1 = (bf16[3,3,128,256]{3,2,1,0:T(8,128)(2,1)}, bf16[3,3,128,256]{3,2,1,0:T(8,128)(2,1)}) fusion(bf16[3,3,256,256]{3,2,1,0:T(8,128)(2,1)} %param.7), kind=kLoop, calls=%fused_computation.28 | loop fusion | bytes 2359296 | tf_op jit(solution)/shard_map/slice | solution.py:227
  33.1 45.0 %all-to-all-done.1 = bf16[8,1,16,64,128]{4,3,2,1,0:T(8,128)(2,1)S(1)} async-done(((bf16[8,1,16,64,128]{4,3,2,1,0:T(8,128)(2,1)}), bf16[8,1,16,64,128]{4,3,2,1,0:T(8,128)(2,1)S(1)}, u32[]{:S(2)}, u32[]{:S(2)}) %all-to-all-start.1) | async-done | bytes 2097184 | tf_op jit(solution)/shard_map/all_to_all | solution.py:216
  78.1 1.3 copy-done.2
  79.4 3.6 %all-to-all-start = ((bf16[8,1,16,64,128]{4,3,2,1,0:T(8,128)(2,1)}), bf16[8,1,16,64,128]{4,3,2,1,0:T(8,128)(2,1)S(1)}, u32[]{:S(2)}, u32[]{:S(2)}) async-start(bf16[8,1,16,64,128]{4,3,2,1,0:T(8,128)(2,1)} %bitcast.67), calls=%async_computation | async-start | bytes 4194304 | tf_op jit(solution)/shard_map/all_to_all | solution.py:216
  83.0 3.6 %pad_slice_fusion.2 = (bf16[1,130,63,128]{3,2,1,0:T(8,128)(2,1)S(1)}, bf16[1,130,63,128]{3,2,1,0:T(8,128)(2,1)S(1)}) fusion(bf16[1,128,64,128]{3,2,1,0:T(8,128)(2,1)} %bitcast.64), kind=kLoop, calls=%fused_computation.26 | loop fusion | bytes 6290432 | tf_op jit(solution)/shard_map/slice | solution.py:24
  86.7 1.8 pad.11.refs_1_
  88.5 1.8 concatenate.21.refs_2_
  90.3 2.5 %concatenate.20.refs_0_ = bf16[1,130,64,128]{3,2,1,0:T(8,128)(2,1)} pad(bf16[1,130,63,128]{3,2,1,0:T(8,128)(2,1)S(1)} %get-tuple-element.25, bf16[]{:T(256)} %constant.80.clone.1), padding=0_0x0_0x1_0x0_0 | pad | bytes 4226562 | tf_op jit(solution)/shard_map/concatenate | solution.py:19
  92.8 17.7 %shard_map.69 = (f32[1,128,64,256]{3,2,1,0:T(8,128)}, f32[1,256,1152]{2,1,0:T(8,128)}) custom-call(bf16[1,130,64,128]{3,2,1,0:T(8,128)(2,1)} %concatenate.20.refs_0_, bf16[1,130,64,128]{3,2,1,0:T(8,128)(2,1)} %pad.11.refs_1_, bf16[1,130,64,128]{3,2,1,0:T(8,128)(2,1)} %concatenate.21.refs_2_, bf16[1152,256]{1,0:T(8,128)(2,1)} %bitcast.75, ...), custom_call_target="tpu_custom_call" | custom-call | flops 9663676416 | bytes 26345472 | tf_op jit(solution)/shard_map/pallas_call | solution.py:155
  110.5 1.1 dynamic-slice_bitcast_fusion.1
  111.6 0.1 collective-permute-start.1
  111.7 2.0 %collective-permute-done.1 = f32[2,2,2,2,8,1152]{5,4,3,2,1,0:T(8,128)S(1)} collective-permute-done((f32[2,2,2,2,8,1152]{5,4,3,2,1,0:T(8,128)S(1)}, f32[2,2,2,2,8,1152]{5,4,3,2,1,0:T(8,128)S(1)}, u32[]{:S(2)}, u32[]{:S(2)}) %collective-permute-start.1) | collective-permute-done | bytes 589856 | tf_op jit(solution)/shard_map/ppermute | solution.py:195
  113.6 1.1 bitcast_add_fusion.1
  114.8 1.6 collective-permute-start.2
  116.4 7.5 %collective-permute-done.2 = f32[2,2,2,8,1152]{4,3,2,1,0:T(8,128)S(1)} collective-permute-done((f32[2,2,2,8,1152]{4,3,2,1,0:T(8,128)S(1)}, f32[2,2,2,8,1152]{4,3,2,1,0:T(8,128)S(1)}, u32[]{:S(2)}, u32[]{:S(2)}) %collective-permute-start.2) | collective-permute-done | bytes 294944 | tf_op jit(solution)/shard_map/ppermute | solution.py:195
  124.0 2.1 %collective-permute-start.3 = (f32[2,2,8,1152]{3,2,1,0:T(8,128)S(1)}, f32[2,2,8,1152]{3,2,1,0:T(8,128)S(1)}, u32[]{:S(2)}, u32[]{:S(2)}) collective-permute-start(f32[2,2,8,1152]{3,2,1,0:T(8,128)S(1)} %dynamic-slice_bitcast_fusion.5), channel_id=1, source_target_pairs={{0,1},{1,0},{2,3},{3,2},{4,5},{5,4},{6,7},{7,6},{8,9},{9,8},{10,11... | collective-permute-start | bytes 442376 | tf_op jit(solution)/shard_map/ppermute | solution.py:195
  126.1 3.3 %collective-permute-done.3 = f32[2,2,8,1152]{3,2,1,0:T(8,128)S(1)} collective-permute-done((f32[2,2,8,1152]{3,2,1,0:T(8,128)S(1)}, f32[2,2,8,1152]{3,2,1,0:T(8,128)S(1)}, u32[]{:S(2)}, u32[]{:S(2)}) %collective-permute-start.3) | collective-permute-done | bytes 147488 | tf_op jit(solution)/shard_map/ppermute | solution.py:195
  129.4 2.0 %collective-permute-start.4 = (f32[2,8,1152]{2,1,0:T(8,128)S(1)}, f32[2,8,1152]{2,1,0:T(8,128)S(1)}, u32[]{:S(2)}, u32[]{:S(2)}) collective-permute-start(f32[2,8,1152]{2,1,0:T(8,128)S(1)} %dynamic-slice_bitcast_fusion.7), channel_id=1, source_target_pairs={{0,2},{1,3},{2,0},{3,1},{4,6},{5,7},{6,4},{7,5},{8,10},{9,11},{10,... | collective-permute-start | bytes 221192 | tf_op jit(solution)/shard_map/ppermute | solution.py:195
  131.4 0.1 all-to-all-done
  131.5 2.3 %collective-permute-done.4 = f32[2,8,1152]{2,1,0:T(8,128)S(1)} collective-permute-done((f32[2,8,1152]{2,1,0:T(8,128)S(1)}, f32[2,8,1152]{2,1,0:T(8,128)S(1)}, u32[]{:S(2)}, u32[]{:S(2)}) %collective-permute-start.4) | collective-permute-done | bytes 73760 | tf_op jit(solution)/shard_map/ppermute | solution.py:195
  133.9 2.8 %collective-permute-start.5 = (f32[8,1152]{1,0:T(8,128)S(1)}, f32[8,1152]{1,0:T(8,128)S(1)}, u32[]{:S(2)}, u32[]{:S(2)}) collective-permute-start(f32[8,1152]{1,0:T(8,128)S(1)} %dynamic-slice_bitcast_fusion.9), channel_id=1, source_target_pairs={{0,4},{1,5},{2,6},{3,7},{4,0},{5,1},{6,2},{7,3},{8,12},{9,13},{10,... | collective-permute-start | bytes 110600 | tf_op jit(solution)/shard_map/ppermute | solution.py:195
  136.7 1.2 pad_slice_fusion
  137.9 1.8 pad.12.refs_1_
  139.7 1.8 concatenate.23.refs_2_
  141.4 2.6 %concatenate.22.refs_0_ = bf16[1,130,64,128]{3,2,1,0:T(8,128)(2,1)} pad(bf16[1,130,63,128]{3,2,1,0:T(8,128)(2,1)S(1)} %get-tuple-element.23, bf16[]{:T(256)} %constant.80.clone.1), padding=0_0x0_0x1_0x0_0 | pad | bytes 4226562 | tf_op jit(solution)/shard_map/concatenate | solution.py:19
  144.0 17.8 %shard_map.70 = (bf16[1,128,64,256]{3,2,1,0:T(8,128)(2,1)}, f32[1,256,1152]{2,1,0:T(8,128)}) custom-call(bf16[1,130,64,128]{3,2,1,0:T(8,128)(2,1)} %concatenate.22.refs_0_, bf16[1,130,64,128]{3,2,1,0:T(8,128)(2,1)} %pad.12.refs_1_, bf16[1,130,64,128]{3,2,1,0:T(8,128)(2,1)} %concatenate.23.refs_2_, bf16[1152,256]{1,0:T(8,128)(2,1)} %bitcast.74, ...), custom_call_target="tpu_custom_call" | custom-call | flops 9663676416 | bytes 26345472 | tf_op jit(solution)/shard_map/pallas_call | solution.py:155
  161.8 1.2 dynamic-slice_bitcast_fusion
  163.0 0.1 collective-permute-start.6
  163.0 2.0 %collective-permute-done.6 = f32[2,2,2,2,8,1152]{5,4,3,2,1,0:T(8,128)S(1)} collective-permute-done((f32[2,2,2,2,8,1152]{5,4,3,2,1,0:T(8,128)S(1)}, f32[2,2,2,2,8,1152]{5,4,3,2,1,0:T(8,128)S(1)}, u32[]{:S(2)}, u32[]{:S(2)}) %collective-permute-start.6) | collective-permute-done | bytes 589856 | tf_op jit(solution)/shard_map/ppermute | solution.py:195
  165.0 1.1 bitcast_add_fusion
  166.2 1.9 collective-permute-start.7
  168.1 7.3 %collective-permute-done.7 = f32[2,2,2,8,1152]{4,3,2,1,0:T(8,128)S(1)} collective-permute-done((f32[2,2,2,8,1152]{4,3,2,1,0:T(8,128)S(1)}, f32[2,2,2,8,1152]{4,3,2,1,0:T(8,128)S(1)}, u32[]{:S(2)}, u32[]{:S(2)}) %collective-permute-start.7) | collective-permute-done | bytes 294944 | tf_op jit(solution)/shard_map/ppermute | solution.py:195
  175.5 1.6 collective-permute-start.8
  177.0 3.6 %collective-permute-done.8 = f32[2,2,8,1152]{3,2,1,0:T(8,128)S(1)} collective-permute-done((f32[2,2,8,1152]{3,2,1,0:T(8,128)S(1)}, f32[2,2,8,1152]{3,2,1,0:T(8,128)S(1)}, u32[]{:S(2)}, u32[]{:S(2)}) %collective-permute-start.8) | collective-permute-done | bytes 147488 | tf_op jit(solution)/shard_map/ppermute | solution.py:195
  180.7 1.5 collective-permute-start.9
  182.2 3.0 %collective-permute-done.9 = f32[2,8,1152]{2,1,0:T(8,128)S(1)} collective-permute-done((f32[2,8,1152]{2,1,0:T(8,128)S(1)}, f32[2,8,1152]{2,1,0:T(8,128)S(1)}, u32[]{:S(2)}, u32[]{:S(2)}) %collective-permute-start.9) | collective-permute-done | bytes 73760 | tf_op jit(solution)/shard_map/ppermute | solution.py:195
  185.2 0.7 collective-permute-start.10
  185.9 4.2 %collective-permute-done.10 = f32[8,1152]{1,0:T(8,128)S(1)} collective-permute-done((f32[8,1152]{1,0:T(8,128)S(1)}, f32[8,1152]{1,0:T(8,128)S(1)}, u32[]{:S(2)}, u32[]{:S(2)}) %collective-permute-start.10) | collective-permute-done | bytes 36896 | tf_op jit(solution)/shard_map/ppermute | solution.py:195
  190.1 0.6 pad_maximum_fusion
  (25 shorter events, 0.3 us)
Async XLA Ops:
  0.6 6.6 %copy-start = (bf16[3,3,128,256]{3,2,1,0:T(8,128)(2,1)S(1)}, bf16[3,3,128,256]{3,2,1,0:T(8,128)(2,1)}, u32[]{:S(2)}) copy-start(bf16[3,3,128,256]{3,2,1,0:T(8,128)(2,1)} %param.6) | copy-start | bytes 1769476
  1.7 10.4 %collective-permute-start = (bf16[8,1,128,128]{3,2,1,0:T(8,128)(2,1)S(1)}, bf16[8,1,128,128]{3,2,1,0:T(8,128)(2,1)S(1)}, u32[]{:S(2)}, u32[]{:S(2)}) collective-permute-start(bf16[8,1,128,128]{3,2,1,0:T(8,128)(2,1)S(1)} %slice.21), channel_id=1, source_target_pairs={{0,1},{1,2},{2,3},{3,4},{4,5},{5,6},{6,7},{8,9},{9,10},{10,11},{11... | collective-permute-start | bytes 786440 | tf_op jit(solution)/shard_map/ppermute | solution.py:14
  12.1 0.7 copy-start.4
  23.9 54.2 %all-to-all-start.1 = ((bf16[8,1,16,64,128]{4,3,2,1,0:T(8,128)(2,1)}), bf16[8,1,16,64,128]{4,3,2,1,0:T(8,128)(2,1)S(1)}, u32[]{:S(2)}, u32[]{:S(2)}) async-start(bf16[8,1,16,64,128]{4,3,2,1,0:T(8,128)(2,1)} %bitcast.68), calls=%async_computation.1 | async-start | bytes 4194304 | tf_op jit(solution)/shard_map/all_to_all | solution.py:216
  78.1 1.3 copy-start.2
  79.4 52.1 %all-to-all-start = ((bf16[8,1,16,64,128]{4,3,2,1,0:T(8,128)(2,1)}), bf16[8,1,16,64,128]{4,3,2,1,0:T(8,128)(2,1)S(1)}, u32[]{:S(2)}, u32[]{:S(2)}) async-start(bf16[8,1,16,64,128]{4,3,2,1,0:T(8,128)(2,1)} %bitcast.67), calls=%async_computation | async-start | bytes 4194304 | tf_op jit(solution)/shard_map/all_to_all | solution.py:216
  83.0 3.6 %copy-start.3 = (bf16[8,1,16,64,128]{4,3,2,1,0:T(8,128)(2,1)S(1)}, bf16[8,1,16,64,128]{4,3,2,1,0:T(8,128)(2,1)}, u32[]{:S(2)}) copy-start(bf16[8,1,16,64,128]{4,3,2,1,0:T(8,128)(2,1)} %copy-done.2) | copy-start | bytes 6291460
  111.6 2.1 %collective-permute-start.1 = (f32[2,2,2,2,8,1152]{5,4,3,2,1,0:T(8,128)S(1)}, f32[2,2,2,2,8,1152]{5,4,3,2,1,0:T(8,128)S(1)}, u32[]{:S(2)}, u32[]{:S(2)}) collective-permute-start(f32[2,2,2,2,8,1152]{5,4,3,2,1,0:T(8,128)S(1)} %dynamic-slice_bitcast_fusion.1), channel_id=1, source_target_pairs={{0,8},{1,9},{2,10},{3,11},{4,12},{5,13},{6,14},{7,15},{8,0},{9,1},... | collective-permute-start | bytes 1769480 | tf_op jit(solution)/shard_map/ppermute | solution.py:195
  114.8 9.1 %collective-permute-start.2 = (f32[2,2,2,8,1152]{4,3,2,1,0:T(8,128)S(1)}, f32[2,2,2,8,1152]{4,3,2,1,0:T(8,128)S(1)}, u32[]{:S(2)}, u32[]{:S(2)}) collective-permute-start(f32[2,2,2,8,1152]{4,3,2,1,0:T(8,128)S(1)} %dynamic-slice_bitcast_fusion.3), channel_id=1, source_target_pairs={{0,16},{1,17},{2,18},{3,19},{4,20},{5,21},{6,22},{7,23},{8,24},{9,... | collective-permute-start | bytes 884744 | tf_op jit(solution)/shard_map/ppermute | solution.py:195
  124.0 5.4 %collective-permute-start.3 = (f32[2,2,8,1152]{3,2,1,0:T(8,128)S(1)}, f32[2,2,8,1152]{3,2,1,0:T(8,128)S(1)}, u32[]{:S(2)}, u32[]{:S(2)}) collective-permute-start(f32[2,2,8,1152]{3,2,1,0:T(8,128)S(1)} %dynamic-slice_bitcast_fusion.5), channel_id=1, source_target_pairs={{0,1},{1,0},{2,3},{3,2},{4,5},{5,4},{6,7},{7,6},{8,9},{9,8},{10,11... | collective-permute-start | bytes 442376 | tf_op jit(solution)/shard_map/ppermute | solution.py:195
  129.4 4.4 %collective-permute-start.4 = (f32[2,8,1152]{2,1,0:T(8,128)S(1)}, f32[2,8,1152]{2,1,0:T(8,128)S(1)}, u32[]{:S(2)}, u32[]{:S(2)}) collective-permute-start(f32[2,8,1152]{2,1,0:T(8,128)S(1)} %dynamic-slice_bitcast_fusion.7), channel_id=1, source_target_pairs={{0,2},{1,3},{2,0},{3,1},{4,6},{5,7},{6,4},{7,5},{8,10},{9,11},{10,... | collective-permute-start | bytes 221192 | tf_op jit(solution)/shard_map/ppermute | solution.py:195
  133.9 10.1 %collective-permute-start.5 = (f32[8,1152]{1,0:T(8,128)S(1)}, f32[8,1152]{1,0:T(8,128)S(1)}, u32[]{:S(2)}, u32[]{:S(2)}) collective-permute-start(f32[8,1152]{1,0:T(8,128)S(1)} %dynamic-slice_bitcast_fusion.9), channel_id=1, source_target_pairs={{0,4},{1,5},{2,6},{3,7},{4,0},{5,1},{6,2},{7,3},{8,12},{9,13},{10,... | collective-permute-start | bytes 110600 | tf_op jit(solution)/shard_map/ppermute | solution.py:195
  161.8 29.0 %copy-start.1 = (bf16[3,3,128,256]{3,2,1,0:T(8,128)(2,1)S(1)}, bf16[3,3,128,256]{3,2,1,0:T(8,128)(2,1)}, u32[]{:S(2)}) copy-start(bf16[3,3,128,256]{3,2,1,0:T(8,128)(2,1)} %param.6) | copy-start | bytes 1769476
  163.0 2.1 %collective-permute-start.6 = (f32[2,2,2,2,8,1152]{5,4,3,2,1,0:T(8,128)S(1)}, f32[2,2,2,2,8,1152]{5,4,3,2,1,0:T(8,128)S(1)}, u32[]{:S(2)}, u32[]{:S(2)}) collective-permute-start(f32[2,2,2,2,8,1152]{5,4,3,2,1,0:T(8,128)S(1)} %dynamic-slice_bitcast_fusion), channel_id=1, source_target_pairs={{0,8},{1,9},{2,10},{3,11},{4,12},{5,13},{6,14},{7,15},{8,0},{9,1},... | collective-permute-start | bytes 1769480 | tf_op jit(solution)/shard_map/ppermute | solution.py:195
  166.2 9.2 %collective-permute-start.7 = (f32[2,2,2,8,1152]{4,3,2,1,0:T(8,128)S(1)}, f32[2,2,2,8,1152]{4,3,2,1,0:T(8,128)S(1)}, u32[]{:S(2)}, u32[]{:S(2)}) collective-permute-start(f32[2,2,2,8,1152]{4,3,2,1,0:T(8,128)S(1)} %dynamic-slice_bitcast_fusion.2), channel_id=1, source_target_pairs={{0,1},{1,0},{2,3},{3,2},{4,5},{5,4},{6,7},{7,6},{8,9},{9,8},{10,11... | collective-permute-start | bytes 884744 | tf_op jit(solution)/shard_map/ppermute | solution.py:195
  175.5 5.2 %collective-permute-start.8 = (f32[2,2,8,1152]{3,2,1,0:T(8,128)S(1)}, f32[2,2,8,1152]{3,2,1,0:T(8,128)S(1)}, u32[]{:S(2)}, u32[]{:S(2)}) collective-permute-start(f32[2,2,8,1152]{3,2,1,0:T(8,128)S(1)} %dynamic-slice_bitcast_fusion.4), channel_id=1, source_target_pairs={{0,16},{1,17},{2,18},{3,19},{4,20},{5,21},{6,22},{7,23},{8,24},{9,... | collective-permute-start | bytes 442376 | tf_op jit(solution)/shard_map/ppermute | solution.py:195
  180.7 4.4 %collective-permute-start.9 = (f32[2,8,1152]{2,1,0:T(8,128)S(1)}, f32[2,8,1152]{2,1,0:T(8,128)S(1)}, u32[]{:S(2)}, u32[]{:S(2)}) collective-permute-start(f32[2,8,1152]{2,1,0:T(8,128)S(1)} %dynamic-slice_bitcast_fusion.6), channel_id=1, source_target_pairs={{0,2},{1,3},{2,0},{3,1},{4,6},{5,7},{6,4},{7,5},{8,10},{9,11},{10,... | collective-permute-start | bytes 221192 | tf_op jit(solution)/shard_map/ppermute | solution.py:195
  185.2 4.9 %collective-permute-start.10 = (f32[8,1152]{1,0:T(8,128)S(1)}, f32[8,1152]{1,0:T(8,128)S(1)}, u32[]{:S(2)}, u32[]{:S(2)}) collective-permute-start(f32[8,1152]{1,0:T(8,128)S(1)} %dynamic-slice_bitcast_fusion.8), channel_id=1, source_target_pairs={{0,4},{1,5},{2,6},{3,7},{4,0},{5,1},{6,2},{7,3},{8,12},{9,13},{10,... | collective-permute-start | bytes 110600 | tf_op jit(solution)/shard_map/ppermute | solution.py:195

commit v12 on v9

--- a/solution.py
+++ b/solution.py
@@ -135,7 +135,7 @@
 def second_stage(hidden, weight, grad, prev, out_dtype):
     owned, out_rows, out_cols, inputs = hidden.shape
     outputs = weight.shape[-1]
-    rows = min(16, out_rows)
+    rows = min(32, out_rows)
     row_padded = jnp.pad(hidden, ((0, 0), (1, 1), (0, 0), (0, 0)))
     shifted = [shift_cols_right(row_padded), row_padded, shift_cols_left(row_padded)]
     full = pl.BlockSpec((None, out_rows + 2, out_cols, inputs), lambda n, i: (n, 0, 0, 0))

time: 184 us -> 183 us (level)
  no operation moved by 1% of the time
where the time goes in v12:
time: 183 us
  blocking collectives  54.4 us (30%)
  Pallas kernels  45.3 us (25%)
  waiting for transfers between devices  40.9 us (22%)
  local copies, waits for them, and re-layouts  21.9 us (12%)
  starting transfers between devices  17.8 us (10%)
    all_to_all x1, blocking collectives, local(): lax.all_to_all(local_hidden.reshape(tiles, owned, half_rows, width // 2,...  54.4 us
    pallas_call x2, Pallas kernels, second_stage(): pl.pallas_call(functools.partial(second_kernel, rows=rows, carry=prev is...  34.1 us
    all_to_all x1, waiting for transfers between devices, local(): lax.all_to_all(local_hidden.reshape(tiles, owned, half_rows, width // 2,...  20.8 us
    ppermute x10, waiting for transfers between devices, halving_reduce_scatter(): buf = keep + lax.ppermute(send, axes, pairs)  16.7 us
    pallas_call x1, Pallas kernels, first_stage(): pl.pallas_call(first_kernel, grid=(images,), in_specs=[pl.BlockSpec((None...  11.1 us
    ppermute x10, starting transfers between devices, halving_reduce_scatter(): buf = keep + lax.ppermute(send, axes, pairs)  9.35 us
    concatenate x2, local copies, waits for them, and re-layouts, shift_cols_right(): return jnp.concatenate([zero_col, slab[:, :, :-1]], axis=2)  5.06 us
    ppermute x1, starting transfers between devices, shifted_2(): return lax.ppermute(shard, axis, pairs)  4.86 us
  transfers between devices with their start and end apart: 12, of which 10 were waited for; matrix products, arithmetic and copies ran while one was open for 10% of the time, Pallas kernels for 19%

profile of v12, /device:TPU:0, one launch (start us, length us, event | category | flops | bytes accessed | tf_op | source)
XLA Modules:
  0.0 182.7 jit_solution(1221202251674318728)
XLA Ops:
  0.6 0.0 copy-start
  0.6 1.0 slice.21
  1.7 4.9 %collective-permute-start = (bf16[8,1,128,128]{3,2,1,0:T(8,128)(2,1)S(1)}, bf16[8,1,128,128]{3,2,1,0:T(8,128)(2,1)S(1)}, u32[]{:S(2)}, u32[]{:S(2)}) collective-permute-start(bf16[8,1,128,128]{3,2,1,0:T(8,128)(2,1)S(1)} %slice.21), channel_id=1, source_target_pairs={{0,1},{1,2},{2,3},{3,4},{4,5},{5,6},{6,7},{8,9},{9,10},{10,11},{11... | collective-permute-start | bytes 786440 | tf_op jit(solution)/shard_map/ppermute | solution.py:14
  6.6 0.7 pad_clamp_fusion
  7.2 0.6 gather_fusion
  7.8 0.9 copy.8
  8.7 3.4 %collective-permute-done.up_ref = bf16[8,1,128,128]{3,2,1,0:T(8,128)(2,1)S(1)} collective-permute-done((bf16[8,1,128,128]{3,2,1,0:T(8,128)(2,1)S(1)}, bf16[8,1,128,128]{3,2,1,0:T(8,128)(2,1)S(1)}, u32[]{:S(2)}, u32[]{:S(2)}) %collective-permute-start) | collective-permute-done | bytes 262176 | tf_op jit(solution)/shard_map/ppermute | solution.py:14
  12.1 0.7 copy-done.6
  12.8 11.1 %shard_map.68 = (bf16[8,16,64,128]{3,2,1,0:T(8,128)(2,1)}, bf16[8,16,64,128]{3,2,1,0:T(8,128)(2,1)}) custom-call(bf16[8,32,128,128]{3,2,1,0:T(8,128)(2,1)} %x_ref.1, bf16[8,1,128,128]{3,2,1,0:T(8,128)(2,1)} %copy-done.6, bf16[1152,256]{1,0:T(8,128)(2,1)} %bitcast.69), custom_call_target="tpu_custom_call" | custom-call | flops 4831838208 | bytes 12582912 | tf_op jit(solution)/shard_map/pallas_call | solution.py:76
  23.9 54.4 %all_to_all.21 = bf16[8,1,16,64,128]{4,3,2,1,0:T(8,128)(2,1)} all-to-all(bf16[8,1,16,64,128]{4,3,2,1,0:T(8,128)(2,1)} %bitcast.64), channel_id=1, replica_groups=mesh['group'=4,'tile'=8] {'tile'}, dimensions={0} | all-to-all | bytes 4194304 | tf_op jit(solution)/shard_map/all_to_all | solution.py:216
  78.3 3.6 %all-to-all-start = ((bf16[8,1,16,64,128]{4,3,2,1,0:T(8,128)(2,1)}), bf16[8,1,16,64,128]{4,3,2,1,0:T(8,128)(2,1)S(1)}, u32[]{:S(2)}, u32[]{:S(2)}) async-start(bf16[8,1,16,64,128]{4,3,2,1,0:T(8,128)(2,1)} %bitcast.63), calls=%async_computation | async-start | bytes 4194304 | tf_op jit(solution)/shard_map/all_to_all | solution.py:216
  81.9 2.5 %fusion = (bf16[3,3,128,256]{3,2,1,0:T(8,128)(2,1)}, bf16[3,3,128,256]{3,2,1,0:T(8,128)(2,1)}) fusion(bf16[3,3,256,256]{3,2,1,0:T(8,128)(2,1)} %param.7), kind=kLoop, calls=%fused_computation.27 | loop fusion | bytes 2359296 | tf_op jit(solution)/shard_map/slice | solution.py:228
  84.4 1.8 pad.11.refs_1_
  86.3 1.3 pad_slice_fusion.2
  87.6 1.8 concatenate.21.refs_2_
  89.4 2.5 %concatenate.20.refs_0_ = bf16[1,130,64,128]{3,2,1,0:T(8,128)(2,1)} pad(bf16[1,130,63,128]{3,2,1,0:T(8,128)(2,1)S(1)} %get-tuple-element.21, bf16[]{:T(256)} %constant.80.clone.1), padding=0_0x0_0x1_0x0_0 | pad | bytes 4226562 | tf_op jit(solution)/shard_map/concatenate | solution.py:19
  91.8 16.9 %shard_map.69 = (f32[1,128,64,256]{3,2,1,0:T(8,128)}, f32[1,256,1152]{2,1,0:T(8,128)}) custom-call(bf16[1,130,64,128]{3,2,1,0:T(8,128)(2,1)} %concatenate.20.refs_0_, bf16[1,130,64,128]{3,2,1,0:T(8,128)(2,1)} %pad.11.refs_1_, bf16[1,130,64,128]{3,2,1,0:T(8,128)(2,1)} %concatenate.21.refs_2_, bf16[1152,256]{1,0:T(8,128)(2,1)} %bitcast.71, ...), custom_call_target="tpu_custom_call" | custom-call | flops 9663676416 | bytes 26345472 | tf_op jit(solution)/shard_map/pallas_call | solution.py:155
  108.8 20.8 %all-to-all-done = bf16[8,1,16,64,128]{4,3,2,1,0:T(8,128)(2,1)S(1)} async-done(((bf16[8,1,16,64,128]{4,3,2,1,0:T(8,128)(2,1)}), bf16[8,1,16,64,128]{4,3,2,1,0:T(8,128)(2,1)S(1)}, u32[]{:S(2)}, u32[]{:S(2)}) %all-to-all-start) | async-done | bytes 2097184 | tf_op jit(solution)/shard_map/all_to_all | solution.py:216
  129.5 1.8 pad.12.refs_1_
  131.3 1.2 pad_slice_fusion
  132.5 0.0 copy-done.3
  132.6 0.1 collective-permute-start.1
  132.7 1.8 concatenate.23.refs_2_
  134.5 2.6 %concatenate.22.refs_0_ = bf16[1,130,64,128]{3,2,1,0:T(8,128)(2,1)} pad(bf16[1,130,63,128]{3,2,1,0:T(8,128)(2,1)S(1)} %get-tuple-element.19, bf16[]{:T(256)} %constant.80.clone.1), padding=0_0x0_0x1_0x0_0 | pad | bytes 4226562 | tf_op jit(solution)/shard_map/concatenate | solution.py:19
  137.0 17.2 %shard_map.70 = (bf16[1,128,64,256]{3,2,1,0:T(8,128)(2,1)}, f32[1,256,1152]{2,1,0:T(8,128)}) custom-call(bf16[1,130,64,128]{3,2,1,0:T(8,128)(2,1)} %concatenate.22.refs_0_, bf16[1,130,64,128]{3,2,1,0:T(8,128)(2,1)} %pad.12.refs_1_, bf16[1,130,64,128]{3,2,1,0:T(8,128)(2,1)} %concatenate.23.refs_2_, bf16[1152,256]{1,0:T(8,128)(2,1)} %bitcast.70, ...), custom_call_target="tpu_custom_call" | custom-call | flops 9663676416 | bytes 26345472 | tf_op jit(solution)/shard_map/pallas_call | solution.py:155
  154.3 1.2 dynamic-slice_bitcast_fusion
  155.5 0.6 collective-permute-start.6
  156.0 0.0 collective-permute-done.1
  156.1 0.1 bitcast_add_fusion.1
  156.2 1.6 collective-permute-start.2
  157.7 0.1 bitcast_add_fusion
  157.8 0.0 copy-start.1
  157.9 1.5 collective-permute-start.7
  159.4 5.8 %collective-permute-done.2 = f32[2,2,2,8,1152]{4,3,2,1,0:T(8,128)S(1)} collective-permute-done((f32[2,2,2,8,1152]{4,3,2,1,0:T(8,128)S(1)}, f32[2,2,2,8,1152]{4,3,2,1,0:T(8,128)S(1)}, u32[]{:S(2)}, u32[]{:S(2)}) %collective-permute-start.2) | collective-permute-done | bytes 294944 | tf_op jit(solution)/shard_map/ppermute | solution.py:195
  165.2 1.5 collective-permute-start.3
  166.8 0.4 collective-permute-done.7
  167.2 1.6 collective-permute-start.8
  168.8 1.6 collective-permute-done.3
  170.5 0.1 collective-permute-start.4
  170.6 2.0 %collective-permute-done.8 = f32[2,2,8,1152]{3,2,1,0:T(8,128)S(1)} collective-permute-done((f32[2,2,8,1152]{3,2,1,0:T(8,128)S(1)}, f32[2,2,8,1152]{3,2,1,0:T(8,128)S(1)}, u32[]{:S(2)}, u32[]{:S(2)}) %collective-permute-start.8) | collective-permute-done | bytes 147488 | tf_op jit(solution)/shard_map/ppermute | solution.py:195
  172.6 0.1 collective-permute-start.9
  172.7 2.7 %collective-permute-done.4 = f32[2,8,1152]{2,1,0:T(8,128)S(1)} collective-permute-done((f32[2,8,1152]{2,1,0:T(8,128)S(1)}, f32[2,8,1152]{2,1,0:T(8,128)S(1)}, u32[]{:S(2)}, u32[]{:S(2)}) %collective-permute-start.4) | collective-permute-done | bytes 73760 | tf_op jit(solution)/shard_map/ppermute | solution.py:195
  175.4 0.9 collective-permute-start.5
  176.3 0.7 collective-permute-done.9
  177.1 1.4 collective-permute-start.10
  178.5 1.9 %collective-permute-done.5 = f32[8,1152]{1,0:T(8,128)S(1)} collective-permute-done((f32[8,1152]{1,0:T(8,128)S(1)}, f32[8,1152]{1,0:T(8,128)S(1)}, u32[]{:S(2)}, u32[]{:S(2)}) %collective-permute-start.5) | collective-permute-done | bytes 36896 | tf_op jit(solution)/shard_map/ppermute | solution.py:195
  180.5 1.5 collective-permute-done.10
  182.0 0.6 pad_maximum_fusion
  (28 shorter events, 0.4 us)
Async XLA Ops:
  0.6 6.6 %copy-start = (bf16[3,3,128,256]{3,2,1,0:T(8,128)(2,1)S(1)}, bf16[3,3,128,256]{3,2,1,0:T(8,128)(2,1)}, u32[]{:S(2)}) copy-start(bf16[3,3,128,256]{3,2,1,0:T(8,128)(2,1)} %param.6) | copy-start | bytes 1769476
  1.7 10.4 %collective-permute-start = (bf16[8,1,128,128]{3,2,1,0:T(8,128)(2,1)S(1)}, bf16[8,1,128,128]{3,2,1,0:T(8,128)(2,1)S(1)}, u32[]{:S(2)}, u32[]{:S(2)}) collective-permute-start(bf16[8,1,128,128]{3,2,1,0:T(8,128)(2,1)S(1)} %slice.21), channel_id=1, source_target_pairs={{0,1},{1,2},{2,3},{3,4},{4,5},{5,6},{6,7},{8,9},{9,10},{10,11},{11... | collective-permute-start | bytes 786440 | tf_op jit(solution)/shard_map/ppermute | solution.py:14
  12.1 0.7 copy-start.6
  78.3 51.3 %all-to-all-start = ((bf16[8,1,16,64,128]{4,3,2,1,0:T(8,128)(2,1)}), bf16[8,1,16,64,128]{4,3,2,1,0:T(8,128)(2,1)S(1)}, u32[]{:S(2)}, u32[]{:S(2)}) async-start(bf16[8,1,16,64,128]{4,3,2,1,0:T(8,128)(2,1)} %bitcast.63), calls=%async_computation | async-start | bytes 4194304 | tf_op jit(solution)/shard_map/all_to_all | solution.py:216
  81.9 2.5 %copy-start.2 = (bf16[8,1,16,64,128]{4,3,2,1,0:T(8,128)(2,1)S(1)}, bf16[8,1,16,64,128]{4,3,2,1,0:T(8,128)(2,1)}, u32[]{:S(2)}) copy-start(bf16[8,1,16,64,128]{4,3,2,1,0:T(8,128)(2,1)} %all_to_all.21) | copy-start | bytes 6291460
  131.3 1.3 copy-start.3
  132.6 23.4 %collective-permute-start.1 = (f32[2,2,2,2,8,1152]{5,4,3,2,1,0:T(8,128)S(1)}, f32[2,2,2,2,8,1152]{5,4,3,2,1,0:T(8,128)S(1)}, u32[]{:S(2)}, u32[]{:S(2)}) collective-permute-start(f32[2,2,2,2,8,1152]{5,4,3,2,1,0:T(8,128)S(1)} %dynamic-slice_bitcast_fusion.1), channel_id=1, source_target_pairs={{0,8},{1,9},{2,10},{3,11},{4,12},{5,13},{6,14},{7,15},{8,0},{9,1},... | collective-permute-start | bytes 1769480 | tf_op jit(solution)/shard_map/ppermute | solution.py:195
  137.0 19.0 %copy-start.4 = (f32[1,256,1152]{2,1,0:T(8,128)S(1)}, f32[1,256,1152]{2,1,0:T(8,128)}, u32[]{:S(2)}) copy-start(f32[1,256,1152]{2,1,0:T(8,128)} %get-tuple-element.16) | copy-start | bytes 3538948
  154.3 3.5 %copy-start.5 = (f32[1,256,1152]{2,1,0:T(8,128)S(1)}, f32[1,256,1152]{2,1,0:T(8,128)}, u32[]{:S(2)}) copy-start(f32[1,256,1152]{2,1,0:T(8,128)} %get-tuple-element.17) | copy-start | bytes 3538948
  155.5 2.3 %collective-permute-start.6 = (f32[2,2,2,2,8,1152]{5,4,3,2,1,0:T(8,128)S(1)}, f32[2,2,2,2,8,1152]{5,4,3,2,1,0:T(8,128)S(1)}, u32[]{:S(2)}, u32[]{:S(2)}) collective-permute-start(f32[2,2,2,2,8,1152]{5,4,3,2,1,0:T(8,128)S(1)} %dynamic-slice_bitcast_fusion), channel_id=1, source_target_pairs={{0,8},{1,9},{2,10},{3,11},{4,12},{5,13},{6,14},{7,15},{8,0},{9,1},... | collective-permute-start | bytes 1769480 | tf_op jit(solution)/shard_map/ppermute | solution.py:195
  156.2 9.0 %collective-permute-start.2 = (f32[2,2,2,8,1152]{4,3,2,1,0:T(8,128)S(1)}, f32[2,2,2,8,1152]{4,3,2,1,0:T(8,128)S(1)}, u32[]{:S(2)}, u32[]{:S(2)}) collective-permute-start(f32[2,2,2,8,1152]{4,3,2,1,0:T(8,128)S(1)} %dynamic-slice_bitcast_fusion.3), channel_id=1, source_target_pairs={{0,16},{1,17},{2,18},{3,19},{4,20},{5,21},{6,22},{7,23},{8,24},{9,... | collective-permute-start | bytes 884744 | tf_op jit(solution)/shard_map/ppermute | solution.py:195
  157.8 24.8 %copy-start.1 = (bf16[3,3,128,256]{3,2,1,0:T(8,128)(2,1)S(1)}, bf16[3,3,128,256]{3,2,1,0:T(8,128)(2,1)}, u32[]{:S(2)}) copy-start(bf16[3,3,128,256]{3,2,1,0:T(8,128)(2,1)} %param.6) | copy-start | bytes 1769476
  157.9 9.3 %collective-permute-start.7 = (f32[2,2,2,8,1152]{4,3,2,1,0:T(8,128)S(1)}, f32[2,2,2,8,1152]{4,3,2,1,0:T(8,128)S(1)}, u32[]{:S(2)}, u32[]{:S(2)}) collective-permute-start(f32[2,2,2,8,1152]{4,3,2,1,0:T(8,128)S(1)} %dynamic-slice_bitcast_fusion.2), channel_id=1, source_target_pairs={{0,1},{1,0},{2,3},{3,2},{4,5},{5,4},{6,7},{7,6},{8,9},{9,8},{10,11... | collective-permute-start | bytes 884744 | tf_op jit(solution)/shard_map/ppermute | solution.py:195
  165.2 5.2 %collective-permute-start.3 = (f32[2,2,8,1152]{3,2,1,0:T(8,128)S(1)}, f32[2,2,8,1152]{3,2,1,0:T(8,128)S(1)}, u32[]{:S(2)}, u32[]{:S(2)}) collective-permute-start(f32[2,2,8,1152]{3,2,1,0:T(8,128)S(1)} %dynamic-slice_bitcast_fusion.5), channel_id=1, source_target_pairs={{0,1},{1,0},{2,3},{3,2},{4,5},{5,4},{6,7},{7,6},{8,9},{9,8},{10,11... | collective-permute-start | bytes 442376 | tf_op jit(solution)/shard_map/ppermute | solution.py:195
  167.2 5.3 %collective-permute-start.8 = (f32[2,2,8,1152]{3,2,1,0:T(8,128)S(1)}, f32[2,2,8,1152]{3,2,1,0:T(8,128)S(1)}, u32[]{:S(2)}, u32[]{:S(2)}) collective-permute-start(f32[2,2,8,1152]{3,2,1,0:T(8,128)S(1)} %dynamic-slice_bitcast_fusion.4), channel_id=1, source_target_pairs={{0,16},{1,17},{2,18},{3,19},{4,20},{5,21},{6,22},{7,23},{8,24},{9,... | collective-permute-start | bytes 442376 | tf_op jit(solution)/shard_map/ppermute | solution.py:195
  170.5 4.9 %collective-permute-start.4 = (f32[2,8,1152]{2,1,0:T(8,128)S(1)}, f32[2,8,1152]{2,1,0:T(8,128)S(1)}, u32[]{:S(2)}, u32[]{:S(2)}) collective-permute-start(f32[2,8,1152]{2,1,0:T(8,128)S(1)} %dynamic-slice_bitcast_fusion.7), channel_id=1, source_target_pairs={{0,2},{1,3},{2,0},{3,1},{4,6},{5,7},{6,4},{7,5},{8,10},{9,11},{10,... | collective-permute-start | bytes 221192 | tf_op jit(solution)/shard_map/ppermute | solution.py:195
  172.6 4.5 %collective-permute-start.9 = (f32[2,8,1152]{2,1,0:T(8,128)S(1)}, f32[2,8,1152]{2,1,0:T(8,128)S(1)}, u32[]{:S(2)}, u32[]{:S(2)}) collective-permute-start(f32[2,8,1152]{2,1,0:T(8,128)S(1)} %dynamic-slice_bitcast_fusion.6), channel_id=1, source_target_pairs={{0,2},{1,3},{2,0},{3,1},{4,6},{5,7},{6,4},{7,5},{8,10},{9,11},{10,... | collective-permute-start | bytes 221192 | tf_op jit(solution)/shard_map/ppermute | solution.py:195
  175.4 5.0 %collective-permute-start.5 = (f32[8,1152]{1,0:T(8,128)S(1)}, f32[8,1152]{1,0:T(8,128)S(1)}, u32[]{:S(2)}, u32[]{:S(2)}) collective-permute-start(f32[8,1152]{1,0:T(8,128)S(1)} %dynamic-slice_bitcast_fusion.9), channel_id=1, source_target_pairs={{0,4},{1,5},{2,6},{3,7},{4,0},{5,1},{6,2},{7,3},{8,12},{9,13},{10,... | collective-permute-start | bytes 110600 | tf_op jit(solution)/shard_map/ppermute | solution.py:195
  177.1 4.9 %collective-permute-start.10 = (f32[8,1152]{1,0:T(8,128)S(1)}, f32[8,1152]{1,0:T(8,128)S(1)}, u32[]{:S(2)}, u32[]{:S(2)}) collective-permute-start(f32[8,1152]{1,0:T(8,128)S(1)} %dynamic-slice_bitcast_fusion.8), channel_id=1, source_target_pairs={{0,4},{1,5},{2,6},{3,7},{4,0},{5,1},{6,2},{7,3},{8,12},{9,13},{10,... | collective-permute-start | bytes 110600 | tf_op jit(solution)/shard_map/ppermute | solution.py:195

commit v13 on v12

--- a/solution.py
+++ b/solution.py
@@ -97,16 +97,15 @@
 
 def second_kernel(*refs, rows, carry):
     if carry:
-        left_ref, mid_ref, right_ref, weight_ref, grad_ref, prev_ref, out_ref, wgrad_ref, acc_ref = refs
+        src_ref, weight_ref, grad_ref, prev_ref, out_ref, wgrad_ref, acc_ref = refs
     else:
-        left_ref, mid_ref, right_ref, weight_ref, grad_ref, out_ref, wgrad_ref, acc_ref = refs
+        src_ref, weight_ref, grad_ref, out_ref, wgrad_ref, acc_ref = refs
     step = pl.program_id(1)
     _, width, outputs = out_ref.shape
-    inputs = mid_ref.shape[-1]
-    sources = (left_ref, mid_ref, right_ref)
+    inputs = src_ref.shape[-1]
     patches = jnp.concatenate(
         [
-            sources[tap % 3][pl.ds(step * rows + tap // 3, rows)].reshape(rows * width, inputs)
+            src_ref[tap % 3, pl.ds(step * rows + tap // 3, rows)].reshape(rows * width, inputs)
             for tap in range(9)
         ],
         axis=-1,
@@ -137,17 +136,15 @@
     outputs = weight.shape[-1]
     rows = min(32, out_rows)
     row_padded = jnp.pad(hidden, ((0, 0), (1, 1), (0, 0), (0, 0)))
-    shifted = [shift_cols_right(row_padded), row_padded, shift_cols_left(row_padded)]
-    full = pl.BlockSpec((None, out_rows + 2, out_cols, inputs), lambda n, i: (n, 0, 0, 0))
+    shifted = jnp.stack([shift_cols_right(row_padded), row_padded, shift_cols_left(row_padded)], axis=1)
+    full = pl.BlockSpec((None, 3, out_rows + 2, out_cols, inputs), lambda n, i: (n, 0, 0, 0, 0))
     block = pl.BlockSpec((None, rows, out_cols, outputs), lambda n, i: (n, i, 0, 0))
     in_specs = [
-        full,
-        full,
         full,
         pl.BlockSpec((9 * inputs, outputs), lambda n, i: (0, 0)),
         pl.BlockSpec((None, rows * out_cols, outputs), lambda n, i: (n, i, 0)),
     ]
-    operands = [*shifted, weight.reshape(9 * inputs, outputs), grad]
+    operands = [shifted, weight.reshape(9 * inputs, outputs), grad]
     if prev is not None:
         in_specs.append(block)
         operands.append(prev)

time: 183 us -> 183 us (level)
  local copies, waits for them, and re-layouts: 21.9 us -> 14.3 us
  other arithmetic: 1.57 us -> 8.11 us
    concatenate x4 -> x0, local copies, waits for them, and re-layouts: 8.62 us -> none  [the longest x2 5.06 us: shift_cols_right(): return jnp.concatenate([zero_col, slab[:, :, :-1]], axis=2)]
    another operation x0 -> x2, other arithmetic: none -> 6.54 us  [second_stage(): jnp.stack([shift_cols_right(row_padded), row_padded, shift_cols_left(row_...]
    another operation x0 -> x5, local copies, waits for them, and re-layouts: none -> 4.33 us  [second_stage(): jnp.stack([shift_cols_right(row_padded), row_padded, shift_cols_left(row_...]
    pad x2 -> x0, local copies, waits for them, and re-layouts: 3.6 us -> none  [second_stage(): row_padded = jnp.pad(hidden, ((0, 0), (1, 1), (0, 0), (0, 0)))]
where the time goes in v13:
time: 183 us; the launch traced here: 182 us
  blocking collectives  54.4 us (30%)
  Pallas kernels  45.1 us (25%)
  waiting for transfers between devices  41.5 us (23%)
  starting transfers between devices  17.8 us (10%)
  local copies, waits for them, and re-layouts  14.3 us (8%)
  other arithmetic  8.11 us (4%)
    all_to_all x1, blocking collectives, local(): lax.all_to_all(local_hidden.reshape(tiles, owned, half_rows, width // 2,...  54.4 us
    pallas_call x2, Pallas kernels, second_stage(): pl.pallas_call(functools.partial(second_kernel, rows=rows, carry=prev is...  34 us
    all_to_all x1, waiting for transfers between devices, local(): lax.all_to_all(local_hidden.reshape(tiles, owned, half_rows, width // 2,...  21.4 us
    ppermute x10, waiting for transfers between devices, halving_reduce_scatter(): buf = keep + lax.ppermute(send, axes, pairs)  16.7 us
    pallas_call x1, Pallas kernels, first_stage(): pl.pallas_call(first_kernel, grid=(images,), in_specs=[pl.BlockSpec((None...  11.1 us
    ppermute x10, starting transfers between devices, halving_reduce_scatter(): buf = keep + lax.ppermute(send, axes, pairs)  9.35 us
    another operation x2, other arithmetic, second_stage(): jnp.stack([shift_cols_right(row_padded), row_padded, shift_cols_left(row_...  6.54 us
    ppermute x1, starting transfers between devices, shifted_2(): return lax.ppermute(shard, axis, pairs)  4.86 us
  transfers between devices with their start and end apart: 12, of which 10 were waited for; matrix products, arithmetic and copies ran while one was open for 10% of the time, Pallas kernels for 19%

profile of v13, /device:TPU:0, one launch (start us, length us, event | category | flops | bytes accessed | tf_op | source)
XLA Modules:
  0.0 182.1 jit_solution(16184992740233456704)
XLA Ops:
  0.6 0.0 copy-start
  0.6 1.0 slice.21
  1.7 4.9 %collective-permute-start = (bf16[8,1,128,128]{3,2,1,0:T(8,128)(2,1)S(1)}, bf16[8,1,128,128]{3,2,1,0:T(8,128)(2,1)S(1)}, u32[]{:S(2)}, u32[]{:S(2)}) collective-permute-start(bf16[8,1,128,128]{3,2,1,0:T(8,128)(2,1)S(1)} %slice.21), channel_id=1, source_target_pairs={{0,1},{1,2},{2,3},{3,4},{4,5},{5,6},{6,7},{8,9},{9,10},{10,11},{11... | collective-permute-start | bytes 786440 | tf_op jit(solution)/shard_map/ppermute | solution.py:14
  6.6 0.7 pad_clamp_fusion
  7.2 0.6 gather_fusion
  7.8 0.9 copy.8
  8.7 3.4 %collective-permute-done.up_ref = bf16[8,1,128,128]{3,2,1,0:T(8,128)(2,1)S(1)} collective-permute-done((bf16[8,1,128,128]{3,2,1,0:T(8,128)(2,1)S(1)}, bf16[8,1,128,128]{3,2,1,0:T(8,128)(2,1)S(1)}, u32[]{:S(2)}, u32[]{:S(2)}) %collective-permute-start) | collective-permute-done | bytes 262176 | tf_op jit(solution)/shard_map/ppermute | solution.py:14
  12.1 0.7 copy-done.6
  12.8 11.1 %shard_map.68 = (bf16[8,16,64,128]{3,2,1,0:T(8,128)(2,1)}, bf16[8,16,64,128]{3,2,1,0:T(8,128)(2,1)}) custom-call(bf16[8,32,128,128]{3,2,1,0:T(8,128)(2,1)} %x_ref.1, bf16[8,1,128,128]{3,2,1,0:T(8,128)(2,1)} %copy-done.6, bf16[1152,256]{1,0:T(8,128)(2,1)} %bitcast.81), custom_call_target="tpu_custom_call" | custom-call | flops 4831838208 | bytes 12582912 | tf_op jit(solution)/shard_map/pallas_call | solution.py:76
  23.9 54.4 %all_to_all.21 = bf16[8,1,16,64,128]{4,3,2,1,0:T(8,128)(2,1)} all-to-all(bf16[8,1,16,64,128]{4,3,2,1,0:T(8,128)(2,1)} %bitcast.76), channel_id=1, replica_groups=mesh['group'=4,'tile'=8] {'tile'}, dimensions={0} | all-to-all | bytes 4194304 | tf_op jit(solution)/shard_map/all_to_all | solution.py:213
  78.3 3.6 %all-to-all-start = ((bf16[8,1,16,64,128]{4,3,2,1,0:T(8,128)(2,1)}), bf16[8,1,16,64,128]{4,3,2,1,0:T(8,128)(2,1)S(1)}, u32[]{:S(2)}, u32[]{:S(2)}) async-start(bf16[8,1,16,64,128]{4,3,2,1,0:T(8,128)(2,1)} %bitcast.75), calls=%async_computation | async-start | bytes 4194304 | tf_op jit(solution)/shard_map/all_to_all | solution.py:213
  81.9 2.5 %fusion = (bf16[3,3,128,256]{3,2,1,0:T(8,128)(2,1)}, bf16[3,3,128,256]{3,2,1,0:T(8,128)(2,1)}) fusion(bf16[3,3,256,256]{3,2,1,0:T(8,128)(2,1)} %param.7), kind=kLoop, calls=%fused_computation.35 | loop fusion | bytes 2359296 | tf_op jit(solution)/shard_map/slice | solution.py:225
  84.4 0.4 pad_bitcast_fusion.5
  84.8 1.4 pad_slice_fusion.3
  86.3 1.8 pad_bitcast_fusion.2
  88.1 3.3 %pad_maximum_fusion.refs_0_ = bf16[1,3,130,64,128]{4,3,2,1,0:T(8,128)(2,1)} fusion(bf16[1,1,130,64,128]{4,3,2,1,0:T(8,128)(2,1)S(1)} %get-tuple-element.24, bf16[1,1,130,64,128]{4,3,2,1,0:T(8,128)(2,1)S(1)} %pad_bitcast_fusion.5, bf16[1,1,130,64,128]{4,3,2,1,0:T(8,128)(2,1)S(1)} %get-tuple-element.25), kind=kLoop, calls=%fused_computation.1 | loop fusion | flops 6389760 | bytes 12779520 | tf_op jit(solution)/shard_map/stack | solution.py:139
  91.3 16.8 %shard_map.69 = (f32[1,128,64,256]{3,2,1,0:T(8,128)}, f32[1,256,1152]{2,1,0:T(8,128)}) custom-call(bf16[1,3,130,64,128]{4,3,2,1,0:T(8,128)(2,1)} %pad_maximum_fusion.refs_0_, bf16[1152,256]{1,0:T(8,128)(2,1)} %bitcast.83, bf16[1,8192,256]{2,1,0:T(8,128)(2,1)} %bitcast.86), custom_call_target="tpu_custom_call" | custom-call | flops 9663676416 | bytes 26345472 | tf_op jit(solution)/shard_map/pallas_call | solution.py:152
  108.1 21.4 %all-to-all-done = bf16[8,1,16,64,128]{4,3,2,1,0:T(8,128)(2,1)S(1)} async-done(((bf16[8,1,16,64,128]{4,3,2,1,0:T(8,128)(2,1)}), bf16[8,1,16,64,128]{4,3,2,1,0:T(8,128)(2,1)S(1)}, u32[]{:S(2)}, u32[]{:S(2)}) %all-to-all-start) | async-done | bytes 2097184 | tf_op jit(solution)/shard_map/all_to_all | solution.py:213
  129.5 0.4 pad_bitcast_fusion.4
  130.0 1.4 pad_slice_fusion.1
  131.4 0.1 collective-permute-start.1
  131.5 1.3 pad_bitcast_fusion.1
  132.8 0.4 pad_bitcast_fusion
  133.2 3.3 %pad_maximum_fusion.1.refs_0_ = bf16[1,3,130,64,128]{4,3,2,1,0:T(8,128)(2,1)} fusion(bf16[1,1,130,64,128]{4,3,2,1,0:T(8,128)(2,1)S(1)} %pad_bitcast_fusion, bf16[1,1,130,64,128]{4,3,2,1,0:T(8,128)(2,1)S(1)} %pad_bitcast_fusion.4, bf16[1,1,130,64,128]{4,3,2,1,0:T(8,128)(2,1)S(1)} %pad_bitcast_fusion.1), kind=kLoop, calls=%fused_computation.2 | loop fusion | flops 6389760 | bytes 12779520 | tf_op jit(solution)/shard_map/stack | solution.py:139
  136.5 17.2 %shard_map.70 = (bf16[1,128,64,256]{3,2,1,0:T(8,128)(2,1)}, f32[1,256,1152]{2,1,0:T(8,128)}) custom-call(bf16[1,3,130,64,128]{4,3,2,1,0:T(8,128)(2,1)} %pad_maximum_fusion.1.refs_0_, bf16[1152,256]{1,0:T(8,128)(2,1)} %bitcast.82, bf16[1,8192,256]{2,1,0:T(8,128)(2,1)} %bitcast.87, f32[1,128,64,256]{3,2,1,0:T(8,128)} %get-tuple-element.14.refs_3_), custom_call_target="tpu_custom_call" | custom-call | flops 9663676416 | bytes 26345472 | tf_op jit(solution)/shard_map/pallas_call | solution.py:152
  153.7 1.2 dynamic-slice_bitcast_fusion
  154.9 0.6 collective-permute-start.6
  155.5 0.1 bitcast_add_fusion.1
  155.6 1.6 collective-permute-start.2
  157.2 0.0 collective-permute-done.6
  157.2 0.1 bitcast_add_fusion
  157.2 0.0 copy-start.1
  157.3 1.5 collective-permute-start.7
  158.8 5.8 %collective-permute-done.2 = f32[2,2,2,8,1152]{4,3,2,1,0:T(8,128)S(1)} collective-permute-done((f32[2,2,2,8,1152]{4,3,2,1,0:T(8,128)S(1)}, f32[2,2,2,8,1152]{4,3,2,1,0:T(8,128)S(1)}, u32[]{:S(2)}, u32[]{:S(2)}) %collective-permute-start.2) | collective-permute-done | bytes 294944 | tf_op jit(solution)/shard_map/ppermute | solution.py:192
  164.7 1.5 collective-permute-start.3
  166.2 0.4 collective-permute-done.7
  166.6 1.6 collective-permute-start.8
  168.2 1.6 collective-permute-done.3
  169.9 0.1 collective-permute-start.4
  170.0 2.0 %collective-permute-done.8 = f32[2,2,8,1152]{3,2,1,0:T(8,128)S(1)} collective-permute-done((f32[2,2,8,1152]{3,2,1,0:T(8,128)S(1)}, f32[2,2,8,1152]{3,2,1,0:T(8,128)S(1)}, u32[]{:S(2)}, u32[]{:S(2)}) %collective-permute-start.8) | collective-permute-done | bytes 147488 | tf_op jit(solution)/shard_map/ppermute | solution.py:192
  172.0 0.1 collective-permute-start.9
  172.1 2.7 %collective-permute-done.4 = f32[2,8,1152]{2,1,0:T(8,128)S(1)} collective-permute-done((f32[2,8,1152]{2,1,0:T(8,128)S(1)}, f32[2,8,1152]{2,1,0:T(8,128)S(1)}, u32[]{:S(2)}, u32[]{:S(2)}) %collective-permute-start.4) | collective-permute-done | bytes 73760 | tf_op jit(solution)/shard_map/ppermute | solution.py:192
  174.9 0.9 collective-permute-start.5
  175.7 0.7 collective-permute-done.9
  176.5 1.4 collective-permute-start.10
  177.9 1.9 %collective-permute-done.5 = f32[8,1152]{1,0:T(8,128)S(1)} collective-permute-done((f32[8,1152]{1,0:T(8,128)S(1)}, f32[8,1152]{1,0:T(8,128)S(1)}, u32[]{:S(2)}, u32[]{:S(2)}) %collective-permute-start.5) | collective-permute-done | bytes 36896 | tf_op jit(solution)/shard_map/ppermute | solution.py:192
  179.9 1.5 collective-permute-done.10
  181.4 0.6 pad_maximum_fusion.2
  (29 shorter events, 0.4 us)
Async XLA Ops:
  0.6 6.6 %copy-start = (bf16[3,3,128,256]{3,2,1,0:T(8,128)(2,1)S(1)}, bf16[3,3,128,256]{3,2,1,0:T(8,128)(2,1)}, u32[]{:S(2)}) copy-start(bf16[3,3,128,256]{3,2,1,0:T(8,128)(2,1)} %param.6) | copy-start | bytes 1769476
  1.7 10.4 %collective-permute-start = (bf16[8,1,128,128]{3,2,1,0:T(8,128)(2,1)S(1)}, bf16[8,1,128,128]{3,2,1,0:T(8,128)(2,1)S(1)}, u32[]{:S(2)}, u32[]{:S(2)}) collective-permute-start(bf16[8,1,128,128]{3,2,1,0:T(8,128)(2,1)S(1)} %slice.21), channel_id=1, source_target_pairs={{0,1},{1,2},{2,3},{3,4},{4,5},{5,6},{6,7},{8,9},{9,10},{10,11},{11... | collective-permute-start | bytes 786440 | tf_op jit(solution)/shard_map/ppermute | solution.py:14
  12.1 0.7 copy-start.6
  78.3 51.3 %all-to-all-start = ((bf16[8,1,16,64,128]{4,3,2,1,0:T(8,128)(2,1)}), bf16[8,1,16,64,128]{4,3,2,1,0:T(8,128)(2,1)S(1)}, u32[]{:S(2)}, u32[]{:S(2)}) async-start(bf16[8,1,16,64,128]{4,3,2,1,0:T(8,128)(2,1)} %bitcast.75), calls=%async_computation | async-start | bytes 4194304 | tf_op jit(solution)/shard_map/all_to_all | solution.py:213
  81.9 2.5 %copy-start.2 = (bf16[8,1,16,64,128]{4,3,2,1,0:T(8,128)(2,1)S(1)}, bf16[8,1,16,64,128]{4,3,2,1,0:T(8,128)(2,1)}, u32[]{:S(2)}) copy-start(bf16[8,1,16,64,128]{4,3,2,1,0:T(8,128)(2,1)} %all_to_all.21) | copy-start | bytes 6291460
  129.9 1.4 copy-start.3
  131.4 24.1 %collective-permute-start.1 = (f32[2,2,2,2,8,1152]{5,4,3,2,1,0:T(8,128)S(1)}, f32[2,2,2,2,8,1152]{5,4,3,2,1,0:T(8,128)S(1)}, u32[]{:S(2)}, u32[]{:S(2)}) collective-permute-start(f32[2,2,2,2,8,1152]{5,4,3,2,1,0:T(8,128)S(1)} %dynamic-slice_bitcast_fusion.1), channel_id=1, source_target_pairs={{0,8},{1,9},{2,10},{3,11},{4,12},{5,13},{6,14},{7,15},{8,0},{9,1},... | collective-permute-start | bytes 1769480 | tf_op jit(solution)/shard_map/ppermute | solution.py:192
  136.5 19.0 %copy-start.4 = (f32[1,256,1152]{2,1,0:T(8,128)S(1)}, f32[1,256,1152]{2,1,0:T(8,128)}, u32[]{:S(2)}) copy-start(f32[1,256,1152]{2,1,0:T(8,128)} %get-tuple-element.16) | copy-start | bytes 3538948
  153.7 3.5 %copy-start.5 = (f32[1,256,1152]{2,1,0:T(8,128)S(1)}, f32[1,256,1152]{2,1,0:T(8,128)}, u32[]{:S(2)}) copy-start(f32[1,256,1152]{2,1,0:T(8,128)} %get-tuple-element.17) | copy-start | bytes 3538948
  154.9 2.3 %collective-permute-start.6 = (f32[2,2,2,2,8,1152]{5,4,3,2,1,0:T(8,128)S(1)}, f32[2,2,2,2,8,1152]{5,4,3,2,1,0:T(8,128)S(1)}, u32[]{:S(2)}, u32[]{:S(2)}) collective-permute-start(f32[2,2,2,2,8,1152]{5,4,3,2,1,0:T(8,128)S(1)} %dynamic-slice_bitcast_fusion), channel_id=1, source_target_pairs={{0,8},{1,9},{2,10},{3,11},{4,12},{5,13},{6,14},{7,15},{8,0},{9,1},... | collective-permute-start | bytes 1769480 | tf_op jit(solution)/shard_map/ppermute | solution.py:192
  155.6 9.0 %collective-permute-start.2 = (f32[2,2,2,8,1152]{4,3,2,1,0:T(8,128)S(1)}, f32[2,2,2,8,1152]{4,3,2,1,0:T(8,128)S(1)}, u32[]{:S(2)}, u32[]{:S(2)}) collective-permute-start(f32[2,2,2,8,1152]{4,3,2,1,0:T(8,128)S(1)} %dynamic-slice_bitcast_fusion.3), channel_id=1, source_target_pairs={{0,16},{1,17},{2,18},{3,19},{4,20},{5,21},{6,22},{7,23},{8,24},{9,... | collective-permute-start | bytes 884744 | tf_op jit(solution)/shard_map/ppermute | solution.py:192
  157.2 24.8 %copy-start.1 = (bf16[3,3,128,256]{3,2,1,0:T(8,128)(2,1)S(1)}, bf16[3,3,128,256]{3,2,1,0:T(8,128)(2,1)}, u32[]{:S(2)}) copy-start(bf16[3,3,128,256]{3,2,1,0:T(8,128)(2,1)} %param.6) | copy-start | bytes 1769476
  157.3 9.3 %collective-permute-start.7 = (f32[2,2,2,8,1152]{4,3,2,1,0:T(8,128)S(1)}, f32[2,2,2,8,1152]{4,3,2,1,0:T(8,128)S(1)}, u32[]{:S(2)}, u32[]{:S(2)}) collective-permute-start(f32[2,2,2,8,1152]{4,3,2,1,0:T(8,128)S(1)} %dynamic-slice_bitcast_fusion.2), channel_id=1, source_target_pairs={{0,1},{1,0},{2,3},{3,2},{4,5},{5,4},{6,7},{7,6},{8,9},{9,8},{10,11... | collective-permute-start | bytes 884744 | tf_op jit(solution)/shard_map/ppermute | solution.py:192
  164.7 5.2 %collective-permute-start.3 = (f32[2,2,8,1152]{3,2,1,0:T(8,128)S(1)}, f32[2,2,8,1152]{3,2,1,0:T(8,128)S(1)}, u32[]{:S(2)}, u32[]{:S(2)}) collective-permute-start(f32[2,2,8,1152]{3,2,1,0:T(8,128)S(1)} %dynamic-slice_bitcast_fusion.5), channel_id=1, source_target_pairs={{0,1},{1,0},{2,3},{3,2},{4,5},{5,4},{6,7},{7,6},{8,9},{9,8},{10,11... | collective-permute-start | bytes 442376 | tf_op jit(solution)/shard_map/ppermute | solution.py:192
  166.6 5.3 %collective-permute-start.8 = (f32[2,2,8,1152]{3,2,1,0:T(8,128)S(1)}, f32[2,2,8,1152]{3,2,1,0:T(8,128)S(1)}, u32[]{:S(2)}, u32[]{:S(2)}) collective-permute-start(f32[2,2,8,1152]{3,2,1,0:T(8,128)S(1)} %dynamic-slice_bitcast_fusion.4), channel_id=1, source_target_pairs={{0,16},{1,17},{2,18},{3,19},{4,20},{5,21},{6,22},{7,23},{8,24},{9,... | collective-permute-start | bytes 442376 | tf_op jit(solution)/shard_map/ppermute | solution.py:192
  169.9 4.9 %collective-permute-start.4 = (f32[2,8,1152]{2,1,0:T(8,128)S(1)}, f32[2,8,1152]{2,1,0:T(8,128)S(1)}, u32[]{:S(2)}, u32[]{:S(2)}) collective-permute-start(f32[2,8,1152]{2,1,0:T(8,128)S(1)} %dynamic-slice_bitcast_fusion.7), channel_id=1, source_target_pairs={{0,2},{1,3},{2,0},{3,1},{4,6},{5,7},{6,4},{7,5},{8,10},{9,11},{10,... | collective-permute-start | bytes 221192 | tf_op jit(solution)/shard_map/ppermute | solution.py:192
  172.0 4.5 %collective-permute-start.9 = (f32[2,8,1152]{2,1,0:T(8,128)S(1)}, f32[2,8,1152]{2,1,0:T(8,128)S(1)}, u32[]{:S(2)}, u32[]{:S(2)}) collective-permute-start(f32[2,8,1152]{2,1,0:T(8,128)S(1)} %dynamic-slice_bitcast_fusion.6), channel_id=1, source_target_pairs={{0,2},{1,3},{2,0},{3,1},{4,6},{5,7},{6,4},{7,5},{8,10},{9,11},{10,... | collective-permute-start | bytes 221192 | tf_op jit(solution)/shard_map/ppermute | solution.py:192
  174.9 5.0 %collective-permute-start.5 = (f32[8,1152]{1,0:T(8,128)S(1)}, f32[8,1152]{1,0:T(8,128)S(1)}, u32[]{:S(2)}, u32[]{:S(2)}) collective-permute-start(f32[8,1152]{1,0:T(8,128)S(1)} %dynamic-slice_bitcast_fusion.9), channel_id=1, source_target_pairs={{0,4},{1,5},{2,6},{3,7},{4,0},{5,1},{6,2},{7,3},{8,12},{9,13},{10,... | collective-permute-start | bytes 110600 | tf_op jit(solution)/shard_map/ppermute | solution.py:192
  176.5 4.9 %collective-permute-start.10 = (f32[8,1152]{1,0:T(8,128)S(1)}, f32[8,1152]{1,0:T(8,128)S(1)}, u32[]{:S(2)}, u32[]{:S(2)}) collective-permute-start(f32[8,1152]{1,0:T(8,128)S(1)} %dynamic-slice_bitcast_fusion.8), channel_id=1, source_target_pairs={{0,4},{1,5},{2,6},{3,7},{4,0},{5,1},{6,2},{7,3},{8,12},{9,13},{10,... | collective-permute-start | bytes 110600 | tf_op jit(solution)/shard_map/ppermute | solution.py:192

commit v14 on v13

--- a/solution.py
+++ b/solution.py
@@ -189,7 +189,7 @@
         keep = lax.dynamic_index_in_dim(buf, mine, axis=axis, keepdims=False)
         send = lax.dynamic_index_in_dim(buf, 1 - mine, axis=axis, keepdims=False)
         pairs = [(i, i ^ (1 << bit)) for i in range(devices)]
-        buf = keep + lax.ppermute(send, axes, pairs)
+        buf = keep + lax.ppermute(send.astype(jnp.bfloat16), axes, pairs).astype(jnp.float32)
         remaining.pop(axis)
     return buf
 

time: 183 us -> 179 us (0.978)
  waiting for transfers between devices: 41.5 us -> 36.1 us
    ppermute x10, waiting for transfers between devices: 16.7 us -> 11.3 us  [halving_reduce_scatter(): lax.ppermute(send.astype(jnp.bfloat16), axes, pairs).astype(jnp.float32)]
    convert_element_type x0 -> x10, local copies, waits for them, and re-layouts: none -> 2.47 us  [halving_reduce_scatter(): send.astype(jnp.bfloat16)]
  transfers between devices with their start and end apart: 12 -> 12, of which waited for: 10 -> 9; matrix products, arithmetic and copies ran while one was open for 10% -> 10% of each run, Pallas kernels for 19% -> 19%
where the time goes in v14:
time: 179 us; the launch traced here: 178 us
  blocking collectives  54.4 us (30%)
  Pallas kernels  45.1 us (25%)
  waiting for transfers between devices  36.1 us (20%)
  starting transfers between devices  18.1 us (10%)
  local copies, waits for them, and re-layouts  15.4 us (9%)
  other arithmetic  8.02 us (4%)
    all_to_all x1, blocking collectives, local(): lax.all_to_all(local_hidden.reshape(tiles, owned, half_rows, width // 2,...  54.4 us
    pallas_call x2, Pallas kernels, second_stage(): pl.pallas_call(functools.partial(second_kernel, rows=rows, carry=prev is...  34 us
    all_to_all x1, waiting for transfers between devices, local(): lax.all_to_all(local_hidden.reshape(tiles, owned, half_rows, width // 2,...  21.4 us
    ppermute x10, waiting for transfers between devices, halving_reduce_scatter(): lax.ppermute(send.astype(jnp.bfloat16), axes, pairs).astype(jnp.float32)  11.3 us
    pallas_call x1, Pallas kernels, first_stage(): pl.pallas_call(first_kernel, grid=(images,), in_specs=[pl.BlockSpec((None...  11.1 us
    ppermute x10, starting transfers between devices, halving_reduce_scatter(): lax.ppermute(send.astype(jnp.bfloat16), axes, pairs).astype(jnp.float32)  9.66 us
    another operation x2, other arithmetic, second_stage(): jnp.stack([shift_cols_right(row_padded), row_padded, shift_cols_left(row_...  6.48 us
    ppermute x1, starting transfers between devices, shifted_2(): return lax.ppermute(shard, axis, pairs)  4.86 us
  transfers between devices with their start and end apart: 12, of which 9 were waited for; matrix products, arithmetic and copies ran while one was open for 10% of the time, Pallas kernels for 19%

profile of v14, /device:TPU:0, one launch (start us, length us, event | category | flops | bytes accessed | tf_op | source)
XLA Modules:
  0.0 177.9 jit_solution(15909808589486578877)
XLA Ops:
  0.6 0.0 copy-start
  0.6 1.0 slice.21
  1.7 4.9 %collective-permute-start = (bf16[8,1,128,128]{3,2,1,0:T(8,128)(2,1)S(1)}, bf16[8,1,128,128]{3,2,1,0:T(8,128)(2,1)S(1)}, u32[]{:S(2)}, u32[]{:S(2)}) collective-permute-start(bf16[8,1,128,128]{3,2,1,0:T(8,128)(2,1)S(1)} %slice.21), channel_id=1, source_target_pairs={{0,1},{1,2},{2,3},{3,4},{4,5},{5,6},{6,7},{8,9},{9,10},{10,11},{11... | collective-permute-start | bytes 786440 | tf_op jit(solution)/shard_map/ppermute | solution.py:14
  6.6 0.7 pad_clamp_fusion
  7.2 0.6 gather_fusion
  7.8 0.9 copy.8
  8.7 3.4 %collective-permute-done.up_ref = bf16[8,1,128,128]{3,2,1,0:T(8,128)(2,1)S(1)} collective-permute-done((bf16[8,1,128,128]{3,2,1,0:T(8,128)(2,1)S(1)}, bf16[8,1,128,128]{3,2,1,0:T(8,128)(2,1)S(1)}, u32[]{:S(2)}, u32[]{:S(2)}) %collective-permute-start) | collective-permute-done | bytes 262176 | tf_op jit(solution)/shard_map/ppermute | solution.py:14
  12.1 0.7 copy-done.5
  12.8 11.1 %shard_map.68 = (bf16[8,16,64,128]{3,2,1,0:T(8,128)(2,1)}, bf16[8,16,64,128]{3,2,1,0:T(8,128)(2,1)}) custom-call(bf16[8,32,128,128]{3,2,1,0:T(8,128)(2,1)} %x_ref.1, bf16[8,1,128,128]{3,2,1,0:T(8,128)(2,1)} %copy-done.5, bf16[1152,256]{1,0:T(8,128)(2,1)} %bitcast.81), custom_call_target="tpu_custom_call" | custom-call | flops 4831838208 | bytes 12582912 | tf_op jit(solution)/shard_map/pallas_call | solution.py:76
  23.9 54.4 %all_to_all.21 = bf16[8,1,16,64,128]{4,3,2,1,0:T(8,128)(2,1)} all-to-all(bf16[8,1,16,64,128]{4,3,2,1,0:T(8,128)(2,1)} %bitcast.76), channel_id=1, replica_groups=mesh['group'=4,'tile'=8] {'tile'}, dimensions={0} | all-to-all | bytes 4194304 | tf_op jit(solution)/shard_map/all_to_all | solution.py:213
  78.3 3.6 %all-to-all-start = ((bf16[8,1,16,64,128]{4,3,2,1,0:T(8,128)(2,1)}), bf16[8,1,16,64,128]{4,3,2,1,0:T(8,128)(2,1)S(1)}, u32[]{:S(2)}, u32[]{:S(2)}) async-start(bf16[8,1,16,64,128]{4,3,2,1,0:T(8,128)(2,1)} %bitcast.75), calls=%async_computation | async-start | bytes 4194304 | tf_op jit(solution)/shard_map/all_to_all | solution.py:213
  81.9 2.5 %fusion.10 = (bf16[3,3,128,256]{3,2,1,0:T(8,128)(2,1)}, bf16[3,3,128,256]{3,2,1,0:T(8,128)(2,1)}) fusion(bf16[3,3,256,256]{3,2,1,0:T(8,128)(2,1)} %param.7), kind=kLoop, calls=%fused_computation.45 | loop fusion | bytes 2359296 | tf_op jit(solution)/shard_map/slice | solution.py:225
  84.4 0.4 pad_bitcast_fusion.5
  84.8 1.4 pad_slice_fusion.3
  86.3 1.8 %pad_bitcast_fusion.2 = (bf16[1,1,130,64,128]{4,3,2,1,0:T(8,128)(2,1)S(1)}, bf16[1,1,130,64,128]{4,3,2,1,0:T(8,128)(2,1)S(1)}) fusion(bf16[1,130,63,128]{3,2,1,0:T(8,128)(2,1)S(1)} %get-tuple-element.21, bf16[1,130,63,128]{3,2,1,0:T(8,128)(2,1)S(1)} %get-tuple-element.20), kind=kLoop, calls=%fused_computation.5 | loop fusion | bytes 8453120 | tf_op jit(solution)/shard_map/stack | solution.py:139
  88.1 3.2 %pad_maximum_fusion.refs_0_ = bf16[1,3,130,64,128]{4,3,2,1,0:T(8,128)(2,1)} fusion(bf16[1,1,130,64,128]{4,3,2,1,0:T(8,128)(2,1)S(1)} %get-tuple-element.24, bf16[1,1,130,64,128]{4,3,2,1,0:T(8,128)(2,1)S(1)} %pad_bitcast_fusion.5, bf16[1,1,130,64,128]{4,3,2,1,0:T(8,128)(2,1)S(1)} %get-tuple-element.25), kind=kLoop, calls=%fused_computation.1 | loop fusion | flops 6389760 | bytes 12779520 | tf_op jit(solution)/shard_map/stack | solution.py:139
  91.3 16.8 %shard_map.69 = (f32[1,128,64,256]{3,2,1,0:T(8,128)}, f32[1,256,1152]{2,1,0:T(8,128)}) custom-call(bf16[1,3,130,64,128]{4,3,2,1,0:T(8,128)(2,1)} %pad_maximum_fusion.refs_0_, bf16[1152,256]{1,0:T(8,128)(2,1)} %bitcast.83, bf16[1,8192,256]{2,1,0:T(8,128)(2,1)} %bitcast.86), custom_call_target="tpu_custom_call" | custom-call | flops 9663676416 | bytes 26345472 | tf_op jit(solution)/shard_map/pallas_call | solution.py:152
  108.1 21.4 %all-to-all-done = bf16[8,1,16,64,128]{4,3,2,1,0:T(8,128)(2,1)S(1)} async-done(((bf16[8,1,16,64,128]{4,3,2,1,0:T(8,128)(2,1)}), bf16[8,1,16,64,128]{4,3,2,1,0:T(8,128)(2,1)S(1)}, u32[]{:S(2)}, u32[]{:S(2)}) %all-to-all-start) | async-done | bytes 2097184 | tf_op jit(solution)/shard_map/all_to_all | solution.py:213
  129.5 0.4 pad_bitcast_fusion.4
  129.9 1.4 pad_slice_fusion.1
  131.3 1.1 fusion
  132.4 0.1 collective-permute-start.1
  132.5 1.3 pad_bitcast_fusion.1
  133.8 0.4 pad_bitcast_fusion
  134.2 3.2 %pad_maximum_fusion.1.refs_0_ = bf16[1,3,130,64,128]{4,3,2,1,0:T(8,128)(2,1)} fusion(bf16[1,1,130,64,128]{4,3,2,1,0:T(8,128)(2,1)S(1)} %pad_bitcast_fusion, bf16[1,1,130,64,128]{4,3,2,1,0:T(8,128)(2,1)S(1)} %pad_bitcast_fusion.4, bf16[1,1,130,64,128]{4,3,2,1,0:T(8,128)(2,1)S(1)} %pad_bitcast_fusion.1), kind=kLoop, calls=%fused_computation.2 | loop fusion | flops 6389760 | bytes 12779520 | tf_op jit(solution)/shard_map/stack | solution.py:139
  137.5 17.2 %shard_map.70 = (bf16[1,128,64,256]{3,2,1,0:T(8,128)(2,1)}, f32[1,256,1152]{2,1,0:T(8,128)}) custom-call(bf16[1,3,130,64,128]{4,3,2,1,0:T(8,128)(2,1)} %pad_maximum_fusion.1.refs_0_, bf16[1152,256]{1,0:T(8,128)(2,1)} %bitcast.82, bf16[1,8192,256]{2,1,0:T(8,128)(2,1)} %bitcast.87, f32[1,128,64,256]{3,2,1,0:T(8,128)} %get-tuple-element.14.refs_3_), custom_call_target="tpu_custom_call" | custom-call | flops 9663676416 | bytes 26345472 | tf_op jit(solution)/shard_map/pallas_call | solution.py:152
  154.7 1.2 fusion.1
  155.9 0.6 collective-permute-start.6
  156.4 0.0 collective-permute-done.1
  156.5 0.1 bitcast_add_fusion.1
  156.6 1.6 collective-permute-start.2
  158.1 0.0 collective-permute-done.6
  158.1 0.1 bitcast_add_fusion
  158.2 1.5 collective-permute-start.7
  159.8 2.6 %collective-permute-done.2 = bf16[2,2,2,8,1152]{4,3,2,1,0:T(8,128)(2,1)S(1)} collective-permute-done((bf16[2,2,2,8,1152]{4,3,2,1,0:T(8,128)(2,1)S(1)}, bf16[2,2,2,8,1152]{4,3,2,1,0:T(8,128)(2,1)S(1)}, u32[]{:S(2)}, u32[]{:S(2)}) %collective-permute-start.2) | collective-permute-done | bytes 147488 | tf_op jit(solution)/shard_map/ppermute | solution.py:192
  162.5 1.5 collective-permute-start.3
  164.0 1.6 collective-permute-start.8
  165.6 1.3 collective-permute-done.3
  166.9 0.1 collective-permute-start.4
  167.0 1.5 collective-permute-done.8
  168.5 0.6 collective-permute-start.9
  169.1 1.8 %collective-permute-done.4 = bf16[2,8,1152]{2,1,0:T(8,128)(2,1)S(1)} collective-permute-done((bf16[2,8,1152]{2,1,0:T(8,128)(2,1)S(1)}, bf16[2,8,1152]{2,1,0:T(8,128)(2,1)S(1)}, u32[]{:S(2)}, u32[]{:S(2)}) %collective-permute-start.4) | collective-permute-done | bytes 36896 | tf_op jit(solution)/shard_map/ppermute | solution.py:192
  171.0 0.6 collective-permute-start.5
  171.6 0.9 collective-permute-done.9
  172.6 1.5 collective-permute-start.10
  174.1 1.6 collective-permute-done.5
  175.7 1.6 collective-permute-done.10
  177.3 0.6 pad_maximum_fusion.2
  (27 shorter events, 0.3 us)
Async XLA Ops:
  0.6 6.6 %copy-start = (bf16[3,3,128,256]{3,2,1,0:T(8,128)(2,1)S(1)}, bf16[3,3,128,256]{3,2,1,0:T(8,128)(2,1)}, u32[]{:S(2)}) copy-start(bf16[3,3,128,256]{3,2,1,0:T(8,128)(2,1)} %param.6) | copy-start | bytes 1769476
  1.7 10.4 %collective-permute-start = (bf16[8,1,128,128]{3,2,1,0:T(8,128)(2,1)S(1)}, bf16[8,1,128,128]{3,2,1,0:T(8,128)(2,1)S(1)}, u32[]{:S(2)}, u32[]{:S(2)}) collective-permute-start(bf16[8,1,128,128]{3,2,1,0:T(8,128)(2,1)S(1)} %slice.21), channel_id=1, source_target_pairs={{0,1},{1,2},{2,3},{3,4},{4,5},{5,6},{6,7},{8,9},{9,10},{10,11},{11... | collective-permute-start | bytes 786440 | tf_op jit(solution)/shard_map/ppermute | solution.py:14
  12.1 0.7 copy-start.5
  78.3 51.3 %all-to-all-start = ((bf16[8,1,16,64,128]{4,3,2,1,0:T(8,128)(2,1)}), bf16[8,1,16,64,128]{4,3,2,1,0:T(8,128)(2,1)S(1)}, u32[]{:S(2)}, u32[]{:S(2)}) async-start(bf16[8,1,16,64,128]{4,3,2,1,0:T(8,128)(2,1)} %bitcast.75), calls=%async_computation | async-start | bytes 4194304 | tf_op jit(solution)/shard_map/all_to_all | solution.py:213
  81.9 2.5 %copy-start.2 = (bf16[8,1,16,64,128]{4,3,2,1,0:T(8,128)(2,1)S(1)}, bf16[8,1,16,64,128]{4,3,2,1,0:T(8,128)(2,1)}, u32[]{:S(2)}) copy-start(bf16[8,1,16,64,128]{4,3,2,1,0:T(8,128)(2,1)} %all_to_all.21) | copy-start | bytes 6291460
  132.4 24.0 %collective-permute-start.1 = (bf16[2,2,2,2,8,1152]{5,4,3,2,1,0:T(8,128)(2,1)S(1)}, bf16[2,2,2,2,8,1152]{5,4,3,2,1,0:T(8,128)(2,1)S(1)}, u32[]{:S(2)}, u32[]{:S(2)}) collective-permute-start(bf16[2,2,2,2,8,1152]{5,4,3,2,1,0:T(8,128)(2,1)S(1)} %fusion), channel_id=1, source_target_pairs={{0,8},{1,9},{2,10},{3,11},{4,12},{5,13},{6,14},{7,15},{8,0},{9,1},... | collective-permute-start | bytes 884744 | tf_op jit(solution)/shard_map/ppermute | solution.py:192
  137.5 19.0 %copy-start.3 = (f32[1,256,1152]{2,1,0:T(8,128)S(1)}, f32[1,256,1152]{2,1,0:T(8,128)}, u32[]{:S(2)}) copy-start(f32[1,256,1152]{2,1,0:T(8,128)} %get-tuple-element.16) | copy-start | bytes 3538948
  154.7 3.5 %copy-start.4 = (f32[1,256,1152]{2,1,0:T(8,128)S(1)}, f32[1,256,1152]{2,1,0:T(8,128)}, u32[]{:S(2)}) copy-start(f32[1,256,1152]{2,1,0:T(8,128)} %get-tuple-element.17) | copy-start | bytes 3538948
  155.9 2.3 %collective-permute-start.6 = (bf16[2,2,2,2,8,1152]{5,4,3,2,1,0:T(8,128)(2,1)S(1)}, bf16[2,2,2,2,8,1152]{5,4,3,2,1,0:T(8,128)(2,1)S(1)}, u32[]{:S(2)}, u32[]{:S(2)}) collective-permute-start(bf16[2,2,2,2,8,1152]{5,4,3,2,1,0:T(8,128)(2,1)S(1)} %fusion.1), channel_id=1, source_target_pairs={{0,8},{1,9},{2,10},{3,11},{4,12},{5,13},{6,14},{7,15},{8,0},{9,1},... | collective-permute-start | bytes 884744 | tf_op jit(solution)/shard_map/ppermute | solution.py:192
  156.6 5.9 %collective-permute-start.2 = (bf16[2,2,2,8,1152]{4,3,2,1,0:T(8,128)(2,1)S(1)}, bf16[2,2,2,8,1152]{4,3,2,1,0:T(8,128)(2,1)S(1)}, u32[]{:S(2)}, u32[]{:S(2)}) collective-permute-start(bf16[2,2,2,8,1152]{4,3,2,1,0:T(8,128)(2,1)S(1)} %fusion.2), channel_id=1, source_target_pairs={{0,16},{1,17},{2,18},{3,19},{4,20},{5,21},{6,22},{7,23},{8,24},{9,... | collective-permute-start | bytes 442376 | tf_op jit(solution)/shard_map/ppermute | solution.py:192
  158.1 19.8 %copy-start.1 = (bf16[3,3,128,256]{3,2,1,0:T(8,128)(2,1)S(1)}, bf16[3,3,128,256]{3,2,1,0:T(8,128)(2,1)}, u32[]{:S(2)}) copy-start(bf16[3,3,128,256]{3,2,1,0:T(8,128)(2,1)} %param.6) | copy-start | bytes 1769476
  158.2 5.7 %collective-permute-start.7 = (bf16[2,2,2,8,1152]{4,3,2,1,0:T(8,128)(2,1)S(1)}, bf16[2,2,2,8,1152]{4,3,2,1,0:T(8,128)(2,1)S(1)}, u32[]{:S(2)}, u32[]{:S(2)}) collective-permute-start(bf16[2,2,2,8,1152]{4,3,2,1,0:T(8,128)(2,1)S(1)} %fusion.3), channel_id=1, source_target_pairs={{0,1},{1,0},{2,3},{3,2},{4,5},{5,4},{6,7},{7,6},{8,9},{9,8},{10,11... | collective-permute-start | bytes 442376 | tf_op jit(solution)/shard_map/ppermute | solution.py:192
  162.5 4.4 %collective-permute-start.3 = (bf16[2,2,8,1152]{3,2,1,0:T(8,128)(2,1)S(1)}, bf16[2,2,8,1152]{3,2,1,0:T(8,128)(2,1)S(1)}, u32[]{:S(2)}, u32[]{:S(2)}) collective-permute-start(bf16[2,2,8,1152]{3,2,1,0:T(8,128)(2,1)S(1)} %fusion.4), channel_id=1, source_target_pairs={{0,1},{1,0},{2,3},{3,2},{4,5},{5,4},{6,7},{7,6},{8,9},{9,8},{10,11... | collective-permute-start | bytes 221192 | tf_op jit(solution)/shard_map/ppermute | solution.py:192
  164.0 4.4 %collective-permute-start.8 = (bf16[2,2,8,1152]{3,2,1,0:T(8,128)(2,1)S(1)}, bf16[2,2,8,1152]{3,2,1,0:T(8,128)(2,1)S(1)}, u32[]{:S(2)}, u32[]{:S(2)}) collective-permute-start(bf16[2,2,8,1152]{3,2,1,0:T(8,128)(2,1)S(1)} %fusion.5), channel_id=1, source_target_pairs={{0,16},{1,17},{2,18},{3,19},{4,20},{5,21},{6,22},{7,23},{8,24},{9,... | collective-permute-start | bytes 221192 | tf_op jit(solution)/shard_map/ppermute | solution.py:192
  166.9 4.0 %collective-permute-start.4 = (bf16[2,8,1152]{2,1,0:T(8,128)(2,1)S(1)}, bf16[2,8,1152]{2,1,0:T(8,128)(2,1)S(1)}, u32[]{:S(2)}, u32[]{:S(2)}) collective-permute-start(bf16[2,8,1152]{2,1,0:T(8,128)(2,1)S(1)} %fusion.6), channel_id=1, source_target_pairs={{0,2},{1,3},{2,0},{3,1},{4,6},{5,7},{6,4},{7,5},{8,10},{9,11},{10,... | collective-permute-start | bytes 110600 | tf_op jit(solution)/shard_map/ppermute | solution.py:192
  168.5 4.0 %collective-permute-start.9 = (bf16[2,8,1152]{2,1,0:T(8,128)(2,1)S(1)}, bf16[2,8,1152]{2,1,0:T(8,128)(2,1)S(1)}, u32[]{:S(2)}, u32[]{:S(2)}) collective-permute-start(bf16[2,8,1152]{2,1,0:T(8,128)(2,1)S(1)} %fusion.7), channel_id=1, source_target_pairs={{0,2},{1,3},{2,0},{3,1},{4,6},{5,7},{6,4},{7,5},{8,10},{9,11},{10,... | collective-permute-start | bytes 110600 | tf_op jit(solution)/shard_map/ppermute | solution.py:192
  171.0 4.7 %collective-permute-start.5 = (bf16[8,1152]{1,0:T(8,128)(2,1)S(1)}, bf16[8,1152]{1,0:T(8,128)(2,1)S(1)}, u32[]{:S(2)}, u32[]{:S(2)}) collective-permute-start(bf16[8,1152]{1,0:T(8,128)(2,1)S(1)} %fusion.8), channel_id=1, source_target_pairs={{0,4},{1,5},{2,6},{3,7},{4,0},{5,1},{6,2},{7,3},{8,12},{9,13},{10,... | collective-permute-start | bytes 55304 | tf_op jit(solution)/shard_map/ppermute | solution.py:192
  172.6 4.7 %collective-permute-start.10 = (bf16[8,1152]{1,0:T(8,128)(2,1)S(1)}, bf16[8,1152]{1,0:T(8,128)(2,1)S(1)}, u32[]{:S(2)}, u32[]{:S(2)}) collective-permute-start(bf16[8,1152]{1,0:T(8,128)(2,1)S(1)} %fusion.9), channel_id=1, source_target_pairs={{0,4},{1,5},{2,6},{3,7},{4,0},{5,1},{6,2},{7,3},{8,12},{9,13},{10,... | collective-permute-start | bytes 55304 | tf_op jit(solution)/shard_map/ppermute | solution.py:192

commit v15 on v14

--- a/solution.py
+++ b/solution.py
@@ -183,13 +183,16 @@
     rows = partial.shape[0] // devices
     buf = partial.reshape((2,) * bits + (rows,) + partial.shape[1:])
     remaining = list(range(bits - 1, -1, -1))
-    for bit in order:
+    for position, bit in enumerate(order):
         axis = remaining.index(bit)
         mine = (me >> bit) & 1
         keep = lax.dynamic_index_in_dim(buf, mine, axis=axis, keepdims=False)
         send = lax.dynamic_index_in_dim(buf, 1 - mine, axis=axis, keepdims=False)
         pairs = [(i, i ^ (1 << bit)) for i in range(devices)]
-        buf = keep + lax.ppermute(send.astype(jnp.bfloat16), axes, pairs).astype(jnp.float32)
+        if position == 1:
+            buf = keep + lax.ppermute(send.astype(jnp.bfloat16), axes, pairs).astype(jnp.float32)
+        else:
+            buf = keep + lax.ppermute(send, axes, pairs)
         remaining.pop(axis)
     return buf
 

time: 179 us -> 179 us (level)
  waiting for transfers between devices: 36.1 us -> 38.3 us
    ppermute x0 -> x8, waiting for transfers between devices: none -> 10.5 us  [halving_reduce_scatter(): buf = keep + lax.ppermute(send, axes, pairs)]
    ppermute x10 -> x2, waiting for transfers between devices: 11.3 us -> 3.03 us  [halving_reduce_scatter(): lax.ppermute(send.astype(jnp.bfloat16), axes, pairs).astype(jnp.float32)]
    ppermute x10 -> x2, starting transfers between devices: 9.66 us -> 3.1 us  [halving_reduce_scatter(): lax.ppermute(send.astype(jnp.bfloat16), axes, pairs).astype(jnp.float32)]
    ppermute x0 -> x8, starting transfers between devices: none -> 6.26 us  [halving_reduce_scatter(): buf = keep + lax.ppermute(send, axes, pairs)]
    convert_element_type x10 -> x2, local copies, waits for them, and re-layouts: 2.47 us -> 0.05 us  [halving_reduce_scatter(): send.astype(jnp.bfloat16)]
  transfers between devices with their start and end apart: 12 -> 12, of which waited for: 9 -> 10; matrix products, arithmetic and copies ran while one was open for 10% -> 10% of each run, Pallas kernels for 19% -> 19%
where the time goes in v15:
time: 179 us
  blocking collectives  54.4 us (30%)
  Pallas kernels  45.1 us (25%)
  waiting for transfers between devices  38.3 us (21%)
  starting transfers between devices  17.8 us (10%)
  local copies, waits for them, and re-layouts  14.3 us (8%)
  other arithmetic  8.09 us (5%)
    all_to_all x1, blocking collectives, local(): lax.all_to_all(local_hidden.reshape(tiles, owned, half_rows, width // 2,...  54.4 us
    pallas_call x2, Pallas kernels, second_stage(): pl.pallas_call(functools.partial(second_kernel, rows=rows, carry=prev is...  34 us
    all_to_all x1, waiting for transfers between devices, local(): lax.all_to_all(local_hidden.reshape(tiles, owned, half_rows, width // 2,...  21.4 us
    pallas_call x1, Pallas kernels, first_stage(): pl.pallas_call(first_kernel, grid=(images,), in_specs=[pl.BlockSpec((None...  11.1 us
    ppermute x8, waiting for transfers between devices, halving_reduce_scatter(): buf = keep + lax.ppermute(send, axes, pairs)  10.5 us
    another operation x2, other arithmetic, second_stage(): jnp.stack([shift_cols_right(row_padded), row_padded, shift_cols_left(row_...  6.54 us
    ppermute x8, starting transfers between devices, halving_reduce_scatter(): buf = keep + lax.ppermute(send, axes, pairs)  6.26 us
    ppermute x1, starting transfers between devices, shifted_2(): return lax.ppermute(shard, axis, pairs)  4.86 us
  transfers between devices with their start and end apart: 12, of which 10 were waited for; matrix products, arithmetic and copies ran while one was open for 10% of the time, Pallas kernels for 19%

profile of v15, /device:TPU:0, one launch (start us, length us, event | category | flops | bytes accessed | tf_op | source)
XLA Modules:
  0.0 178.9 jit_solution(6590477144564912026)
XLA Ops:
  0.6 0.0 copy-start
  0.6 1.0 slice.21
  1.7 4.9 %collective-permute-start = (bf16[8,1,128,128]{3,2,1,0:T(8,128)(2,1)S(1)}, bf16[8,1,128,128]{3,2,1,0:T(8,128)(2,1)S(1)}, u32[]{:S(2)}, u32[]{:S(2)}) collective-permute-start(bf16[8,1,128,128]{3,2,1,0:T(8,128)(2,1)S(1)} %slice.21), channel_id=1, source_target_pairs={{0,1},{1,2},{2,3},{3,4},{4,5},{5,6},{6,7},{8,9},{9,10},{10,11},{11... | collective-permute-start | bytes 786440 | tf_op jit(solution)/shard_map/ppermute | solution.py:14
  6.6 0.7 pad_clamp_fusion
  7.2 0.6 gather_fusion
  7.8 0.9 copy.8
  8.7 3.4 %collective-permute-done.up_ref = bf16[8,1,128,128]{3,2,1,0:T(8,128)(2,1)S(1)} collective-permute-done((bf16[8,1,128,128]{3,2,1,0:T(8,128)(2,1)S(1)}, bf16[8,1,128,128]{3,2,1,0:T(8,128)(2,1)S(1)}, u32[]{:S(2)}, u32[]{:S(2)}) %collective-permute-start) | collective-permute-done | bytes 262176 | tf_op jit(solution)/shard_map/ppermute | solution.py:14
  12.1 0.7 copy-done.6
  12.8 11.1 %shard_map.68 = (bf16[8,16,64,128]{3,2,1,0:T(8,128)(2,1)}, bf16[8,16,64,128]{3,2,1,0:T(8,128)(2,1)}) custom-call(bf16[8,32,128,128]{3,2,1,0:T(8,128)(2,1)} %x_ref.1, bf16[8,1,128,128]{3,2,1,0:T(8,128)(2,1)} %copy-done.6, bf16[1152,256]{1,0:T(8,128)(2,1)} %bitcast.81), custom_call_target="tpu_custom_call" | custom-call | flops 4831838208 | bytes 12582912 | tf_op jit(solution)/shard_map/pallas_call | solution.py:76
  23.9 54.4 %all_to_all.21 = bf16[8,1,16,64,128]{4,3,2,1,0:T(8,128)(2,1)} all-to-all(bf16[8,1,16,64,128]{4,3,2,1,0:T(8,128)(2,1)} %bitcast.76), channel_id=1, replica_groups=mesh['group'=4,'tile'=8] {'tile'}, dimensions={0} | all-to-all | bytes 4194304 | tf_op jit(solution)/shard_map/all_to_all | solution.py:216
  78.3 3.6 %all-to-all-start = ((bf16[8,1,16,64,128]{4,3,2,1,0:T(8,128)(2,1)}), bf16[8,1,16,64,128]{4,3,2,1,0:T(8,128)(2,1)S(1)}, u32[]{:S(2)}, u32[]{:S(2)}) async-start(bf16[8,1,16,64,128]{4,3,2,1,0:T(8,128)(2,1)} %bitcast.75), calls=%async_computation | async-start | bytes 4194304 | tf_op jit(solution)/shard_map/all_to_all | solution.py:216
  81.9 2.5 %fusion.2 = (bf16[3,3,128,256]{3,2,1,0:T(8,128)(2,1)}, bf16[3,3,128,256]{3,2,1,0:T(8,128)(2,1)}) fusion(bf16[3,3,256,256]{3,2,1,0:T(8,128)(2,1)} %param.7), kind=kLoop, calls=%fused_computation.37 | loop fusion | bytes 2359296 | tf_op jit(solution)/shard_map/slice | solution.py:228
  84.4 0.4 pad_bitcast_fusion.5
  84.8 1.4 pad_slice_fusion.3
  86.3 1.8 pad_bitcast_fusion.2
  88.1 3.3 %pad_maximum_fusion.refs_0_ = bf16[1,3,130,64,128]{4,3,2,1,0:T(8,128)(2,1)} fusion(bf16[1,1,130,64,128]{4,3,2,1,0:T(8,128)(2,1)S(1)} %get-tuple-element.24, bf16[1,1,130,64,128]{4,3,2,1,0:T(8,128)(2,1)S(1)} %pad_bitcast_fusion.5, bf16[1,1,130,64,128]{4,3,2,1,0:T(8,128)(2,1)S(1)} %get-tuple-element.25), kind=kLoop, calls=%fused_computation.1 | loop fusion | flops 6389760 | bytes 12779520 | tf_op jit(solution)/shard_map/stack | solution.py:139
  91.3 16.8 %shard_map.69 = (f32[1,128,64,256]{3,2,1,0:T(8,128)}, f32[1,256,1152]{2,1,0:T(8,128)}) custom-call(bf16[1,3,130,64,128]{4,3,2,1,0:T(8,128)(2,1)} %pad_maximum_fusion.refs_0_, bf16[1152,256]{1,0:T(8,128)(2,1)} %bitcast.83, bf16[1,8192,256]{2,1,0:T(8,128)(2,1)} %bitcast.86), custom_call_target="tpu_custom_call" | custom-call | flops 9663676416 | bytes 26345472 | tf_op jit(solution)/shard_map/pallas_call | solution.py:152
  108.1 21.4 %all-to-all-done = bf16[8,1,16,64,128]{4,3,2,1,0:T(8,128)(2,1)S(1)} async-done(((bf16[8,1,16,64,128]{4,3,2,1,0:T(8,128)(2,1)}), bf16[8,1,16,64,128]{4,3,2,1,0:T(8,128)(2,1)S(1)}, u32[]{:S(2)}, u32[]{:S(2)}) %all-to-all-start) | async-done | bytes 2097184 | tf_op jit(solution)/shard_map/all_to_all | solution.py:216
  129.5 0.4 pad_bitcast_fusion.4
  130.0 1.4 pad_slice_fusion.1
  131.4 0.1 collective-permute-start.1
  131.5 1.3 pad_bitcast_fusion.1
  132.8 0.4 pad_bitcast_fusion
  133.2 3.3 %pad_maximum_fusion.1.refs_0_ = bf16[1,3,130,64,128]{4,3,2,1,0:T(8,128)(2,1)} fusion(bf16[1,1,130,64,128]{4,3,2,1,0:T(8,128)(2,1)S(1)} %pad_bitcast_fusion, bf16[1,1,130,64,128]{4,3,2,1,0:T(8,128)(2,1)S(1)} %pad_bitcast_fusion.4, bf16[1,1,130,64,128]{4,3,2,1,0:T(8,128)(2,1)S(1)} %pad_bitcast_fusion.1), kind=kLoop, calls=%fused_computation.2 | loop fusion | flops 6389760 | bytes 12779520 | tf_op jit(solution)/shard_map/stack | solution.py:139
  136.5 17.2 %shard_map.70 = (bf16[1,128,64,256]{3,2,1,0:T(8,128)(2,1)}, f32[1,256,1152]{2,1,0:T(8,128)}) custom-call(bf16[1,3,130,64,128]{4,3,2,1,0:T(8,128)(2,1)} %pad_maximum_fusion.1.refs_0_, bf16[1152,256]{1,0:T(8,128)(2,1)} %bitcast.82, bf16[1,8192,256]{2,1,0:T(8,128)(2,1)} %bitcast.87, f32[1,128,64,256]{3,2,1,0:T(8,128)} %get-tuple-element.14.refs_3_), custom_call_target="tpu_custom_call" | custom-call | flops 9663676416 | bytes 26345472 | tf_op jit(solution)/shard_map/pallas_call | solution.py:152
  153.7 1.2 dynamic-slice_bitcast_fusion
  154.9 0.6 collective-permute-start.6
  155.5 0.0 collective-permute-done.1
  155.5 0.1 bitcast_add_fusion.1
  155.6 1.6 collective-permute-start.2
  157.2 0.1 bitcast_add_fusion
  157.2 0.0 copy-start.1
  157.3 1.5 collective-permute-start.7
  158.8 2.6 %collective-permute-done.2 = bf16[2,2,2,8,1152]{4,3,2,1,0:T(8,128)(2,1)S(1)} collective-permute-done((bf16[2,2,2,8,1152]{4,3,2,1,0:T(8,128)(2,1)S(1)}, bf16[2,2,2,8,1152]{4,3,2,1,0:T(8,128)(2,1)S(1)}, u32[]{:S(2)}, u32[]{:S(2)}) %collective-permute-start.2) | collective-permute-done | bytes 147488 | tf_op jit(solution)/shard_map/ppermute | solution.py:193
  161.5 1.5 collective-permute-start.3
  163.0 0.4 collective-permute-done.7
  163.5 1.6 collective-permute-start.8
  165.1 1.6 collective-permute-done.3
  166.8 0.1 collective-permute-start.4
  166.8 2.0 %collective-permute-done.8 = f32[2,2,8,1152]{3,2,1,0:T(8,128)S(1)} collective-permute-done((f32[2,2,8,1152]{3,2,1,0:T(8,128)S(1)}, f32[2,2,8,1152]{3,2,1,0:T(8,128)S(1)}, u32[]{:S(2)}, u32[]{:S(2)}) %collective-permute-start.8) | collective-permute-done | bytes 147488 | tf_op jit(solution)/shard_map/ppermute | solution.py:195
  168.8 0.1 collective-permute-start.9
  169.0 2.7 %collective-permute-done.4 = f32[2,8,1152]{2,1,0:T(8,128)S(1)} collective-permute-done((f32[2,8,1152]{2,1,0:T(8,128)S(1)}, f32[2,8,1152]{2,1,0:T(8,128)S(1)}, u32[]{:S(2)}, u32[]{:S(2)}) %collective-permute-start.4) | collective-permute-done | bytes 73760 | tf_op jit(solution)/shard_map/ppermute | solution.py:195
  171.7 0.9 collective-permute-start.5
  172.6 0.7 collective-permute-done.9
  173.3 1.4 collective-permute-start.10
  174.8 1.9 %collective-permute-done.5 = f32[8,1152]{1,0:T(8,128)S(1)} collective-permute-done((f32[8,1152]{1,0:T(8,128)S(1)}, f32[8,1152]{1,0:T(8,128)S(1)}, u32[]{:S(2)}, u32[]{:S(2)}) %collective-permute-start.5) | collective-permute-done | bytes 36896 | tf_op jit(solution)/shard_map/ppermute | solution.py:195
  176.7 1.5 collective-permute-done.10
  178.3 0.6 pad_maximum_fusion.2
  (29 shorter events, 0.4 us)
Async XLA Ops:
  0.6 6.6 %copy-start = (bf16[3,3,128,256]{3,2,1,0:T(8,128)(2,1)S(1)}, bf16[3,3,128,256]{3,2,1,0:T(8,128)(2,1)}, u32[]{:S(2)}) copy-start(bf16[3,3,128,256]{3,2,1,0:T(8,128)(2,1)} %param.6) | copy-start | bytes 1769476
  1.7 10.4 %collective-permute-start = (bf16[8,1,128,128]{3,2,1,0:T(8,128)(2,1)S(1)}, bf16[8,1,128,128]{3,2,1,0:T(8,128)(2,1)S(1)}, u32[]{:S(2)}, u32[]{:S(2)}) collective-permute-start(bf16[8,1,128,128]{3,2,1,0:T(8,128)(2,1)S(1)} %slice.21), channel_id=1, source_target_pairs={{0,1},{1,2},{2,3},{3,4},{4,5},{5,6},{6,7},{8,9},{9,10},{10,11},{11... | collective-permute-start | bytes 786440 | tf_op jit(solution)/shard_map/ppermute | solution.py:14
  12.1 0.7 copy-start.6
  78.3 51.3 %all-to-all-start = ((bf16[8,1,16,64,128]{4,3,2,1,0:T(8,128)(2,1)}), bf16[8,1,16,64,128]{4,3,2,1,0:T(8,128)(2,1)S(1)}, u32[]{:S(2)}, u32[]{:S(2)}) async-start(bf16[8,1,16,64,128]{4,3,2,1,0:T(8,128)(2,1)} %bitcast.75), calls=%async_computation | async-start | bytes 4194304 | tf_op jit(solution)/shard_map/all_to_all | solution.py:216
  81.9 2.5 %copy-start.2 = (bf16[8,1,16,64,128]{4,3,2,1,0:T(8,128)(2,1)S(1)}, bf16[8,1,16,64,128]{4,3,2,1,0:T(8,128)(2,1)}, u32[]{:S(2)}) copy-start(bf16[8,1,16,64,128]{4,3,2,1,0:T(8,128)(2,1)} %all_to_all.21) | copy-start | bytes 6291460
  129.9 1.4 copy-start.3
  131.4 24.1 %collective-permute-start.1 = (f32[2,2,2,2,8,1152]{5,4,3,2,1,0:T(8,128)S(1)}, f32[2,2,2,2,8,1152]{5,4,3,2,1,0:T(8,128)S(1)}, u32[]{:S(2)}, u32[]{:S(2)}) collective-permute-start(f32[2,2,2,2,8,1152]{5,4,3,2,1,0:T(8,128)S(1)} %dynamic-slice_bitcast_fusion.1), channel_id=1, source_target_pairs={{0,8},{1,9},{2,10},{3,11},{4,12},{5,13},{6,14},{7,15},{8,0},{9,1},... | collective-permute-start | bytes 1769480 | tf_op jit(solution)/shard_map/ppermute | solution.py:195
  136.5 19.0 %copy-start.4 = (f32[1,256,1152]{2,1,0:T(8,128)S(1)}, f32[1,256,1152]{2,1,0:T(8,128)}, u32[]{:S(2)}) copy-start(f32[1,256,1152]{2,1,0:T(8,128)} %get-tuple-element.16) | copy-start | bytes 3538948
  153.7 3.5 %copy-start.5 = (f32[1,256,1152]{2,1,0:T(8,128)S(1)}, f32[1,256,1152]{2,1,0:T(8,128)}, u32[]{:S(2)}) copy-start(f32[1,256,1152]{2,1,0:T(8,128)} %get-tuple-element.17) | copy-start | bytes 3538948
  154.9 2.3 %collective-permute-start.6 = (f32[2,2,2,2,8,1152]{5,4,3,2,1,0:T(8,128)S(1)}, f32[2,2,2,2,8,1152]{5,4,3,2,1,0:T(8,128)S(1)}, u32[]{:S(2)}, u32[]{:S(2)}) collective-permute-start(f32[2,2,2,2,8,1152]{5,4,3,2,1,0:T(8,128)S(1)} %dynamic-slice_bitcast_fusion), channel_id=1, source_target_pairs={{0,8},{1,9},{2,10},{3,11},{4,12},{5,13},{6,14},{7,15},{8,0},{9,1},... | collective-permute-start | bytes 1769480 | tf_op jit(solution)/shard_map/ppermute | solution.py:195
  155.6 5.9 %collective-permute-start.2 = (bf16[2,2,2,8,1152]{4,3,2,1,0:T(8,128)(2,1)S(1)}, bf16[2,2,2,8,1152]{4,3,2,1,0:T(8,128)(2,1)S(1)}, u32[]{:S(2)}, u32[]{:S(2)}) collective-permute-start(bf16[2,2,2,8,1152]{4,3,2,1,0:T(8,128)(2,1)S(1)} %fusion), channel_id=1, source_target_pairs={{0,16},{1,17},{2,18},{3,19},{4,20},{5,21},{6,22},{7,23},{8,24},{9,... | collective-permute-start | bytes 442376 | tf_op jit(solution)/shard_map/ppermute | solution.py:193
  157.2 21.7 %copy-start.1 = (bf16[3,3,128,256]{3,2,1,0:T(8,128)(2,1)S(1)}, bf16[3,3,128,256]{3,2,1,0:T(8,128)(2,1)}, u32[]{:S(2)}) copy-start(bf16[3,3,128,256]{3,2,1,0:T(8,128)(2,1)} %param.6) | copy-start | bytes 1769476
  157.3 6.1 %collective-permute-start.7 = (bf16[2,2,2,8,1152]{4,3,2,1,0:T(8,128)(2,1)S(1)}, bf16[2,2,2,8,1152]{4,3,2,1,0:T(8,128)(2,1)S(1)}, u32[]{:S(2)}, u32[]{:S(2)}) collective-permute-start(bf16[2,2,2,8,1152]{4,3,2,1,0:T(8,128)(2,1)S(1)} %fusion.1), channel_id=1, source_target_pairs={{0,1},{1,0},{2,3},{3,2},{4,5},{5,4},{6,7},{7,6},{8,9},{9,8},{10,11... | collective-permute-start | bytes 442376 | tf_op jit(solution)/shard_map/ppermute | solution.py:193
  161.5 5.2 %collective-permute-start.3 = (f32[2,2,8,1152]{3,2,1,0:T(8,128)S(1)}, f32[2,2,8,1152]{3,2,1,0:T(8,128)S(1)}, u32[]{:S(2)}, u32[]{:S(2)}) collective-permute-start(f32[2,2,8,1152]{3,2,1,0:T(8,128)S(1)} %dynamic-slice_bitcast_fusion.3), channel_id=1, source_target_pairs={{0,1},{1,0},{2,3},{3,2},{4,5},{5,4},{6,7},{7,6},{8,9},{9,8},{10,11... | collective-permute-start | bytes 442376 | tf_op jit(solution)/shard_map/ppermute | solution.py:195
  163.5 5.3 %collective-permute-start.8 = (f32[2,2,8,1152]{3,2,1,0:T(8,128)S(1)}, f32[2,2,8,1152]{3,2,1,0:T(8,128)S(1)}, u32[]{:S(2)}, u32[]{:S(2)}) collective-permute-start(f32[2,2,8,1152]{3,2,1,0:T(8,128)S(1)} %dynamic-slice_bitcast_fusion.2), channel_id=1, source_target_pairs={{0,16},{1,17},{2,18},{3,19},{4,20},{5,21},{6,22},{7,23},{8,24},{9,... | collective-permute-start | bytes 442376 | tf_op jit(solution)/shard_map/ppermute | solution.py:195
  166.8 4.9 %collective-permute-start.4 = (f32[2,8,1152]{2,1,0:T(8,128)S(1)}, f32[2,8,1152]{2,1,0:T(8,128)S(1)}, u32[]{:S(2)}, u32[]{:S(2)}) collective-permute-start(f32[2,8,1152]{2,1,0:T(8,128)S(1)} %dynamic-slice_bitcast_fusion.5), channel_id=1, source_target_pairs={{0,2},{1,3},{2,0},{3,1},{4,6},{5,7},{6,4},{7,5},{8,10},{9,11},{10,... | collective-permute-start | bytes 221192 | tf_op jit(solution)/shard_map/ppermute | solution.py:195
  168.8 4.5 %collective-permute-start.9 = (f32[2,8,1152]{2,1,0:T(8,128)S(1)}, f32[2,8,1152]{2,1,0:T(8,128)S(1)}, u32[]{:S(2)}, u32[]{:S(2)}) collective-permute-start(f32[2,8,1152]{2,1,0:T(8,128)S(1)} %dynamic-slice_bitcast_fusion.4), channel_id=1, source_target_pairs={{0,2},{1,3},{2,0},{3,1},{4,6},{5,7},{6,4},{7,5},{8,10},{9,11},{10,... | collective-permute-start | bytes 221192 | tf_op jit(solution)/shard_map/ppermute | solution.py:195
  171.7 5.0 %collective-permute-start.5 = (f32[8,1152]{1,0:T(8,128)S(1)}, f32[8,1152]{1,0:T(8,128)S(1)}, u32[]{:S(2)}, u32[]{:S(2)}) collective-permute-start(f32[8,1152]{1,0:T(8,128)S(1)} %dynamic-slice_bitcast_fusion.7), channel_id=1, source_target_pairs={{0,4},{1,5},{2,6},{3,7},{4,0},{5,1},{6,2},{7,3},{8,12},{9,13},{10,... | collective-permute-start | bytes 110600 | tf_op jit(solution)/shard_map/ppermute | solution.py:195
  173.3 4.9 %collective-permute-start.10 = (f32[8,1152]{1,0:T(8,128)S(1)}, f32[8,1152]{1,0:T(8,128)S(1)}, u32[]{:S(2)}, u32[]{:S(2)}) collective-permute-start(f32[8,1152]{1,0:T(8,128)S(1)} %dynamic-slice_bitcast_fusion.6), channel_id=1, source_target_pairs={{0,4},{1,5},{2,6},{3,7},{4,0},{5,1},{6,2},{7,3},{8,12},{9,13},{10,... | collective-permute-start | bytes 110600 | tf_op jit(solution)/shard_map/ppermute | solution.py:195

commit v16 on v13

--- a/solution.py
+++ b/solution.py
@@ -45,10 +45,10 @@
     return jnp.maximum(total, 0.0).astype(jnp.bfloat16)
 
 
-def first_kernel(x_ref, up_ref, w_ref, low_ref, high_ref, scratch):
+def first_kernel(x_ref, w_ref, low_ref, high_ref, scratch):
     rows, width, inputs = x_ref.shape
     out_rows, out_cols = rows // 2, width // 2
-    scratch[0] = up_ref[0].astype(jnp.float32)
+    scratch[0] = jnp.zeros(scratch.shape[1:], jnp.float32)
     scratch[1:] = x_ref[...].astype(jnp.float32)
     first_col = lax.broadcasted_iota(jnp.int32, (out_rows, out_cols, inputs), 1) == 0
     pieces = []
@@ -67,32 +67,73 @@
     high_ref[...] = hidden[..., half:]
 
 
+def first_row_kernel(x_ref, up_ref, w_ref, _low, _high, low_ref, high_ref, scratch):
+    images, _, width, inputs = x_ref.shape
+    out_cols = width // 2
+    scratch[:, 0] = up_ref[:, 0].astype(jnp.float32)
+    scratch[:, 1:] = x_ref[...].astype(jnp.float32)
+    first_col = lax.broadcasted_iota(jnp.int32, (images, out_cols, inputs), 1) == 0
+    pieces = []
+    for tap_row in range(3):
+        even = scratch[:, tap_row, pl.ds(0, out_cols, stride=2), :]
+        odd = scratch[:, tap_row, pl.ds(1, out_cols, stride=2), :]
+        left = jnp.where(first_col, 0.0, pltpu.roll(odd, 1, 1))
+        pieces += [even, odd, left]
+    patches = jnp.concatenate(
+        [p.astype(jnp.bfloat16).reshape(images * out_cols, inputs) for p in pieces], axis=-1
+    )
+    total = jnp.dot(patches, w_ref[...], preferred_element_type=jnp.float32)
+    hidden = jnp.maximum(total, 0.0).astype(jnp.bfloat16).reshape(images, 1, out_cols, -1)
+    half = low_ref.shape[-1]
+    low_ref[...] = hidden[..., :half]
+    high_ref[...] = hidden[..., half:]
+
+
 def first_stage(maps, upper_row, first_weight, part):
     images, rows, width, inputs = maps.shape
     outputs = first_weight.shape[3]
     weight = first_weight[:, jnp.array([1, 2, 0])].reshape(9 * inputs, outputs)
+    shape = jax.ShapeDtypeStruct((images, rows // 2, width // 2, part), jnp.bfloat16)
+    params = pltpu.CompilerParams(dimension_semantics=("arbitrary",), vmem_limit_bytes=60 * 1024 * 1024)
+    weight_spec = pl.BlockSpec((9 * inputs, outputs), lambda n: (0, 0))
+
+    def cost(out_rows):
+        return pl.CostEstimate(
+            flops=2 * images * out_rows * (width // 2) * 9 * inputs * outputs,
+            transcendentals=0,
+            bytes_accessed=images * out_rows * 2 * width * inputs * 2 + images * out_rows * (width // 2) * outputs * 2,
+        )
+
     out_block = pl.BlockSpec((None, rows // 2, width // 2, part), lambda n: (n, 0, 0, 0))
-    shape = jax.ShapeDtypeStruct((images, rows // 2, width // 2, part), jnp.bfloat16)
-    return pl.pallas_call(
+    low, high = pl.pallas_call(
         first_kernel,
         grid=(images,),
-        in_specs=[
-            pl.BlockSpec((None, rows, width, inputs), lambda n: (n, 0, 0, 0)),
-            pl.BlockSpec((None, 1, width, inputs), lambda n: (n, 0, 0, 0)),
-            pl.BlockSpec((9 * inputs, outputs), lambda n: (0, 0)),
-        ],
+        in_specs=[pl.BlockSpec((None, rows, width, inputs), lambda n: (n, 0, 0, 0)), weight_spec],
         out_specs=[out_block, out_block],
         out_shape=[shape, shape],
         scratch_shapes=[pltpu.VMEM((rows + 1, width, inputs), jnp.float32)],
-        compiler_params=pltpu.CompilerParams(
-            dimension_semantics=("arbitrary",), vmem_limit_bytes=60 * 1024 * 1024
-        ),
-        cost_estimate=pl.CostEstimate(
-            flops=2 * images * (rows // 2) * (width // 2) * 9 * inputs * outputs,
-            transcendentals=0,
-            bytes_accessed=maps.size * 2 + images * (rows // 2) * (width // 2) * outputs * 2,
-        ),
-    )(maps, upper_row, weight)
+        compiler_params=params,
+        cost_estimate=cost(rows // 2),
+    )(maps, weight)
+    row_block = pl.BlockSpec((images, 1, width // 2, part), lambda n: (0, 0, 0, 0))
+    anywhere = pl.BlockSpec(memory_space=pl.ANY)
+    return pl.pallas_call(
+        first_row_kernel,
+        grid=(1,),
+        in_specs=[
+            pl.BlockSpec((images, 2, width, inputs), lambda n: (0, 0, 0, 0)),
+            pl.BlockSpec((images, 1, width, inputs), lambda n: (0, 0, 0, 0)),
+            weight_spec,
+            anywhere,
+            anywhere,
+        ],
+        out_specs=[row_block, row_block],
+        out_shape=[shape, shape],
+        scratch_shapes=[pltpu.VMEM((images, 3, width, inputs), jnp.float32)],
+        input_output_aliases={3: 0, 4: 1},
+        compiler_params=params,
+        cost_estimate=cost(1),
+    )(maps, upper_row, weight, low, high)
 
 
 def second_kernel(*refs, rows, carry):

time: 183 us -> 180 us (0.984)
  waiting for transfers between devices: 41.5 us -> 38.1 us
  Pallas kernels: 45.1 us -> 47.5 us
    ppermute x1, waiting for transfers between devices: 3.38 us -> 0.01 us  [shifted_2(): return lax.ppermute(shard, axis, pairs)]
    pallas_call x0 -> x1, Pallas kernels: none -> 2.52 us  [first_stage(): pl.pallas_call(first_row_kernel, grid=(1,), in_specs=[pl.BlockSpec((image...]
  transfers between devices with their start and end apart: 12 -> 12, of which waited for: 10 -> 9; matrix products, arithmetic and copies ran while one was open for 10% -> 10% of each run, Pallas kernels for 19% -> 25%
where the time goes in v16:
time: 180 us
  blocking collectives  53 us (29%)
  Pallas kernels  47.5 us (26%)
  waiting for transfers between devices  38.1 us (21%)
  starting transfers between devices  17.9 us (10%)
  local copies, waits for them, and re-layouts  14.3 us (8%)
  other arithmetic  8.05 us (4%)
    all_to_all x1, blocking collectives, local(): lax.all_to_all(local_hidden.reshape(tiles, owned, half_rows, width // 2,...  53 us
    pallas_call x2, Pallas kernels, second_stage(): pl.pallas_call(functools.partial(second_kernel, rows=rows, carry=prev is...  34 us
    all_to_all x1, waiting for transfers between devices, local(): lax.all_to_all(local_hidden.reshape(tiles, owned, half_rows, width // 2,...  21.5 us
    ppermute x10, waiting for transfers between devices, halving_reduce_scatter(): buf = keep + lax.ppermute(send, axes, pairs)  16.6 us
    pallas_call x1, Pallas kernels, first_stage(): pl.pallas_call(first_kernel, grid=(images,), in_specs=[pl.BlockSpec((None...  11 us
    ppermute x10, starting transfers between devices, halving_reduce_scatter(): buf = keep + lax.ppermute(send, axes, pairs)  9.45 us
    another operation x2, other arithmetic, second_stage(): jnp.stack([shift_cols_right(row_padded), row_padded, shift_cols_left(row_...  6.48 us
    ppermute x1, starting transfers between devices, shifted_2(): return lax.ppermute(shard, axis, pairs)  4.86 us
  transfers between devices with their start and end apart: 12, of which 9 were waited for; matrix products, arithmetic and copies ran while one was open for 10% of the time, Pallas kernels for 25%

profile of v16, /device:TPU:0, one launch (start us, length us, event | category | flops | bytes accessed | tf_op | source)
XLA Modules:
  0.0 179.8 jit_solution(5395638157155610191)
XLA Ops:
  0.6 0.0 copy-start
  0.6 1.0 slice.21
  1.7 4.9 %collective-permute-start = (bf16[8,1,128,128]{3,2,1,0:T(8,128)(2,1)S(1)}, bf16[8,1,128,128]{3,2,1,0:T(8,128)(2,1)S(1)}, u32[]{:S(2)}, u32[]{:S(2)}) collective-permute-start(bf16[8,1,128,128]{3,2,1,0:T(8,128)(2,1)S(1)} %slice.21), channel_id=1, source_target_pairs={{0,1},{1,2},{2,3},{3,4},{4,5},{5,6},{6,7},{8,9},{9,10},{10,11},{11... | collective-permute-start | bytes 786440 | tf_op jit(solution)/shard_map/ppermute | solution.py:14
  6.6 0.7 pad_clamp_fusion
  7.2 0.6 gather_fusion
  7.8 0.9 copy.10
  8.7 11.0 %shard_map.68 = (bf16[8,16,64,128]{3,2,1,0:T(8,128)(2,1)}, bf16[8,16,64,128]{3,2,1,0:T(8,128)(2,1)}) custom-call(bf16[8,32,128,128]{3,2,1,0:T(8,128)(2,1)} %x_ref.3, bf16[1152,256]{1,0:T(8,128)(2,1)} %bitcast.76), custom_call_target="tpu_custom_call" | custom-call | flops 4831838208 | bytes 12582912 | tf_op jit(solution)/shard_map/pallas_call | solution.py:108
  19.7 0.0 collective-permute-done.up_ref
  19.7 0.7 copy-done.6
  20.4 2.5 %shard_map.69 = (bf16[8,16,64,128]{3,2,1,0:T(8,128)(2,1)}, bf16[8,16,64,128]{3,2,1,0:T(8,128)(2,1)}) custom-call(bf16[8,32,128,128]{3,2,1,0:T(8,128)(2,1)} %x_ref.3, bf16[8,1,128,128]{3,2,1,0:T(8,128)(2,1)} %copy-done.6, bf16[1152,256]{1,0:T(8,128)(2,1)} %bitcast.77, ...), custom_call_target="tpu_custom_call", output_to_operand_aliasing={{0}: (3, {}), {1}: (4, {})} | custom-call | flops 301989888 | bytes 786432 | tf_op jit(solution)/shard_map/pallas_call | solution.py:120
  23.0 53.0 %all_to_all.21 = bf16[8,1,16,64,128]{4,3,2,1,0:T(8,128)(2,1)} all-to-all(bf16[8,1,16,64,128]{4,3,2,1,0:T(8,128)(2,1)} %bitcast.74), channel_id=1, replica_groups=mesh['group'=4,'tile'=8] {'tile'}, dimensions={0} | all-to-all | bytes 4194304 | tf_op jit(solution)/shard_map/all_to_all | solution.py:254
  76.0 3.6 %all-to-all-start = ((bf16[8,1,16,64,128]{4,3,2,1,0:T(8,128)(2,1)}), bf16[8,1,16,64,128]{4,3,2,1,0:T(8,128)(2,1)S(1)}, u32[]{:S(2)}, u32[]{:S(2)}) async-start(bf16[8,1,16,64,128]{4,3,2,1,0:T(8,128)(2,1)} %bitcast.75), calls=%async_computation | async-start | bytes 4194304 | tf_op jit(solution)/shard_map/all_to_all | solution.py:254
  79.6 2.5 %fusion = (bf16[3,3,128,256]{3,2,1,0:T(8,128)(2,1)}, bf16[3,3,128,256]{3,2,1,0:T(8,128)(2,1)}) fusion(bf16[3,3,256,256]{3,2,1,0:T(8,128)(2,1)} %param.7), kind=kLoop, calls=%fused_computation.35 | loop fusion | bytes 2359296 | tf_op jit(solution)/shard_map/slice | solution.py:266
  82.1 0.4 pad_bitcast_fusion.5
  82.5 1.4 pad_slice_fusion.3
  84.0 1.8 pad_bitcast_fusion.2
  85.8 3.2 %pad_maximum_fusion.refs_0_ = bf16[1,3,130,64,128]{4,3,2,1,0:T(8,128)(2,1)} fusion(bf16[1,1,130,64,128]{4,3,2,1,0:T(8,128)(2,1)S(1)} %get-tuple-element.28, bf16[1,1,130,64,128]{4,3,2,1,0:T(8,128)(2,1)S(1)} %pad_bitcast_fusion.5, bf16[1,1,130,64,128]{4,3,2,1,0:T(8,128)(2,1)S(1)} %get-tuple-element.29), kind=kLoop, calls=%fused_computation.1 | loop fusion | flops 6389760 | bytes 12779520 | tf_op jit(solution)/shard_map/stack | solution.py:180
  89.0 16.8 %shard_map.70 = (f32[1,128,64,256]{3,2,1,0:T(8,128)}, f32[1,256,1152]{2,1,0:T(8,128)}) custom-call(bf16[1,3,130,64,128]{4,3,2,1,0:T(8,128)(2,1)} %pad_maximum_fusion.refs_0_, bf16[1152,256]{1,0:T(8,128)(2,1)} %bitcast.84, bf16[1,8192,256]{2,1,0:T(8,128)(2,1)} %bitcast.87), custom_call_target="tpu_custom_call" | custom-call | flops 9663676416 | bytes 26345472 | tf_op jit(solution)/shard_map/pallas_call | solution.py:193
  105.8 21.5 %all-to-all-done = bf16[8,1,16,64,128]{4,3,2,1,0:T(8,128)(2,1)S(1)} async-done(((bf16[8,1,16,64,128]{4,3,2,1,0:T(8,128)(2,1)}), bf16[8,1,16,64,128]{4,3,2,1,0:T(8,128)(2,1)S(1)}, u32[]{:S(2)}, u32[]{:S(2)}) %all-to-all-start) | async-done | bytes 2097184 | tf_op jit(solution)/shard_map/all_to_all | solution.py:254
  127.3 0.4 pad_bitcast_fusion.4
  127.7 1.4 pad_slice_fusion.1
  129.2 0.1 collective-permute-start.1
  129.3 1.3 pad_bitcast_fusion.1
  130.5 0.4 pad_bitcast_fusion
  131.0 3.2 %pad_maximum_fusion.1.refs_0_ = bf16[1,3,130,64,128]{4,3,2,1,0:T(8,128)(2,1)} fusion(bf16[1,1,130,64,128]{4,3,2,1,0:T(8,128)(2,1)S(1)} %pad_bitcast_fusion, bf16[1,1,130,64,128]{4,3,2,1,0:T(8,128)(2,1)S(1)} %pad_bitcast_fusion.4, bf16[1,1,130,64,128]{4,3,2,1,0:T(8,128)(2,1)S(1)} %pad_bitcast_fusion.1), kind=kLoop, calls=%fused_computation.2 | loop fusion | flops 6389760 | bytes 12779520 | tf_op jit(solution)/shard_map/stack | solution.py:180
  134.2 17.2 %shard_map.71 = (bf16[1,128,64,256]{3,2,1,0:T(8,128)(2,1)}, f32[1,256,1152]{2,1,0:T(8,128)}) custom-call(bf16[1,3,130,64,128]{4,3,2,1,0:T(8,128)(2,1)} %pad_maximum_fusion.1.refs_0_, bf16[1152,256]{1,0:T(8,128)(2,1)} %bitcast.83, bf16[1,8192,256]{2,1,0:T(8,128)(2,1)} %bitcast.88, f32[1,128,64,256]{3,2,1,0:T(8,128)} %get-tuple-element.18.refs_3_), custom_call_target="tpu_custom_call" | custom-call | flops 9663676416 | bytes 26345472 | tf_op jit(solution)/shard_map/pallas_call | solution.py:193
  151.4 1.2 dynamic-slice_bitcast_fusion
  152.6 0.6 collective-permute-start.6
  153.2 0.1 bitcast_add_fusion.1
  153.3 1.6 collective-permute-start.2
  154.9 0.1 bitcast_add_fusion
  155.0 0.0 copy-start.1
  155.0 1.5 collective-permute-start.7
  156.5 5.8 %collective-permute-done.2 = f32[2,2,2,8,1152]{4,3,2,1,0:T(8,128)S(1)} collective-permute-done((f32[2,2,2,8,1152]{4,3,2,1,0:T(8,128)S(1)}, f32[2,2,2,8,1152]{4,3,2,1,0:T(8,128)S(1)}, u32[]{:S(2)}, u32[]{:S(2)}) %collective-permute-start.2) | collective-permute-done | bytes 294944 | tf_op jit(solution)/shard_map/ppermute | solution.py:233
  162.4 1.5 collective-permute-start.3
  163.9 0.4 collective-permute-done.7
  164.4 1.6 collective-permute-start.8
  166.0 1.6 collective-permute-done.3
  167.6 0.1 collective-permute-start.4
  167.7 2.0 %collective-permute-done.8 = f32[2,2,8,1152]{3,2,1,0:T(8,128)S(1)} collective-permute-done((f32[2,2,8,1152]{3,2,1,0:T(8,128)S(1)}, f32[2,2,8,1152]{3,2,1,0:T(8,128)S(1)}, u32[]{:S(2)}, u32[]{:S(2)}) %collective-permute-start.8) | collective-permute-done | bytes 147488 | tf_op jit(solution)/shard_map/ppermute | solution.py:233
  169.7 0.1 collective-permute-start.9
  169.9 2.7 %collective-permute-done.4 = f32[2,8,1152]{2,1,0:T(8,128)S(1)} collective-permute-done((f32[2,8,1152]{2,1,0:T(8,128)S(1)}, f32[2,8,1152]{2,1,0:T(8,128)S(1)}, u32[]{:S(2)}, u32[]{:S(2)}) %collective-permute-start.4) | collective-permute-done | bytes 73760 | tf_op jit(solution)/shard_map/ppermute | solution.py:233
  172.6 1.0 collective-permute-start.5
  173.6 0.6 collective-permute-done.9
  174.2 1.4 collective-permute-start.10
  175.7 1.9 %collective-permute-done.5 = f32[8,1152]{1,0:T(8,128)S(1)} collective-permute-done((f32[8,1152]{1,0:T(8,128)S(1)}, f32[8,1152]{1,0:T(8,128)S(1)}, u32[]{:S(2)}, u32[]{:S(2)}) %collective-permute-start.5) | collective-permute-done | bytes 36896 | tf_op jit(solution)/shard_map/ppermute | solution.py:233
  177.6 1.5 collective-permute-done.10
  179.2 0.6 pad_maximum_fusion.2
  (30 shorter events, 0.4 us)
Async XLA Ops:
  0.6 6.6 %copy-start = (bf16[3,3,128,256]{3,2,1,0:T(8,128)(2,1)S(1)}, bf16[3,3,128,256]{3,2,1,0:T(8,128)(2,1)}, u32[]{:S(2)}) copy-start(bf16[3,3,128,256]{3,2,1,0:T(8,128)(2,1)} %param.6) | copy-start | bytes 1769476
  1.7 18.0 %collective-permute-start = (bf16[8,1,128,128]{3,2,1,0:T(8,128)(2,1)S(1)}, bf16[8,1,128,128]{3,2,1,0:T(8,128)(2,1)S(1)}, u32[]{:S(2)}, u32[]{:S(2)}) collective-permute-start(bf16[8,1,128,128]{3,2,1,0:T(8,128)(2,1)S(1)} %slice.21), channel_id=1, source_target_pairs={{0,1},{1,2},{2,3},{3,4},{4,5},{5,6},{6,7},{8,9},{9,10},{10,11},{11... | collective-permute-start | bytes 786440 | tf_op jit(solution)/shard_map/ppermute | solution.py:14
  19.7 0.7 copy-start.6
  76.0 51.3 %all-to-all-start = ((bf16[8,1,16,64,128]{4,3,2,1,0:T(8,128)(2,1)}), bf16[8,1,16,64,128]{4,3,2,1,0:T(8,128)(2,1)S(1)}, u32[]{:S(2)}, u32[]{:S(2)}) async-start(bf16[8,1,16,64,128]{4,3,2,1,0:T(8,128)(2,1)} %bitcast.75), calls=%async_computation | async-start | bytes 4194304 | tf_op jit(solution)/shard_map/all_to_all | solution.py:254
  79.6 2.5 %copy-start.2 = (bf16[8,1,16,64,128]{4,3,2,1,0:T(8,128)(2,1)S(1)}, bf16[8,1,16,64,128]{4,3,2,1,0:T(8,128)(2,1)}, u32[]{:S(2)}) copy-start(bf16[8,1,16,64,128]{4,3,2,1,0:T(8,128)(2,1)} %all_to_all.21) | copy-start | bytes 6291460
  127.7 1.4 copy-start.3
  129.2 24.0 %collective-permute-start.1 = (f32[2,2,2,2,8,1152]{5,4,3,2,1,0:T(8,128)S(1)}, f32[2,2,2,2,8,1152]{5,4,3,2,1,0:T(8,128)S(1)}, u32[]{:S(2)}, u32[]{:S(2)}) collective-permute-start(f32[2,2,2,2,8,1152]{5,4,3,2,1,0:T(8,128)S(1)} %dynamic-slice_bitcast_fusion.1), channel_id=1, source_target_pairs={{0,8},{1,9},{2,10},{3,11},{4,12},{5,13},{6,14},{7,15},{8,0},{9,1},... | collective-permute-start | bytes 1769480 | tf_op jit(solution)/shard_map/ppermute | solution.py:233
  134.2 19.0 %copy-start.4 = (f32[1,256,1152]{2,1,0:T(8,128)S(1)}, f32[1,256,1152]{2,1,0:T(8,128)}, u32[]{:S(2)}) copy-start(f32[1,256,1152]{2,1,0:T(8,128)} %get-tuple-element.20) | copy-start | bytes 3538948
  151.4 3.5 %copy-start.5 = (f32[1,256,1152]{2,1,0:T(8,128)S(1)}, f32[1,256,1152]{2,1,0:T(8,128)}, u32[]{:S(2)}) copy-start(f32[1,256,1152]{2,1,0:T(8,128)} %get-tuple-element.21) | copy-start | bytes 3538948
  152.6 2.3 %collective-permute-start.6 = (f32[2,2,2,2,8,1152]{5,4,3,2,1,0:T(8,128)S(1)}, f32[2,2,2,2,8,1152]{5,4,3,2,1,0:T(8,128)S(1)}, u32[]{:S(2)}, u32[]{:S(2)}) collective-permute-start(f32[2,2,2,2,8,1152]{5,4,3,2,1,0:T(8,128)S(1)} %dynamic-slice_bitcast_fusion), channel_id=1, source_target_pairs={{0,8},{1,9},{2,10},{3,11},{4,12},{5,13},{6,14},{7,15},{8,0},{9,1},... | collective-permute-start | bytes 1769480 | tf_op jit(solution)/shard_map/ppermute | solution.py:233
  153.3 9.0 %collective-permute-start.2 = (f32[2,2,2,8,1152]{4,3,2,1,0:T(8,128)S(1)}, f32[2,2,2,8,1152]{4,3,2,1,0:T(8,128)S(1)}, u32[]{:S(2)}, u32[]{:S(2)}) collective-permute-start(f32[2,2,2,8,1152]{4,3,2,1,0:T(8,128)S(1)} %dynamic-slice_bitcast_fusion.3), channel_id=1, source_target_pairs={{0,16},{1,17},{2,18},{3,19},{4,20},{5,21},{6,22},{7,23},{8,24},{9,... | collective-permute-start | bytes 884744 | tf_op jit(solution)/shard_map/ppermute | solution.py:233
  155.0 24.8 %copy-start.1 = (bf16[3,3,128,256]{3,2,1,0:T(8,128)(2,1)S(1)}, bf16[3,3,128,256]{3,2,1,0:T(8,128)(2,1)}, u32[]{:S(2)}) copy-start(bf16[3,3,128,256]{3,2,1,0:T(8,128)(2,1)} %param.6) | copy-start | bytes 1769476
  155.0 9.3 %collective-permute-start.7 = (f32[2,2,2,8,1152]{4,3,2,1,0:T(8,128)S(1)}, f32[2,2,2,8,1152]{4,3,2,1,0:T(8,128)S(1)}, u32[]{:S(2)}, u32[]{:S(2)}) collective-permute-start(f32[2,2,2,8,1152]{4,3,2,1,0:T(8,128)S(1)} %dynamic-slice_bitcast_fusion.2), channel_id=1, source_target_pairs={{0,1},{1,0},{2,3},{3,2},{4,5},{5,4},{6,7},{7,6},{8,9},{9,8},{10,11... | collective-permute-start | bytes 884744 | tf_op jit(solution)/shard_map/ppermute | solution.py:233
  162.4 5.2 %collective-permute-start.3 = (f32[2,2,8,1152]{3,2,1,0:T(8,128)S(1)}, f32[2,2,8,1152]{3,2,1,0:T(8,128)S(1)}, u32[]{:S(2)}, u32[]{:S(2)}) collective-permute-start(f32[2,2,8,1152]{3,2,1,0:T(8,128)S(1)} %dynamic-slice_bitcast_fusion.5), channel_id=1, source_target_pairs={{0,1},{1,0},{2,3},{3,2},{4,5},{5,4},{6,7},{7,6},{8,9},{9,8},{10,11... | collective-permute-start | bytes 442376 | tf_op jit(solution)/shard_map/ppermute | solution.py:233
  164.4 5.3 %collective-permute-start.8 = (f32[2,2,8,1152]{3,2,1,0:T(8,128)S(1)}, f32[2,2,8,1152]{3,2,1,0:T(8,128)S(1)}, u32[]{:S(2)}, u32[]{:S(2)}) collective-permute-start(f32[2,2,8,1152]{3,2,1,0:T(8,128)S(1)} %dynamic-slice_bitcast_fusion.4), channel_id=1, source_target_pairs={{0,16},{1,17},{2,18},{3,19},{4,20},{5,21},{6,22},{7,23},{8,24},{9,... | collective-permute-start | bytes 442376 | tf_op jit(solution)/shard_map/ppermute | solution.py:233
  167.6 4.9 %collective-permute-start.4 = (f32[2,8,1152]{2,1,0:T(8,128)S(1)}, f32[2,8,1152]{2,1,0:T(8,128)S(1)}, u32[]{:S(2)}, u32[]{:S(2)}) collective-permute-start(f32[2,8,1152]{2,1,0:T(8,128)S(1)} %dynamic-slice_bitcast_fusion.7), channel_id=1, source_target_pairs={{0,2},{1,3},{2,0},{3,1},{4,6},{5,7},{6,4},{7,5},{8,10},{9,11},{10,... | collective-permute-start | bytes 221192 | tf_op jit(solution)/shard_map/ppermute | solution.py:233
  169.7 4.5 %collective-permute-start.9 = (f32[2,8,1152]{2,1,0:T(8,128)S(1)}, f32[2,8,1152]{2,1,0:T(8,128)S(1)}, u32[]{:S(2)}, u32[]{:S(2)}) collective-permute-start(f32[2,8,1152]{2,1,0:T(8,128)S(1)} %dynamic-slice_bitcast_fusion.6), channel_id=1, source_target_pairs={{0,2},{1,3},{2,0},{3,1},{4,6},{5,7},{6,4},{7,5},{8,10},{9,11},{10,... | collective-permute-start | bytes 221192 | tf_op jit(solution)/shard_map/ppermute | solution.py:233
  172.6 5.0 %collective-permute-start.5 = (f32[8,1152]{1,0:T(8,128)S(1)}, f32[8,1152]{1,0:T(8,128)S(1)}, u32[]{:S(2)}, u32[]{:S(2)}) collective-permute-start(f32[8,1152]{1,0:T(8,128)S(1)} %dynamic-slice_bitcast_fusion.9), channel_id=1, source_target_pairs={{0,4},{1,5},{2,6},{3,7},{4,0},{5,1},{6,2},{7,3},{8,12},{9,13},{10,... | collective-permute-start | bytes 110600 | tf_op jit(solution)/shard_map/ppermute | solution.py:233
  174.2 4.9 %collective-permute-start.10 = (f32[8,1152]{1,0:T(8,128)S(1)}, f32[8,1152]{1,0:T(8,128)S(1)}, u32[]{:S(2)}, u32[]{:S(2)}) collective-permute-start(f32[8,1152]{1,0:T(8,128)S(1)} %dynamic-slice_bitcast_fusion.8), channel_id=1, source_target_pairs={{0,4},{1,5},{2,6},{3,7},{4,0},{5,1},{6,2},{7,3},{8,12},{9,13},{10,... | collective-permute-start | bytes 110600 | tf_op jit(solution)/shard_map/ppermute | solution.py:233

commit v17 on v16

--- a/solution.py
+++ b/solution.py
@@ -56,7 +56,7 @@
         even = scratch[pl.ds(tap_row, out_rows, stride=2), pl.ds(0, out_cols, stride=2), :]
         odd = scratch[pl.ds(tap_row, out_rows, stride=2), pl.ds(1, out_cols, stride=2), :]
         left = jnp.where(first_col, 0.0, pltpu.roll(odd, 1, 1))
-        pieces += [even, odd, left]
+        pieces += [left, even, odd]
     patches = jnp.concatenate(
         [p.astype(jnp.bfloat16).reshape(out_rows * out_cols, inputs) for p in pieces], axis=-1
     )
@@ -78,7 +78,7 @@
         even = scratch[:, tap_row, pl.ds(0, out_cols, stride=2), :]
         odd = scratch[:, tap_row, pl.ds(1, out_cols, stride=2), :]
         left = jnp.where(first_col, 0.0, pltpu.roll(odd, 1, 1))
-        pieces += [even, odd, left]
+        pieces += [left, even, odd]
     patches = jnp.concatenate(
         [p.astype(jnp.bfloat16).reshape(images * out_cols, inputs) for p in pieces], axis=-1
     )
@@ -92,7 +92,7 @@
 def first_stage(maps, upper_row, first_weight, part):
     images, rows, width, inputs = maps.shape
     outputs = first_weight.shape[3]
-    weight = first_weight[:, jnp.array([1, 2, 0])].reshape(9 * inputs, outputs)
+    weight = first_weight.reshape(9 * inputs, outputs)
     shape = jax.ShapeDtypeStruct((images, rows // 2, width // 2, part), jnp.bfloat16)
     params = pltpu.CompilerParams(dimension_semantics=("arbitrary",), vmem_limit_bytes=60 * 1024 * 1024)
     weight_spec = pl.BlockSpec((9 * inputs, outputs), lambda n: (0, 0))

time: 180 us -> 178 us (0.989)
  local copies, waits for them, and re-layouts: 14.3 us -> 12.3 us
  transfers between devices with their start and end apart: 12 -> 12, of which waited for: 9 -> 9; matrix products, arithmetic and copies ran while one was open for 10% -> 8% of each run, Pallas kernels for 25% -> 25%
where the time goes in v17:
time: 178 us
  blocking collectives  53 us (30%)
  Pallas kernels  47.4 us (27%)
  waiting for transfers between devices  38.6 us (22%)
  starting transfers between devices  18 us (10%)
  local copies, waits for them, and re-layouts  12.3 us (7%)
  other arithmetic  7.39 us (4%)
    all_to_all x1, blocking collectives, local(): lax.all_to_all(local_hidden.reshape(tiles, owned, half_rows, width // 2,...  53 us
    pallas_call x2, Pallas kernels, second_stage(): pl.pallas_call(functools.partial(second_kernel, rows=rows, carry=prev is...  33.8 us
    all_to_all x1, waiting for transfers between devices, local(): lax.all_to_all(local_hidden.reshape(tiles, owned, half_rows, width // 2,...  22 us
    ppermute x10, waiting for transfers between devices, halving_reduce_scatter(): buf = keep + lax.ppermute(send, axes, pairs)  16.6 us
    pallas_call x1, Pallas kernels, first_stage(): pl.pallas_call(first_kernel, grid=(images,), in_specs=[pl.BlockSpec((None...  11 us
    ppermute x10, starting transfers between devices, halving_reduce_scatter(): buf = keep + lax.ppermute(send, axes, pairs)  9.44 us
    another operation x2, other arithmetic, second_stage(): jnp.stack([shift_cols_right(row_padded), row_padded, shift_cols_left(row_...  6.48 us
    ppermute x1, starting transfers between devices, shifted_2(): return lax.ppermute(shard, axis, pairs)  4.86 us
  transfers between devices with their start and end apart: 12, of which 9 were waited for; matrix products, arithmetic and copies ran while one was open for 8% of the time, Pallas kernels for 25%

profile of v17, /device:TPU:0, one launch (start us, length us, event | category | flops | bytes accessed | tf_op | source)
XLA Modules:
  0.0 177.7 jit_solution(17656920737106024341)
XLA Ops:
  0.6 1.0 slice.21
  1.6 4.9 %collective-permute-start = (bf16[8,1,128,128]{3,2,1,0:T(8,128)(2,1)S(1)}, bf16[8,1,128,128]{3,2,1,0:T(8,128)(2,1)S(1)}, u32[]{:S(2)}, u32[]{:S(2)}) collective-permute-start(bf16[8,1,128,128]{3,2,1,0:T(8,128)(2,1)S(1)} %slice.21), channel_id=1, source_target_pairs={{0,1},{1,2},{2,3},{3,4},{4,5},{5,6},{6,7},{8,9},{9,10},{10,11},{11... | collective-permute-start | bytes 786440 | tf_op jit(solution)/shard_map/ppermute | solution.py:14
  6.5 11.0 %shard_map.59 = (bf16[8,16,64,128]{3,2,1,0:T(8,128)(2,1)}, bf16[8,16,64,128]{3,2,1,0:T(8,128)(2,1)}) custom-call(bf16[8,32,128,128]{3,2,1,0:T(8,128)(2,1)} %x_ref.3, bf16[1152,256]{1,0:T(8,128)(2,1)} %bitcast.79), custom_call_target="tpu_custom_call" | custom-call | flops 4831838208 | bytes 12582912 | tf_op jit(solution)/shard_map/pallas_call | solution.py:108
  17.5 0.0 collective-permute-done.up_ref
  17.5 0.7 copy-done.4
  18.2 2.6 %shard_map.60 = (bf16[8,16,64,128]{3,2,1,0:T(8,128)(2,1)}, bf16[8,16,64,128]{3,2,1,0:T(8,128)(2,1)}) custom-call(bf16[8,32,128,128]{3,2,1,0:T(8,128)(2,1)} %x_ref.3, bf16[8,1,128,128]{3,2,1,0:T(8,128)(2,1)} %copy-done.4, bf16[1152,256]{1,0:T(8,128)(2,1)} %bitcast.80, ...), custom_call_target="tpu_custom_call", output_to_operand_aliasing={{0}: (3, {}), {1}: (4, {})} | custom-call | flops 301989888 | bytes 786432 | tf_op jit(solution)/shard_map/pallas_call | solution.py:120
  20.8 53.0 %all_to_all.21 = bf16[8,1,16,64,128]{4,3,2,1,0:T(8,128)(2,1)} all-to-all(bf16[8,1,16,64,128]{4,3,2,1,0:T(8,128)(2,1)} %bitcast.73), channel_id=1, replica_groups=mesh['group'=4,'tile'=8] {'tile'}, dimensions={0} | all-to-all | bytes 4194304 | tf_op jit(solution)/shard_map/all_to_all | solution.py:254
  73.8 3.7 %all-to-all-start = ((bf16[8,1,16,64,128]{4,3,2,1,0:T(8,128)(2,1)}), bf16[8,1,16,64,128]{4,3,2,1,0:T(8,128)(2,1)S(1)}, u32[]{:S(2)}, u32[]{:S(2)}) async-start(bf16[8,1,16,64,128]{4,3,2,1,0:T(8,128)(2,1)} %bitcast.74), calls=%async_computation | async-start | bytes 4194304 | tf_op jit(solution)/shard_map/all_to_all | solution.py:254
  77.6 1.1 fusion
  78.7 0.9 copy-done
  79.6 0.4 pad_bitcast_fusion.5
  80.0 1.4 pad_slice_fusion.3
  81.5 1.8 %pad_bitcast_fusion.2 = (bf16[1,1,130,64,128]{4,3,2,1,0:T(8,128)(2,1)S(1)}, bf16[1,1,130,64,128]{4,3,2,1,0:T(8,128)(2,1)S(1)}) fusion(bf16[1,130,63,128]{3,2,1,0:T(8,128)(2,1)S(1)} %get-tuple-element.25, bf16[1,130,63,128]{3,2,1,0:T(8,128)(2,1)S(1)} %get-tuple-element.24), kind=kLoop, calls=%fused_computation.4 | loop fusion | bytes 8453120 | tf_op jit(solution)/shard_map/stack | solution.py:180
  83.2 3.2 %pad_maximum_fusion.refs_0_ = bf16[1,3,130,64,128]{4,3,2,1,0:T(8,128)(2,1)} fusion(bf16[1,1,130,64,128]{4,3,2,1,0:T(8,128)(2,1)S(1)} %get-tuple-element.28, bf16[1,1,130,64,128]{4,3,2,1,0:T(8,128)(2,1)S(1)} %pad_bitcast_fusion.5, bf16[1,1,130,64,128]{4,3,2,1,0:T(8,128)(2,1)S(1)} %get-tuple-element.29), kind=kLoop, calls=%fused_computation | loop fusion | flops 6389760 | bytes 12779520 | tf_op jit(solution)/shard_map/stack | solution.py:180
  86.5 16.7 %shard_map.61 = (f32[1,128,64,256]{3,2,1,0:T(8,128)}, f32[1,256,1152]{2,1,0:T(8,128)}) custom-call(bf16[1,3,130,64,128]{4,3,2,1,0:T(8,128)(2,1)} %pad_maximum_fusion.refs_0_, bf16[1152,256]{1,0:T(8,128)(2,1)} %bitcast.82, bf16[1,8192,256]{2,1,0:T(8,128)(2,1)} %bitcast.85), custom_call_target="tpu_custom_call" | custom-call | flops 9663676416 | bytes 26345472 | tf_op jit(solution)/shard_map/pallas_call | solution.py:193
  103.2 22.0 %all-to-all-done = bf16[8,1,16,64,128]{4,3,2,1,0:T(8,128)(2,1)S(1)} async-done(((bf16[8,1,16,64,128]{4,3,2,1,0:T(8,128)(2,1)}), bf16[8,1,16,64,128]{4,3,2,1,0:T(8,128)(2,1)S(1)}, u32[]{:S(2)}, u32[]{:S(2)}) %all-to-all-start) | async-done | bytes 2097184 | tf_op jit(solution)/shard_map/all_to_all | solution.py:254
  125.2 0.4 pad_bitcast_fusion.4
  125.7 0.0 copy-start.2
  125.7 1.4 pad_slice_fusion.1
  127.1 0.0 copy-done.2
  127.1 0.1 collective-permute-start.1
  127.2 1.3 pad_bitcast_fusion.1
  128.5 0.4 pad_bitcast_fusion
  128.9 3.2 %pad_maximum_fusion.1.refs_0_ = bf16[1,3,130,64,128]{4,3,2,1,0:T(8,128)(2,1)} fusion(bf16[1,1,130,64,128]{4,3,2,1,0:T(8,128)(2,1)S(1)} %pad_bitcast_fusion, bf16[1,1,130,64,128]{4,3,2,1,0:T(8,128)(2,1)S(1)} %pad_bitcast_fusion.4, bf16[1,1,130,64,128]{4,3,2,1,0:T(8,128)(2,1)S(1)} %pad_bitcast_fusion.1), kind=kLoop, calls=%fused_computation.1 | loop fusion | flops 6389760 | bytes 12779520 | tf_op jit(solution)/shard_map/stack | solution.py:180
  132.2 17.1 %shard_map.62 = (bf16[1,128,64,256]{3,2,1,0:T(8,128)(2,1)}, f32[1,256,1152]{2,1,0:T(8,128)}) custom-call(bf16[1,3,130,64,128]{4,3,2,1,0:T(8,128)(2,1)} %pad_maximum_fusion.1.refs_0_, bf16[1152,256]{1,0:T(8,128)(2,1)} %bitcast.81, bf16[1,8192,256]{2,1,0:T(8,128)(2,1)} %bitcast.86, f32[1,128,64,256]{3,2,1,0:T(8,128)} %get-tuple-element.18.refs_3_), custom_call_target="tpu_custom_call" | custom-call | flops 9663676416 | bytes 26345472 | tf_op jit(solution)/shard_map/pallas_call | solution.py:193
  149.3 1.2 dynamic-slice_bitcast_fusion
  150.5 0.6 collective-permute-start.6
  151.1 0.0 collective-permute-done.1
  151.1 0.1 bitcast_add_fusion.1
  151.2 1.6 collective-permute-start.2
  152.8 0.0 collective-permute-done.6
  152.8 0.1 bitcast_add_fusion
  152.9 1.5 collective-permute-start.7
  154.4 5.8 %collective-permute-done.2 = f32[2,2,2,8,1152]{4,3,2,1,0:T(8,128)S(1)} collective-permute-done((f32[2,2,2,8,1152]{4,3,2,1,0:T(8,128)S(1)}, f32[2,2,2,8,1152]{4,3,2,1,0:T(8,128)S(1)}, u32[]{:S(2)}, u32[]{:S(2)}) %collective-permute-start.2) | collective-permute-done | bytes 294944 | tf_op jit(solution)/shard_map/ppermute | solution.py:233
  160.2 1.5 collective-permute-start.3
  161.7 0.4 collective-permute-done.7
  162.2 1.6 collective-permute-start.8
  163.8 1.6 collective-permute-done.3
  165.5 0.1 collective-permute-start.4
  165.6 2.0 %collective-permute-done.8 = f32[2,2,8,1152]{3,2,1,0:T(8,128)S(1)} collective-permute-done((f32[2,2,8,1152]{3,2,1,0:T(8,128)S(1)}, f32[2,2,8,1152]{3,2,1,0:T(8,128)S(1)}, u32[]{:S(2)}, u32[]{:S(2)}) %collective-permute-start.8) | collective-permute-done | bytes 147488 | tf_op jit(solution)/shard_map/ppermute | solution.py:233
  167.6 0.1 collective-permute-start.9
  167.7 2.7 %collective-permute-done.4 = f32[2,8,1152]{2,1,0:T(8,128)S(1)} collective-permute-done((f32[2,8,1152]{2,1,0:T(8,128)S(1)}, f32[2,8,1152]{2,1,0:T(8,128)S(1)}, u32[]{:S(2)}, u32[]{:S(2)}) %collective-permute-start.4) | collective-permute-done | bytes 73760 | tf_op jit(solution)/shard_map/ppermute | solution.py:233
  170.4 1.0 collective-permute-start.5
  171.4 0.7 collective-permute-done.9
  172.1 1.4 collective-permute-start.10
  173.5 1.9 %collective-permute-done.5 = f32[8,1152]{1,0:T(8,128)S(1)} collective-permute-done((f32[8,1152]{1,0:T(8,128)S(1)}, f32[8,1152]{1,0:T(8,128)S(1)}, u32[]{:S(2)}, u32[]{:S(2)}) %collective-permute-start.5) | collective-permute-done | bytes 36896 | tf_op jit(solution)/shard_map/ppermute | solution.py:233
  175.5 1.6 collective-permute-done.10
  177.0 0.6 pad_maximum_fusion.2
  (23 shorter events, 0.4 us)
Async XLA Ops:
  1.6 15.9 %collective-permute-start = (bf16[8,1,128,128]{3,2,1,0:T(8,128)(2,1)S(1)}, bf16[8,1,128,128]{3,2,1,0:T(8,128)(2,1)S(1)}, u32[]{:S(2)}, u32[]{:S(2)}) collective-permute-start(bf16[8,1,128,128]{3,2,1,0:T(8,128)(2,1)S(1)} %slice.21), channel_id=1, source_target_pairs={{0,1},{1,2},{2,3},{3,4},{4,5},{5,6},{6,7},{8,9},{9,10},{10,11},{11... | collective-permute-start | bytes 786440 | tf_op jit(solution)/shard_map/ppermute | solution.py:14
  17.5 0.7 copy-start.4
  73.8 3.8 %copy-start.1 = (bf16[3,3,256,256]{3,2,1,0:T(8,128)(2,1)S(1)}, bf16[3,3,256,256]{3,2,1,0:T(8,128)(2,1)}, u32[]{:S(2)}) copy-start(bf16[3,3,256,256]{3,2,1,0:T(8,128)(2,1)} %param.6) | copy-start | bytes 3538948
  73.8 51.4 %all-to-all-start = ((bf16[8,1,16,64,128]{4,3,2,1,0:T(8,128)(2,1)}), bf16[8,1,16,64,128]{4,3,2,1,0:T(8,128)(2,1)S(1)}, u32[]{:S(2)}, u32[]{:S(2)}) async-start(bf16[8,1,16,64,128]{4,3,2,1,0:T(8,128)(2,1)} %bitcast.74), calls=%async_computation | async-start | bytes 4194304 | tf_op jit(solution)/shard_map/all_to_all | solution.py:254
  77.6 2.0 %copy-start = (bf16[8,1,16,64,128]{4,3,2,1,0:T(8,128)(2,1)S(1)}, bf16[8,1,16,64,128]{4,3,2,1,0:T(8,128)(2,1)}, u32[]{:S(2)}) copy-start(bf16[8,1,16,64,128]{4,3,2,1,0:T(8,128)(2,1)} %all_to_all.21) | copy-start | bytes 6291460
  125.7 1.4 copy-start.2
  127.1 23.9 %collective-permute-start.1 = (f32[2,2,2,2,8,1152]{5,4,3,2,1,0:T(8,128)S(1)}, f32[2,2,2,2,8,1152]{5,4,3,2,1,0:T(8,128)S(1)}, u32[]{:S(2)}, u32[]{:S(2)}) collective-permute-start(f32[2,2,2,2,8,1152]{5,4,3,2,1,0:T(8,128)S(1)} %dynamic-slice_bitcast_fusion.1), channel_id=1, source_target_pairs={{0,8},{1,9},{2,10},{3,11},{4,12},{5,13},{6,14},{7,15},{8,0},{9,1},... | collective-permute-start | bytes 1769480 | tf_op jit(solution)/shard_map/ppermute | solution.py:233
  149.3 3.5 %copy-start.3 = (f32[1,256,1152]{2,1,0:T(8,128)S(1)}, f32[1,256,1152]{2,1,0:T(8,128)}, u32[]{:S(2)}) copy-start(f32[1,256,1152]{2,1,0:T(8,128)} %get-tuple-element.21) | copy-start | bytes 3538948
  150.5 2.3 %collective-permute-start.6 = (f32[2,2,2,2,8,1152]{5,4,3,2,1,0:T(8,128)S(1)}, f32[2,2,2,2,8,1152]{5,4,3,2,1,0:T(8,128)S(1)}, u32[]{:S(2)}, u32[]{:S(2)}) collective-permute-start(f32[2,2,2,2,8,1152]{5,4,3,2,1,0:T(8,128)S(1)} %dynamic-slice_bitcast_fusion), channel_id=1, source_target_pairs={{0,8},{1,9},{2,10},{3,11},{4,12},{5,13},{6,14},{7,15},{8,0},{9,1},... | collective-permute-start | bytes 1769480 | tf_op jit(solution)/shard_map/ppermute | solution.py:233
  151.2 9.0 %collective-permute-start.2 = (f32[2,2,2,8,1152]{4,3,2,1,0:T(8,128)S(1)}, f32[2,2,2,8,1152]{4,3,2,1,0:T(8,128)S(1)}, u32[]{:S(2)}, u32[]{:S(2)}) collective-permute-start(f32[2,2,2,8,1152]{4,3,2,1,0:T(8,128)S(1)} %dynamic-slice_bitcast_fusion.3), channel_id=1, source_target_pairs={{0,16},{1,17},{2,18},{3,19},{4,20},{5,21},{6,22},{7,23},{8,24},{9,... | collective-permute-start | bytes 884744 | tf_op jit(solution)/shard_map/ppermute | solution.py:233
  152.9 9.3 %collective-permute-start.7 = (f32[2,2,2,8,1152]{4,3,2,1,0:T(8,128)S(1)}, f32[2,2,2,8,1152]{4,3,2,1,0:T(8,128)S(1)}, u32[]{:S(2)}, u32[]{:S(2)}) collective-permute-start(f32[2,2,2,8,1152]{4,3,2,1,0:T(8,128)S(1)} %dynamic-slice_bitcast_fusion.2), channel_id=1, source_target_pairs={{0,1},{1,0},{2,3},{3,2},{4,5},{5,4},{6,7},{7,6},{8,9},{9,8},{10,11... | collective-permute-start | bytes 884744 | tf_op jit(solution)/shard_map/ppermute | solution.py:233
  160.2 5.2 %collective-permute-start.3 = (f32[2,2,8,1152]{3,2,1,0:T(8,128)S(1)}, f32[2,2,8,1152]{3,2,1,0:T(8,128)S(1)}, u32[]{:S(2)}, u32[]{:S(2)}) collective-permute-start(f32[2,2,8,1152]{3,2,1,0:T(8,128)S(1)} %dynamic-slice_bitcast_fusion.5), channel_id=1, source_target_pairs={{0,1},{1,0},{2,3},{3,2},{4,5},{5,4},{6,7},{7,6},{8,9},{9,8},{10,11... | collective-permute-start | bytes 442376 | tf_op jit(solution)/shard_map/ppermute | solution.py:233
  162.2 5.3 %collective-permute-start.8 = (f32[2,2,8,1152]{3,2,1,0:T(8,128)S(1)}, f32[2,2,8,1152]{3,2,1,0:T(8,128)S(1)}, u32[]{:S(2)}, u32[]{:S(2)}) collective-permute-start(f32[2,2,8,1152]{3,2,1,0:T(8,128)S(1)} %dynamic-slice_bitcast_fusion.4), channel_id=1, source_target_pairs={{0,16},{1,17},{2,18},{3,19},{4,20},{5,21},{6,22},{7,23},{8,24},{9,... | collective-permute-start | bytes 442376 | tf_op jit(solution)/shard_map/ppermute | solution.py:233
  165.5 4.9 %collective-permute-start.4 = (f32[2,8,1152]{2,1,0:T(8,128)S(1)}, f32[2,8,1152]{2,1,0:T(8,128)S(1)}, u32[]{:S(2)}, u32[]{:S(2)}) collective-permute-start(f32[2,8,1152]{2,1,0:T(8,128)S(1)} %dynamic-slice_bitcast_fusion.7), channel_id=1, source_target_pairs={{0,2},{1,3},{2,0},{3,1},{4,6},{5,7},{6,4},{7,5},{8,10},{9,11},{10,... | collective-permute-start | bytes 221192 | tf_op jit(solution)/shard_map/ppermute | solution.py:233
  167.6 4.5 %collective-permute-start.9 = (f32[2,8,1152]{2,1,0:T(8,128)S(1)}, f32[2,8,1152]{2,1,0:T(8,128)S(1)}, u32[]{:S(2)}, u32[]{:S(2)}) collective-permute-start(f32[2,8,1152]{2,1,0:T(8,128)S(1)} %dynamic-slice_bitcast_fusion.6), channel_id=1, source_target_pairs={{0,2},{1,3},{2,0},{3,1},{4,6},{5,7},{6,4},{7,5},{8,10},{9,11},{10,... | collective-permute-start | bytes 221192 | tf_op jit(solution)/shard_map/ppermute | solution.py:233
  170.4 5.0 %collective-permute-start.5 = (f32[8,1152]{1,0:T(8,128)S(1)}, f32[8,1152]{1,0:T(8,128)S(1)}, u32[]{:S(2)}, u32[]{:S(2)}) collective-permute-start(f32[8,1152]{1,0:T(8,128)S(1)} %dynamic-slice_bitcast_fusion.9), channel_id=1, source_target_pairs={{0,4},{1,5},{2,6},{3,7},{4,0},{5,1},{6,2},{7,3},{8,12},{9,13},{10,... | collective-permute-start | bytes 110600 | tf_op jit(solution)/shard_map/ppermute | solution.py:233
  172.1 4.9 %collective-permute-start.10 = (f32[8,1152]{1,0:T(8,128)S(1)}, f32[8,1152]{1,0:T(8,128)S(1)}, u32[]{:S(2)}, u32[]{:S(2)}) collective-permute-start(f32[8,1152]{1,0:T(8,128)S(1)} %dynamic-slice_bitcast_fusion.8), channel_id=1, source_target_pairs={{0,4},{1,5},{2,6},{3,7},{4,0},{5,1},{6,2},{7,3},{8,12},{9,13},{10,... | collective-permute-start | bytes 110600 | tf_op jit(solution)/shard_map/ppermute | solution.py:233

commit v18 on v17

--- a/solution.py
+++ b/solution.py
@@ -220,7 +220,7 @@
     core = tiles.bit_length() - 1
     high = [b for b in range(bits) if b > core]
     low = [b for b in range(core)]
-    order = [core] + (low[:1] + high + low[1:] if swap else high + low)
+    order = [core] + (low[:2] + high + low[2:] if swap else high + low)
     rows = partial.shape[0] // devices
     buf = partial.reshape((2,) * bits + (rows,) + partial.shape[1:])
     remaining = list(range(bits - 1, -1, -1))

time: 178 us -> 179 us (level)
  transfers between devices with their start and end apart: 12 -> 12, of which waited for: 9 -> 8; matrix products, arithmetic and copies ran while one was open for 8% -> 8% of each run, Pallas kernels for 25% -> 25%
where the time goes in v18:
time: 179 us; the launch traced here: 178 us
  blocking collectives  53 us (30%)
  Pallas kernels  47.4 us (26%)
  waiting for transfers between devices  39.9 us (22%)
  starting transfers between devices  17.6 us (10%)
  local copies, waits for them, and re-layouts  12.3 us (7%)
  other arithmetic  7.39 us (4%)
    all_to_all x1, blocking collectives, local(): lax.all_to_all(local_hidden.reshape(tiles, owned, half_rows, width // 2,...  53 us
    pallas_call x2, Pallas kernels, second_stage(): pl.pallas_call(functools.partial(second_kernel, rows=rows, carry=prev is...  33.8 us
    all_to_all x1, waiting for transfers between devices, local(): lax.all_to_all(local_hidden.reshape(tiles, owned, half_rows, width // 2,...  22 us
    ppermute x10, waiting for transfers between devices, halving_reduce_scatter(): buf = keep + lax.ppermute(send, axes, pairs)  17.9 us
    pallas_call x1, Pallas kernels, first_stage(): pl.pallas_call(first_kernel, grid=(images,), in_specs=[pl.BlockSpec((None...  11 us
    ppermute x10, starting transfers between devices, halving_reduce_scatter(): buf = keep + lax.ppermute(send, axes, pairs)  9.03 us
    another operation x2, other arithmetic, second_stage(): jnp.stack([shift_cols_right(row_padded), row_padded, shift_cols_left(row_...  6.48 us
    ppermute x1, starting transfers between devices, shifted_2(): return lax.ppermute(shard, axis, pairs)  4.86 us
  transfers between devices with their start and end apart: 12, of which 8 were waited for; matrix products, arithmetic and copies ran while one was open for 8% of the time, Pallas kernels for 25%

profile of v18, /device:TPU:0, one launch (start us, length us, event | category | flops | bytes accessed | tf_op | source)
XLA Modules:
  0.0 178.5 jit_solution(14762909650439881682)
XLA Ops:
  0.6 1.0 slice.21
  1.6 4.9 %collective-permute-start = (bf16[8,1,128,128]{3,2,1,0:T(8,128)(2,1)S(1)}, bf16[8,1,128,128]{3,2,1,0:T(8,128)(2,1)S(1)}, u32[]{:S(2)}, u32[]{:S(2)}) collective-permute-start(bf16[8,1,128,128]{3,2,1,0:T(8,128)(2,1)S(1)} %slice.21), channel_id=1, source_target_pairs={{0,1},{1,2},{2,3},{3,4},{4,5},{5,6},{6,7},{8,9},{9,10},{10,11},{11... | collective-permute-start | bytes 786440 | tf_op jit(solution)/shard_map/ppermute | solution.py:14
  6.5 11.0 %shard_map.59 = (bf16[8,16,64,128]{3,2,1,0:T(8,128)(2,1)}, bf16[8,16,64,128]{3,2,1,0:T(8,128)(2,1)}) custom-call(bf16[8,32,128,128]{3,2,1,0:T(8,128)(2,1)} %x_ref.3, bf16[1152,256]{1,0:T(8,128)(2,1)} %bitcast.79), custom_call_target="tpu_custom_call" | custom-call | flops 4831838208 | bytes 12582912 | tf_op jit(solution)/shard_map/pallas_call | solution.py:108
  17.5 0.0 collective-permute-done.up_ref
  17.5 0.7 copy-done.4
  18.2 2.6 %shard_map.60 = (bf16[8,16,64,128]{3,2,1,0:T(8,128)(2,1)}, bf16[8,16,64,128]{3,2,1,0:T(8,128)(2,1)}) custom-call(bf16[8,32,128,128]{3,2,1,0:T(8,128)(2,1)} %x_ref.3, bf16[8,1,128,128]{3,2,1,0:T(8,128)(2,1)} %copy-done.4, bf16[1152,256]{1,0:T(8,128)(2,1)} %bitcast.80, ...), custom_call_target="tpu_custom_call", output_to_operand_aliasing={{0}: (3, {}), {1}: (4, {})} | custom-call | flops 301989888 | bytes 786432 | tf_op jit(solution)/shard_map/pallas_call | solution.py:120
  20.8 53.0 %all_to_all.21 = bf16[8,1,16,64,128]{4,3,2,1,0:T(8,128)(2,1)} all-to-all(bf16[8,1,16,64,128]{4,3,2,1,0:T(8,128)(2,1)} %bitcast.73), channel_id=1, replica_groups=mesh['group'=4,'tile'=8] {'tile'}, dimensions={0} | all-to-all | bytes 4194304 | tf_op jit(solution)/shard_map/all_to_all | solution.py:254
  73.8 3.7 %all-to-all-start = ((bf16[8,1,16,64,128]{4,3,2,1,0:T(8,128)(2,1)}), bf16[8,1,16,64,128]{4,3,2,1,0:T(8,128)(2,1)S(1)}, u32[]{:S(2)}, u32[]{:S(2)}) async-start(bf16[8,1,16,64,128]{4,3,2,1,0:T(8,128)(2,1)} %bitcast.74), calls=%async_computation | async-start | bytes 4194304 | tf_op jit(solution)/shard_map/all_to_all | solution.py:254
  77.6 1.1 fusion
  78.7 0.9 copy-done
  79.6 0.4 pad_bitcast_fusion.5
  80.0 1.4 pad_slice_fusion.3
  81.5 1.8 pad_bitcast_fusion.2
  83.2 3.2 %pad_maximum_fusion.refs_0_ = bf16[1,3,130,64,128]{4,3,2,1,0:T(8,128)(2,1)} fusion(bf16[1,1,130,64,128]{4,3,2,1,0:T(8,128)(2,1)S(1)} %get-tuple-element.28, bf16[1,1,130,64,128]{4,3,2,1,0:T(8,128)(2,1)S(1)} %pad_bitcast_fusion.5, bf16[1,1,130,64,128]{4,3,2,1,0:T(8,128)(2,1)S(1)} %get-tuple-element.29), kind=kLoop, calls=%fused_computation | loop fusion | flops 6389760 | bytes 12779520 | tf_op jit(solution)/shard_map/stack | solution.py:180
  86.5 16.7 %shard_map.61 = (f32[1,128,64,256]{3,2,1,0:T(8,128)}, f32[1,256,1152]{2,1,0:T(8,128)}) custom-call(bf16[1,3,130,64,128]{4,3,2,1,0:T(8,128)(2,1)} %pad_maximum_fusion.refs_0_, bf16[1152,256]{1,0:T(8,128)(2,1)} %bitcast.82, bf16[1,8192,256]{2,1,0:T(8,128)(2,1)} %bitcast.85), custom_call_target="tpu_custom_call" | custom-call | flops 9663676416 | bytes 26345472 | tf_op jit(solution)/shard_map/pallas_call | solution.py:193
  103.2 22.0 %all-to-all-done = bf16[8,1,16,64,128]{4,3,2,1,0:T(8,128)(2,1)S(1)} async-done(((bf16[8,1,16,64,128]{4,3,2,1,0:T(8,128)(2,1)}), bf16[8,1,16,64,128]{4,3,2,1,0:T(8,128)(2,1)S(1)}, u32[]{:S(2)}, u32[]{:S(2)}) %all-to-all-start) | async-done | bytes 2097184 | tf_op jit(solution)/shard_map/all_to_all | solution.py:254
  125.2 0.4 pad_bitcast_fusion.4
  125.7 0.0 copy-start.2
  125.7 1.4 pad_slice_fusion.1
  127.1 0.0 copy-done.2
  127.1 0.1 collective-permute-start.1
  127.2 1.3 pad_bitcast_fusion.1
  128.5 0.4 pad_bitcast_fusion
  128.9 3.2 %pad_maximum_fusion.1.refs_0_ = bf16[1,3,130,64,128]{4,3,2,1,0:T(8,128)(2,1)} fusion(bf16[1,1,130,64,128]{4,3,2,1,0:T(8,128)(2,1)S(1)} %pad_bitcast_fusion, bf16[1,1,130,64,128]{4,3,2,1,0:T(8,128)(2,1)S(1)} %pad_bitcast_fusion.4, bf16[1,1,130,64,128]{4,3,2,1,0:T(8,128)(2,1)S(1)} %pad_bitcast_fusion.1), kind=kLoop, calls=%fused_computation.1 | loop fusion | flops 6389760 | bytes 12779520 | tf_op jit(solution)/shard_map/stack | solution.py:180
  132.2 17.1 %shard_map.62 = (bf16[1,128,64,256]{3,2,1,0:T(8,128)(2,1)}, f32[1,256,1152]{2,1,0:T(8,128)}) custom-call(bf16[1,3,130,64,128]{4,3,2,1,0:T(8,128)(2,1)} %pad_maximum_fusion.1.refs_0_, bf16[1152,256]{1,0:T(8,128)(2,1)} %bitcast.81, bf16[1,8192,256]{2,1,0:T(8,128)(2,1)} %bitcast.86, f32[1,128,64,256]{3,2,1,0:T(8,128)} %get-tuple-element.18.refs_3_), custom_call_target="tpu_custom_call" | custom-call | flops 9663676416 | bytes 26345472 | tf_op jit(solution)/shard_map/pallas_call | solution.py:193
  149.3 1.2 dynamic-slice_bitcast_fusion
  150.5 0.6 collective-permute-start.6
  151.1 0.0 collective-permute-done.1
  151.1 0.1 bitcast_add_fusion.1
  151.2 1.6 collective-permute-start.2
  152.8 0.0 collective-permute-done.6
  152.8 0.1 bitcast_add_fusion
  152.9 1.5 collective-permute-start.7
  154.4 5.8 %collective-permute-done.2 = f32[2,2,2,8,1152]{4,3,2,1,0:T(8,128)S(1)} collective-permute-done((f32[2,2,2,8,1152]{4,3,2,1,0:T(8,128)S(1)}, f32[2,2,2,8,1152]{4,3,2,1,0:T(8,128)S(1)}, u32[]{:S(2)}, u32[]{:S(2)}) %collective-permute-start.2) | collective-permute-done | bytes 294944 | tf_op jit(solution)/shard_map/ppermute | solution.py:233
  160.2 1.5 collective-permute-start.3
  161.7 0.4 collective-permute-done.7
  162.2 0.1 collective-permute-start.8
  162.3 3.2 %collective-permute-done.3 = f32[2,2,8,1152]{3,2,1,0:T(8,128)S(1)} collective-permute-done((f32[2,2,8,1152]{3,2,1,0:T(8,128)S(1)}, f32[2,2,8,1152]{3,2,1,0:T(8,128)S(1)}, u32[]{:S(2)}, u32[]{:S(2)}) %collective-permute-start.3) | collective-permute-done | bytes 147488 | tf_op jit(solution)/shard_map/ppermute | solution.py:233
  165.5 0.1 collective-permute-start.4
  165.6 2.7 %collective-permute-done.8 = f32[2,2,8,1152]{3,2,1,0:T(8,128)S(1)} collective-permute-done((f32[2,2,8,1152]{3,2,1,0:T(8,128)S(1)}, f32[2,2,8,1152]{3,2,1,0:T(8,128)S(1)}, u32[]{:S(2)}, u32[]{:S(2)}) %collective-permute-start.8) | collective-permute-done | bytes 147488 | tf_op jit(solution)/shard_map/ppermute | solution.py:233
  168.4 1.7 collective-permute-start.9
  170.0 0.0 collective-permute-done.4
  170.1 1.0 collective-permute-start.5
  171.0 1.7 collective-permute-done.9
  172.8 1.0 collective-permute-start.10
  173.8 1.3 collective-permute-done.5
  175.1 2.7 %collective-permute-done.10 = f32[8,1152]{1,0:T(8,128)S(1)} collective-permute-done((f32[8,1152]{1,0:T(8,128)S(1)}, f32[8,1152]{1,0:T(8,128)S(1)}, u32[]{:S(2)}, u32[]{:S(2)}) %collective-permute-start.10) | collective-permute-done | bytes 36896 | tf_op jit(solution)/shard_map/ppermute | solution.py:233
  177.9 0.6 pad_maximum_fusion.2
  (23 shorter events, 0.4 us)
Async XLA Ops:
  1.6 15.9 %collective-permute-start = (bf16[8,1,128,128]{3,2,1,0:T(8,128)(2,1)S(1)}, bf16[8,1,128,128]{3,2,1,0:T(8,128)(2,1)S(1)}, u32[]{:S(2)}, u32[]{:S(2)}) collective-permute-start(bf16[8,1,128,128]{3,2,1,0:T(8,128)(2,1)S(1)} %slice.21), channel_id=1, source_target_pairs={{0,1},{1,2},{2,3},{3,4},{4,5},{5,6},{6,7},{8,9},{9,10},{10,11},{11... | collective-permute-start | bytes 786440 | tf_op jit(solution)/shard_map/ppermute | solution.py:14
  17.5 0.7 copy-start.4
  73.8 3.8 %copy-start.1 = (bf16[3,3,256,256]{3,2,1,0:T(8,128)(2,1)S(1)}, bf16[3,3,256,256]{3,2,1,0:T(8,128)(2,1)}, u32[]{:S(2)}) copy-start(bf16[3,3,256,256]{3,2,1,0:T(8,128)(2,1)} %param.6) | copy-start | bytes 3538948
  73.8 51.4 %all-to-all-start = ((bf16[8,1,16,64,128]{4,3,2,1,0:T(8,128)(2,1)}), bf16[8,1,16,64,128]{4,3,2,1,0:T(8,128)(2,1)S(1)}, u32[]{:S(2)}, u32[]{:S(2)}) async-start(bf16[8,1,16,64,128]{4,3,2,1,0:T(8,128)(2,1)} %bitcast.74), calls=%async_computation | async-start | bytes 4194304 | tf_op jit(solution)/shard_map/all_to_all | solution.py:254
  77.6 2.0 %copy-start = (bf16[8,1,16,64,128]{4,3,2,1,0:T(8,128)(2,1)S(1)}, bf16[8,1,16,64,128]{4,3,2,1,0:T(8,128)(2,1)}, u32[]{:S(2)}) copy-start(bf16[8,1,16,64,128]{4,3,2,1,0:T(8,128)(2,1)} %all_to_all.21) | copy-start | bytes 6291460
  125.7 1.4 copy-start.2
  127.1 23.9 %collective-permute-start.1 = (f32[2,2,2,2,8,1152]{5,4,3,2,1,0:T(8,128)S(1)}, f32[2,2,2,2,8,1152]{5,4,3,2,1,0:T(8,128)S(1)}, u32[]{:S(2)}, u32[]{:S(2)}) collective-permute-start(f32[2,2,2,2,8,1152]{5,4,3,2,1,0:T(8,128)S(1)} %dynamic-slice_bitcast_fusion.1), channel_id=1, source_target_pairs={{0,8},{1,9},{2,10},{3,11},{4,12},{5,13},{6,14},{7,15},{8,0},{9,1},... | collective-permute-start | bytes 1769480 | tf_op jit(solution)/shard_map/ppermute | solution.py:233
  149.3 3.5 %copy-start.3 = (f32[1,256,1152]{2,1,0:T(8,128)S(1)}, f32[1,256,1152]{2,1,0:T(8,128)}, u32[]{:S(2)}) copy-start(f32[1,256,1152]{2,1,0:T(8,128)} %get-tuple-element.21) | copy-start | bytes 3538948
  150.5 2.3 %collective-permute-start.6 = (f32[2,2,2,2,8,1152]{5,4,3,2,1,0:T(8,128)S(1)}, f32[2,2,2,2,8,1152]{5,4,3,2,1,0:T(8,128)S(1)}, u32[]{:S(2)}, u32[]{:S(2)}) collective-permute-start(f32[2,2,2,2,8,1152]{5,4,3,2,1,0:T(8,128)S(1)} %dynamic-slice_bitcast_fusion), channel_id=1, source_target_pairs={{0,8},{1,9},{2,10},{3,11},{4,12},{5,13},{6,14},{7,15},{8,0},{9,1},... | collective-permute-start | bytes 1769480 | tf_op jit(solution)/shard_map/ppermute | solution.py:233
  151.2 9.0 %collective-permute-start.2 = (f32[2,2,2,8,1152]{4,3,2,1,0:T(8,128)S(1)}, f32[2,2,2,8,1152]{4,3,2,1,0:T(8,128)S(1)}, u32[]{:S(2)}, u32[]{:S(2)}) collective-permute-start(f32[2,2,2,8,1152]{4,3,2,1,0:T(8,128)S(1)} %dynamic-slice_bitcast_fusion.3), channel_id=1, source_target_pairs={{0,16},{1,17},{2,18},{3,19},{4,20},{5,21},{6,22},{7,23},{8,24},{9,... | collective-permute-start | bytes 884744 | tf_op jit(solution)/shard_map/ppermute | solution.py:233
  152.9 9.3 %collective-permute-start.7 = (f32[2,2,2,8,1152]{4,3,2,1,0:T(8,128)S(1)}, f32[2,2,2,8,1152]{4,3,2,1,0:T(8,128)S(1)}, u32[]{:S(2)}, u32[]{:S(2)}) collective-permute-start(f32[2,2,2,8,1152]{4,3,2,1,0:T(8,128)S(1)} %dynamic-slice_bitcast_fusion.2), channel_id=1, source_target_pairs={{0,1},{1,0},{2,3},{3,2},{4,5},{5,4},{6,7},{7,6},{8,9},{9,8},{10,11... | collective-permute-start | bytes 884744 | tf_op jit(solution)/shard_map/ppermute | solution.py:233
  160.2 5.2 %collective-permute-start.3 = (f32[2,2,8,1152]{3,2,1,0:T(8,128)S(1)}, f32[2,2,8,1152]{3,2,1,0:T(8,128)S(1)}, u32[]{:S(2)}, u32[]{:S(2)}) collective-permute-start(f32[2,2,8,1152]{3,2,1,0:T(8,128)S(1)} %dynamic-slice_bitcast_fusion.5), channel_id=1, source_target_pairs={{0,1},{1,0},{2,3},{3,2},{4,5},{5,4},{6,7},{7,6},{8,9},{9,8},{10,11... | collective-permute-start | bytes 442376 | tf_op jit(solution)/shard_map/ppermute | solution.py:233
  162.2 6.1 %collective-permute-start.8 = (f32[2,2,8,1152]{3,2,1,0:T(8,128)S(1)}, f32[2,2,8,1152]{3,2,1,0:T(8,128)S(1)}, u32[]{:S(2)}, u32[]{:S(2)}) collective-permute-start(f32[2,2,8,1152]{3,2,1,0:T(8,128)S(1)} %dynamic-slice_bitcast_fusion.4), channel_id=1, source_target_pairs={{0,2},{1,3},{2,0},{3,1},{4,6},{5,7},{6,4},{7,5},{8,10},{9,11},{10,... | collective-permute-start | bytes 442376 | tf_op jit(solution)/shard_map/ppermute | solution.py:233
  165.5 4.5 %collective-permute-start.4 = (f32[2,8,1152]{2,1,0:T(8,128)S(1)}, f32[2,8,1152]{2,1,0:T(8,128)S(1)}, u32[]{:S(2)}, u32[]{:S(2)}) collective-permute-start(f32[2,8,1152]{2,1,0:T(8,128)S(1)} %dynamic-slice_bitcast_fusion.7), channel_id=1, source_target_pairs={{0,2},{1,3},{2,0},{3,1},{4,6},{5,7},{6,4},{7,5},{8,10},{9,11},{10,... | collective-permute-start | bytes 221192 | tf_op jit(solution)/shard_map/ppermute | solution.py:233
  168.4 4.4 %collective-permute-start.9 = (f32[2,8,1152]{2,1,0:T(8,128)S(1)}, f32[2,8,1152]{2,1,0:T(8,128)S(1)}, u32[]{:S(2)}, u32[]{:S(2)}) collective-permute-start(f32[2,8,1152]{2,1,0:T(8,128)S(1)} %dynamic-slice_bitcast_fusion.6), channel_id=1, source_target_pairs={{0,16},{1,17},{2,18},{3,19},{4,20},{5,21},{6,22},{7,23},{8,24},{9,... | collective-permute-start | bytes 221192 | tf_op jit(solution)/shard_map/ppermute | solution.py:233
  170.1 5.0 %collective-permute-start.5 = (f32[8,1152]{1,0:T(8,128)S(1)}, f32[8,1152]{1,0:T(8,128)S(1)}, u32[]{:S(2)}, u32[]{:S(2)}) collective-permute-start(f32[8,1152]{1,0:T(8,128)S(1)} %dynamic-slice_bitcast_fusion.9), channel_id=1, source_target_pairs={{0,4},{1,5},{2,6},{3,7},{4,0},{5,1},{6,2},{7,3},{8,12},{9,13},{10,... | collective-permute-start | bytes 110600 | tf_op jit(solution)/shard_map/ppermute | solution.py:233
  172.8 5.0 %collective-permute-start.10 = (f32[8,1152]{1,0:T(8,128)S(1)}, f32[8,1152]{1,0:T(8,128)S(1)}, u32[]{:S(2)}, u32[]{:S(2)}) collective-permute-start(f32[8,1152]{1,0:T(8,128)S(1)} %dynamic-slice_bitcast_fusion.8), channel_id=1, source_target_pairs={{0,4},{1,5},{2,6},{3,7},{4,0},{5,1},{6,2},{7,3},{8,12},{9,13},{10,... | collective-permute-start | bytes 110600 | tf_op jit(solution)/shard_map/ppermute | solution.py:233

commit v19 on v17

--- a/solution.py
+++ b/solution.py
@@ -46,22 +46,22 @@
 
 
 def first_kernel(x_ref, w_ref, low_ref, high_ref, scratch):
-    rows, width, inputs = x_ref.shape
+    images, rows, width, inputs = x_ref.shape
     out_rows, out_cols = rows // 2, width // 2
-    scratch[0] = jnp.zeros(scratch.shape[1:], jnp.float32)
-    scratch[1:] = x_ref[...].astype(jnp.float32)
-    first_col = lax.broadcasted_iota(jnp.int32, (out_rows, out_cols, inputs), 1) == 0
+    scratch[:, 0] = jnp.zeros((images,) + scratch.shape[2:], jnp.float32)
+    scratch[:, 1:] = x_ref[...].astype(jnp.float32)
+    first_col = lax.broadcasted_iota(jnp.int32, (images, out_rows, out_cols, inputs), 2) == 0
     pieces = []
     for tap_row in range(3):
-        even = scratch[pl.ds(tap_row, out_rows, stride=2), pl.ds(0, out_cols, stride=2), :]
-        odd = scratch[pl.ds(tap_row, out_rows, stride=2), pl.ds(1, out_cols, stride=2), :]
-        left = jnp.where(first_col, 0.0, pltpu.roll(odd, 1, 1))
+        even = scratch[:, pl.ds(tap_row, out_rows, stride=2), pl.ds(0, out_cols, stride=2), :]
+        odd = scratch[:, pl.ds(tap_row, out_rows, stride=2), pl.ds(1, out_cols, stride=2), :]
+        left = jnp.where(first_col, 0.0, pltpu.roll(odd, 1, 2))
         pieces += [left, even, odd]
     patches = jnp.concatenate(
-        [p.astype(jnp.bfloat16).reshape(out_rows * out_cols, inputs) for p in pieces], axis=-1
+        [p.astype(jnp.bfloat16).reshape(images * out_rows * out_cols, inputs) for p in pieces], axis=-1
     )
     total = jnp.dot(patches, w_ref[...], preferred_element_type=jnp.float32)
-    hidden = jnp.maximum(total, 0.0).astype(jnp.bfloat16).reshape(out_rows, out_cols, -1)
+    hidden = jnp.maximum(total, 0.0).astype(jnp.bfloat16).reshape(images, out_rows, out_cols, -1)
     half = low_ref.shape[-1]
     low_ref[...] = hidden[..., :half]
     high_ref[...] = hidden[..., half:]
@@ -104,14 +104,15 @@
             bytes_accessed=images * out_rows * 2 * width * inputs * 2 + images * out_rows * (width // 2) * outputs * 2,
         )
 
-    out_block = pl.BlockSpec((None, rows // 2, width // 2, part), lambda n: (n, 0, 0, 0))
+    per = 2 if images % 2 == 0 else 1
+    out_block = pl.BlockSpec((per, rows // 2, width // 2, part), lambda n: (n, 0, 0, 0))
     low, high = pl.pallas_call(
         first_kernel,
-        grid=(images,),
-        in_specs=[pl.BlockSpec((None, rows, width, inputs), lambda n: (n, 0, 0, 0)), weight_spec],
+        grid=(images // per,),
+        in_specs=[pl.BlockSpec((per, rows, width, inputs), lambda n: (n, 0, 0, 0)), weight_spec],
         out_specs=[out_block, out_block],
         out_shape=[shape, shape],
-        scratch_shapes=[pltpu.VMEM((rows + 1, width, inputs), jnp.float32)],
+        scratch_shapes=[pltpu.VMEM((per, rows + 1, width, inputs), jnp.float32)],
         compiler_params=params,
         cost_estimate=cost(rows // 2),
     )(maps, weight)

time: 178 us -> 177 us (level)
  no operation moved by 1% of the time
where the time goes in v19:
time: 177 us; the launch traced here: 176 us
  blocking collectives  53 us (30%)
  Pallas kernels  45.9 us (26%)
  waiting for transfers between devices  39 us (22%)
  starting transfers between devices  17.8 us (10%)
  local copies, waits for them, and re-layouts  12.3 us (7%)
  other arithmetic  7.39 us (4%)
    all_to_all x1, blocking collectives, local(): lax.all_to_all(local_hidden.reshape(tiles, owned, half_rows, width // 2,...  53 us
    pallas_call x2, Pallas kernels, second_stage(): pl.pallas_call(functools.partial(second_kernel, rows=rows, carry=prev is...  33.8 us
    all_to_all x1, waiting for transfers between devices, local(): lax.all_to_all(local_hidden.reshape(tiles, owned, half_rows, width // 2,...  21.9 us
    ppermute x10, waiting for transfers between devices, halving_reduce_scatter(): buf = keep + lax.ppermute(send, axes, pairs)  17 us
    pallas_call x1, Pallas kernels, first_stage(): pl.pallas_call(first_kernel, grid=(images // per,), in_specs=[pl.BlockSpe...  9.51 us
    ppermute x10, starting transfers between devices, halving_reduce_scatter(): buf = keep + lax.ppermute(send, axes, pairs)  9.01 us
    another operation x2, other arithmetic, second_stage(): jnp.stack([shift_cols_right(row_padded), row_padded, shift_cols_left(row_...  6.48 us
    ppermute x1, starting transfers between devices, shifted_2(): return lax.ppermute(shard, axis, pairs)  4.86 us
  transfers between devices with their start and end apart: 12, of which 9 were waited for; matrix products, arithmetic and copies ran while one was open for 8% of the time, Pallas kernels for 25%

profile of v19, /device:TPU:0, one launch (start us, length us, event | category | flops | bytes accessed | tf_op | source)
XLA Modules:
  0.0 176.2 jit_solution(14338743008580236346)
XLA Ops:
  0.6 1.0 slice.21
  1.6 4.9 %collective-permute-start = (bf16[8,1,128,128]{3,2,1,0:T(8,128)(2,1)S(1)}, bf16[8,1,128,128]{3,2,1,0:T(8,128)(2,1)S(1)}, u32[]{:S(2)}, u32[]{:S(2)}) collective-permute-start(bf16[8,1,128,128]{3,2,1,0:T(8,128)(2,1)S(1)} %slice.21), channel_id=1, source_target_pairs={{0,1},{1,2},{2,3},{3,4},{4,5},{5,6},{6,7},{8,9},{9,10},{10,11},{11... | collective-permute-start | bytes 786440 | tf_op jit(solution)/shard_map/ppermute | solution.py:14
  6.5 9.5 %shard_map.59 = (bf16[8,16,64,128]{3,2,1,0:T(8,128)(2,1)}, bf16[8,16,64,128]{3,2,1,0:T(8,128)(2,1)}) custom-call(bf16[8,32,128,128]{3,2,1,0:T(8,128)(2,1)} %x_ref.3, bf16[1152,256]{1,0:T(8,128)(2,1)} %bitcast.79), custom_call_target="tpu_custom_call" | custom-call | flops 4831838208 | bytes 12582912 | tf_op jit(solution)/shard_map/pallas_call | solution.py:109
  16.0 0.0 collective-permute-done.up_ref
  16.0 0.7 copy-done.4
  16.7 2.6 %shard_map.60 = (bf16[8,16,64,128]{3,2,1,0:T(8,128)(2,1)}, bf16[8,16,64,128]{3,2,1,0:T(8,128)(2,1)}) custom-call(bf16[8,32,128,128]{3,2,1,0:T(8,128)(2,1)} %x_ref.3, bf16[8,1,128,128]{3,2,1,0:T(8,128)(2,1)} %copy-done.4, bf16[1152,256]{1,0:T(8,128)(2,1)} %bitcast.80, ...), custom_call_target="tpu_custom_call", output_to_operand_aliasing={{0}: (3, {}), {1}: (4, {})} | custom-call | flops 301989888 | bytes 786432 | tf_op jit(solution)/shard_map/pallas_call | solution.py:121
  19.3 53.0 %all_to_all.21 = bf16[8,1,16,64,128]{4,3,2,1,0:T(8,128)(2,1)} all-to-all(bf16[8,1,16,64,128]{4,3,2,1,0:T(8,128)(2,1)} %bitcast.73), channel_id=1, replica_groups=mesh['group'=4,'tile'=8] {'tile'}, dimensions={0} | all-to-all | bytes 4194304 | tf_op jit(solution)/shard_map/all_to_all | solution.py:255
  72.3 3.9 %all-to-all-start = ((bf16[8,1,16,64,128]{4,3,2,1,0:T(8,128)(2,1)}), bf16[8,1,16,64,128]{4,3,2,1,0:T(8,128)(2,1)S(1)}, u32[]{:S(2)}, u32[]{:S(2)}) async-start(bf16[8,1,16,64,128]{4,3,2,1,0:T(8,128)(2,1)} %bitcast.74), calls=%async_computation | async-start | bytes 4194304 | tf_op jit(solution)/shard_map/all_to_all | solution.py:255
  76.2 1.1 fusion
  77.3 0.9 copy-done
  78.2 0.4 pad_bitcast_fusion.5
  78.7 1.4 pad_slice_fusion.3
  80.1 1.8 %pad_bitcast_fusion.2 = (bf16[1,1,130,64,128]{4,3,2,1,0:T(8,128)(2,1)S(1)}, bf16[1,1,130,64,128]{4,3,2,1,0:T(8,128)(2,1)S(1)}) fusion(bf16[1,130,63,128]{3,2,1,0:T(8,128)(2,1)S(1)} %get-tuple-element.25, bf16[1,130,63,128]{3,2,1,0:T(8,128)(2,1)S(1)} %get-tuple-element.24), kind=kLoop, calls=%fused_computation.4 | loop fusion | bytes 8453120 | tf_op jit(solution)/shard_map/stack | solution.py:181
  81.9 3.2 %pad_maximum_fusion.refs_0_ = bf16[1,3,130,64,128]{4,3,2,1,0:T(8,128)(2,1)} fusion(bf16[1,1,130,64,128]{4,3,2,1,0:T(8,128)(2,1)S(1)} %get-tuple-element.28, bf16[1,1,130,64,128]{4,3,2,1,0:T(8,128)(2,1)S(1)} %pad_bitcast_fusion.5, bf16[1,1,130,64,128]{4,3,2,1,0:T(8,128)(2,1)S(1)} %get-tuple-element.29), kind=kLoop, calls=%fused_computation | loop fusion | flops 6389760 | bytes 12779520 | tf_op jit(solution)/shard_map/stack | solution.py:181
  85.2 16.7 %shard_map.61 = (f32[1,128,64,256]{3,2,1,0:T(8,128)}, f32[1,256,1152]{2,1,0:T(8,128)}) custom-call(bf16[1,3,130,64,128]{4,3,2,1,0:T(8,128)(2,1)} %pad_maximum_fusion.refs_0_, bf16[1152,256]{1,0:T(8,128)(2,1)} %bitcast.82, bf16[1,8192,256]{2,1,0:T(8,128)(2,1)} %bitcast.85), custom_call_target="tpu_custom_call" | custom-call | flops 9663676416 | bytes 26345472 | tf_op jit(solution)/shard_map/pallas_call | solution.py:194
  101.9 21.9 %all-to-all-done = bf16[8,1,16,64,128]{4,3,2,1,0:T(8,128)(2,1)S(1)} async-done(((bf16[8,1,16,64,128]{4,3,2,1,0:T(8,128)(2,1)}), bf16[8,1,16,64,128]{4,3,2,1,0:T(8,128)(2,1)S(1)}, u32[]{:S(2)}, u32[]{:S(2)}) %all-to-all-start) | async-done | bytes 2097184 | tf_op jit(solution)/shard_map/all_to_all | solution.py:255
  123.8 0.4 pad_bitcast_fusion.4
  124.2 0.0 copy-start.2
  124.3 1.4 pad_slice_fusion.1
  125.6 0.0 copy-done.2
  125.7 0.1 collective-permute-start.1
  125.8 1.3 pad_bitcast_fusion.1
  127.1 0.4 pad_bitcast_fusion
  127.5 3.2 %pad_maximum_fusion.1.refs_0_ = bf16[1,3,130,64,128]{4,3,2,1,0:T(8,128)(2,1)} fusion(bf16[1,1,130,64,128]{4,3,2,1,0:T(8,128)(2,1)S(1)} %pad_bitcast_fusion, bf16[1,1,130,64,128]{4,3,2,1,0:T(8,128)(2,1)S(1)} %pad_bitcast_fusion.4, bf16[1,1,130,64,128]{4,3,2,1,0:T(8,128)(2,1)S(1)} %pad_bitcast_fusion.1), kind=kLoop, calls=%fused_computation.1 | loop fusion | flops 6389760 | bytes 12779520 | tf_op jit(solution)/shard_map/stack | solution.py:181
  130.7 17.1 %shard_map.62 = (bf16[1,128,64,256]{3,2,1,0:T(8,128)(2,1)}, f32[1,256,1152]{2,1,0:T(8,128)}) custom-call(bf16[1,3,130,64,128]{4,3,2,1,0:T(8,128)(2,1)} %pad_maximum_fusion.1.refs_0_, bf16[1152,256]{1,0:T(8,128)(2,1)} %bitcast.81, bf16[1,8192,256]{2,1,0:T(8,128)(2,1)} %bitcast.86, f32[1,128,64,256]{3,2,1,0:T(8,128)} %get-tuple-element.18.refs_3_), custom_call_target="tpu_custom_call" | custom-call | flops 9663676416 | bytes 26345472 | tf_op jit(solution)/shard_map/pallas_call | solution.py:194
  147.8 1.2 dynamic-slice_bitcast_fusion
  149.1 0.6 collective-permute-start.6
  149.6 0.0 collective-permute-done.1
  149.6 0.1 bitcast_add_fusion.1
  149.7 1.6 collective-permute-start.2
  151.3 0.0 collective-permute-done.6
  151.3 0.1 bitcast_add_fusion
  151.4 1.4 collective-permute-start.7
  152.8 5.9 %collective-permute-done.2 = f32[2,2,2,8,1152]{4,3,2,1,0:T(8,128)S(1)} collective-permute-done((f32[2,2,2,8,1152]{4,3,2,1,0:T(8,128)S(1)}, f32[2,2,2,8,1152]{4,3,2,1,0:T(8,128)S(1)}, u32[]{:S(2)}, u32[]{:S(2)}) %collective-permute-start.2) | collective-permute-done | bytes 294944 | tf_op jit(solution)/shard_map/ppermute | solution.py:234
  158.8 1.4 collective-permute-start.3
  160.2 0.5 collective-permute-done.7
  160.8 1.6 collective-permute-start.8
  162.4 1.7 collective-permute-done.3
  164.1 0.1 collective-permute-start.4
  164.1 2.0 %collective-permute-done.8 = f32[2,2,8,1152]{3,2,1,0:T(8,128)S(1)} collective-permute-done((f32[2,2,8,1152]{3,2,1,0:T(8,128)S(1)}, f32[2,2,8,1152]{3,2,1,0:T(8,128)S(1)}, u32[]{:S(2)}, u32[]{:S(2)}) %collective-permute-start.8) | collective-permute-done | bytes 147488 | tf_op jit(solution)/shard_map/ppermute | solution.py:234
  166.1 0.1 collective-permute-start.9
  166.3 2.7 %collective-permute-done.4 = f32[2,8,1152]{2,1,0:T(8,128)S(1)} collective-permute-done((f32[2,8,1152]{2,1,0:T(8,128)S(1)}, f32[2,8,1152]{2,1,0:T(8,128)S(1)}, u32[]{:S(2)}, u32[]{:S(2)}) %collective-permute-start.4) | collective-permute-done | bytes 73760 | tf_op jit(solution)/shard_map/ppermute | solution.py:234
  169.0 0.7 collective-permute-start.5
  169.7 0.9 collective-permute-done.9
  170.6 1.5 collective-permute-start.10
  172.1 1.9 %collective-permute-done.5 = f32[8,1152]{1,0:T(8,128)S(1)} collective-permute-done((f32[8,1152]{1,0:T(8,128)S(1)}, f32[8,1152]{1,0:T(8,128)S(1)}, u32[]{:S(2)}, u32[]{:S(2)}) %collective-permute-start.5) | collective-permute-done | bytes 36896 | tf_op jit(solution)/shard_map/ppermute | solution.py:234
  174.1 1.5 collective-permute-done.10
  175.6 0.6 pad_maximum_fusion.2
  (23 shorter events, 0.4 us)
Async XLA Ops:
  1.6 14.4 %collective-permute-start = (bf16[8,1,128,128]{3,2,1,0:T(8,128)(2,1)S(1)}, bf16[8,1,128,128]{3,2,1,0:T(8,128)(2,1)S(1)}, u32[]{:S(2)}, u32[]{:S(2)}) collective-permute-start(bf16[8,1,128,128]{3,2,1,0:T(8,128)(2,1)S(1)} %slice.21), channel_id=1, source_target_pairs={{0,1},{1,2},{2,3},{3,4},{4,5},{5,6},{6,7},{8,9},{9,10},{10,11},{11... | collective-permute-start | bytes 786440 | tf_op jit(solution)/shard_map/ppermute | solution.py:14
  16.0 0.7 copy-start.4
  72.3 3.9 %copy-start.1 = (bf16[3,3,256,256]{3,2,1,0:T(8,128)(2,1)S(1)}, bf16[3,3,256,256]{3,2,1,0:T(8,128)(2,1)}, u32[]{:S(2)}) copy-start(bf16[3,3,256,256]{3,2,1,0:T(8,128)(2,1)} %param.6) | copy-start | bytes 3538948
  72.3 51.5 %all-to-all-start = ((bf16[8,1,16,64,128]{4,3,2,1,0:T(8,128)(2,1)}), bf16[8,1,16,64,128]{4,3,2,1,0:T(8,128)(2,1)S(1)}, u32[]{:S(2)}, u32[]{:S(2)}) async-start(bf16[8,1,16,64,128]{4,3,2,1,0:T(8,128)(2,1)} %bitcast.74), calls=%async_computation | async-start | bytes 4194304 | tf_op jit(solution)/shard_map/all_to_all | solution.py:255
  76.2 2.0 %copy-start = (bf16[8,1,16,64,128]{4,3,2,1,0:T(8,128)(2,1)S(1)}, bf16[8,1,16,64,128]{4,3,2,1,0:T(8,128)(2,1)}, u32[]{:S(2)}) copy-start(bf16[8,1,16,64,128]{4,3,2,1,0:T(8,128)(2,1)} %all_to_all.21) | copy-start | bytes 6291460
  124.2 1.4 copy-start.2
  125.7 23.9 %collective-permute-start.1 = (f32[2,2,2,2,8,1152]{5,4,3,2,1,0:T(8,128)S(1)}, f32[2,2,2,2,8,1152]{5,4,3,2,1,0:T(8,128)S(1)}, u32[]{:S(2)}, u32[]{:S(2)}) collective-permute-start(f32[2,2,2,2,8,1152]{5,4,3,2,1,0:T(8,128)S(1)} %dynamic-slice_bitcast_fusion.1), channel_id=1, source_target_pairs={{0,8},{1,9},{2,10},{3,11},{4,12},{5,13},{6,14},{7,15},{8,0},{9,1},... | collective-permute-start | bytes 1769480 | tf_op jit(solution)/shard_map/ppermute | solution.py:234
  147.8 3.5 %copy-start.3 = (f32[1,256,1152]{2,1,0:T(8,128)S(1)}, f32[1,256,1152]{2,1,0:T(8,128)}, u32[]{:S(2)}) copy-start(f32[1,256,1152]{2,1,0:T(8,128)} %get-tuple-element.21) | copy-start | bytes 3538948
  149.1 2.3 %collective-permute-start.6 = (f32[2,2,2,2,8,1152]{5,4,3,2,1,0:T(8,128)S(1)}, f32[2,2,2,2,8,1152]{5,4,3,2,1,0:T(8,128)S(1)}, u32[]{:S(2)}, u32[]{:S(2)}) collective-permute-start(f32[2,2,2,2,8,1152]{5,4,3,2,1,0:T(8,128)S(1)} %dynamic-slice_bitcast_fusion), channel_id=1, source_target_pairs={{0,8},{1,9},{2,10},{3,11},{4,12},{5,13},{6,14},{7,15},{8,0},{9,1},... | collective-permute-start | bytes 1769480 | tf_op jit(solution)/shard_map/ppermute | solution.py:234
  149.7 9.0 %collective-permute-start.2 = (f32[2,2,2,8,1152]{4,3,2,1,0:T(8,128)S(1)}, f32[2,2,2,8,1152]{4,3,2,1,0:T(8,128)S(1)}, u32[]{:S(2)}, u32[]{:S(2)}) collective-permute-start(f32[2,2,2,8,1152]{4,3,2,1,0:T(8,128)S(1)} %dynamic-slice_bitcast_fusion.3), channel_id=1, source_target_pairs={{0,16},{1,17},{2,18},{3,19},{4,20},{5,21},{6,22},{7,23},{8,24},{9,... | collective-permute-start | bytes 884744 | tf_op jit(solution)/shard_map/ppermute | solution.py:234
  151.4 9.3 %collective-permute-start.7 = (f32[2,2,2,8,1152]{4,3,2,1,0:T(8,128)S(1)}, f32[2,2,2,8,1152]{4,3,2,1,0:T(8,128)S(1)}, u32[]{:S(2)}, u32[]{:S(2)}) collective-permute-start(f32[2,2,2,8,1152]{4,3,2,1,0:T(8,128)S(1)} %dynamic-slice_bitcast_fusion.2), channel_id=1, source_target_pairs={{0,1},{1,0},{2,3},{3,2},{4,5},{5,4},{6,7},{7,6},{8,9},{9,8},{10,11... | collective-permute-start | bytes 884744 | tf_op jit(solution)/shard_map/ppermute | solution.py:234
  158.8 5.2 %collective-permute-start.3 = (f32[2,2,8,1152]{3,2,1,0:T(8,128)S(1)}, f32[2,2,8,1152]{3,2,1,0:T(8,128)S(1)}, u32[]{:S(2)}, u32[]{:S(2)}) collective-permute-start(f32[2,2,8,1152]{3,2,1,0:T(8,128)S(1)} %dynamic-slice_bitcast_fusion.5), channel_id=1, source_target_pairs={{0,1},{1,0},{2,3},{3,2},{4,5},{5,4},{6,7},{7,6},{8,9},{9,8},{10,11... | collective-permute-start | bytes 442376 | tf_op jit(solution)/shard_map/ppermute | solution.py:234
  160.8 5.3 %collective-permute-start.8 = (f32[2,2,8,1152]{3,2,1,0:T(8,128)S(1)}, f32[2,2,8,1152]{3,2,1,0:T(8,128)S(1)}, u32[]{:S(2)}, u32[]{:S(2)}) collective-permute-start(f32[2,2,8,1152]{3,2,1,0:T(8,128)S(1)} %dynamic-slice_bitcast_fusion.4), channel_id=1, source_target_pairs={{0,16},{1,17},{2,18},{3,19},{4,20},{5,21},{6,22},{7,23},{8,24},{9,... | collective-permute-start | bytes 442376 | tf_op jit(solution)/shard_map/ppermute | solution.py:234
  164.1 4.9 %collective-permute-start.4 = (f32[2,8,1152]{2,1,0:T(8,128)S(1)}, f32[2,8,1152]{2,1,0:T(8,128)S(1)}, u32[]{:S(2)}, u32[]{:S(2)}) collective-permute-start(f32[2,8,1152]{2,1,0:T(8,128)S(1)} %dynamic-slice_bitcast_fusion.7), channel_id=1, source_target_pairs={{0,2},{1,3},{2,0},{3,1},{4,6},{5,7},{6,4},{7,5},{8,10},{9,11},{10,... | collective-permute-start | bytes 221192 | tf_op jit(solution)/shard_map/ppermute | solution.py:234
  166.1 4.4 %collective-permute-start.9 = (f32[2,8,1152]{2,1,0:T(8,128)S(1)}, f32[2,8,1152]{2,1,0:T(8,128)S(1)}, u32[]{:S(2)}, u32[]{:S(2)}) collective-permute-start(f32[2,8,1152]{2,1,0:T(8,128)S(1)} %dynamic-slice_bitcast_fusion.6), channel_id=1, source_target_pairs={{0,2},{1,3},{2,0},{3,1},{4,6},{5,7},{6,4},{7,5},{8,10},{9,11},{10,... | collective-permute-start | bytes 221192 | tf_op jit(solution)/shard_map/ppermute | solution.py:234
  169.0 5.0 %collective-permute-start.5 = (f32[8,1152]{1,0:T(8,128)S(1)}, f32[8,1152]{1,0:T(8,128)S(1)}, u32[]{:S(2)}, u32[]{:S(2)}) collective-permute-start(f32[8,1152]{1,0:T(8,128)S(1)} %dynamic-slice_bitcast_fusion.9), channel_id=1, source_target_pairs={{0,4},{1,5},{2,6},{3,7},{4,0},{5,1},{6,2},{7,3},{8,12},{9,13},{10,... | collective-permute-start | bytes 110600 | tf_op jit(solution)/shard_map/ppermute | solution.py:234
  170.6 4.9 %collective-permute-start.10 = (f32[8,1152]{1,0:T(8,128)S(1)}, f32[8,1152]{1,0:T(8,128)S(1)}, u32[]{:S(2)}, u32[]{:S(2)}) collective-permute-start(f32[8,1152]{1,0:T(8,128)S(1)} %dynamic-slice_bitcast_fusion.8), channel_id=1, source_target_pairs={{0,4},{1,5},{2,6},{3,7},{4,0},{5,1},{6,2},{7,3},{8,12},{9,13},{10,... | collective-permute-start | bytes 110600 | tf_op jit(solution)/shard_map/ppermute | solution.py:234

commit v20 on v19

--- a/solution.py
+++ b/solution.py
@@ -104,7 +104,7 @@
             bytes_accessed=images * out_rows * 2 * width * inputs * 2 + images * out_rows * (width // 2) * outputs * 2,
         )
 
-    per = 2 if images % 2 == 0 else 1
+    per = 4 if images % 4 == 0 else 1
     out_block = pl.BlockSpec((per, rows // 2, width // 2, part), lambda n: (n, 0, 0, 0))
     low, high = pl.pallas_call(
         first_kernel,

time: 177 us -> 177 us (level)
  no operation moved by 1% of the time
where the time goes in v20:
time: 177 us; the launch traced here: 176 us
  blocking collectives  53 us (30%)
  Pallas kernels  46 us (26%)
  waiting for transfers between devices  39 us (22%)
  starting transfers between devices  17.8 us (10%)
  local copies, waits for them, and re-layouts  12.3 us (7%)
  other arithmetic  7.39 us (4%)
    all_to_all x1, blocking collectives, local(): lax.all_to_all(local_hidden.reshape(tiles, owned, half_rows, width // 2,...  53 us
    pallas_call x2, Pallas kernels, second_stage(): pl.pallas_call(functools.partial(second_kernel, rows=rows, carry=prev is...  33.8 us
    all_to_all x1, waiting for transfers between devices, local(): lax.all_to_all(local_hidden.reshape(tiles, owned, half_rows, width // 2,...  21.9 us
    ppermute x10, waiting for transfers between devices, halving_reduce_scatter(): buf = keep + lax.ppermute(send, axes, pairs)  17 us
    pallas_call x1, Pallas kernels, first_stage(): pl.pallas_call(first_kernel, grid=(images // per,), in_specs=[pl.BlockSpe...  9.59 us
    ppermute x10, starting transfers between devices, halving_reduce_scatter(): buf = keep + lax.ppermute(send, axes, pairs)  9.02 us
    another operation x2, other arithmetic, second_stage(): jnp.stack([shift_cols_right(row_padded), row_padded, shift_cols_left(row_...  6.48 us
    ppermute x1, starting transfers between devices, shifted_2(): return lax.ppermute(shard, axis, pairs)  4.86 us
  transfers between devices with their start and end apart: 12, of which 9 were waited for; matrix products, arithmetic and copies ran while one was open for 8% of the time, Pallas kernels for 25%

profile of v20, /device:TPU:0, one launch (start us, length us, event | category | flops | bytes accessed | tf_op | source)
XLA Modules:
  0.0 176.3 jit_solution(18119336466789604281)
XLA Ops:
  0.6 1.0 slice.21
  1.6 4.9 %collective-permute-start = (bf16[8,1,128,128]{3,2,1,0:T(8,128)(2,1)S(1)}, bf16[8,1,128,128]{3,2,1,0:T(8,128)(2,1)S(1)}, u32[]{:S(2)}, u32[]{:S(2)}) collective-permute-start(bf16[8,1,128,128]{3,2,1,0:T(8,128)(2,1)S(1)} %slice.21), channel_id=1, source_target_pairs={{0,1},{1,2},{2,3},{3,4},{4,5},{5,6},{6,7},{8,9},{9,10},{10,11},{11... | collective-permute-start | bytes 786440 | tf_op jit(solution)/shard_map/ppermute | solution.py:14
  6.5 9.6 %shard_map.59 = (bf16[8,16,64,128]{3,2,1,0:T(8,128)(2,1)}, bf16[8,16,64,128]{3,2,1,0:T(8,128)(2,1)}) custom-call(bf16[8,32,128,128]{3,2,1,0:T(8,128)(2,1)} %x_ref.3, bf16[1152,256]{1,0:T(8,128)(2,1)} %bitcast.79), custom_call_target="tpu_custom_call" | custom-call | flops 4831838208 | bytes 12582912 | tf_op jit(solution)/shard_map/pallas_call | solution.py:109
  16.1 0.0 collective-permute-done.up_ref
  16.1 0.7 copy-done.4
  16.8 2.6 %shard_map.60 = (bf16[8,16,64,128]{3,2,1,0:T(8,128)(2,1)}, bf16[8,16,64,128]{3,2,1,0:T(8,128)(2,1)}) custom-call(bf16[8,32,128,128]{3,2,1,0:T(8,128)(2,1)} %x_ref.3, bf16[8,1,128,128]{3,2,1,0:T(8,128)(2,1)} %copy-done.4, bf16[1152,256]{1,0:T(8,128)(2,1)} %bitcast.80, ...), custom_call_target="tpu_custom_call", output_to_operand_aliasing={{0}: (3, {}), {1}: (4, {})} | custom-call | flops 301989888 | bytes 786432 | tf_op jit(solution)/shard_map/pallas_call | solution.py:121
  19.3 53.0 %all_to_all.21 = bf16[8,1,16,64,128]{4,3,2,1,0:T(8,128)(2,1)} all-to-all(bf16[8,1,16,64,128]{4,3,2,1,0:T(8,128)(2,1)} %bitcast.73), channel_id=1, replica_groups=mesh['group'=4,'tile'=8] {'tile'}, dimensions={0} | all-to-all | bytes 4194304 | tf_op jit(solution)/shard_map/all_to_all | solution.py:255
  72.4 3.9 %all-to-all-start = ((bf16[8,1,16,64,128]{4,3,2,1,0:T(8,128)(2,1)}), bf16[8,1,16,64,128]{4,3,2,1,0:T(8,128)(2,1)S(1)}, u32[]{:S(2)}, u32[]{:S(2)}) async-start(bf16[8,1,16,64,128]{4,3,2,1,0:T(8,128)(2,1)} %bitcast.74), calls=%async_computation | async-start | bytes 4194304 | tf_op jit(solution)/shard_map/all_to_all | solution.py:255
  76.3 0.0 copy-done.1
  76.3 1.1 fusion
  77.4 0.9 copy-done
  78.3 0.4 pad_bitcast_fusion.5
  78.8 1.4 pad_slice_fusion.3
  80.2 1.8 %pad_bitcast_fusion.2 = (bf16[1,1,130,64,128]{4,3,2,1,0:T(8,128)(2,1)S(1)}, bf16[1,1,130,64,128]{4,3,2,1,0:T(8,128)(2,1)S(1)}) fusion(bf16[1,130,63,128]{3,2,1,0:T(8,128)(2,1)S(1)} %get-tuple-element.25, bf16[1,130,63,128]{3,2,1,0:T(8,128)(2,1)S(1)} %get-tuple-element.24), kind=kLoop, calls=%fused_computation.4 | loop fusion | bytes 8453120 | tf_op jit(solution)/shard_map/stack | solution.py:181
  82.0 3.2 %pad_maximum_fusion.refs_0_ = bf16[1,3,130,64,128]{4,3,2,1,0:T(8,128)(2,1)} fusion(bf16[1,1,130,64,128]{4,3,2,1,0:T(8,128)(2,1)S(1)} %get-tuple-element.28, bf16[1,1,130,64,128]{4,3,2,1,0:T(8,128)(2,1)S(1)} %pad_bitcast_fusion.5, bf16[1,1,130,64,128]{4,3,2,1,0:T(8,128)(2,1)S(1)} %get-tuple-element.29), kind=kLoop, calls=%fused_computation | loop fusion | flops 6389760 | bytes 12779520 | tf_op jit(solution)/shard_map/stack | solution.py:181
  85.2 16.7 %shard_map.61 = (f32[1,128,64,256]{3,2,1,0:T(8,128)}, f32[1,256,1152]{2,1,0:T(8,128)}) custom-call(bf16[1,3,130,64,128]{4,3,2,1,0:T(8,128)(2,1)} %pad_maximum_fusion.refs_0_, bf16[1152,256]{1,0:T(8,128)(2,1)} %bitcast.82, bf16[1,8192,256]{2,1,0:T(8,128)(2,1)} %bitcast.85), custom_call_target="tpu_custom_call" | custom-call | flops 9663676416 | bytes 26345472 | tf_op jit(solution)/shard_map/pallas_call | solution.py:194
  102.0 21.9 %all-to-all-done = bf16[8,1,16,64,128]{4,3,2,1,0:T(8,128)(2,1)S(1)} async-done(((bf16[8,1,16,64,128]{4,3,2,1,0:T(8,128)(2,1)}), bf16[8,1,16,64,128]{4,3,2,1,0:T(8,128)(2,1)S(1)}, u32[]{:S(2)}, u32[]{:S(2)}) %all-to-all-start) | async-done | bytes 2097184 | tf_op jit(solution)/shard_map/all_to_all | solution.py:255
  123.9 0.4 pad_bitcast_fusion.4
  124.3 0.0 copy-start.2
  124.3 1.4 pad_slice_fusion.1
  125.8 0.1 collective-permute-start.1
  125.9 1.3 pad_bitcast_fusion.1
  127.1 0.4 pad_bitcast_fusion
  127.6 3.2 %pad_maximum_fusion.1.refs_0_ = bf16[1,3,130,64,128]{4,3,2,1,0:T(8,128)(2,1)} fusion(bf16[1,1,130,64,128]{4,3,2,1,0:T(8,128)(2,1)S(1)} %pad_bitcast_fusion, bf16[1,1,130,64,128]{4,3,2,1,0:T(8,128)(2,1)S(1)} %pad_bitcast_fusion.4, bf16[1,1,130,64,128]{4,3,2,1,0:T(8,128)(2,1)S(1)} %pad_bitcast_fusion.1), kind=kLoop, calls=%fused_computation.1 | loop fusion | flops 6389760 | bytes 12779520 | tf_op jit(solution)/shard_map/stack | solution.py:181
  130.8 17.1 %shard_map.62 = (bf16[1,128,64,256]{3,2,1,0:T(8,128)(2,1)}, f32[1,256,1152]{2,1,0:T(8,128)}) custom-call(bf16[1,3,130,64,128]{4,3,2,1,0:T(8,128)(2,1)} %pad_maximum_fusion.1.refs_0_, bf16[1152,256]{1,0:T(8,128)(2,1)} %bitcast.81, bf16[1,8192,256]{2,1,0:T(8,128)(2,1)} %bitcast.86, f32[1,128,64,256]{3,2,1,0:T(8,128)} %get-tuple-element.18.refs_3_), custom_call_target="tpu_custom_call" | custom-call | flops 9663676416 | bytes 26345472 | tf_op jit(solution)/shard_map/pallas_call | solution.py:194
  147.9 1.2 dynamic-slice_bitcast_fusion
  149.2 0.6 collective-permute-start.6
  149.7 0.0 collective-permute-done.1
  149.7 0.1 bitcast_add_fusion.1
  149.8 1.6 collective-permute-start.2
  151.4 0.0 collective-permute-done.6
  151.4 0.1 bitcast_add_fusion
  151.5 1.4 collective-permute-start.7
  152.9 5.9 %collective-permute-done.2 = f32[2,2,2,8,1152]{4,3,2,1,0:T(8,128)S(1)} collective-permute-done((f32[2,2,2,8,1152]{4,3,2,1,0:T(8,128)S(1)}, f32[2,2,2,8,1152]{4,3,2,1,0:T(8,128)S(1)}, u32[]{:S(2)}, u32[]{:S(2)}) %collective-permute-start.2) | collective-permute-done | bytes 294944 | tf_op jit(solution)/shard_map/ppermute | solution.py:234
  158.9 1.4 collective-permute-start.3
  160.3 0.5 collective-permute-done.7
  160.9 1.6 collective-permute-start.8
  162.5 1.6 collective-permute-done.3
  164.2 0.1 collective-permute-start.4
  164.2 2.0 %collective-permute-done.8 = f32[2,2,8,1152]{3,2,1,0:T(8,128)S(1)} collective-permute-done((f32[2,2,8,1152]{3,2,1,0:T(8,128)S(1)}, f32[2,2,8,1152]{3,2,1,0:T(8,128)S(1)}, u32[]{:S(2)}, u32[]{:S(2)}) %collective-permute-start.8) | collective-permute-done | bytes 147488 | tf_op jit(solution)/shard_map/ppermute | solution.py:234
  166.2 0.1 collective-permute-start.9
  166.4 2.7 %collective-permute-done.4 = f32[2,8,1152]{2,1,0:T(8,128)S(1)} collective-permute-done((f32[2,8,1152]{2,1,0:T(8,128)S(1)}, f32[2,8,1152]{2,1,0:T(8,128)S(1)}, u32[]{:S(2)}, u32[]{:S(2)}) %collective-permute-start.4) | collective-permute-done | bytes 73760 | tf_op jit(solution)/shard_map/ppermute | solution.py:234
  169.1 0.7 collective-permute-start.5
  169.8 0.9 collective-permute-done.9
  170.7 1.4 collective-permute-start.10
  172.2 1.9 %collective-permute-done.5 = f32[8,1152]{1,0:T(8,128)S(1)} collective-permute-done((f32[8,1152]{1,0:T(8,128)S(1)}, f32[8,1152]{1,0:T(8,128)S(1)}, u32[]{:S(2)}, u32[]{:S(2)}) %collective-permute-start.5) | collective-permute-done | bytes 36896 | tf_op jit(solution)/shard_map/ppermute | solution.py:234
  174.1 1.5 collective-permute-done.10
  175.7 0.6 pad_maximum_fusion.2
  (23 shorter events, 0.4 us)
Async XLA Ops:
  1.6 14.5 %collective-permute-start = (bf16[8,1,128,128]{3,2,1,0:T(8,128)(2,1)S(1)}, bf16[8,1,128,128]{3,2,1,0:T(8,128)(2,1)S(1)}, u32[]{:S(2)}, u32[]{:S(2)}) collective-permute-start(bf16[8,1,128,128]{3,2,1,0:T(8,128)(2,1)S(1)} %slice.21), channel_id=1, source_target_pairs={{0,1},{1,2},{2,3},{3,4},{4,5},{5,6},{6,7},{8,9},{9,10},{10,11},{11... | collective-permute-start | bytes 786440 | tf_op jit(solution)/shard_map/ppermute | solution.py:14
  16.1 0.7 copy-start.4
  72.4 3.9 %copy-start.1 = (bf16[3,3,256,256]{3,2,1,0:T(8,128)(2,1)S(1)}, bf16[3,3,256,256]{3,2,1,0:T(8,128)(2,1)}, u32[]{:S(2)}) copy-start(bf16[3,3,256,256]{3,2,1,0:T(8,128)(2,1)} %param.6) | copy-start | bytes 3538948
  72.4 51.5 %all-to-all-start = ((bf16[8,1,16,64,128]{4,3,2,1,0:T(8,128)(2,1)}), bf16[8,1,16,64,128]{4,3,2,1,0:T(8,128)(2,1)S(1)}, u32[]{:S(2)}, u32[]{:S(2)}) async-start(bf16[8,1,16,64,128]{4,3,2,1,0:T(8,128)(2,1)} %bitcast.74), calls=%async_computation | async-start | bytes 4194304 | tf_op jit(solution)/shard_map/all_to_all | solution.py:255
  76.3 2.0 %copy-start = (bf16[8,1,16,64,128]{4,3,2,1,0:T(8,128)(2,1)S(1)}, bf16[8,1,16,64,128]{4,3,2,1,0:T(8,128)(2,1)}, u32[]{:S(2)}) copy-start(bf16[8,1,16,64,128]{4,3,2,1,0:T(8,128)(2,1)} %all_to_all.21) | copy-start | bytes 6291460
  124.3 1.4 copy-start.2
  125.8 23.9 %collective-permute-start.1 = (f32[2,2,2,2,8,1152]{5,4,3,2,1,0:T(8,128)S(1)}, f32[2,2,2,2,8,1152]{5,4,3,2,1,0:T(8,128)S(1)}, u32[]{:S(2)}, u32[]{:S(2)}) collective-permute-start(f32[2,2,2,2,8,1152]{5,4,3,2,1,0:T(8,128)S(1)} %dynamic-slice_bitcast_fusion.1), channel_id=1, source_target_pairs={{0,8},{1,9},{2,10},{3,11},{4,12},{5,13},{6,14},{7,15},{8,0},{9,1},... | collective-permute-start | bytes 1769480 | tf_op jit(solution)/shard_map/ppermute | solution.py:234
  147.9 3.5 %copy-start.3 = (f32[1,256,1152]{2,1,0:T(8,128)S(1)}, f32[1,256,1152]{2,1,0:T(8,128)}, u32[]{:S(2)}) copy-start(f32[1,256,1152]{2,1,0:T(8,128)} %get-tuple-element.21) | copy-start | bytes 3538948
  149.2 2.3 %collective-permute-start.6 = (f32[2,2,2,2,8,1152]{5,4,3,2,1,0:T(8,128)S(1)}, f32[2,2,2,2,8,1152]{5,4,3,2,1,0:T(8,128)S(1)}, u32[]{:S(2)}, u32[]{:S(2)}) collective-permute-start(f32[2,2,2,2,8,1152]{5,4,3,2,1,0:T(8,128)S(1)} %dynamic-slice_bitcast_fusion), channel_id=1, source_target_pairs={{0,8},{1,9},{2,10},{3,11},{4,12},{5,13},{6,14},{7,15},{8,0},{9,1},... | collective-permute-start | bytes 1769480 | tf_op jit(solution)/shard_map/ppermute | solution.py:234
  149.8 9.0 %collective-permute-start.2 = (f32[2,2,2,8,1152]{4,3,2,1,0:T(8,128)S(1)}, f32[2,2,2,8,1152]{4,3,2,1,0:T(8,128)S(1)}, u32[]{:S(2)}, u32[]{:S(2)}) collective-permute-start(f32[2,2,2,8,1152]{4,3,2,1,0:T(8,128)S(1)} %dynamic-slice_bitcast_fusion.3), channel_id=1, source_target_pairs={{0,16},{1,17},{2,18},{3,19},{4,20},{5,21},{6,22},{7,23},{8,24},{9,... | collective-permute-start | bytes 884744 | tf_op jit(solution)/shard_map/ppermute | solution.py:234
  151.5 9.3 %collective-permute-start.7 = (f32[2,2,2,8,1152]{4,3,2,1,0:T(8,128)S(1)}, f32[2,2,2,8,1152]{4,3,2,1,0:T(8,128)S(1)}, u32[]{:S(2)}, u32[]{:S(2)}) collective-permute-start(f32[2,2,2,8,1152]{4,3,2,1,0:T(8,128)S(1)} %dynamic-slice_bitcast_fusion.2), channel_id=1, source_target_pairs={{0,1},{1,0},{2,3},{3,2},{4,5},{5,4},{6,7},{7,6},{8,9},{9,8},{10,11... | collective-permute-start | bytes 884744 | tf_op jit(solution)/shard_map/ppermute | solution.py:234
  158.9 5.2 %collective-permute-start.3 = (f32[2,2,8,1152]{3,2,1,0:T(8,128)S(1)}, f32[2,2,8,1152]{3,2,1,0:T(8,128)S(1)}, u32[]{:S(2)}, u32[]{:S(2)}) collective-permute-start(f32[2,2,8,1152]{3,2,1,0:T(8,128)S(1)} %dynamic-slice_bitcast_fusion.5), channel_id=1, source_target_pairs={{0,1},{1,0},{2,3},{3,2},{4,5},{5,4},{6,7},{7,6},{8,9},{9,8},{10,11... | collective-permute-start | bytes 442376 | tf_op jit(solution)/shard_map/ppermute | solution.py:234
  160.9 5.3 %collective-permute-start.8 = (f32[2,2,8,1152]{3,2,1,0:T(8,128)S(1)}, f32[2,2,8,1152]{3,2,1,0:T(8,128)S(1)}, u32[]{:S(2)}, u32[]{:S(2)}) collective-permute-start(f32[2,2,8,1152]{3,2,1,0:T(8,128)S(1)} %dynamic-slice_bitcast_fusion.4), channel_id=1, source_target_pairs={{0,16},{1,17},{2,18},{3,19},{4,20},{5,21},{6,22},{7,23},{8,24},{9,... | collective-permute-start | bytes 442376 | tf_op jit(solution)/shard_map/ppermute | solution.py:234
  164.2 4.9 %collective-permute-start.4 = (f32[2,8,1152]{2,1,0:T(8,128)S(1)}, f32[2,8,1152]{2,1,0:T(8,128)S(1)}, u32[]{:S(2)}, u32[]{:S(2)}) collective-permute-start(f32[2,8,1152]{2,1,0:T(8,128)S(1)} %dynamic-slice_bitcast_fusion.7), channel_id=1, source_target_pairs={{0,2},{1,3},{2,0},{3,1},{4,6},{5,7},{6,4},{7,5},{8,10},{9,11},{10,... | collective-permute-start | bytes 221192 | tf_op jit(solution)/shard_map/ppermute | solution.py:234
  166.2 4.5 %collective-permute-start.9 = (f32[2,8,1152]{2,1,0:T(8,128)S(1)}, f32[2,8,1152]{2,1,0:T(8,128)S(1)}, u32[]{:S(2)}, u32[]{:S(2)}) collective-permute-start(f32[2,8,1152]{2,1,0:T(8,128)S(1)} %dynamic-slice_bitcast_fusion.6), channel_id=1, source_target_pairs={{0,2},{1,3},{2,0},{3,1},{4,6},{5,7},{6,4},{7,5},{8,10},{9,11},{10,... | collective-permute-start | bytes 221192 | tf_op jit(solution)/shard_map/ppermute | solution.py:234
  169.1 5.0 %collective-permute-start.5 = (f32[8,1152]{1,0:T(8,128)S(1)}, f32[8,1152]{1,0:T(8,128)S(1)}, u32[]{:S(2)}, u32[]{:S(2)}) collective-permute-start(f32[8,1152]{1,0:T(8,128)S(1)} %dynamic-slice_bitcast_fusion.9), channel_id=1, source_target_pairs={{0,4},{1,5},{2,6},{3,7},{4,0},{5,1},{6,2},{7,3},{8,12},{9,13},{10,... | collective-permute-start | bytes 110600 | tf_op jit(solution)/shard_map/ppermute | solution.py:234
  170.7 4.9 %collective-permute-start.10 = (f32[8,1152]{1,0:T(8,128)S(1)}, f32[8,1152]{1,0:T(8,128)S(1)}, u32[]{:S(2)}, u32[]{:S(2)}) collective-permute-start(f32[8,1152]{1,0:T(8,128)S(1)} %dynamic-slice_bitcast_fusion.8), channel_id=1, source_target_pairs={{0,4},{1,5},{2,6},{3,7},{4,0},{5,1},{6,2},{7,3},{8,12},{9,13},{10,... | collective-permute-start | bytes 110600 | tf_op jit(solution)/shard_map/ppermute | solution.py:234

commit v21 on v20

--- a/solution.py
+++ b/solution.py
@@ -176,7 +176,7 @@
 def second_stage(hidden, weight, grad, prev, out_dtype):
     owned, out_rows, out_cols, inputs = hidden.shape
     outputs = weight.shape[-1]
-    rows = min(32, out_rows)
+    rows = min(64, out_rows)
     row_padded = jnp.pad(hidden, ((0, 0), (1, 1), (0, 0), (0, 0)))
     shifted = jnp.stack([shift_cols_right(row_padded), row_padded, shift_cols_left(row_padded)], axis=1)
     full = pl.BlockSpec((None, 3, out_rows + 2, out_cols, inputs), lambda n, i: (n, 0, 0, 0, 0))

time: 177 us -> 177 us (level)
  no operation moved by 1% of the time
where the time goes in v21:
time: 177 us
  blocking collectives  53 us (30%)
  Pallas kernels  47.1 us (27%)
  waiting for transfers between devices  38.5 us (22%)
  starting transfers between devices  17.8 us (10%)
  local copies, waits for them, and re-layouts  12.3 us (7%)
  other arithmetic  7.39 us (4%)
    all_to_all x1, blocking collectives, local(): lax.all_to_all(local_hidden.reshape(tiles, owned, half_rows, width // 2,...  53 us
    pallas_call x2, Pallas kernels, second_stage(): pl.pallas_call(functools.partial(second_kernel, rows=rows, carry=prev is...  34.9 us
    all_to_all x1, waiting for transfers between devices, local(): lax.all_to_all(local_hidden.reshape(tiles, owned, half_rows, width // 2,...  21.5 us
    ppermute x10, waiting for transfers between devices, halving_reduce_scatter(): buf = keep + lax.ppermute(send, axes, pairs)  17 us
    pallas_call x1, Pallas kernels, first_stage(): pl.pallas_call(first_kernel, grid=(images // per,), in_specs=[pl.BlockSpe...  9.59 us
    ppermute x10, starting transfers between devices, halving_reduce_scatter(): buf = keep + lax.ppermute(send, axes, pairs)  9.02 us
    another operation x2, other arithmetic, second_stage(): jnp.stack([shift_cols_right(row_padded), row_padded, shift_cols_left(row_...  6.48 us
    ppermute x1, starting transfers between devices, shifted_2(): return lax.ppermute(shard, axis, pairs)  4.86 us
  transfers between devices with their start and end apart: 12, of which 9 were waited for; matrix products, arithmetic and copies ran while one was open for 8% of the time, Pallas kernels for 25%

profile of v21, /device:TPU:0, one launch (start us, length us, event | category | flops | bytes accessed | tf_op | source)
XLA Modules:
  0.0 177.0 jit_solution(14000454466752131026)
XLA Ops:
  0.6 1.0 slice.21
  1.6 4.9 %collective-permute-start = (bf16[8,1,128,128]{3,2,1,0:T(8,128)(2,1)S(1)}, bf16[8,1,128,128]{3,2,1,0:T(8,128)(2,1)S(1)}, u32[]{:S(2)}, u32[]{:S(2)}) collective-permute-start(bf16[8,1,128,128]{3,2,1,0:T(8,128)(2,1)S(1)} %slice.21), channel_id=1, source_target_pairs={{0,1},{1,2},{2,3},{3,4},{4,5},{5,6},{6,7},{8,9},{9,10},{10,11},{11... | collective-permute-start | bytes 786440 | tf_op jit(solution)/shard_map/ppermute | solution.py:14
  6.5 9.6 %shard_map.59 = (bf16[8,16,64,128]{3,2,1,0:T(8,128)(2,1)}, bf16[8,16,64,128]{3,2,1,0:T(8,128)(2,1)}) custom-call(bf16[8,32,128,128]{3,2,1,0:T(8,128)(2,1)} %x_ref.3, bf16[1152,256]{1,0:T(8,128)(2,1)} %bitcast.79), custom_call_target="tpu_custom_call" | custom-call | flops 4831838208 | bytes 12582912 | tf_op jit(solution)/shard_map/pallas_call | solution.py:109
  16.1 0.0 collective-permute-done.up_ref
  16.1 0.7 copy-done.4
  16.8 2.6 %shard_map.60 = (bf16[8,16,64,128]{3,2,1,0:T(8,128)(2,1)}, bf16[8,16,64,128]{3,2,1,0:T(8,128)(2,1)}) custom-call(bf16[8,32,128,128]{3,2,1,0:T(8,128)(2,1)} %x_ref.3, bf16[8,1,128,128]{3,2,1,0:T(8,128)(2,1)} %copy-done.4, bf16[1152,256]{1,0:T(8,128)(2,1)} %bitcast.80, ...), custom_call_target="tpu_custom_call", output_to_operand_aliasing={{0}: (3, {}), {1}: (4, {})} | custom-call | flops 301989888 | bytes 786432 | tf_op jit(solution)/shard_map/pallas_call | solution.py:121
  19.3 53.0 %all_to_all.21 = bf16[8,1,16,64,128]{4,3,2,1,0:T(8,128)(2,1)} all-to-all(bf16[8,1,16,64,128]{4,3,2,1,0:T(8,128)(2,1)} %bitcast.73), channel_id=1, replica_groups=mesh['group'=4,'tile'=8] {'tile'}, dimensions={0} | all-to-all | bytes 4194304 | tf_op jit(solution)/shard_map/all_to_all | solution.py:255
  72.4 3.9 %all-to-all-start = ((bf16[8,1,16,64,128]{4,3,2,1,0:T(8,128)(2,1)}), bf16[8,1,16,64,128]{4,3,2,1,0:T(8,128)(2,1)S(1)}, u32[]{:S(2)}, u32[]{:S(2)}) async-start(bf16[8,1,16,64,128]{4,3,2,1,0:T(8,128)(2,1)} %bitcast.74), calls=%async_computation | async-start | bytes 4194304 | tf_op jit(solution)/shard_map/all_to_all | solution.py:255
  76.3 0.0 copy-done.1
  76.3 1.1 fusion
  77.4 0.9 copy-done
  78.3 0.4 pad_bitcast_fusion.5
  78.8 1.4 pad_slice_fusion.3
  80.2 1.8 %pad_bitcast_fusion.2 = (bf16[1,1,130,64,128]{4,3,2,1,0:T(8,128)(2,1)S(1)}, bf16[1,1,130,64,128]{4,3,2,1,0:T(8,128)(2,1)S(1)}) fusion(bf16[1,130,63,128]{3,2,1,0:T(8,128)(2,1)S(1)} %get-tuple-element.25, bf16[1,130,63,128]{3,2,1,0:T(8,128)(2,1)S(1)} %get-tuple-element.24), kind=kLoop, calls=%fused_computation.4 | loop fusion | bytes 8453120 | tf_op jit(solution)/shard_map/stack | solution.py:181
  82.0 3.2 %pad_maximum_fusion.refs_0_ = bf16[1,3,130,64,128]{4,3,2,1,0:T(8,128)(2,1)} fusion(bf16[1,1,130,64,128]{4,3,2,1,0:T(8,128)(2,1)S(1)} %get-tuple-element.28, bf16[1,1,130,64,128]{4,3,2,1,0:T(8,128)(2,1)S(1)} %pad_bitcast_fusion.5, bf16[1,1,130,64,128]{4,3,2,1,0:T(8,128)(2,1)S(1)} %get-tuple-element.29), kind=kLoop, calls=%fused_computation | loop fusion | flops 6389760 | bytes 12779520 | tf_op jit(solution)/shard_map/stack | solution.py:181
  85.2 17.2 %shard_map.61 = (f32[1,128,64,256]{3,2,1,0:T(8,128)}, f32[1,256,1152]{2,1,0:T(8,128)}) custom-call(bf16[1,3,130,64,128]{4,3,2,1,0:T(8,128)(2,1)} %pad_maximum_fusion.refs_0_, bf16[1152,256]{1,0:T(8,128)(2,1)} %bitcast.82, bf16[1,8192,256]{2,1,0:T(8,128)(2,1)} %bitcast.85), custom_call_target="tpu_custom_call" | custom-call | flops 9663676416 | bytes 26345472 | tf_op jit(solution)/shard_map/pallas_call | solution.py:194
  102.4 21.5 %all-to-all-done = bf16[8,1,16,64,128]{4,3,2,1,0:T(8,128)(2,1)S(1)} async-done(((bf16[8,1,16,64,128]{4,3,2,1,0:T(8,128)(2,1)}), bf16[8,1,16,64,128]{4,3,2,1,0:T(8,128)(2,1)S(1)}, u32[]{:S(2)}, u32[]{:S(2)}) %all-to-all-start) | async-done | bytes 2097184 | tf_op jit(solution)/shard_map/all_to_all | solution.py:255
  123.9 0.4 pad_bitcast_fusion.4
  124.3 0.0 copy-start.2
  124.3 1.4 pad_slice_fusion.1
  125.8 0.1 collective-permute-start.1
  125.9 1.3 pad_bitcast_fusion.1
  127.1 0.4 pad_bitcast_fusion
  127.6 3.2 %pad_maximum_fusion.1.refs_0_ = bf16[1,3,130,64,128]{4,3,2,1,0:T(8,128)(2,1)} fusion(bf16[1,1,130,64,128]{4,3,2,1,0:T(8,128)(2,1)S(1)} %pad_bitcast_fusion, bf16[1,1,130,64,128]{4,3,2,1,0:T(8,128)(2,1)S(1)} %pad_bitcast_fusion.4, bf16[1,1,130,64,128]{4,3,2,1,0:T(8,128)(2,1)S(1)} %pad_bitcast_fusion.1), kind=kLoop, calls=%fused_computation.1 | loop fusion | flops 6389760 | bytes 12779520 | tf_op jit(solution)/shard_map/stack | solution.py:181
  130.8 17.8 %shard_map.62 = (bf16[1,128,64,256]{3,2,1,0:T(8,128)(2,1)}, f32[1,256,1152]{2,1,0:T(8,128)}) custom-call(bf16[1,3,130,64,128]{4,3,2,1,0:T(8,128)(2,1)} %pad_maximum_fusion.1.refs_0_, bf16[1152,256]{1,0:T(8,128)(2,1)} %bitcast.81, bf16[1,8192,256]{2,1,0:T(8,128)(2,1)} %bitcast.86, f32[1,128,64,256]{3,2,1,0:T(8,128)} %get-tuple-element.18.refs_3_), custom_call_target="tpu_custom_call" | custom-call | flops 9663676416 | bytes 26345472 | tf_op jit(solution)/shard_map/pallas_call | solution.py:194
  148.6 1.2 dynamic-slice_bitcast_fusion
  149.8 0.6 collective-permute-start.6
  150.4 0.0 collective-permute-done.1
  150.4 0.1 bitcast_add_fusion.1
  150.5 1.6 collective-permute-start.2
  152.1 0.0 collective-permute-done.6
  152.1 0.1 bitcast_add_fusion
  152.2 1.4 collective-permute-start.7
  153.6 5.9 %collective-permute-done.2 = f32[2,2,2,8,1152]{4,3,2,1,0:T(8,128)S(1)} collective-permute-done((f32[2,2,2,8,1152]{4,3,2,1,0:T(8,128)S(1)}, f32[2,2,2,8,1152]{4,3,2,1,0:T(8,128)S(1)}, u32[]{:S(2)}, u32[]{:S(2)}) %collective-permute-start.2) | collective-permute-done | bytes 294944 | tf_op jit(solution)/shard_map/ppermute | solution.py:234
  159.6 1.4 collective-permute-start.3
  161.0 0.5 collective-permute-done.7
  161.5 1.6 collective-permute-start.8
  163.1 1.6 collective-permute-done.3
  164.8 0.1 collective-permute-start.4
  164.9 2.0 %collective-permute-done.8 = f32[2,2,8,1152]{3,2,1,0:T(8,128)S(1)} collective-permute-done((f32[2,2,8,1152]{3,2,1,0:T(8,128)S(1)}, f32[2,2,8,1152]{3,2,1,0:T(8,128)S(1)}, u32[]{:S(2)}, u32[]{:S(2)}) %collective-permute-start.8) | collective-permute-done | bytes 147488 | tf_op jit(solution)/shard_map/ppermute | solution.py:234
  166.9 0.1 collective-permute-start.9
  167.0 2.7 %collective-permute-done.4 = f32[2,8,1152]{2,1,0:T(8,128)S(1)} collective-permute-done((f32[2,8,1152]{2,1,0:T(8,128)S(1)}, f32[2,8,1152]{2,1,0:T(8,128)S(1)}, u32[]{:S(2)}, u32[]{:S(2)}) %collective-permute-start.4) | collective-permute-done | bytes 73760 | tf_op jit(solution)/shard_map/ppermute | solution.py:234
  169.8 0.7 collective-permute-start.5
  170.5 0.9 collective-permute-done.9
  171.4 1.4 collective-permute-start.10
  172.8 1.9 %collective-permute-done.5 = f32[8,1152]{1,0:T(8,128)S(1)} collective-permute-done((f32[8,1152]{1,0:T(8,128)S(1)}, f32[8,1152]{1,0:T(8,128)S(1)}, u32[]{:S(2)}, u32[]{:S(2)}) %collective-permute-start.5) | collective-permute-done | bytes 36896 | tf_op jit(solution)/shard_map/ppermute | solution.py:234
  174.8 1.5 collective-permute-done.10
  176.3 0.6 pad_maximum_fusion.2
  (23 shorter events, 0.4 us)
Async XLA Ops:
  1.6 14.5 %collective-permute-start = (bf16[8,1,128,128]{3,2,1,0:T(8,128)(2,1)S(1)}, bf16[8,1,128,128]{3,2,1,0:T(8,128)(2,1)S(1)}, u32[]{:S(2)}, u32[]{:S(2)}) collective-permute-start(bf16[8,1,128,128]{3,2,1,0:T(8,128)(2,1)S(1)} %slice.21), channel_id=1, source_target_pairs={{0,1},{1,2},{2,3},{3,4},{4,5},{5,6},{6,7},{8,9},{9,10},{10,11},{11... | collective-permute-start | bytes 786440 | tf_op jit(solution)/shard_map/ppermute | solution.py:14
  16.1 0.7 copy-start.4
  72.4 3.9 %copy-start.1 = (bf16[3,3,256,256]{3,2,1,0:T(8,128)(2,1)S(1)}, bf16[3,3,256,256]{3,2,1,0:T(8,128)(2,1)}, u32[]{:S(2)}) copy-start(bf16[3,3,256,256]{3,2,1,0:T(8,128)(2,1)} %param.6) | copy-start | bytes 3538948
  72.4 51.5 %all-to-all-start = ((bf16[8,1,16,64,128]{4,3,2,1,0:T(8,128)(2,1)}), bf16[8,1,16,64,128]{4,3,2,1,0:T(8,128)(2,1)S(1)}, u32[]{:S(2)}, u32[]{:S(2)}) async-start(bf16[8,1,16,64,128]{4,3,2,1,0:T(8,128)(2,1)} %bitcast.74), calls=%async_computation | async-start | bytes 4194304 | tf_op jit(solution)/shard_map/all_to_all | solution.py:255
  76.3 2.0 %copy-start = (bf16[8,1,16,64,128]{4,3,2,1,0:T(8,128)(2,1)S(1)}, bf16[8,1,16,64,128]{4,3,2,1,0:T(8,128)(2,1)}, u32[]{:S(2)}) copy-start(bf16[8,1,16,64,128]{4,3,2,1,0:T(8,128)(2,1)} %all_to_all.21) | copy-start | bytes 6291460
  124.3 1.4 copy-start.2
  125.8 24.6 %collective-permute-start.1 = (f32[2,2,2,2,8,1152]{5,4,3,2,1,0:T(8,128)S(1)}, f32[2,2,2,2,8,1152]{5,4,3,2,1,0:T(8,128)S(1)}, u32[]{:S(2)}, u32[]{:S(2)}) collective-permute-start(f32[2,2,2,2,8,1152]{5,4,3,2,1,0:T(8,128)S(1)} %dynamic-slice_bitcast_fusion.1), channel_id=1, source_target_pairs={{0,8},{1,9},{2,10},{3,11},{4,12},{5,13},{6,14},{7,15},{8,0},{9,1},... | collective-permute-start | bytes 1769480 | tf_op jit(solution)/shard_map/ppermute | solution.py:234
  148.6 3.5 %copy-start.3 = (f32[1,256,1152]{2,1,0:T(8,128)S(1)}, f32[1,256,1152]{2,1,0:T(8,128)}, u32[]{:S(2)}) copy-start(f32[1,256,1152]{2,1,0:T(8,128)} %get-tuple-element.21) | copy-start | bytes 3538948
  149.8 2.3 %collective-permute-start.6 = (f32[2,2,2,2,8,1152]{5,4,3,2,1,0:T(8,128)S(1)}, f32[2,2,2,2,8,1152]{5,4,3,2,1,0:T(8,128)S(1)}, u32[]{:S(2)}, u32[]{:S(2)}) collective-permute-start(f32[2,2,2,2,8,1152]{5,4,3,2,1,0:T(8,128)S(1)} %dynamic-slice_bitcast_fusion), channel_id=1, source_target_pairs={{0,8},{1,9},{2,10},{3,11},{4,12},{5,13},{6,14},{7,15},{8,0},{9,1},... | collective-permute-start | bytes 1769480 | tf_op jit(solution)/shard_map/ppermute | solution.py:234
  150.5 9.0 %collective-permute-start.2 = (f32[2,2,2,8,1152]{4,3,2,1,0:T(8,128)S(1)}, f32[2,2,2,8,1152]{4,3,2,1,0:T(8,128)S(1)}, u32[]{:S(2)}, u32[]{:S(2)}) collective-permute-start(f32[2,2,2,8,1152]{4,3,2,1,0:T(8,128)S(1)} %dynamic-slice_bitcast_fusion.3), channel_id=1, source_target_pairs={{0,16},{1,17},{2,18},{3,19},{4,20},{5,21},{6,22},{7,23},{8,24},{9,... | collective-permute-start | bytes 884744 | tf_op jit(solution)/shard_map/ppermute | solution.py:234
  152.2 9.3 %collective-permute-start.7 = (f32[2,2,2,8,1152]{4,3,2,1,0:T(8,128)S(1)}, f32[2,2,2,8,1152]{4,3,2,1,0:T(8,128)S(1)}, u32[]{:S(2)}, u32[]{:S(2)}) collective-permute-start(f32[2,2,2,8,1152]{4,3,2,1,0:T(8,128)S(1)} %dynamic-slice_bitcast_fusion.2), channel_id=1, source_target_pairs={{0,1},{1,0},{2,3},{3,2},{4,5},{5,4},{6,7},{7,6},{8,9},{9,8},{10,11... | collective-permute-start | bytes 884744 | tf_op jit(solution)/shard_map/ppermute | solution.py:234
  159.6 5.2 %collective-permute-start.3 = (f32[2,2,8,1152]{3,2,1,0:T(8,128)S(1)}, f32[2,2,8,1152]{3,2,1,0:T(8,128)S(1)}, u32[]{:S(2)}, u32[]{:S(2)}) collective-permute-start(f32[2,2,8,1152]{3,2,1,0:T(8,128)S(1)} %dynamic-slice_bitcast_fusion.5), channel_id=1, source_target_pairs={{0,1},{1,0},{2,3},{3,2},{4,5},{5,4},{6,7},{7,6},{8,9},{9,8},{10,11... | collective-permute-start | bytes 442376 | tf_op jit(solution)/shard_map/ppermute | solution.py:234
  161.5 5.3 %collective-permute-start.8 = (f32[2,2,8,1152]{3,2,1,0:T(8,128)S(1)}, f32[2,2,8,1152]{3,2,1,0:T(8,128)S(1)}, u32[]{:S(2)}, u32[]{:S(2)}) collective-permute-start(f32[2,2,8,1152]{3,2,1,0:T(8,128)S(1)} %dynamic-slice_bitcast_fusion.4), channel_id=1, source_target_pairs={{0,16},{1,17},{2,18},{3,19},{4,20},{5,21},{6,22},{7,23},{8,24},{9,... | collective-permute-start | bytes 442376 | tf_op jit(solution)/shard_map/ppermute | solution.py:234
  164.8 4.9 %collective-permute-start.4 = (f32[2,8,1152]{2,1,0:T(8,128)S(1)}, f32[2,8,1152]{2,1,0:T(8,128)S(1)}, u32[]{:S(2)}, u32[]{:S(2)}) collective-permute-start(f32[2,8,1152]{2,1,0:T(8,128)S(1)} %dynamic-slice_bitcast_fusion.7), channel_id=1, source_target_pairs={{0,2},{1,3},{2,0},{3,1},{4,6},{5,7},{6,4},{7,5},{8,10},{9,11},{10,... | collective-permute-start | bytes 221192 | tf_op jit(solution)/shard_map/ppermute | solution.py:234
  166.9 4.5 %collective-permute-start.9 = (f32[2,8,1152]{2,1,0:T(8,128)S(1)}, f32[2,8,1152]{2,1,0:T(8,128)S(1)}, u32[]{:S(2)}, u32[]{:S(2)}) collective-permute-start(f32[2,8,1152]{2,1,0:T(8,128)S(1)} %dynamic-slice_bitcast_fusion.6), channel_id=1, source_target_pairs={{0,2},{1,3},{2,0},{3,1},{4,6},{5,7},{6,4},{7,5},{8,10},{9,11},{10,... | collective-permute-start | bytes 221192 | tf_op jit(solution)/shard_map/ppermute | solution.py:234
  169.8 5.0 %collective-permute-start.5 = (f32[8,1152]{1,0:T(8,128)S(1)}, f32[8,1152]{1,0:T(8,128)S(1)}, u32[]{:S(2)}, u32[]{:S(2)}) collective-permute-start(f32[8,1152]{1,0:T(8,128)S(1)} %dynamic-slice_bitcast_fusion.9), channel_id=1, source_target_pairs={{0,4},{1,5},{2,6},{3,7},{4,0},{5,1},{6,2},{7,3},{8,12},{9,13},{10,... | collective-permute-start | bytes 110600 | tf_op jit(solution)/shard_map/ppermute | solution.py:234
  171.4 4.9 %collective-permute-start.10 = (f32[8,1152]{1,0:T(8,128)S(1)}, f32[8,1152]{1,0:T(8,128)S(1)}, u32[]{:S(2)}, u32[]{:S(2)}) collective-permute-start(f32[8,1152]{1,0:T(8,128)S(1)} %dynamic-slice_bitcast_fusion.8), channel_id=1, source_target_pairs={{0,4},{1,5},{2,6},{3,7},{4,0},{5,1},{6,2},{7,3},{8,12},{9,13},{10,... | collective-permute-start | bytes 110600 | tf_op jit(solution)/shard_map/ppermute | solution.py:234

commit v22 on v20

--- a/solution.py
+++ b/solution.py
@@ -178,7 +178,11 @@
     outputs = weight.shape[-1]
     rows = min(32, out_rows)
     row_padded = jnp.pad(hidden, ((0, 0), (1, 1), (0, 0), (0, 0)))
-    shifted = jnp.stack([shift_cols_right(row_padded), row_padded, shift_cols_left(row_padded)], axis=1)
+    zero = jnp.zeros((), hidden.dtype)
+    none = (0, 0, 0)
+    right = lax.pad(row_padded, zero, [none, none, (1, -1, 0), none])
+    left = lax.pad(row_padded, zero, [none, none, (-1, 1, 0), none])
+    shifted = jnp.stack([right, row_padded, left], axis=1)
     full = pl.BlockSpec((None, 3, out_rows + 2, out_cols, inputs), lambda n, i: (n, 0, 0, 0, 0))
     block = pl.BlockSpec((None, rows, out_cols, outputs), lambda n, i: (n, i, 0, 0))
     in_specs = [

time: 177 us -> 178 us (level)
    slice x2 -> x0, local copies, waits for them, and re-layouts: 2.82 us -> none  [shift_cols_right(): return jnp.concatenate([zero_col, slab[:, :, :-1]], axis=2)]
    another operation x5 -> x4, local copies, waits for them, and re-layouts: 4.33 us -> 6.89 us  [second_stage(): shifted = jnp.stack([right, row_padded, left], axis=1)]
  transfers between devices with their start and end apart: 12 -> 12, of which waited for: 9 -> 9; matrix products, arithmetic and copies ran while one was open for 8% -> 9% of each run, Pallas kernels for 25% -> 25%
where the time goes in v22:
time: 178 us
  blocking collectives  53 us (30%)
  Pallas kernels  46.1 us (26%)
  waiting for transfers between devices  39.3 us (22%)
  starting transfers between devices  17.8 us (10%)
  local copies, waits for them, and re-layouts  13.1 us (7%)
  other arithmetic  7.44 us (4%)
    all_to_all x1, blocking collectives, local(): lax.all_to_all(local_hidden.reshape(tiles, owned, half_rows, width // 2,...  53 us
    pallas_call x2, Pallas kernels, second_stage(): pl.pallas_call(functools.partial(second_kernel, rows=rows, carry=prev is...  34 us
    all_to_all x1, waiting for transfers between devices, local(): lax.all_to_all(local_hidden.reshape(tiles, owned, half_rows, width // 2,...  21.8 us
    ppermute x10, waiting for transfers between devices, halving_reduce_scatter(): buf = keep + lax.ppermute(send, axes, pairs)  17.4 us
    pallas_call x1, Pallas kernels, first_stage(): pl.pallas_call(first_kernel, grid=(images // per,), in_specs=[pl.BlockSpe...  9.58 us
    ppermute x10, starting transfers between devices, halving_reduce_scatter(): buf = keep + lax.ppermute(send, axes, pairs)  9.02 us
    another operation x4, local copies, waits for them, and re-layouts, second_stage(): shifted = jnp.stack([right, row_padded, left], axis=1)  6.89 us
    another operation x2, other arithmetic, second_stage(): shifted = jnp.stack([right, row_padded, left], axis=1)  6.54 us
  transfers between devices with their start and end apart: 12, of which 9 were waited for; matrix products, arithmetic and copies ran while one was open for 9% of the time, Pallas kernels for 25%

profile of v22, /device:TPU:0, one launch (start us, length us, event | category | flops | bytes accessed | tf_op | source)
XLA Modules:
  0.0 177.6 jit_solution(10724502785917443169)
XLA Ops:
  0.6 1.0 slice.13
  1.6 4.9 %collective-permute-start = (bf16[8,1,128,128]{3,2,1,0:T(8,128)(2,1)S(1)}, bf16[8,1,128,128]{3,2,1,0:T(8,128)(2,1)S(1)}, u32[]{:S(2)}, u32[]{:S(2)}) collective-permute-start(bf16[8,1,128,128]{3,2,1,0:T(8,128)(2,1)S(1)} %slice.13), channel_id=1, source_target_pairs={{0,1},{1,2},{2,3},{3,4},{4,5},{5,6},{6,7},{8,9},{9,10},{10,11},{11... | collective-permute-start | bytes 786440 | tf_op jit(solution)/shard_map/ppermute | solution.py:14
  6.5 9.6 %shard_map.59 = (bf16[8,16,64,128]{3,2,1,0:T(8,128)(2,1)}, bf16[8,16,64,128]{3,2,1,0:T(8,128)(2,1)}) custom-call(bf16[8,32,128,128]{3,2,1,0:T(8,128)(2,1)} %x_ref.3, bf16[1152,256]{1,0:T(8,128)(2,1)} %bitcast.77), custom_call_target="tpu_custom_call" | custom-call | flops 4831838208 | bytes 12582912 | tf_op jit(solution)/shard_map/pallas_call | solution.py:109
  16.1 0.0 collective-permute-done.up_ref
  16.1 0.7 copy-done.4
  16.8 2.6 %shard_map.60 = (bf16[8,16,64,128]{3,2,1,0:T(8,128)(2,1)}, bf16[8,16,64,128]{3,2,1,0:T(8,128)(2,1)}) custom-call(bf16[8,32,128,128]{3,2,1,0:T(8,128)(2,1)} %x_ref.3, bf16[8,1,128,128]{3,2,1,0:T(8,128)(2,1)} %copy-done.4, bf16[1152,256]{1,0:T(8,128)(2,1)} %bitcast.78, ...), custom_call_target="tpu_custom_call", output_to_operand_aliasing={{0}: (3, {}), {1}: (4, {})} | custom-call | flops 301989888 | bytes 786432 | tf_op jit(solution)/shard_map/pallas_call | solution.py:121
  19.3 53.0 %all_to_all.21 = bf16[8,1,16,64,128]{4,3,2,1,0:T(8,128)(2,1)} all-to-all(bf16[8,1,16,64,128]{4,3,2,1,0:T(8,128)(2,1)} %bitcast.71), channel_id=1, replica_groups=mesh['group'=4,'tile'=8] {'tile'}, dimensions={0} | all-to-all | bytes 4194304 | tf_op jit(solution)/shard_map/all_to_all | solution.py:259
  72.3 3.9 %all-to-all-start = ((bf16[8,1,16,64,128]{4,3,2,1,0:T(8,128)(2,1)}), bf16[8,1,16,64,128]{4,3,2,1,0:T(8,128)(2,1)S(1)}, u32[]{:S(2)}, u32[]{:S(2)}) async-start(bf16[8,1,16,64,128]{4,3,2,1,0:T(8,128)(2,1)} %bitcast.72), calls=%async_computation | async-start | bytes 4194304 | tf_op jit(solution)/shard_map/all_to_all | solution.py:259
  76.3 0.0 copy-done.1
  76.3 0.0 copy-start
  76.3 1.1 fusion.4
  77.4 0.9 copy-done
  78.3 1.5 pad_bitcast_fusion.1
  79.8 2.2 %fusion = (bf16[1,1,130,64,128]{4,3,2,1,0:T(8,128)(2,1)S(1)}, bf16[1,1,130,64,128]{4,3,2,1,0:T(8,128)(2,1)S(1)}) fusion(bf16[1,130,64,128]{3,2,1,0:T(8,128)(2,1)S(1)} %get-tuple-element.29), kind=kLoop, calls=%fused_computation.6 | loop fusion | bytes 6389760 | tf_op jit(solution)/shard_map/stack | solution.py:185
  82.0 3.3 %pad_maximum_fusion.refs_0_ = bf16[1,3,130,64,128]{4,3,2,1,0:T(8,128)(2,1)} fusion(bf16[1,1,130,64,128]{4,3,2,1,0:T(8,128)(2,1)S(1)} %get-tuple-element.25, bf16[1,1,130,64,128]{4,3,2,1,0:T(8,128)(2,1)S(1)} %get-tuple-element.28, bf16[1,1,130,64,128]{4,3,2,1,0:T(8,128)(2,1)S(1)} %get-tuple-element.24), kind=kLoop, calls=%fused_computation | loop fusion | flops 6389760 | bytes 12779520 | tf_op jit(solution)/shard_map/stack | solution.py:185
  85.3 16.8 %shard_map.61 = (f32[1,128,64,256]{3,2,1,0:T(8,128)}, f32[1,256,1152]{2,1,0:T(8,128)}) custom-call(bf16[1,3,130,64,128]{4,3,2,1,0:T(8,128)(2,1)} %pad_maximum_fusion.refs_0_, bf16[1152,256]{1,0:T(8,128)(2,1)} %bitcast.80, bf16[1,8192,256]{2,1,0:T(8,128)(2,1)} %bitcast.83), custom_call_target="tpu_custom_call" | custom-call | flops 9663676416 | bytes 26345472 | tf_op jit(solution)/shard_map/pallas_call | solution.py:198
  102.1 21.8 %all-to-all-done = bf16[8,1,16,64,128]{4,3,2,1,0:T(8,128)(2,1)S(1)} async-done(((bf16[8,1,16,64,128]{4,3,2,1,0:T(8,128)(2,1)}), bf16[8,1,16,64,128]{4,3,2,1,0:T(8,128)(2,1)S(1)}, u32[]{:S(2)}, u32[]{:S(2)}) %all-to-all-start) | async-done | bytes 2097184 | tf_op jit(solution)/shard_map/all_to_all | solution.py:259
  123.9 1.1 dynamic-slice_bitcast_fusion.1
  125.0 0.1 collective-permute-start.1
  125.1 1.1 pad_bitcast_fusion
  126.1 2.2 %fusion.2 = (bf16[1,1,130,64,128]{4,3,2,1,0:T(8,128)(2,1)S(1)}, bf16[1,1,130,64,128]{4,3,2,1,0:T(8,128)(2,1)S(1)}) fusion(bf16[1,130,64,128]{3,2,1,0:T(8,128)(2,1)S(1)} %get-tuple-element.27), kind=kLoop, calls=%fused_computation.8 | loop fusion | bytes 6389760 | tf_op jit(solution)/shard_map/stack | solution.py:185
  128.3 3.3 %pad_maximum_fusion.1.refs_0_ = bf16[1,3,130,64,128]{4,3,2,1,0:T(8,128)(2,1)} fusion(bf16[1,1,130,64,128]{4,3,2,1,0:T(8,128)(2,1)S(1)} %get-tuple-element.23, bf16[1,1,130,64,128]{4,3,2,1,0:T(8,128)(2,1)S(1)} %get-tuple-element.26, bf16[1,1,130,64,128]{4,3,2,1,0:T(8,128)(2,1)S(1)} %get-tuple-element.22), kind=kLoop, calls=%fused_computation.1 | loop fusion | flops 6389760 | bytes 12779520 | tf_op jit(solution)/shard_map/stack | solution.py:185
  131.6 17.2 %shard_map.62 = (bf16[1,128,64,256]{3,2,1,0:T(8,128)(2,1)}, f32[1,256,1152]{2,1,0:T(8,128)}) custom-call(bf16[1,3,130,64,128]{4,3,2,1,0:T(8,128)(2,1)} %pad_maximum_fusion.1.refs_0_, bf16[1152,256]{1,0:T(8,128)(2,1)} %bitcast.79, bf16[1,8192,256]{2,1,0:T(8,128)(2,1)} %bitcast.84, f32[1,128,64,256]{3,2,1,0:T(8,128)} %get-tuple-element.18.refs_3_), custom_call_target="tpu_custom_call" | custom-call | flops 9663676416 | bytes 26345472 | tf_op jit(solution)/shard_map/pallas_call | solution.py:198
  148.8 1.2 dynamic-slice_bitcast_fusion
  150.0 0.6 collective-permute-start.6
  150.6 0.0 collective-permute-done.1
  150.6 0.0 copy-done.2
  150.6 0.1 bitcast_add_fusion.1
  150.7 1.6 collective-permute-start.2
  152.3 0.0 collective-permute-done.6
  152.3 0.0 copy-done.3
  152.3 0.1 bitcast_add_fusion
  152.4 1.4 collective-permute-start.7
  153.8 5.9 %collective-permute-done.2 = f32[2,2,2,8,1152]{4,3,2,1,0:T(8,128)S(1)} collective-permute-done((f32[2,2,2,8,1152]{4,3,2,1,0:T(8,128)S(1)}, f32[2,2,2,8,1152]{4,3,2,1,0:T(8,128)S(1)}, u32[]{:S(2)}, u32[]{:S(2)}) %collective-permute-start.2) | collective-permute-done | bytes 294944 | tf_op jit(solution)/shard_map/ppermute | solution.py:238
  159.8 1.4 collective-permute-start.3
  161.2 0.5 collective-permute-done.7
  161.7 1.6 collective-permute-start.8
  163.3 1.7 collective-permute-done.3
  165.0 0.1 collective-permute-start.4
  165.1 1.9 %collective-permute-done.8 = f32[2,2,8,1152]{3,2,1,0:T(8,128)S(1)} collective-permute-done((f32[2,2,8,1152]{3,2,1,0:T(8,128)S(1)}, f32[2,2,8,1152]{3,2,1,0:T(8,128)S(1)}, u32[]{:S(2)}, u32[]{:S(2)}) %collective-permute-start.8) | collective-permute-done | bytes 147488 | tf_op jit(solution)/shard_map/ppermute | solution.py:238
  167.1 0.1 collective-permute-start.9
  167.2 2.7 %collective-permute-done.4 = f32[2,8,1152]{2,1,0:T(8,128)S(1)} collective-permute-done((f32[2,8,1152]{2,1,0:T(8,128)S(1)}, f32[2,8,1152]{2,1,0:T(8,128)S(1)}, u32[]{:S(2)}, u32[]{:S(2)}) %collective-permute-start.4) | collective-permute-done | bytes 73760 | tf_op jit(solution)/shard_map/ppermute | solution.py:238
  169.9 0.7 collective-permute-start.5
  170.7 0.9 collective-permute-done.9
  171.6 1.4 collective-permute-start.10
  173.0 1.9 %collective-permute-done.5 = f32[8,1152]{1,0:T(8,128)S(1)} collective-permute-done((f32[8,1152]{1,0:T(8,128)S(1)}, f32[8,1152]{1,0:T(8,128)S(1)}, u32[]{:S(2)}, u32[]{:S(2)}) %collective-permute-start.5) | collective-permute-done | bytes 36896 | tf_op jit(solution)/shard_map/ppermute | solution.py:238
  175.0 1.9 %collective-permute-done.10 = f32[8,1152]{1,0:T(8,128)S(1)} collective-permute-done((f32[8,1152]{1,0:T(8,128)S(1)}, f32[8,1152]{1,0:T(8,128)S(1)}, u32[]{:S(2)}, u32[]{:S(2)}) %collective-permute-start.10) | collective-permute-done | bytes 36896 | tf_op jit(solution)/shard_map/ppermute | solution.py:238
  176.9 0.6 pad_maximum_fusion.2
  (20 shorter events, 0.3 us)
Async XLA Ops:
  1.6 14.4 %collective-permute-start = (bf16[8,1,128,128]{3,2,1,0:T(8,128)(2,1)S(1)}, bf16[8,1,128,128]{3,2,1,0:T(8,128)(2,1)S(1)}, u32[]{:S(2)}, u32[]{:S(2)}) collective-permute-start(bf16[8,1,128,128]{3,2,1,0:T(8,128)(2,1)S(1)} %slice.13), channel_id=1, source_target_pairs={{0,1},{1,2},{2,3},{3,4},{4,5},{5,6},{6,7},{8,9},{9,10},{10,11},{11... | collective-permute-start | bytes 786440 | tf_op jit(solution)/shard_map/ppermute | solution.py:14
  16.1 0.7 copy-start.4
  72.3 3.9 %copy-start.1 = (bf16[3,3,256,256]{3,2,1,0:T(8,128)(2,1)S(1)}, bf16[3,3,256,256]{3,2,1,0:T(8,128)(2,1)}, u32[]{:S(2)}) copy-start(bf16[3,3,256,256]{3,2,1,0:T(8,128)(2,1)} %param.6) | copy-start | bytes 3538948
  72.3 51.5 %all-to-all-start = ((bf16[8,1,16,64,128]{4,3,2,1,0:T(8,128)(2,1)}), bf16[8,1,16,64,128]{4,3,2,1,0:T(8,128)(2,1)S(1)}, u32[]{:S(2)}, u32[]{:S(2)}) async-start(bf16[8,1,16,64,128]{4,3,2,1,0:T(8,128)(2,1)} %bitcast.72), calls=%async_computation | async-start | bytes 4194304 | tf_op jit(solution)/shard_map/all_to_all | solution.py:259
  76.3 2.0 %copy-start = (bf16[8,1,16,64,128]{4,3,2,1,0:T(8,128)(2,1)S(1)}, bf16[8,1,16,64,128]{4,3,2,1,0:T(8,128)(2,1)}, u32[]{:S(2)}) copy-start(bf16[8,1,16,64,128]{4,3,2,1,0:T(8,128)(2,1)} %all_to_all.21) | copy-start | bytes 6291460
  125.0 25.6 %collective-permute-start.1 = (f32[2,2,2,2,8,1152]{5,4,3,2,1,0:T(8,128)S(1)}, f32[2,2,2,2,8,1152]{5,4,3,2,1,0:T(8,128)S(1)}, u32[]{:S(2)}, u32[]{:S(2)}) collective-permute-start(f32[2,2,2,2,8,1152]{5,4,3,2,1,0:T(8,128)S(1)} %dynamic-slice_bitcast_fusion.1), channel_id=1, source_target_pairs={{0,8},{1,9},{2,10},{3,11},{4,12},{5,13},{6,14},{7,15},{8,0},{9,1},... | collective-permute-start | bytes 1769480 | tf_op jit(solution)/shard_map/ppermute | solution.py:238
  131.6 19.0 %copy-start.2 = (f32[1,256,1152]{2,1,0:T(8,128)S(1)}, f32[1,256,1152]{2,1,0:T(8,128)}, u32[]{:S(2)}) copy-start(f32[1,256,1152]{2,1,0:T(8,128)} %get-tuple-element.20) | copy-start | bytes 3538948
  148.8 3.5 %copy-start.3 = (f32[1,256,1152]{2,1,0:T(8,128)S(1)}, f32[1,256,1152]{2,1,0:T(8,128)}, u32[]{:S(2)}) copy-start(f32[1,256,1152]{2,1,0:T(8,128)} %get-tuple-element.21) | copy-start | bytes 3538948
  150.0 2.3 %collective-permute-start.6 = (f32[2,2,2,2,8,1152]{5,4,3,2,1,0:T(8,128)S(1)}, f32[2,2,2,2,8,1152]{5,4,3,2,1,0:T(8,128)S(1)}, u32[]{:S(2)}, u32[]{:S(2)}) collective-permute-start(f32[2,2,2,2,8,1152]{5,4,3,2,1,0:T(8,128)S(1)} %dynamic-slice_bitcast_fusion), channel_id=1, source_target_pairs={{0,8},{1,9},{2,10},{3,11},{4,12},{5,13},{6,14},{7,15},{8,0},{9,1},... | collective-permute-start | bytes 1769480 | tf_op jit(solution)/shard_map/ppermute | solution.py:238
  150.7 9.0 %collective-permute-start.2 = (f32[2,2,2,8,1152]{4,3,2,1,0:T(8,128)S(1)}, f32[2,2,2,8,1152]{4,3,2,1,0:T(8,128)S(1)}, u32[]{:S(2)}, u32[]{:S(2)}) collective-permute-start(f32[2,2,2,8,1152]{4,3,2,1,0:T(8,128)S(1)} %dynamic-slice_bitcast_fusion.3), channel_id=1, source_target_pairs={{0,16},{1,17},{2,18},{3,19},{4,20},{5,21},{6,22},{7,23},{8,24},{9,... | collective-permute-start | bytes 884744 | tf_op jit(solution)/shard_map/ppermute | solution.py:238
  152.4 9.3 %collective-permute-start.7 = (f32[2,2,2,8,1152]{4,3,2,1,0:T(8,128)S(1)}, f32[2,2,2,8,1152]{4,3,2,1,0:T(8,128)S(1)}, u32[]{:S(2)}, u32[]{:S(2)}) collective-permute-start(f32[2,2,2,8,1152]{4,3,2,1,0:T(8,128)S(1)} %dynamic-slice_bitcast_fusion.2), channel_id=1, source_target_pairs={{0,1},{1,0},{2,3},{3,2},{4,5},{5,4},{6,7},{7,6},{8,9},{9,8},{10,11... | collective-permute-start | bytes 884744 | tf_op jit(solution)/shard_map/ppermute | solution.py:238
  159.8 5.2 %collective-permute-start.3 = (f32[2,2,8,1152]{3,2,1,0:T(8,128)S(1)}, f32[2,2,8,1152]{3,2,1,0:T(8,128)S(1)}, u32[]{:S(2)}, u32[]{:S(2)}) collective-permute-start(f32[2,2,8,1152]{3,2,1,0:T(8,128)S(1)} %dynamic-slice_bitcast_fusion.5), channel_id=1, source_target_pairs={{0,1},{1,0},{2,3},{3,2},{4,5},{5,4},{6,7},{7,6},{8,9},{9,8},{10,11... | collective-permute-start | bytes 442376 | tf_op jit(solution)/shard_map/ppermute | solution.py:238
  161.7 5.3 %collective-permute-start.8 = (f32[2,2,8,1152]{3,2,1,0:T(8,128)S(1)}, f32[2,2,8,1152]{3,2,1,0:T(8,128)S(1)}, u32[]{:S(2)}, u32[]{:S(2)}) collective-permute-start(f32[2,2,8,1152]{3,2,1,0:T(8,128)S(1)} %dynamic-slice_bitcast_fusion.4), channel_id=1, source_target_pairs={{0,16},{1,17},{2,18},{3,19},{4,20},{5,21},{6,22},{7,23},{8,24},{9,... | collective-permute-start | bytes 442376 | tf_op jit(solution)/shard_map/ppermute | solution.py:238
  165.0 4.9 %collective-permute-start.4 = (f32[2,8,1152]{2,1,0:T(8,128)S(1)}, f32[2,8,1152]{2,1,0:T(8,128)S(1)}, u32[]{:S(2)}, u32[]{:S(2)}) collective-permute-start(f32[2,8,1152]{2,1,0:T(8,128)S(1)} %dynamic-slice_bitcast_fusion.7), channel_id=1, source_target_pairs={{0,2},{1,3},{2,0},{3,1},{4,6},{5,7},{6,4},{7,5},{8,10},{9,11},{10,... | collective-permute-start | bytes 221192 | tf_op jit(solution)/shard_map/ppermute | solution.py:238
  167.1 4.5 %collective-permute-start.9 = (f32[2,8,1152]{2,1,0:T(8,128)S(1)}, f32[2,8,1152]{2,1,0:T(8,128)S(1)}, u32[]{:S(2)}, u32[]{:S(2)}) collective-permute-start(f32[2,8,1152]{2,1,0:T(8,128)S(1)} %dynamic-slice_bitcast_fusion.6), channel_id=1, source_target_pairs={{0,2},{1,3},{2,0},{3,1},{4,6},{5,7},{6,4},{7,5},{8,10},{9,11},{10,... | collective-permute-start | bytes 221192 | tf_op jit(solution)/shard_map/ppermute | solution.py:238
  169.9 5.0 %collective-permute-start.5 = (f32[8,1152]{1,0:T(8,128)S(1)}, f32[8,1152]{1,0:T(8,128)S(1)}, u32[]{:S(2)}, u32[]{:S(2)}) collective-permute-start(f32[8,1152]{1,0:T(8,128)S(1)} %dynamic-slice_bitcast_fusion.9), channel_id=1, source_target_pairs={{0,4},{1,5},{2,6},{3,7},{4,0},{5,1},{6,2},{7,3},{8,12},{9,13},{10,... | collective-permute-start | bytes 110600 | tf_op jit(solution)/shard_map/ppermute | solution.py:238
  171.6 5.3 %collective-permute-start.10 = (f32[8,1152]{1,0:T(8,128)S(1)}, f32[8,1152]{1,0:T(8,128)S(1)}, u32[]{:S(2)}, u32[]{:S(2)}) collective-permute-start(f32[8,1152]{1,0:T(8,128)S(1)} %dynamic-slice_bitcast_fusion.8), channel_id=1, source_target_pairs={{0,4},{1,5},{2,6},{3,7},{4,0},{5,1},{6,2},{7,3},{8,12},{9,13},{10,... | collective-permute-start | bytes 110600 | tf_op jit(solution)/shard_map/ppermute | solution.py:238
